TPU v7x, 32 devices: a whole 2x2x4 slice. The times are simulated.
32 devices in a mesh: ctx: 4 (over y, x), pair: 4 (over z), dp: 2 (over core).
Axes of the slice: x: 2, y: 2, z: 4, core: 2. Of those that a mesh axis runs over, the one named last changes fastest.
Arguments:
- queries: bfloat16 [8, 4, 128, 2048], P(('dp', 'ctx'), 'pair'), parts along dimension 0, may hold values from -8 to 8
- resp_keys: bfloat16 [8, 4, 128, 1024], P(('dp', 'ctx'), 'pair'), parts along dimension 0, may hold values from -6 to 6
- resp_values: bfloat16 [8, 4, 128, 1024], P(('dp', 'ctx'), 'pair'), parts along dimension 0, may hold values from -6 to 6
- d_out: bfloat16 [8, 4, 128, 2048], P(('dp', 'ctx'), 'pair'), parts along dimension 0, may hold values from -6 to 6
- prefix_kv: bfloat16 [4, 512, 2, 1024], P('dp', 'ctx', None, 'pair'), parts along dimension 0, may hold values from -8 to 8
- prefix_blocks: int32 [8, 4, 4], P(('dp', 'ctx'), 'pair'), parts along dimension 0, may hold values 0 or 1
- resp_lengths: int32 [8, 4], P(('dp', 'ctx'), 'pair'), parts along dimension 0, may hold values from 32 to 128, as said below
- pair_prompt: int32 [8], P('dp'), parts along dimension 0, may hold values from 0 to 1, as said below
Outputs:
- d_queries: bfloat16 [8, 4, 128, 2048], P(('dp', 'ctx'), 'pair'), parts along dimension 0
- d_resp_keys: bfloat16 [8, 4, 128, 1024], P(('dp', 'ctx'), 'pair'), parts along dimension 0
- d_resp_values: bfloat16 [8, 4, 128, 1024], P(('dp', 'ctx'), 'pair'), parts along dimension 0
- d_prefix: float32 [4, 512, 2, 1024], P('dp', 'ctx', None, 'pair'), parts along dimension 0
There are 2 independent parts, one for each index of `dp`. A program takes and returns all parts, laid end to end along the dimension named above; each array names one. Nothing has to cross between parts.
Inputs may be any that keep to these rules, and one draw needn't show every extreme that they name: `pair_prompt`: each prompt is answered by exactly two indices of pair, one chosen and one rejected response. `resp_lengths`: some response fills all 128 slots.
All inputs are finite; a program needn't handle non-finite values. No bound on the sum of `prefix_blocks` on one device may be relied on, other than what follows from the above.
Results may differ from a plain program's by a relative error of at most 0.012.
The roundings to bfloat16 on the way count: a program that leaves them out, or rounds other values in their place, can miss the bound.
Values may be sent and summed in bfloat16 or wider, within the bound.
No kernel may reach another device: no remote copies, remote signals or barrier semaphores. Data moves between devices by JAX's collectives and lax.ppermute only.
A program may use at most 128 MiB of HBM per device.

v0:
```python
import jax
import jax.numpy as jnp
from jax import lax
from jax.sharding import PartitionSpec as P

KV_HEADS = 8
GROUP = 2
HEAD_DIM = 128
BLOCK = 128


scale_factor = 144.0 ** (-0.5)
neg_big = -1e30


def gather_rows(kv_part):
    return lax.all_gather(kv_part, "ctx", axis=1, tiled=True)


def pick_prompt(kv_part, pair_prompt):
    outgoing = jnp.take(kv_part, pair_prompt, axis=0)
    return lax.all_to_all(outgoing, "pair", split_axis=0, concat_axis=3, tiled=True)


def shards(
    queries, resp_keys, resp_values, d_out, prefix_kv, prefix_blocks, resp_lengths, pair_prompt
):
    prefix_panel = gather_rows(pick_prompt(prefix_kv, pair_prompt))
    prefix_panel = prefix_panel[0]
    resp_rows = queries.shape[2]
    pre_rows = prefix_panel.shape[0]
    n_prompts = prefix_kv.shape[0]
    all_rows = pre_rows + resp_rows
    keys_heads = jnp.transpose(
        jnp.concatenate([prefix_panel[:, 0], resp_keys[0, 0]], 0).reshape(
            all_rows, KV_HEADS, HEAD_DIM
        ),
        (1, 0, 2),
    )
    values_heads = jnp.transpose(
        jnp.concatenate([prefix_panel[:, 1], resp_values[0, 0]], 0).reshape(
            all_rows, KV_HEADS, HEAD_DIM
        ),
        (1, 0, 2),
    )
    query_heads = jnp.transpose(
        queries[0, 0].reshape(resp_rows, KV_HEADS, GROUP, HEAD_DIM), (1, 2, 0, 3)
    )
    positions = jnp.arange(resp_rows, dtype=jnp.int32)
    live_rows = positions < resp_lengths[0, 0]
    grad_rows = jnp.where(live_rows[:, None], d_out[0, 0], jnp.zeros_like(d_out[0, 0]))
    grad_heads = jnp.transpose(
        grad_rows.reshape(resp_rows, KV_HEADS, GROUP, HEAD_DIM), (1, 2, 0, 3)
    )
    visible = prefix_blocks[0, 0] > 0
    prefix_mask = jnp.broadcast_to(visible[:, None], (pre_rows // BLOCK, BLOCK)).reshape(pre_rows)
    causal = positions[:, None] >= positions[None, :]
    allowed = jnp.concatenate(
        [jnp.broadcast_to(prefix_mask[None, :], (resp_rows, pre_rows)), causal], 1
    )

    def one_head(items):
        key_rows, value_rows, query_rows, grad_part = items
        scores = (
            jnp.einsum("jqd,kd->jqk", query_rows, key_rows, preferred_element_type=jnp.float32)
            * scale_factor
        )
        scores = jnp.where(allowed[None], scores, neg_big)
        row_peak = jnp.max(scores, axis=-1, keepdims=True)
        raised = jnp.exp(scores - row_peak)
        weights = raised / jnp.sum(raised, axis=-1, keepdims=True)
        probs_low = weights.astype(jnp.bfloat16)
        attended = jnp.einsum(
            "jqk,kd->jqd", probs_low, value_rows, preferred_element_type=jnp.float32
        )
        attended = lax.optimization_barrier(attended.astype(jnp.bfloat16)).astype(jnp.float32)
        row_delta = jnp.sum(grad_part.astype(jnp.float32) * attended, axis=-1)
        d_probs = jnp.einsum(
            "jqd,kd->jqk", grad_part, value_rows, preferred_element_type=jnp.float32
        )
        ds_low = (weights * (d_probs - row_delta[..., None])).astype(jnp.bfloat16)
        query_grad = (
            jnp.einsum("jqk,kd->jqd", ds_low, key_rows, preferred_element_type=jnp.float32)
            * scale_factor
        )
        key_grad = (
            jnp.einsum("jqk,jqd->kd", ds_low, query_rows, preferred_element_type=jnp.float32)
            * scale_factor
        )
        value_grad = jnp.einsum(
            "jqk,jqd->kd", probs_low, grad_part, preferred_element_type=jnp.float32
        )
        both_grads = jnp.stack([key_grad, value_grad], 1).astype(jnp.bfloat16)
        return (query_grad.astype(jnp.bfloat16), both_grads)

    query_grads, kv_grads = lax.map(one_head, (keys_heads, values_heads, query_heads, grad_heads))
    d_queries = jnp.transpose(query_grads, (2, 0, 1, 3)).reshape(1, 1, resp_rows, -1)
    own_grads = jnp.transpose(kv_grads[:, pre_rows:], (1, 2, 0, 3)).reshape(resp_rows, 2, -1)
    d_resp_keys = own_grads[:, 0].reshape(1, 1, resp_rows, -1)
    d_resp_values = own_grads[:, 1].reshape(1, 1, resp_rows, -1)
    prefix_part = jnp.transpose(kv_grads[:, :pre_rows], (1, 2, 0, 3)).reshape(1, pre_rows, 2, -1)
    pieces = lax.all_to_all(prefix_part, "ctx", split_axis=1, concat_axis=0, tiled=True)
    ctx_total = jnp.sum(pieces.astype(jnp.float32), axis=0).astype(jnp.bfloat16)
    arrived = lax.all_to_all(ctx_total[None], "pair", split_axis=3, concat_axis=0, tiled=True)
    prompt_hits = (pair_prompt[:, None] == jnp.arange(n_prompts, dtype=jnp.int32)[None, :]).astype(
        jnp.float32
    )
    d_prefix = jnp.sum(
        prompt_hits[:, :, None, None, None] * arrived.astype(jnp.float32)[:, None], axis=0
    )
    return (d_queries, d_resp_keys, d_resp_values, d_prefix)


def solution(mesh):
    placed = (
        P(("dp", "ctx"), "pair", None, None),
        P(("dp", "ctx"), "pair", None, None),
        P(("dp", "ctx"), "pair", None, None),
        P(("dp", "ctx"), "pair", None, None),
        P("dp", "ctx", None, "pair"),
        P(("dp", "ctx"), "pair", None),
        P(("dp", "ctx"), "pair"),
        P("dp"),
    )
    return jax.shard_map(
        shards,
        mesh=mesh,
        in_specs=placed,
        out_specs=(
            P(("dp", "ctx"), "pair", None, None),
            P(("dp", "ctx"), "pair", None, None),
            P(("dp", "ctx"), "pair", None, None),
            P("dp", "ctx", None, "pair"),
        ),
        check_vma=False,
    )
```

profile of v0, /device:TPU:0, one launch (start us, length us, event | category | flops | bytes accessed | tf_op | source)
XLA Modules:
  0.0 192.6 jit_solution(804473975615161115)
XLA Ops:
  8.6 1.6 gather_fusion
  10.8 20.7 %all_to_all.39 = bf16[4,128,2,256]{3,2,1,0:T(2,128)(2,1)S(1)} all-to-all(bf16[4,128,2,256]{3,2,1,0:T(2,128)(2,1)S(1)} %broadcast_select_fusion), channel_id=1, replica_groups=mesh['ctx'=4,'pair'=4,'dp'=2] {'pair'}, dimensions={0} | all-to-all | bytes 1048576 | tf_op jit(solution)/shard_map/all_to_all | solution.py:22
  35.3 31.8 %all-gather.2.cloned.1.call-done = bf16[1,512,2,1024]{1,3,2,0:T(8,128)(2,1)} async-done(((bf16[1,128,2,1024]{1,3,2,0:T(8,128)(2,1)}), bf16[1,512,2,1024]{1,3,2,0:T(8,128)(2,1)}) %all-gather.2.cloned.1.call-update) | async-done | bytes 2097168 | tf_op jit(solution)/shard_map/all_gather | solution.py:17
  67.1 1.7 fusion.55
  70.1 50.9 %while.12 = (s32[]{:T(128)}, bf16[8,2,128,128]{3,2,1,0:T(8,128)(2,1)}, bf16[8,640,2,128]{3,1,2,0:T(8,128)(2,1)}, pred[128,640]{1,0:T(8,128)(4,1)S(1)}, bf16[8,2,...) while((s32[]{:T(128)}, ...), condition=%wide.region_4.5_spmd, body=%wide.region_0.4_spmd.sunk | while | flops 254427520 | bytes 6446201 | solution.py:96
  70.1 1.4 fusion.90
  73.3 1.8 fusion.93
  76.4 1.4 fusion.90
  79.6 1.8 fusion.93
  86.0 1.8 fusion.93
  89.1 1.4 fusion.90
  92.4 1.8 fusion.93
  98.7 1.8 fusion.93
  105.1 1.8 fusion.93
  111.4 1.8 fusion.93
  117.8 1.8 fusion.93
  121.0 3.2 %copy.93 = bf16[8,640,2,128]{1,3,0,2:T(8,128)(2,1)S(1)} copy(bf16[8,640,2,128]{3,1,2,0:T(8,128)(2,1)} %get-tuple-element.48) | data formatting | bytes 5242880 | tf_op jit(solution)/shard_map/while | solution.py:96
  124.1 1.5 slice.30
  125.7 6.2 %copy.94 = bf16[1,512,2,1024]{3,2,0,1:T(2,128)(2,1)} copy(bf16[1,512,2,1024]{1,3,2,0:T(8,128)(2,1)} %bitcast.153) | data formatting | bytes 4194304 | tf_op jit(solution)/shard_map/reshape | solution.py:101
  131.9 29.2 %all_to_all.40 = bf16[1,512,2,1024]{3,2,0,1:T(2,128)(2,1)S(1)} all-to-all(bf16[1,512,2,1024]{3,2,0,1:T(2,128)(2,1)} %copy.94), channel_id=1, replica_groups=mesh['ctx'=4,'pair'=4,'dp'=2] {'ctx'}, dimensions={1} | all-to-all | bytes 4194304 | tf_op jit(solution)/shard_map/all_to_all | solution.py:102
  161.1 3.1 %reduce_sum.39 = bf16[128,2,1024]{2,1,0:T(2,128)(2,1)S(1)} reduce(bf16[4,128,2,1024]{3,2,1,0:T(2,128)(2,1)S(1)} %bitcast.152, bf16[]{:T(256)} %constant.29.clone.1), dimensions={0}, to_apply=%region_5.6 | reduce | flops 786432 | bytes 2621442 | tf_op jit(solution)/shard_map/reduce_sum | solution.py:103
  164.2 1.9 copy.95
  166.1 4.6 %all-to-all-start.2 = ((bf16[1,128,2,1024]{1,2,0,3:T(2,128)(2,1)}), bf16[1,128,2,1024]{1,2,0,3:T(2,128)(2,1)S(1)}, u32[]{:S(2)}, u32[]{:S(2)}) async-start(bf16[1,128,2,1024]{1,2,0,3:T(2,128)(2,1)} %copy.95), calls=%async_computation.2 | async-start | bytes 1048576 | tf_op jit(solution)/shard_map/all_to_all | solution.py:104
  174.5 9.3 %all-to-all-done.2 = bf16[1,128,2,1024]{1,2,0,3:T(2,128)(2,1)S(1)} async-done(((bf16[1,128,2,1024]{1,2,0,3:T(2,128)(2,1)}), bf16[1,128,2,1024]{1,2,0,3:T(2,128)(2,1)S(1)}, u32[]{:S(2)}, u32[]{:S(2)}) %all-to-all-start.2) | async-done | bytes 524320 | tf_op jit(solution)/shard_map/all_to_all | solution.py:104
  (124 shorter events, 43.8 us)
Async XLA Ops:
  7.2 1.4 copy-start
  7.2 59.9 %all-gather.2.cloned.1.call-start = ((), (), s32[]{:S(2)}) async-start(), calls=%async_computation.3 | async-start | bytes 2621440 | tf_op jit(solution)/shard_map/all_gather | solution.py:17
  10.2 22.4 %copy-start.1 = (bf16[1,1,128,2048]{3,2,1,0:T(8,128)(2,1)S(1)}, bf16[1,1,128,2048]{3,2,1,0:T(8,128)(2,1)}, u32[]{:S(2)}) copy-start(bf16[1,1,128,2048]{3,2,1,0:T(8,128)(2,1)} %param.10) | copy-start | bytes 1572868
  10.7 22.2 %copy-start.4 = (bf16[1,1,128,1024]{3,2,1,0:T(8,128)(2,1)S(1)}, bf16[1,1,128,1024]{3,2,1,0:T(8,128)(2,1)}, u32[]{:S(2)}) copy-start(bf16[1,1,128,1024]{3,2,1,0:T(8,128)(2,1)} %param.11) | copy-start | bytes 786436
  10.8 22.4 %copy-start.5 = (bf16[1,1,128,1024]{3,2,1,0:T(8,128)(2,1)S(1)}, bf16[1,1,128,1024]{3,2,1,0:T(8,128)(2,1)}, u32[]{:S(2)}) copy-start(bf16[1,1,128,1024]{3,2,1,0:T(8,128)(2,1)} %param.12) | copy-start | bytes 786436
  31.5 1.8 copy-start.2
  32.6 1.6 copy-start.7
  161.1 9.6 %copy-start.6 = (s32[4]{0:T(128)S(1)}, s32[4]{0:T(128)}, u32[]{:S(2)}) copy-start(s32[4]{0:T(128)} %param.17) | copy-start | bytes 52
  161.1 9.7 %copy-start.3 = (bf16[8,2,128,128]{3,2,1,0:T(8,128)(2,1)S(1)}, bf16[8,2,128,128]{3,2,1,0:T(8,128)(2,1)}, u32[]{:S(2)}) copy-start(bf16[8,2,128,128]{3,2,1,0:T(8,128)(2,1)} %get-tuple-element.47) | copy-start | bytes 1572868
  166.1 17.7 %all-to-all-start.2 = ((bf16[1,128,2,1024]{1,2,0,3:T(2,128)(2,1)}), bf16[1,128,2,1024]{1,2,0,3:T(2,128)(2,1)S(1)}, u32[]{:S(2)}, u32[]{:S(2)}) async-start(bf16[1,128,2,1024]{1,2,0,3:T(2,128)(2,1)} %copy.95), calls=%async_computation.2 | async-start | bytes 1048576 | tf_op jit(solution)/shard_map/all_to_all | solution.py:104
Sparse Core Ops, SparseCore 0:
  32.7 34.2 all-gather.1
where the time goes:
time: 194 us; the launch traced here: 193 us
  blocking collectives  50 us (26%)
  waiting for transfers between devices  41.1 us (21%)
  matrix products  34.8 us (18%)
  local copies, waits for them, and re-layouts  31.2 us (16%)
  other arithmetic  15.5 us (8%)
  between operations  14.9 us (8%)
  starting transfers between devices  4.64 us (2%)
    all_gather x1, waiting for transfers between devices, gather_rows(): return lax.all_gather(kv_part, 'ctx', axis=1, tiled=True)  31.8 us
    all_to_all x1, blocking collectives, shards(): lax.all_to_all(prefix_part, 'ctx', split_axis=1, concat_axis=0, tiled=True)  29.2 us
    all_to_all x1, blocking collectives, pick_prompt(): lax.all_to_all(outgoing, 'pair', split_axis=0, concat_axis=3, tiled=True)  20.7 us
    dot_general x8, matrix products, one_head(): jnp.einsum('jqk,kd->jqd', ds_low, key_rows, preferred_element_type=jnp.fl...  14.4 us
    sub x8, matrix products, one_head(): raised = jnp.exp(scores - row_peak)  11.3 us
    all_to_all x1, waiting for transfers between devices, shards(): lax.all_to_all(ctx_total[None], 'pair', split_axis=3, concat_axis=0, tile...  9.32 us
    dynamic_slice x16, local copies, waits for them, and re-layouts, shards(): lax.map(one_head, (keys_heads, values_heads, query_heads, grad_heads))  7.76 us
    reshape x1, local copies, waits for them, and re-layouts, shards(): jnp.transpose(kv_grads[:, :pre_rows], (1, 2, 0, 3))  6.24 us
  transfers between devices with their start and end apart: 2, of which 2 were waited for; matrix products, arithmetic and copies ran while one was open for 3% of the time, Pallas kernels for 0%

commit v1 on v0

v1 whole, which is shorter than its diff:
```python
import functools

import jax
import jax.numpy as jnp
from jax import lax
from jax.experimental import pallas as pl
from jax.experimental.pallas import tpu as pltpu
from jax.sharding import PartitionSpec as P

KV_HEADS = 8
GROUP = 2
HEAD_DIM = 128
BLOCK = 128


scale_factor = 144.0 ** (-0.5)
neg_big = -1e30

NT = (((1,), (1,)), ((), ()))
TN = (((0,), (0,)), ((), ()))


def attention_grad_kernel(blocks_ref, length_ref, q_ref, do_ref, kp_ref, vp_ref, kr_ref, vr_ref,
                          dq_ref, dkr_ref, dvr_ref, dpre_ref):
    resp_rows = q_ref.shape[0]
    pre_rows = kp_ref.shape[0]
    n_blocks = pre_rows // BLOCK
    kp = kp_ref[...]
    vp = vp_ref[...]
    kr = kr_ref[...]
    vr = vr_ref[...]

    col_block = lax.broadcasted_iota(jnp.int32, (1, pre_rows), 1) // BLOCK
    flag = jnp.zeros((1, pre_rows), jnp.int32)
    for b in range(n_blocks):
        flag = jnp.where(col_block == b, blocks_ref[b], flag)
    pre_ok = flag > 0
    row_i = lax.broadcasted_iota(jnp.int32, (resp_rows, resp_rows), 0)
    col_i = lax.broadcasted_iota(jnp.int32, (resp_rows, resp_rows), 1)
    causal = row_i >= col_i
    live = lax.broadcasted_iota(jnp.int32, (resp_rows, 1), 0) < length_ref[0]

    dkp = jnp.zeros((pre_rows, HEAD_DIM), jnp.float32)
    dvp = jnp.zeros((pre_rows, HEAD_DIM), jnp.float32)
    dkr = jnp.zeros((resp_rows, HEAD_DIM), jnp.float32)
    dvr = jnp.zeros((resp_rows, HEAD_DIM), jnp.float32)
    for j in range(GROUP):
        cols = slice(j * HEAD_DIM, (j + 1) * HEAD_DIM)
        qj = q_ref[:, cols]
        doj = jnp.where(live, do_ref[:, cols], jnp.zeros_like(do_ref[:, cols]))
        sp = lax.dot_general(qj, kp, NT, preferred_element_type=jnp.float32) * scale_factor
        sr = lax.dot_general(qj, kr, NT, preferred_element_type=jnp.float32) * scale_factor
        sp = jnp.where(pre_ok, sp, neg_big)
        sr = jnp.where(causal, sr, neg_big)
        peak = jnp.maximum(jnp.max(sp, axis=-1, keepdims=True), jnp.max(sr, axis=-1, keepdims=True))
        ep = jnp.exp(sp - peak)
        er = jnp.exp(sr - peak)
        total = jnp.sum(ep, axis=-1, keepdims=True) + jnp.sum(er, axis=-1, keepdims=True)
        wp = ep / total
        wr = er / total
        pp = wp.astype(jnp.bfloat16)
        pr = wr.astype(jnp.bfloat16)
        att = jnp.dot(pp, vp, preferred_element_type=jnp.float32) + jnp.dot(
            pr, vr, preferred_element_type=jnp.float32)
        att = att.astype(jnp.bfloat16).astype(jnp.float32)
        delta = jnp.sum(doj.astype(jnp.float32) * att, axis=-1, keepdims=True)
        dpp = lax.dot_general(doj, vp, NT, preferred_element_type=jnp.float32)
        dpr = lax.dot_general(doj, vr, NT, preferred_element_type=jnp.float32)
        dsp = (wp * (dpp - delta)).astype(jnp.bfloat16)
        dsr = (wr * (dpr - delta)).astype(jnp.bfloat16)
        dq = (jnp.dot(dsp, kp, preferred_element_type=jnp.float32) + jnp.dot(
            dsr, kr, preferred_element_type=jnp.float32)) * scale_factor
        dq_ref[:, cols] = dq.astype(dq_ref.dtype)
        dkp = dkp + lax.dot_general(dsp, qj, TN, preferred_element_type=jnp.float32)
        dkr = dkr + lax.dot_general(dsr, qj, TN, preferred_element_type=jnp.float32)
        dvp = dvp + lax.dot_general(pp, doj, TN, preferred_element_type=jnp.float32)
        dvr = dvr + lax.dot_general(pr, doj, TN, preferred_element_type=jnp.float32)
    dkr_ref[...] = (dkr * scale_factor).astype(dkr_ref.dtype)
    dvr_ref[...] = dvr.astype(dvr_ref.dtype)
    dpre_ref[0] = (dkp * scale_factor).astype(dpre_ref.dtype)
    dpre_ref[1] = dvp.astype(dpre_ref.dtype)


def attention_grads(blocks, length, q, do, kp, vp, kr, vr):
    resp_rows, q_width = q.shape
    pre_rows, kv_width = kp.shape
    heads = kv_width // HEAD_DIM
    qspec = pl.BlockSpec((resp_rows, GROUP * HEAD_DIM), lambda g, b, n: (0, g))
    pspec = pl.BlockSpec((pre_rows, HEAD_DIM), lambda g, b, n: (0, g))
    rspec = pl.BlockSpec((resp_rows, HEAD_DIM), lambda g, b, n: (0, g))
    flops = 2 * 6 * resp_rows * GROUP * heads * (pre_rows + resp_rows) * HEAD_DIM
    return pl.pallas_call(
        attention_grad_kernel,
        out_shape=(
            jax.ShapeDtypeStruct((resp_rows, q_width), jnp.bfloat16),
            jax.ShapeDtypeStruct((resp_rows, kv_width), jnp.bfloat16),
            jax.ShapeDtypeStruct((resp_rows, kv_width), jnp.bfloat16),
            jax.ShapeDtypeStruct((2, pre_rows, kv_width), jnp.bfloat16),
        ),
        grid_spec=pltpu.PrefetchScalarGridSpec(
            num_scalar_prefetch=2,
            grid=(heads,),
            in_specs=[qspec, qspec, pspec, pspec, rspec, rspec],
            out_specs=[qspec, rspec, rspec,
                       pl.BlockSpec((2, pre_rows, HEAD_DIM), lambda g, b, n: (0, 0, g))],
        ),
        cost_estimate=pl.CostEstimate(
            flops=flops,
            transcendentals=resp_rows * GROUP * heads * (pre_rows + resp_rows),
            bytes_accessed=2 * (2 * resp_rows * q_width + 4 * pre_rows * kv_width + 4 * resp_rows * kv_width),
        ),
    )(blocks, length, q, do, kp, vp, kr, vr)


def shards(
    queries, resp_keys, resp_values, d_out, prefix_kv, prefix_blocks, resp_lengths, pair_prompt
):
    n_prompts = prefix_kv.shape[0]
    kv_planes = jnp.transpose(prefix_kv, (0, 2, 1, 3))
    outgoing = jnp.take(kv_planes, pair_prompt, axis=0)
    mine = lax.all_to_all(outgoing, "pair", split_axis=0, concat_axis=3, tiled=True)
    panel = lax.all_gather(mine, "ctx", axis=2, tiled=True)[0]
    kp = panel[0]
    vp = panel[1]
    pre_rows = kp.shape[0]

    dq, dkr, dvr, dpre = attention_grads(
        prefix_blocks[0, 0], resp_lengths[0, 0].reshape(1), queries[0, 0], d_out[0, 0],
        kp, vp, resp_keys[0, 0], resp_values[0, 0])
    d_queries = dq[None, None]
    d_resp_keys = dkr[None, None]
    d_resp_values = dvr[None, None]

    n_ctx = lax.axis_size("ctx")
    n_pair = lax.axis_size("pair")
    kv_width = dpre.shape[-1]
    pieces = dpre.reshape(2, n_ctx, pre_rows // n_ctx, kv_width)
    pieces = lax.all_to_all(pieces, "ctx", split_axis=1, concat_axis=1, tiled=True)
    ctx_total = jnp.sum(pieces.astype(jnp.float32), axis=1).astype(jnp.bfloat16)
    ctx_total = ctx_total.reshape(2, pre_rows // n_ctx, n_pair, kv_width // n_pair)
    arrived = lax.all_to_all(ctx_total, "pair", split_axis=2, concat_axis=2, tiled=True)
    prompt_hits = (pair_prompt[:, None] == jnp.arange(n_prompts, dtype=jnp.int32)[None, :]).astype(
        jnp.float32
    )
    arrived = jnp.transpose(arrived.astype(jnp.float32), (2, 1, 0, 3))
    d_prefix = jnp.sum(prompt_hits[:, :, None, None, None] * arrived[:, None], axis=0)
    return (d_queries, d_resp_keys, d_resp_values, d_prefix)


def solution(mesh):
    placed = (
        P(("dp", "ctx"), "pair", None, None),
        P(("dp", "ctx"), "pair", None, None),
        P(("dp", "ctx"), "pair", None, None),
        P(("dp", "ctx"), "pair", None, None),
        P("dp", "ctx", None, "pair"),
        P(("dp", "ctx"), "pair", None),
        P(("dp", "ctx"), "pair"),
        P("dp"),
    )
    return jax.shard_map(
        shards,
        mesh=mesh,
        in_specs=placed,
        out_specs=(
            P(("dp", "ctx"), "pair", None, None),
            P(("dp", "ctx"), "pair", None, None),
            P(("dp", "ctx"), "pair", None, None),
            P("dp", "ctx", None, "pair"),
        ),
        check_vma=False,
    )
```

time: 194 us -> 145 us (0.75)
  matrix products: 34.8 us -> 0 us
  local copies, waits for them, and re-layouts: 31.2 us -> 10.6 us
  Pallas kernels: 0 us -> 16 us
  other arithmetic: 15.5 us -> 2.67 us
  waiting for transfers between devices: 41.1 us -> 46.9 us
    dot_general x40 -> x0, matrix products: 23.5 us -> none  [the longest x8 14.4 us: one_head(): jnp.einsum('jqk,kd->jqd', ds_low, key_rows, preferred_element_type=jnp.fl...]
    pallas_call x0 -> x1, Pallas kernels: none -> 16 us  [attention_grads(): pl.pallas_call(attention_grad_kernel, out_shape=(jax.ShapeDtypeStruct((re...]
    sub x8 -> x0, matrix products: 11.3 us -> none  [one_head(): raised = jnp.exp(scores - row_peak)]
    dynamic_slice x16 -> x0, local copies, waits for them, and re-layouts: 7.76 us -> none  [shards(): lax.map(one_head, (keys_heads, values_heads, query_heads, grad_heads))]
    dynamic_update_slice x8 -> x0, other arithmetic: 6.05 us -> none  [shards(): lax.map(one_head, (keys_heads, values_heads, query_heads, grad_heads))]
    reshape x3 -> x2, local copies, waits for them, and re-layouts: 8.54 us -> 2.6 us  [the longest x1 1.76 us: shards(): pieces = dpre.reshape(2, n_ctx, pre_rows // n_ctx, kv_width)]
    reduce_sum x10 -> x2, other arithmetic: 4.25 us -> 0.65 us  [the longest x1 0.42 us: shards(): ctx_total = jnp.sum(pieces.astype(jnp.float32), axis=1).astype(jnp.bfloat16)]
    all_to_all x1, waiting for transfers between devices: 9.32 us -> 12.9 us  [shards(): lax.all_to_all(ctx_total, 'pair', split_axis=2, concat_axis=2, tiled=True)]
  transfers between devices with their start and end apart: 2 -> 2, of which waited for: 2 -> 2; matrix products, arithmetic and copies ran while one was open for 3% -> 0% of each run, Pallas kernels for 0% -> 0%
where the time goes in v1:
time: 145 us; the launch traced here: 144 us
  blocking collectives  48.7 us (34%)
  waiting for transfers between devices  46.9 us (32%)
  Pallas kernels  16 us (11%)
  between operations  14.8 us (10%)
  local copies, waits for them, and re-layouts  10.6 us (7%)
  starting transfers between devices  4.63 us (3%)
  other arithmetic  2.67 us (2%)
    all_gather x1, waiting for transfers between devices, shards(): panel = lax.all_gather(mine, 'ctx', axis=2, tiled=True)[0]  33.9 us
    all_to_all x1, blocking collectives, shards(): lax.all_to_all(pieces, 'ctx', split_axis=1, concat_axis=1, tiled=True)  28.1 us
    all_to_all x1, blocking collectives, shards(): lax.all_to_all(outgoing, 'pair', split_axis=0, concat_axis=3, tiled=True)  20.6 us
    pallas_call x1, Pallas kernels, attention_grads(): pl.pallas_call(attention_grad_kernel, out_shape=(jax.ShapeDtypeStruct((re...  16 us
    all_to_all x1, waiting for transfers between devices, shards(): lax.all_to_all(ctx_total, 'pair', split_axis=2, concat_axis=2, tiled=True)  12.9 us
    all_to_all x1, starting transfers between devices, shards(): lax.all_to_all(ctx_total, 'pair', split_axis=2, concat_axis=2, tiled=True)  4.6 us
    squeeze x1, local copies, waits for them, and re-layouts, shards(): vp = panel[1]  3.02 us
  transfers between devices with their start and end apart: 2, of which 2 were waited for; matrix products, arithmetic and copies ran while one was open for 0% of the time, Pallas kernels for 0%

profile of v1, /device:TPU:0, one launch (start us, length us, event | category | flops | bytes accessed | tf_op | source)
XLA Modules:
  0.0 144.2 jit_solution(15808118463048850393)
XLA Ops:
  7.2 0.0 all-gather.2.cloned.1.call-start
  7.2 0.7 compare_select_fusion
  7.9 0.7 compare_and_fusion
  8.6 1.6 %gather_fusion = bf16[4,2,128,256]{3,1,2,0:T(2,128)(2,1)S(1)} fusion(bf16[2,2,128,256]{3,1,2,0:T(2,128)(2,1)S(1)} %bitcast.22, s32[1024]{0:T(1024)S(1)} %pad_clamp_fusion), kind=kCustom, calls=%fused_computation | custom fusion | bytes 1048592 | tf_op jit(solution)/shard_map/jit(_take)/gather | solution.py:120
  10.2 0.5 broadcast_select_fusion
  10.7 20.6 %all_to_all.28 = bf16[4,2,128,256]{3,1,2,0:T(2,128)(2,1)S(1)} all-to-all(bf16[4,2,128,256]{3,1,2,0:T(2,128)(2,1)S(1)} %broadcast_select_fusion), channel_id=1, replica_groups=mesh['ctx'=4,'pair'=4,'dp'=2] {'pair'}, dimensions={0} | all-to-all | bytes 1048576 | tf_op jit(solution)/shard_map/all_to_all | solution.py:121
  31.3 0.4 copy.21
  31.8 1.2 all_to_all.22
  32.9 0.0 all-gather.2.cloned.1.call-update
  33.6 33.9 %all-gather.2.cloned.1.call-done = bf16[1,2,512,1024]{3,2,1,0:T(8,128)(2,1)} async-done(((bf16[1,2,128,1024]{3,2,1,0:T(8,128)(2,1)}), bf16[1,2,512,1024]{3,2,1,0:T(8,128)(2,1)}) %all-gather.2.cloned.1.call-update) | async-done | bytes 2097168 | tf_op jit(solution)/shard_map/all_gather | solution.py:122
  67.5 3.0 %slice_bitcast_fusion = (bf16[512,1024]{1,0:T(8,128)(2,1)}, bf16[512,1024]{1,0:T(8,128)(2,1)}) fusion(bf16[1,2,512,1024]{3,2,1,0:T(8,128)(2,1)} %all-gather.2.cloned.1.call-done), kind=kLoop, calls=%fused_computation.2 | loop fusion | bytes 4194304 | tf_op jit(solution)/shard_map/squeeze | solution.py:124
  70.5 16.0 %shard_map.111 = (bf16[128,2048]{1,0:T(8,128)(2,1)}, bf16[128,1024]{1,0:T(8,128)(2,1)}, bf16[128,1024]{1,0:T(8,128)(2,1)}, bf16[2,512,1024]{2,1,0:T(8,128)(2,1)}) custom-call(s32[4]{0:T(128)} %bitcast.30, s32[1]{0:T(128)} %bitcast.21.length_ref, bf16[128,2048]{1,0:T(8,128)(2,1)} %bitcast.26, bf16[128,2048]{1,0:T(8,128)(2,1)} %bitcast.27, ...), custom_call_target="tpu_custom_call" | custom-call | flops 2013265920 | bytes 6291456 | tf_op jit(solution)/shard_map/pallas_call | solution.py:92
  86.5 1.8 %copy.22 = bf16[2,4,128,1024]{3,2,0,1:T(8,128)(2,1)S(1)} copy(bf16[2,4,128,1024]{3,2,1,0:T(8,128)(2,1)} %bitcast.23) | data formatting | bytes 4194304 | tf_op jit(solution)/shard_map/reshape | solution.py:137
  88.3 28.1 %all_to_all.29 = bf16[2,4,128,1024]{3,2,0,1:T(8,128)(2,1)S(1)} all-to-all(bf16[2,4,128,1024]{3,2,0,1:T(8,128)(2,1)S(1)} %copy.22), channel_id=1, replica_groups=mesh['ctx'=4,'pair'=4,'dp'=2] {'ctx'}, dimensions={1} | all-to-all | bytes 4194304 | tf_op jit(solution)/shard_map/all_to_all | solution.py:138
  116.4 0.4 reduce_sum.21
  116.8 0.3 copy.24
  117.1 0.8 copy.25
  118.0 4.6 %all-to-all-start.2 = ((bf16[2,128,4,256]{1,3,0,2:T(8,128)(2,1)}), bf16[2,128,4,256]{1,3,0,2:T(8,128)(2,1)S(1)}, u32[]{:S(2)}, u32[]{:S(2)}) async-start(bf16[2,128,4,256]{1,3,0,2:T(8,128)(2,1)} %copy.25), calls=%async_computation.2 | async-start | bytes 1048576 | tf_op jit(solution)/shard_map/all_to_all | solution.py:141
  122.5 0.1 fusion
  122.6 12.9 %all-to-all-done.2 = bf16[2,128,4,256]{1,3,0,2:T(8,128)(2,1)S(1)} async-done(((bf16[2,128,4,256]{1,3,0,2:T(8,128)(2,1)}), bf16[2,128,4,256]{1,3,0,2:T(8,128)(2,1)S(1)}, u32[]{:S(2)}, u32[]{:S(2)}) %all-to-all-start.2) | async-done | bytes 524320 | tf_op jit(solution)/shard_map/all_to_all | solution.py:141
  135.5 0.1 convert_bitcast_fusion
  135.6 0.3 copy.26
  135.9 0.2 multiply_reduce_fusion
  136.2 1.2 copy.27
  (5 shorter events, 0.0 us)
Async XLA Ops:
  7.2 1.4 copy-start
  7.2 60.3 %all-gather.2.cloned.1.call-start = ((), (), s32[]{:S(2)}) async-start(), calls=%async_computation.3 | async-start | bytes 2621440 | tf_op jit(solution)/shard_map/all_gather | solution.py:122
  116.8 5.7 %copy-start.1 = (s32[4]{0:T(128)S(1)}, s32[4]{0:T(128)}, u32[]{:S(2)}) copy-start(s32[4]{0:T(128)} %param.15) | copy-start | bytes 52
  118.0 17.6 %all-to-all-start.2 = ((bf16[2,128,4,256]{1,3,0,2:T(8,128)(2,1)}), bf16[2,128,4,256]{1,3,0,2:T(8,128)(2,1)S(1)}, u32[]{:S(2)}, u32[]{:S(2)}) async-start(bf16[2,128,4,256]{1,3,0,2:T(8,128)(2,1)} %copy.25), calls=%async_computation.2 | async-start | bytes 1048576 | tf_op jit(solution)/shard_map/all_to_all | solution.py:141
Sparse Core Ops, SparseCore 0:
  33.1 34.4 all-gather.1

commit v2 on v1

--- a/solution.py
+++ b/solution.py
@@ -23,10 +23,11 @@
 def attention_grad_kernel(blocks_ref, length_ref, q_ref, do_ref, kp_ref, vp_ref, kr_ref, vr_ref,
                           dq_ref, dkr_ref, dvr_ref, dpre_ref):
     resp_rows = q_ref.shape[0]
-    pre_rows = kp_ref.shape[0]
+    n_ctx, chunk_rows, _ = kp_ref.shape
+    pre_rows = n_ctx * chunk_rows
     n_blocks = pre_rows // BLOCK
-    kp = kp_ref[...]
-    vp = vp_ref[...]
+    kp = kp_ref[...].reshape(pre_rows, HEAD_DIM)
+    vp = vp_ref[...].reshape(pre_rows, HEAD_DIM)
     kr = kr_ref[...]
     vr = vr_ref[...]
 
@@ -77,17 +78,25 @@
         dvr = dvr + lax.dot_general(pr, doj, TN, preferred_element_type=jnp.float32)
     dkr_ref[...] = (dkr * scale_factor).astype(dkr_ref.dtype)
     dvr_ref[...] = dvr.astype(dvr_ref.dtype)
-    dpre_ref[0] = (dkp * scale_factor).astype(dpre_ref.dtype)
-    dpre_ref[1] = dvp.astype(dpre_ref.dtype)
-
-
-def attention_grads(blocks, length, q, do, kp, vp, kr, vr):
+    dpre_ref[:, 0] = (dkp * scale_factor).astype(dpre_ref.dtype).reshape(n_ctx, chunk_rows, HEAD_DIM)
+    dpre_ref[:, 1] = dvp.astype(dpre_ref.dtype).reshape(n_ctx, chunk_rows, HEAD_DIM)
+
+
+def attention_grads(blocks, length, q, do, panel, kr, vr):
     resp_rows, q_width = q.shape
-    pre_rows, kv_width = kp.shape
+    n_ctx, n_pair, _, chunk_rows, chunk_feats = panel.shape
+    kv_width = kr.shape[1]
+    pre_rows = n_ctx * chunk_rows
     heads = kv_width // HEAD_DIM
+    per_chunk = chunk_feats // HEAD_DIM
     qspec = pl.BlockSpec((resp_rows, GROUP * HEAD_DIM), lambda g, b, n: (0, g))
-    pspec = pl.BlockSpec((pre_rows, HEAD_DIM), lambda g, b, n: (0, g))
+    kspec = pl.BlockSpec((n_ctx, None, None, chunk_rows, HEAD_DIM),
+                         lambda g, b, n: (0, g // per_chunk, 0, 0, g % per_chunk))
+    vspec = pl.BlockSpec((n_ctx, None, None, chunk_rows, HEAD_DIM),
+                         lambda g, b, n: (0, g // per_chunk, 1, 0, g % per_chunk))
     rspec = pl.BlockSpec((resp_rows, HEAD_DIM), lambda g, b, n: (0, g))
+    dspec = pl.BlockSpec((n_ctx, None, 2, chunk_rows, HEAD_DIM),
+                         lambda g, b, n: (0, g // per_chunk, 0, 0, g % per_chunk))
     flops = 2 * 6 * resp_rows * GROUP * heads * (pre_rows + resp_rows) * HEAD_DIM
     return pl.pallas_call(
         attention_grad_kernel,
@@ -95,55 +104,106 @@
             jax.ShapeDtypeStruct((resp_rows, q_width), jnp.bfloat16),
             jax.ShapeDtypeStruct((resp_rows, kv_width), jnp.bfloat16),
             jax.ShapeDtypeStruct((resp_rows, kv_width), jnp.bfloat16),
-            jax.ShapeDtypeStruct((2, pre_rows, kv_width), jnp.bfloat16),
+            jax.ShapeDtypeStruct(panel.shape, jnp.bfloat16),
         ),
         grid_spec=pltpu.PrefetchScalarGridSpec(
             num_scalar_prefetch=2,
             grid=(heads,),
-            in_specs=[qspec, qspec, pspec, pspec, rspec, rspec],
-            out_specs=[qspec, rspec, rspec,
-                       pl.BlockSpec((2, pre_rows, HEAD_DIM), lambda g, b, n: (0, 0, g))],
+            in_specs=[qspec, qspec, kspec, vspec, rspec, rspec],
+            out_specs=[qspec, rspec, rspec, dspec],
         ),
         cost_estimate=pl.CostEstimate(
             flops=flops,
             transcendentals=resp_rows * GROUP * heads * (pre_rows + resp_rows),
             bytes_accessed=2 * (2 * resp_rows * q_width + 4 * pre_rows * kv_width + 4 * resp_rows * kv_width),
         ),
-    )(blocks, length, q, do, kp, vp, kr, vr)
+    )(blocks, length, q, do, panel, panel, kr, vr)
+
+
+def ring_shift(x, axis, n, d):
+    return lax.ppermute(x, axis, [(i, (i + d) % n) for i in range(n)])
+
+
+def pair_gather(planes, pair_prompt):
+    n = lax.axis_size("pair")
+    r = lax.axis_index("pair")
+    held = [lax.dynamic_index_in_dim(planes, pair_prompt[r], 0, keepdims=False)]
+    for d in range(1, n):
+        chunk = lax.dynamic_index_in_dim(planes, pair_prompt[(r + d) % n], 0, keepdims=False)
+        held.append(ring_shift(chunk, "pair", n, d))
+    held = jnp.stack(held)
+    return jnp.take(held, (r - jnp.arange(n)) % n, axis=0)
+
+
+def ctx_gather(x):
+    n = lax.axis_size("ctx")
+    if n != 4:
+        return lax.all_gather(x, "ctx", axis=0, tiled=False)
+    c = lax.axis_index("ctx")
+    along_x = [(i, i ^ 1) for i in range(n)]
+    along_y = [(i, i ^ 2) for i in range(n)]
+    from_x = lax.ppermute(x, "ctx", along_x)
+    from_y = lax.ppermute(x, "ctx", along_y)
+    half = x.shape[-2] // 2
+    far_a = lax.ppermute(from_y[..., :half, :], "ctx", along_x)
+    far_b = lax.ppermute(from_x[..., half:, :], "ctx", along_y)
+    held = jnp.stack([x, from_x, from_y, jnp.concatenate([far_a, far_b], -2)])
+    return jnp.take(held, jnp.bitwise_xor(jnp.arange(n), c), axis=0)
+
+
+def ctx_reduce(pieces):
+    n = lax.axis_size("ctx")
+    if n != 4:
+        got = lax.all_to_all(pieces, "ctx", split_axis=0, concat_axis=0, tiled=True)
+        return jnp.sum(got.astype(jnp.float32), axis=0).astype(jnp.bfloat16)
+    c = lax.axis_index("ctx")
+    along_x = [(i, i ^ 1) for i in range(n)]
+    along_y = [(i, i ^ 2) for i in range(n)]
+    mine = lax.dynamic_index_in_dim(pieces, c, 0, keepdims=False)
+    to_x = lax.dynamic_index_in_dim(pieces, jnp.bitwise_xor(c, 1), 0, keepdims=False)
+    to_y = lax.dynamic_index_in_dim(pieces, jnp.bitwise_xor(c, 2), 0, keepdims=False)
+    to_far = lax.dynamic_index_in_dim(pieces, jnp.bitwise_xor(c, 3), 0, keepdims=False)
+    half = to_far.shape[-2] // 2
+    own_x, pass_y = lax.ppermute((to_x, to_far[..., :half, :]), "ctx", along_x)
+    own_y, pass_x = lax.ppermute((to_y, to_far[..., half:, :]), "ctx", along_y)
+    far_a = lax.ppermute(pass_y, "ctx", along_y)
+    far_b = lax.ppermute(pass_x, "ctx", along_x)
+    far = jnp.concatenate([far_a, far_b], -2)
+    total = (mine.astype(jnp.float32) + own_x.astype(jnp.float32)) + (
+        own_y.astype(jnp.float32) + far.astype(jnp.float32))
+    return total.astype(jnp.bfloat16)
+
+
+def pair_reduce(totals, pair_prompt, n_prompts):
+    n = lax.axis_size("pair")
+    r = lax.axis_index("pair")
+    out = None
+    for d in range(n):
+        chunk = lax.dynamic_index_in_dim(totals, (r + d) % n, 0, keepdims=False)
+        got = chunk if d == 0 else ring_shift(chunk, "pair", n, d)
+        source = (r - d) % n
+        hits = (pair_prompt[source] == jnp.arange(n_prompts, dtype=jnp.int32)).astype(jnp.float32)
+        term = hits[:, None, None, None] * jnp.transpose(got.astype(jnp.float32), (1, 0, 2))[None]
+        out = term if out is None else out + term
+    return out
 
 
 def shards(
     queries, resp_keys, resp_values, d_out, prefix_kv, prefix_blocks, resp_lengths, pair_prompt
 ):
     n_prompts = prefix_kv.shape[0]
-    kv_planes = jnp.transpose(prefix_kv, (0, 2, 1, 3))
-    outgoing = jnp.take(kv_planes, pair_prompt, axis=0)
-    mine = lax.all_to_all(outgoing, "pair", split_axis=0, concat_axis=3, tiled=True)
-    panel = lax.all_gather(mine, "ctx", axis=2, tiled=True)[0]
-    kp = panel[0]
-    vp = panel[1]
-    pre_rows = kp.shape[0]
+    planes = jnp.transpose(prefix_kv, (0, 2, 1, 3))
+    panel = ctx_gather(pair_gather(planes, pair_prompt))
 
     dq, dkr, dvr, dpre = attention_grads(
         prefix_blocks[0, 0], resp_lengths[0, 0].reshape(1), queries[0, 0], d_out[0, 0],
-        kp, vp, resp_keys[0, 0], resp_values[0, 0])
+        panel, resp_keys[0, 0], resp_values[0, 0])
     d_queries = dq[None, None]
     d_resp_keys = dkr[None, None]
     d_resp_values = dvr[None, None]
 
-    n_ctx = lax.axis_size("ctx")
-    n_pair = lax.axis_size("pair")
-    kv_width = dpre.shape[-1]
-    pieces = dpre.reshape(2, n_ctx, pre_rows // n_ctx, kv_width)
-    pieces = lax.all_to_all(pieces, "ctx", split_axis=1, concat_axis=1, tiled=True)
-    ctx_total = jnp.sum(pieces.astype(jnp.float32), axis=1).astype(jnp.bfloat16)
-    ctx_total = ctx_total.reshape(2, pre_rows // n_ctx, n_pair, kv_width // n_pair)
-    arrived = lax.all_to_all(ctx_total, "pair", split_axis=2, concat_axis=2, tiled=True)
-    prompt_hits = (pair_prompt[:, None] == jnp.arange(n_prompts, dtype=jnp.int32)[None, :]).astype(
-        jnp.float32
-    )
-    arrived = jnp.transpose(arrived.astype(jnp.float32), (2, 1, 0, 3))
-    d_prefix = jnp.sum(prompt_hits[:, :, None, None, None] * arrived[:, None], axis=0)
+    ctx_total = ctx_reduce(dpre)
+    d_prefix = pair_reduce(ctx_total, pair_prompt, n_prompts)
     return (d_queries, d_resp_keys, d_resp_values, d_prefix)
 
 

time: 145 us -> 113 us (0.78)
  blocking collectives: 48.7 us -> 0 us
  starting transfers between devices: 4.63 us -> 22.1 us
  other arithmetic: 2.67 us -> 9.14 us
  between operations: 14.8 us -> 9.38 us
  local copies, waits for them, and re-layouts: 10.6 us -> 8.11 us
    all_to_all x2 -> x0, blocking collectives: 48.7 us -> none  [the longest x1 28.1 us: shards(): lax.all_to_all(pieces, 'ctx', split_axis=1, concat_axis=1, tiled=True)]
    ppermute x0 -> x16, waiting for transfers between devices: none -> 47.9 us  [the longest x6 17 us: ring_shift(): return lax.ppermute(x, axis, [(i, (i + d) % n) for i in range(n)])]
    all_gather x1 -> x0, waiting for transfers between devices: 33.9 us -> none  [shards(): panel = lax.all_gather(mine, 'ctx', axis=2, tiled=True)[0]]
    ppermute x0 -> x16, starting transfers between devices: none -> 22.1 us  [the longest x6 9.69 us: ring_shift(): return lax.ppermute(x, axis, [(i, (i + d) % n) for i in range(n)])]
    all_to_all x1 -> x0, waiting for transfers between devices: 12.9 us -> none  [shards(): lax.all_to_all(ctx_total, 'pair', split_axis=2, concat_axis=2, tiled=True)]
    all_to_all x1 -> x0, starting transfers between devices: 4.6 us -> none  [shards(): lax.all_to_all(ctx_total, 'pair', split_axis=2, concat_axis=2, tiled=True)]
    convert_element_type x1 -> x3, other arithmetic: 0.07 us -> 3.88 us  [the longest x2 2.56 us: pair_reduce(): (pair_prompt[source] == jnp.arange(n_prompts, dtype=jnp.int32)).astype(jn...]
    reshape x2 -> x0, local copies, waits for them, and re-layouts: 2.6 us -> none  [the longest x1 1.76 us: shards(): pieces = dpre.reshape(2, n_ctx, pre_rows // n_ctx, kv_width)]
  transfers between devices with their start and end apart: 2 -> 16, of which waited for: 2 -> 9; matrix products, arithmetic and copies ran while one was open for 0% -> 3% of each run, Pallas kernels for 0% -> 0%
where the time goes in v2:
time: 113 us
  waiting for transfers between devices  47.9 us (42%)
  starting transfers between devices  22.1 us (20%)
  Pallas kernels  16.3 us (14%)
  between operations  9.38 us (8%)
  other arithmetic  9.14 us (8%)
  local copies, waits for them, and re-layouts  8.11 us (7%)
    ppermute x6, waiting for transfers between devices, ring_shift(): return lax.ppermute(x, axis, [(i, (i + d) % n) for i in range(n)])  17 us
    pallas_call x1, Pallas kernels, attention_grads(): pl.pallas_call(attention_grad_kernel, out_shape=(jax.ShapeDtypeStruct((re...  16.3 us
    ppermute x1, waiting for transfers between devices, ctx_reduce(): far_a = lax.ppermute(pass_y, 'ctx', along_y)  11.7 us
    ppermute x1, waiting for transfers between devices, ctx_gather(): from_y = lax.ppermute(x, 'ctx', along_y)  9.98 us
    ppermute x6, starting transfers between devices, ring_shift(): return lax.ppermute(x, axis, [(i, (i + d) % n) for i in range(n)])  9.69 us
    ppermute x2, waiting for transfers between devices, ctx_reduce(): own_x, pass_y = lax.ppermute((to_x, to_far[..., :half, :]), 'ctx', along_x)  5.2 us
    select_n x2, other arithmetic, ctx_gather(): return jnp.take(held, jnp.bitwise_xor(jnp.arange(n), c), axis=0)  3.16 us
    ppermute x1, waiting for transfers between devices, ctx_gather(): far_a = lax.ppermute(from_y[..., :half, :], 'ctx', along_x)  2.88 us
  transfers between devices with their start and end apart: 16, of which 9 were waited for; matrix products, arithmetic and copies ran while one was open for 3% of the time, Pallas kernels for 0%

profile of v2, /device:TPU:0, one launch (start us, length us, event | category | flops | bytes accessed | tf_op | source)
XLA Modules:
  0.0 112.9 jit_solution(2597230190081300754)
XLA Ops:
  0.7 1.6 %fusion.7 = (s32[1]{0:T(128)}, s32[1]{0:T(128)}, s32[1]{0:T(128)}, s32[1]{0:T(128)}, s32[1]{0:T(128)}, /*index=5*/s32[1]{0:T(128)}, s32[1]{0:T(128)}, s32[1]{0:T(128)}) fusion(s32[4]{0:T(128)} %param.15, s32[]{:T(128)S(6)} %select_n.180, s32[]{:T(128)S(6)} %select_n.186, s32[]{:T(128)S(6)} %select_n.171, s32[]{:T(128)S(6)} %select_n.168, s32[]{:T(128)S(6)} %select_n.165, ...), kind=kLoop, calls=%fused_computation.53 | loop fusion | bytes 96 | tf_op jit(solution)/shard_map/dynamic_slice | solution.py:185
  10.2 1.5 %constant_dynamic-slice_fusion.3 = (bf16[1,128,2,256]{3,2,1,0:T(2,128)(2,1)S(1)}, bf16[1,128,2,256]{3,2,1,0:T(2,128)(2,1)S(1)}, bf16[1,128,2,256]{3,2,1,0:T(2,128)(2,1)S(1)}, bf16[1,128,2,256]{3,2,1,0:T(2,128)(2,1)S(1)}) fusion(bf16[2,128,2,256]{3,2,1,0:T(2,128)(2,1)} %param.12, s32[]{:T(128)S(6)} %select_n.163, s32[]{:T(128)S(6)} %select_n.169, ...), kind=kLoop, calls=%fused_computation.31 | loop fusion | bytes 1048592 | tf_op jit(solution)/shard_map/dynamic-slice
  11.6 5.1 %collective-permute-start.2 = (bf16[2,128,256]{2,1,0:T(8,128)(2,1)S(1)}, bf16[2,128,256]{2,1,0:T(8,128)(2,1)S(1)}, u32[]{:S(2)}, u32[]{:S(2)}) collective-permute-start(bf16[2,128,256]{2,1,0:T(8,128)(2,1)S(1)} %bitcast.78), channel_id=1, source_target_pairs={{0,6},{2,0},{4,2},{6,4},{1,7},{3,1},{5,3},{7,5},{8,14},{10,8},{12,... | collective-permute-start | bytes 393224 | tf_op jit(solution)/shard_map/ppermute | solution.py:124
  18.0 2.7 %collective-permute-done.2 = bf16[2,128,256]{2,1,0:T(8,128)(2,1)S(1)} collective-permute-done((bf16[2,128,256]{2,1,0:T(8,128)(2,1)S(1)}, bf16[2,128,256]{2,1,0:T(8,128)(2,1)S(1)}, u32[]{:S(2)}, u32[]{:S(2)}) %collective-permute-start.2) | collective-permute-done | bytes 131104 | tf_op jit(solution)/shard_map/ppermute | solution.py:124
  20.7 4.4 %collective-permute-done = bf16[2,128,256]{2,1,0:T(8,128)(2,1)S(1)} collective-permute-done((bf16[2,128,256]{2,1,0:T(8,128)(2,1)S(1)}, bf16[2,128,256]{2,1,0:T(8,128)(2,1)S(1)}, u32[]{:S(2)}, u32[]{:S(2)}) %collective-permute-start) | collective-permute-done | bytes 131104 | tf_op jit(solution)/shard_map/ppermute | solution.py:124
  25.1 3.3 %collective-permute-done.1 = bf16[2,128,256]{2,1,0:T(8,128)(2,1)S(1)} collective-permute-done((bf16[2,128,256]{2,1,0:T(8,128)(2,1)S(1)}, bf16[2,128,256]{2,1,0:T(8,128)(2,1)S(1)}, u32[]{:S(2)}, u32[]{:S(2)}) %collective-permute-start.1) | collective-permute-done | bytes 131104 | tf_op jit(solution)/shard_map/ppermute | solution.py:124
  29.2 1.6 %collective-permute-start.4 = (bf16[4,2,128,256]{3,2,1,0:T(8,128)(2,1)S(1)}, bf16[4,2,128,256]{3,2,1,0:T(8,128)(2,1)S(1)}, u32[]{:S(2)}, u32[]{:S(2)}) collective-permute-start(bf16[4,2,128,256]{3,2,1,0:T(8,128)(2,1)S(1)} %broadcast_select_fusion.1), channel_id=1, source_target_pairs={{0,16},{8,24},{16,0},{24,8},{1,17},{9,25},{17,1},{25,9},{2,18},{10... | collective-permute-start | bytes 1572872 | tf_op jit(solution)/shard_map/ppermute | solution.py:146
  30.8 1.5 %collective-permute-start.3 = (bf16[4,2,128,256]{3,2,1,0:T(8,128)(2,1)S(1)}, bf16[4,2,128,256]{3,2,1,0:T(8,128)(2,1)S(1)}, u32[]{:S(2)}, u32[]{:S(2)}) collective-permute-start(bf16[4,2,128,256]{3,2,1,0:T(8,128)(2,1)S(1)} %broadcast_select_fusion.1), channel_id=1, source_target_pairs={{0,8},{8,0},{16,24},{24,16},{1,9},{9,1},{17,25},{25,17},{2,10},{10... | collective-permute-start | bytes 1572872 | tf_op jit(solution)/shard_map/ppermute | solution.py:145
  32.3 10.0 %collective-permute-done.4 = bf16[4,2,128,256]{3,2,1,0:T(8,128)(2,1)S(1)} collective-permute-done((bf16[4,2,128,256]{3,2,1,0:T(8,128)(2,1)S(1)}, bf16[4,2,128,256]{3,2,1,0:T(8,128)(2,1)S(1)}, u32[]{:S(2)}, u32[]{:S(2)}) %collective-permute-start.4) | collective-permute-done | bytes 524320 | tf_op jit(solution)/shard_map/ppermute | solution.py:146
  42.3 1.6 %collective-permute-start.5 = (bf16[4,2,64,256]{3,2,1,0:T(8,128)(2,1)S(1)}, bf16[4,2,64,256]{3,2,1,0:T(8,128)(2,1)S(1)}, u32[]{:S(2)}, u32[]{:S(2)}) collective-permute-start(bf16[4,2,64,256]{3,2,1,0:T(8,128)(2,1)S(1)} %slice.20), channel_id=1, source_target_pairs={{0,8},{8,0},{16,24},{24,16},{1,9},{9,1},{17,25},{25,17},{2,10},{10... | collective-permute-start | bytes 786440 | tf_op jit(solution)/shard_map/ppermute | solution.py:148
  43.8 1.6 %collective-permute-start.6 = (bf16[4,2,64,256]{3,2,1,0:T(8,128)(2,1)S(1)}, bf16[4,2,64,256]{3,2,1,0:T(8,128)(2,1)S(1)}, u32[]{:S(2)}, u32[]{:S(2)}) collective-permute-start(bf16[4,2,64,256]{3,2,1,0:T(8,128)(2,1)S(1)} %slice.21), channel_id=1, source_target_pairs={{0,16},{8,24},{16,0},{24,8},{1,17},{9,25},{17,1},{25,9},{2,18},{10... | collective-permute-start | bytes 786440 | tf_op jit(solution)/shard_map/ppermute | solution.py:149
  46.2 2.9 %collective-permute-done.5 = bf16[4,2,64,256]{3,2,1,0:T(8,128)(2,1)S(1)} collective-permute-done((bf16[4,2,64,256]{3,2,1,0:T(8,128)(2,1)S(1)}, bf16[4,2,64,256]{3,2,1,0:T(8,128)(2,1)S(1)}, u32[]{:S(2)}, u32[]{:S(2)}) %collective-permute-start.5) | collective-permute-done | bytes 262176 | tf_op jit(solution)/shard_map/ppermute | solution.py:148
  50.6 2.0 %gather_fusion.1 = bf16[4,4,2,128,256]{4,3,2,1,0:T(8,128)(2,1)} fusion(bf16[4,4,2,128,256]{4,3,2,1,0:T(8,128)(2,1)S(1)} %pad_maximum_fusion, s32[1024]{0:T(1024)S(1)} %pad_clamp_fusion), kind=kCustom, calls=%fused_computation.1 | custom fusion | bytes 4194320 | tf_op jit(solution)/shard_map/jit(_take)/gather | solution.py:151
  52.6 3.2 %broadcast_select_fusion.kp_ref.vp_ref = bf16[4,4,2,128,256]{4,3,2,1,0:T(8,128)(2,1)} fusion(bf16[4,4,2,128,256]{4,3,2,1,0:T(8,128)(2,1)} %gather_fusion.1, pred[4]{0:T(512)(128)(4,1)S(1)} %get-tuple-element.34), kind=kLoop, calls=%fused_computation.3 | loop fusion | flops 1048576 | bytes 4194308 | tf_op jit(solution)/shard_map/jit(_take)/select_n | solution.py:151
  55.7 16.3 %shard_map.111 = (bf16[128,2048]{1,0:T(8,128)(2,1)}, bf16[128,1024]{1,0:T(8,128)(2,1)}, bf16[128,1024]{1,0:T(8,128)(2,1)}, bf16[4,4,2,128,256]{4,3,2,1,0:T(8,128)(2,1)}) custom-call(s32[4]{0:T(128)} %bitcast.88, s32[1]{0:T(128)} %bitcast.74.length_ref, bf16[128,2048]{1,0:T(8,128)(2,1)} %bitcast.84, bf16[128,2048]{1,0:T(8,128)(2,1)} %bitcast.85, ...), custom_call_target="tpu_custom_call" | custom-call | flops 2013265920 | bytes 6291456 | tf_op jit(solution)/shard_map/pallas_call | solution.py:101
  72.0 1.5 %dynamic-slice_bitcast_fusion = (bf16[4,2,128,256]{3,2,1,0:T(8,128)(2,1)S(1)}, bf16[4,2,128,256]{3,2,1,0:T(8,128)(2,1)S(1)}, bf16[4,2,128,256]{3,2,1,0:T(8,128)(2,1)S(1)}) fusion(bf16[4,4,2,128,256]{4,3,2,1,0:T(8,128)(2,1)} %get-tuple-element.11, s32[]{:T(128)S(6)} %select_n.184, s32[]{:T(128)S(6)} %select_n.183, s32[]{:T(128)S(6)} %select_n.182), kind=kLoop, calls=%fused_computation.11 | loop fusion | bytes 3145740 | tf_op jit(solution)/shard_map/jit(dynamic_index_in_dim)/squeeze | solution.py:165
  73.5 1.5 %collective-permute-start.9 = (bf16[4,2,64,256]{3,2,1,0:T(8,128)(2,1)S(1)}, bf16[4,2,64,256]{3,2,1,0:T(8,128)(2,1)S(1)}, u32[]{:S(2)}, u32[]{:S(2)}) collective-permute-start(bf16[4,2,64,256]{3,2,1,0:T(8,128)(2,1)S(1)} %get-tuple-element.19), channel_id=1, source_target_pairs={{0,8},{8,0},{16,24},{24,16},{1,9},{9,1},{17,25},{25,17},{2,10},{10... | collective-permute-start | bytes 786440 | tf_op jit(solution)/shard_map/ppermute | solution.py:167
  75.7 1.4 %collective-permute-start.8 = (bf16[4,2,128,256]{3,2,1,0:T(8,128)(2,1)S(1)}, bf16[4,2,128,256]{3,2,1,0:T(8,128)(2,1)S(1)}, u32[]{:S(2)}, u32[]{:S(2)}) collective-permute-start(bf16[4,2,128,256]{3,2,1,0:T(8,128)(2,1)S(1)} %get-tuple-element.13), channel_id=1, source_target_pairs={{0,16},{8,24},{16,0},{24,8},{1,17},{9,25},{17,1},{25,9},{2,18},{10... | collective-permute-start | bytes 1572872 | tf_op jit(solution)/shard_map/ppermute | solution.py:168
  77.6 5.2 %collective-permute-done.9 = bf16[4,2,64,256]{3,2,1,0:T(8,128)(2,1)S(1)} collective-permute-done((bf16[4,2,64,256]{3,2,1,0:T(8,128)(2,1)S(1)}, bf16[4,2,64,256]{3,2,1,0:T(8,128)(2,1)S(1)}, u32[]{:S(2)}, u32[]{:S(2)}) %collective-permute-start.9) | collective-permute-done | bytes 262176 | tf_op jit(solution)/shard_map/ppermute | solution.py:167
  82.8 1.5 %collective-permute-start.10 = (bf16[4,2,64,256]{3,2,1,0:T(8,128)(2,1)S(1)}, bf16[4,2,64,256]{3,2,1,0:T(8,128)(2,1)S(1)}, u32[]{:S(2)}, u32[]{:S(2)}) collective-permute-start(bf16[4,2,64,256]{3,2,1,0:T(8,128)(2,1)S(1)} %collective-permute-done.9), channel_id=1, source_target_pairs={{0,16},{8,24},{16,0},{24,8},{1,17},{9,25},{17,1},{25,9},{2,18},{10... | collective-permute-start | bytes 786440 | tf_op jit(solution)/shard_map/ppermute | solution.py:169
  84.9 11.7 %collective-permute-done.10 = bf16[4,2,64,256]{3,2,1,0:T(8,128)(2,1)S(1)} collective-permute-done((bf16[4,2,64,256]{3,2,1,0:T(8,128)(2,1)S(1)}, bf16[4,2,64,256]{3,2,1,0:T(8,128)(2,1)S(1)}, u32[]{:S(2)}, u32[]{:S(2)}) %collective-permute-start.10) | collective-permute-done | bytes 262176 | tf_op jit(solution)/shard_map/ppermute | solution.py:169
  98.0 2.8 %collective-permute-start.15 = (bf16[2,128,256]{2,1,0:T(8,128)(2,1)S(1)}, bf16[2,128,256]{2,1,0:T(8,128)(2,1)S(1)}, u32[]{:S(2)}, u32[]{:S(2)}) collective-permute-start(bf16[2,128,256]{2,1,0:T(8,128)(2,1)S(1)} %get-tuple-element.16), channel_id=1, source_target_pairs={{0,6},{2,0},{4,2},{6,4},{1,7},{3,1},{5,3},{7,5},{8,14},{10,8},{12,... | collective-permute-start | bytes 393224 | tf_op jit(solution)/shard_map/ppermute | solution.py:124
  104.5 6.5 %collective-permute-done.14 = bf16[2,128,256]{2,1,0:T(8,128)(2,1)S(1)} collective-permute-done((bf16[2,128,256]{2,1,0:T(8,128)(2,1)S(1)}, bf16[2,128,256]{2,1,0:T(8,128)(2,1)S(1)}, u32[]{:S(2)}, u32[]{:S(2)}) %collective-permute-start.14) | collective-permute-done | bytes 131104 | tf_op jit(solution)/shard_map/ppermute | solution.py:124
  111.6 1.3 %multiply_add_fusion = f32[2,128,2,256]{3,2,1,0:T(2,128)} fusion(f32[128,2,256]{2,1,0:T(2,128)S(1)} %copy.24, f32[128,2,256]{2,1,0:T(2,128)S(1)} %copy.23, f32[128,2,256]{2,1,0:T(2,128)S(1)} %copy.22, f32[128,2,256]{2,1,0:T(2,128)S(1)} %copy.21, f32[2]{0:T(128)S(1)} %get-tuple-element.35, f32[2]{0:T(128)S(1)} %get-tuple-element.36, ...), kind=kLoop, calls=%fused_computation.10 | loop fusion | flops 917504 | bytes 1572896 | tf_op jit(solution)/shard_map/add | solution.py:187
  (44 shorter events, 11.0 us)
Async XLA Ops:
  11.6 9.0 %collective-permute-start.2 = (bf16[2,128,256]{2,1,0:T(8,128)(2,1)S(1)}, bf16[2,128,256]{2,1,0:T(8,128)(2,1)S(1)}, u32[]{:S(2)}, u32[]{:S(2)}) collective-permute-start(bf16[2,128,256]{2,1,0:T(8,128)(2,1)S(1)} %bitcast.78), channel_id=1, source_target_pairs={{0,6},{2,0},{4,2},{6,4},{1,7},{3,1},{5,3},{7,5},{8,14},{10,8},{12,... | collective-permute-start | bytes 393224 | tf_op jit(solution)/shard_map/ppermute | solution.py:124
  16.8 8.3 %collective-permute-start = (bf16[2,128,256]{2,1,0:T(8,128)(2,1)S(1)}, bf16[2,128,256]{2,1,0:T(8,128)(2,1)S(1)}, u32[]{:S(2)}, u32[]{:S(2)}) collective-permute-start(bf16[2,128,256]{2,1,0:T(8,128)(2,1)S(1)} %bitcast.79), channel_id=1, source_target_pairs={{0,2},{2,4},{4,6},{6,0},{1,3},{3,5},{5,7},{7,1},{8,10},{10,12},{12... | collective-permute-start | bytes 393224 | tf_op jit(solution)/shard_map/ppermute | solution.py:124
  16.9 11.5 %collective-permute-start.1 = (bf16[2,128,256]{2,1,0:T(8,128)(2,1)S(1)}, bf16[2,128,256]{2,1,0:T(8,128)(2,1)S(1)}, u32[]{:S(2)}, u32[]{:S(2)}) collective-permute-start(bf16[2,128,256]{2,1,0:T(8,128)(2,1)S(1)} %bitcast.80), channel_id=1, source_target_pairs={{0,4},{2,6},{4,0},{6,2},{1,5},{3,7},{5,1},{7,3},{8,12},{10,14},{12... | collective-permute-start | bytes 393224 | tf_op jit(solution)/shard_map/ppermute | solution.py:124
  29.2 13.1 %collective-permute-start.4 = (bf16[4,2,128,256]{3,2,1,0:T(8,128)(2,1)S(1)}, bf16[4,2,128,256]{3,2,1,0:T(8,128)(2,1)S(1)}, u32[]{:S(2)}, u32[]{:S(2)}) collective-permute-start(bf16[4,2,128,256]{3,2,1,0:T(8,128)(2,1)S(1)} %broadcast_select_fusion.1), channel_id=1, source_target_pairs={{0,16},{8,24},{16,0},{24,8},{1,17},{9,25},{17,1},{25,9},{2,18},{10... | collective-permute-start | bytes 1572872 | tf_op jit(solution)/shard_map/ppermute | solution.py:146
  30.8 13.1 %collective-permute-start.3 = (bf16[4,2,128,256]{3,2,1,0:T(8,128)(2,1)S(1)}, bf16[4,2,128,256]{3,2,1,0:T(8,128)(2,1)S(1)}, u32[]{:S(2)}, u32[]{:S(2)}) collective-permute-start(bf16[4,2,128,256]{3,2,1,0:T(8,128)(2,1)S(1)} %broadcast_select_fusion.1), channel_id=1, source_target_pairs={{0,8},{8,0},{16,24},{24,16},{1,9},{9,1},{17,25},{25,17},{2,10},{10... | collective-permute-start | bytes 1572872 | tf_op jit(solution)/shard_map/ppermute | solution.py:145
  42.3 6.8 %collective-permute-start.5 = (bf16[4,2,64,256]{3,2,1,0:T(8,128)(2,1)S(1)}, bf16[4,2,64,256]{3,2,1,0:T(8,128)(2,1)S(1)}, u32[]{:S(2)}, u32[]{:S(2)}) collective-permute-start(bf16[4,2,64,256]{3,2,1,0:T(8,128)(2,1)S(1)} %slice.20), channel_id=1, source_target_pairs={{0,8},{8,0},{16,24},{24,16},{1,9},{9,1},{17,25},{25,17},{2,10},{10... | collective-permute-start | bytes 786440 | tf_op jit(solution)/shard_map/ppermute | solution.py:148
  43.8 6.4 %collective-permute-start.6 = (bf16[4,2,64,256]{3,2,1,0:T(8,128)(2,1)S(1)}, bf16[4,2,64,256]{3,2,1,0:T(8,128)(2,1)S(1)}, u32[]{:S(2)}, u32[]{:S(2)}) collective-permute-start(bf16[4,2,64,256]{3,2,1,0:T(8,128)(2,1)S(1)} %slice.21), channel_id=1, source_target_pairs={{0,16},{8,24},{16,0},{24,8},{1,17},{9,25},{17,1},{25,9},{2,18},{10... | collective-permute-start | bytes 786440 | tf_op jit(solution)/shard_map/ppermute | solution.py:149
  73.5 9.3 %collective-permute-start.9 = (bf16[4,2,64,256]{3,2,1,0:T(8,128)(2,1)S(1)}, bf16[4,2,64,256]{3,2,1,0:T(8,128)(2,1)S(1)}, u32[]{:S(2)}, u32[]{:S(2)}) collective-permute-start(bf16[4,2,64,256]{3,2,1,0:T(8,128)(2,1)S(1)} %get-tuple-element.19), channel_id=1, source_target_pairs={{0,8},{8,0},{16,24},{24,16},{1,9},{9,1},{17,25},{25,17},{2,10},{10... | collective-permute-start | bytes 786440 | tf_op jit(solution)/shard_map/ppermute | solution.py:167
  75.0 9.4 %collective-permute-start.11 = (bf16[4,2,64,256]{3,2,1,0:T(8,128)(2,1)S(1)}, bf16[4,2,64,256]{3,2,1,0:T(8,128)(2,1)S(1)}, u32[]{:S(2)}, u32[]{:S(2)}) collective-permute-start(bf16[4,2,64,256]{3,2,1,0:T(8,128)(2,1)S(1)} %get-tuple-element.20), channel_id=1, source_target_pairs={{0,16},{8,24},{16,0},{24,8},{1,17},{9,25},{17,1},{25,9},{2,18},{10... | collective-permute-start | bytes 786440 | tf_op jit(solution)/shard_map/ppermute | solution.py:168
  75.7 21.0 %collective-permute-start.8 = (bf16[4,2,128,256]{3,2,1,0:T(8,128)(2,1)S(1)}, bf16[4,2,128,256]{3,2,1,0:T(8,128)(2,1)S(1)}, u32[]{:S(2)}, u32[]{:S(2)}) collective-permute-start(bf16[4,2,128,256]{3,2,1,0:T(8,128)(2,1)S(1)} %get-tuple-element.13), channel_id=1, source_target_pairs={{0,16},{8,24},{16,0},{24,8},{1,17},{9,25},{17,1},{25,9},{2,18},{10... | collective-permute-start | bytes 1572872 | tf_op jit(solution)/shard_map/ppermute | solution.py:168
  77.0 19.6 %collective-permute-start.7 = (bf16[4,2,128,256]{3,2,1,0:T(8,128)(2,1)S(1)}, bf16[4,2,128,256]{3,2,1,0:T(8,128)(2,1)S(1)}, u32[]{:S(2)}, u32[]{:S(2)}) collective-permute-start(bf16[4,2,128,256]{3,2,1,0:T(8,128)(2,1)S(1)} %get-tuple-element.14), channel_id=1, source_target_pairs={{0,8},{8,0},{16,24},{24,16},{1,9},{9,1},{17,25},{25,17},{2,10},{10... | collective-permute-start | bytes 1572872 | tf_op jit(solution)/shard_map/ppermute | solution.py:167
  82.8 13.8 %collective-permute-start.10 = (bf16[4,2,64,256]{3,2,1,0:T(8,128)(2,1)S(1)}, bf16[4,2,64,256]{3,2,1,0:T(8,128)(2,1)S(1)}, u32[]{:S(2)}, u32[]{:S(2)}) collective-permute-start(bf16[4,2,64,256]{3,2,1,0:T(8,128)(2,1)S(1)} %collective-permute-done.9), channel_id=1, source_target_pairs={{0,16},{8,24},{16,0},{24,8},{1,17},{9,25},{17,1},{25,9},{2,18},{10... | collective-permute-start | bytes 786440 | tf_op jit(solution)/shard_map/ppermute | solution.py:169
  84.4 12.3 %collective-permute-start.12 = (bf16[4,2,64,256]{3,2,1,0:T(8,128)(2,1)S(1)}, bf16[4,2,64,256]{3,2,1,0:T(8,128)(2,1)S(1)}, u32[]{:S(2)}, u32[]{:S(2)}) collective-permute-start(bf16[4,2,64,256]{3,2,1,0:T(8,128)(2,1)S(1)} %collective-permute-done.11), channel_id=1, source_target_pairs={{0,8},{8,0},{16,24},{24,16},{1,9},{9,1},{17,25},{25,17},{2,10},{10... | collective-permute-start | bytes 786440 | tf_op jit(solution)/shard_map/ppermute | solution.py:170
  98.0 6.3 %collective-permute-start.15 = (bf16[2,128,256]{2,1,0:T(8,128)(2,1)S(1)}, bf16[2,128,256]{2,1,0:T(8,128)(2,1)S(1)}, u32[]{:S(2)}, u32[]{:S(2)}) collective-permute-start(bf16[2,128,256]{2,1,0:T(8,128)(2,1)S(1)} %get-tuple-element.16), channel_id=1, source_target_pairs={{0,6},{2,0},{4,2},{6,4},{1,7},{3,1},{5,3},{7,5},{8,14},{10,8},{12,... | collective-permute-start | bytes 393224 | tf_op jit(solution)/shard_map/ppermute | solution.py:124
  103.7 7.4 %collective-permute-start.14 = (bf16[2,128,256]{2,1,0:T(8,128)(2,1)S(1)}, bf16[2,128,256]{2,1,0:T(8,128)(2,1)S(1)}, u32[]{:S(2)}, u32[]{:S(2)}) collective-permute-start(bf16[2,128,256]{2,1,0:T(8,128)(2,1)S(1)} %get-tuple-element.17), channel_id=1, source_target_pairs={{0,4},{2,6},{4,0},{6,2},{1,5},{3,7},{5,1},{7,3},{8,12},{10,14},{12... | collective-permute-start | bytes 393224 | tf_op jit(solution)/shard_map/ppermute | solution.py:124
  103.7 7.6 %collective-permute-start.13 = (bf16[2,128,256]{2,1,0:T(8,128)(2,1)S(1)}, bf16[2,128,256]{2,1,0:T(8,128)(2,1)S(1)}, u32[]{:S(2)}, u32[]{:S(2)}) collective-permute-start(bf16[2,128,256]{2,1,0:T(8,128)(2,1)S(1)} %get-tuple-element.18), channel_id=1, source_target_pairs={{0,2},{2,4},{4,6},{6,0},{1,3},{3,5},{5,7},{7,1},{8,10},{10,12},{12... | collective-permute-start | bytes 393224 | tf_op jit(solution)/shard_map/ppermute | solution.py:124

commit v3 on v2

--- a/solution.py
+++ b/solution.py
@@ -20,7 +20,7 @@
 TN = (((0,), (0,)), ((), ()))
 
 
-def attention_grad_kernel(blocks_ref, length_ref, q_ref, do_ref, kp_ref, vp_ref, kr_ref, vr_ref,
+def attention_grad_kernel(blocks_ref, length_ref, pair_ref, q_ref, do_ref, kp_ref, vp_ref, kr_ref, vr_ref,
                           dq_ref, dkr_ref, dvr_ref, dpre_ref):
     resp_rows = q_ref.shape[0]
     n_ctx, chunk_rows, _ = kp_ref.shape
@@ -82,21 +82,25 @@
     dpre_ref[:, 1] = dvp.astype(dpre_ref.dtype).reshape(n_ctx, chunk_rows, HEAD_DIM)
 
 
-def attention_grads(blocks, length, q, do, panel, kr, vr):
+def attention_grads(blocks, length, pair_index, q, do, panel, kr, vr):
     resp_rows, q_width = q.shape
     n_ctx, n_pair, _, chunk_rows, chunk_feats = panel.shape
     kv_width = kr.shape[1]
     pre_rows = n_ctx * chunk_rows
     heads = kv_width // HEAD_DIM
     per_chunk = chunk_feats // HEAD_DIM
-    qspec = pl.BlockSpec((resp_rows, GROUP * HEAD_DIM), lambda g, b, n: (0, g))
+
+    def head(g, r):
+        return ((r[0] + n_pair - g // per_chunk) % n_pair) * per_chunk + g % per_chunk
+
+    qspec = pl.BlockSpec((resp_rows, GROUP * HEAD_DIM), lambda g, b, n, r: (0, head(g, r)))
     kspec = pl.BlockSpec((n_ctx, None, None, chunk_rows, HEAD_DIM),
-                         lambda g, b, n: (0, g // per_chunk, 0, 0, g % per_chunk))
+                         lambda g, b, n, r: (0, g // per_chunk, 0, 0, g % per_chunk))
     vspec = pl.BlockSpec((n_ctx, None, None, chunk_rows, HEAD_DIM),
-                         lambda g, b, n: (0, g // per_chunk, 1, 0, g % per_chunk))
-    rspec = pl.BlockSpec((resp_rows, HEAD_DIM), lambda g, b, n: (0, g))
+                         lambda g, b, n, r: (0, g // per_chunk, 1, 0, g % per_chunk))
+    rspec = pl.BlockSpec((resp_rows, HEAD_DIM), lambda g, b, n, r: (0, head(g, r)))
     dspec = pl.BlockSpec((n_ctx, None, 2, chunk_rows, HEAD_DIM),
-                         lambda g, b, n: (0, g // per_chunk, 0, 0, g % per_chunk))
+                         lambda g, b, n, r: (0, g // per_chunk, 0, 0, g % per_chunk))
     flops = 2 * 6 * resp_rows * GROUP * heads * (pre_rows + resp_rows) * HEAD_DIM
     return pl.pallas_call(
         attention_grad_kernel,
@@ -107,7 +111,7 @@
             jax.ShapeDtypeStruct(panel.shape, jnp.bfloat16),
         ),
         grid_spec=pltpu.PrefetchScalarGridSpec(
-            num_scalar_prefetch=2,
+            num_scalar_prefetch=3,
             grid=(heads,),
             in_specs=[qspec, qspec, kspec, vspec, rspec, rspec],
             out_specs=[qspec, rspec, rspec, dspec],
@@ -117,7 +121,7 @@
             transcendentals=resp_rows * GROUP * heads * (pre_rows + resp_rows),
             bytes_accessed=2 * (2 * resp_rows * q_width + 4 * pre_rows * kv_width + 4 * resp_rows * kv_width),
         ),
-    )(blocks, length, q, do, panel, panel, kr, vr)
+    )(blocks, length, pair_index, q, do, panel, panel, kr, vr)
 
 
 def ring_shift(x, axis, n, d):
@@ -131,14 +135,13 @@
     for d in range(1, n):
         chunk = lax.dynamic_index_in_dim(planes, pair_prompt[(r + d) % n], 0, keepdims=False)
         held.append(ring_shift(chunk, "pair", n, d))
-    held = jnp.stack(held)
-    return jnp.take(held, (r - jnp.arange(n)) % n, axis=0)
+    return jnp.stack(held)
 
 
 def ctx_gather(x):
     n = lax.axis_size("ctx")
     if n != 4:
-        return lax.all_gather(x, "ctx", axis=0, tiled=False)
+        return lax.all_gather(x, "ctx", axis=0, tiled=False), jnp.arange(n, dtype=jnp.int32)
     c = lax.axis_index("ctx")
     along_x = [(i, i ^ 1) for i in range(n)]
     along_y = [(i, i ^ 2) for i in range(n)]
@@ -148,7 +151,7 @@
     far_a = lax.ppermute(from_y[..., :half, :], "ctx", along_x)
     far_b = lax.ppermute(from_x[..., half:, :], "ctx", along_y)
     held = jnp.stack([x, from_x, from_y, jnp.concatenate([far_a, far_b], -2)])
-    return jnp.take(held, jnp.bitwise_xor(jnp.arange(n), c), axis=0)
+    return held, jnp.bitwise_xor(jnp.arange(n, dtype=jnp.int32), c)
 
 
 def ctx_reduce(pieces):
@@ -156,13 +159,9 @@
     if n != 4:
         got = lax.all_to_all(pieces, "ctx", split_axis=0, concat_axis=0, tiled=True)
         return jnp.sum(got.astype(jnp.float32), axis=0).astype(jnp.bfloat16)
-    c = lax.axis_index("ctx")
     along_x = [(i, i ^ 1) for i in range(n)]
     along_y = [(i, i ^ 2) for i in range(n)]
-    mine = lax.dynamic_index_in_dim(pieces, c, 0, keepdims=False)
-    to_x = lax.dynamic_index_in_dim(pieces, jnp.bitwise_xor(c, 1), 0, keepdims=False)
-    to_y = lax.dynamic_index_in_dim(pieces, jnp.bitwise_xor(c, 2), 0, keepdims=False)
-    to_far = lax.dynamic_index_in_dim(pieces, jnp.bitwise_xor(c, 3), 0, keepdims=False)
+    mine, to_x, to_y, to_far = pieces[0], pieces[1], pieces[2], pieces[3]
     half = to_far.shape[-2] // 2
     own_x, pass_y = lax.ppermute((to_x, to_far[..., :half, :]), "ctx", along_x)
     own_y, pass_x = lax.ppermute((to_y, to_far[..., half:, :]), "ctx", along_y)
@@ -179,7 +178,7 @@
     r = lax.axis_index("pair")
     out = None
     for d in range(n):
-        chunk = lax.dynamic_index_in_dim(totals, (r + d) % n, 0, keepdims=False)
+        chunk = totals[(n - d) % n]
         got = chunk if d == 0 else ring_shift(chunk, "pair", n, d)
         source = (r - d) % n
         hits = (pair_prompt[source] == jnp.arange(n_prompts, dtype=jnp.int32)).astype(jnp.float32)
@@ -193,11 +192,13 @@
 ):
     n_prompts = prefix_kv.shape[0]
     planes = jnp.transpose(prefix_kv, (0, 2, 1, 3))
-    panel = ctx_gather(pair_gather(planes, pair_prompt))
+    panel, sources = ctx_gather(pair_gather(planes, pair_prompt))
+    chunk_blocks = panel.shape[3] // BLOCK
+    flags = prefix_blocks[0, 0].reshape(-1, chunk_blocks)[sources].reshape(-1)
 
     dq, dkr, dvr, dpre = attention_grads(
-        prefix_blocks[0, 0], resp_lengths[0, 0].reshape(1), queries[0, 0], d_out[0, 0],
-        panel, resp_keys[0, 0], resp_values[0, 0])
+        flags, resp_lengths[0, 0].reshape(1), lax.axis_index("pair").reshape(1).astype(jnp.int32),
+        queries[0, 0], d_out[0, 0], panel, resp_keys[0, 0], resp_values[0, 0])
     d_queries = dq[None, None]
     d_resp_keys = dkr[None, None]
     d_resp_values = dvr[None, None]

time: 113 us -> 110 us (0.973)
  other arithmetic: 9.14 us -> 7.02 us
  local copies, waits for them, and re-layouts: 8.11 us -> 6.71 us
    ppermute x1, waiting for transfers between devices: 0.01 us -> 9.98 us  [ctx_gather(): from_x = lax.ppermute(x, 'ctx', along_x)]
    ppermute x1, waiting for transfers between devices: 9.98 us -> 0.01 us  [ctx_gather(): from_y = lax.ppermute(x, 'ctx', along_y)]
    select_n x5 -> x1, other arithmetic: 3.41 us -> 0.01 us  [shards(): flags = prefix_blocks[0, 0].reshape(-1, chunk_blocks)[sources].reshape(-1)]
    ppermute x1, waiting for transfers between devices: 2.88 us -> 1.24 us  [ctx_gather(): far_a = lax.ppermute(from_y[..., :half, :], 'ctx', along_x)]
    gather x2 -> x1, local copies, waits for them, and re-layouts: 2.57 us -> 1.14 us  [shards(): flags = prefix_blocks[0, 0].reshape(-1, chunk_blocks)[sources].reshape(-1)]
    another operation x2 -> x3, other arithmetic: 0.3 us -> 1.72 us  [ctx_gather(): held = jnp.stack([x, from_x, from_y, jnp.concatenate([far_a, far_b], -2)])]
  transfers between devices with their start and end apart: 16 -> 16, of which waited for: 9 -> 10; matrix products, arithmetic and copies ran while one was open for 3% -> 4% of each run, Pallas kernels for 0% -> 0%
where the time goes in v3:
time: 110 us; the launch traced here: 109 us
  waiting for transfers between devices  47.5 us (43%)
  starting transfers between devices  21.9 us (20%)
  Pallas kernels  16.7 us (15%)
  between operations  9.36 us (9%)
  other arithmetic  7.02 us (6%)
  local copies, waits for them, and re-layouts  6.71 us (6%)
    ppermute x6, waiting for transfers between devices, ring_shift(): return lax.ppermute(x, axis, [(i, (i + d) % n) for i in range(n)])  17 us
    pallas_call x1, Pallas kernels, attention_grads(): pl.pallas_call(attention_grad_kernel, out_shape=(jax.ShapeDtypeStruct((re...  16.7 us
    ppermute x1, waiting for transfers between devices, ctx_reduce(): far_a = lax.ppermute(pass_y, 'ctx', along_y)  12.1 us
    ppermute x1, waiting for transfers between devices, ctx_gather(): from_x = lax.ppermute(x, 'ctx', along_x)  9.98 us
    ppermute x6, starting transfers between devices, ring_shift(): return lax.ppermute(x, axis, [(i, (i + d) % n) for i in range(n)])  9.68 us
    ppermute x2, waiting for transfers between devices, ctx_reduce(): own_x, pass_y = lax.ppermute((to_x, to_far[..., :half, :]), 'ctx', along_x)  5.19 us
    convert_element_type x2, other arithmetic, pair_reduce(): (pair_prompt[source] == jnp.arange(n_prompts, dtype=jnp.int32)).astype(jn...  2.52 us
  transfers between devices with their start and end apart: 16, of which 10 were waited for; matrix products, arithmetic and copies ran while one was open for 4% of the time, Pallas kernels for 0%

profile of v3, /device:TPU:0, one launch (start us, length us, event | category | flops | bytes accessed | tf_op | source)
XLA Modules:
  0.0 109.2 jit_solution(7185666058638057836)
XLA Ops:
  0.8 1.6 %fusion.5 = (s32[1]{0:T(128)}, s32[1]{0:T(128)}, s32[1]{0:T(128)}, s32[1]{0:T(128)}, s32[1]{0:T(128)}, /*index=5*/s32[1]{0:T(128)}, s32[1]{0:T(128)}, s32[1]{0:T(128)}) fusion(s32[4]{0:T(128)} %param.15, s32[]{:T(128)S(6)} %select_n.91, s32[]{:T(128)S(6)} %select_n.93, s32[]{:T(128)S(6)} %select_n.88, s32[]{:T(128)S(6)} %select_n.85, s32[]{:T(128)S(6)} %select_n.82, ...), kind=kLoop, calls=%fused_computation.36 | loop fusion | bytes 96 | tf_op jit(solution)/shard_map/dynamic_slice | solution.py:184
  10.2 1.5 %constant_dynamic-slice_fusion.3 = (bf16[1,128,2,256]{3,2,1,0:T(2,128)(2,1)S(1)}, bf16[1,128,2,256]{3,2,1,0:T(2,128)(2,1)S(1)}, bf16[1,128,2,256]{3,2,1,0:T(2,128)(2,1)S(1)}, bf16[1,128,2,256]{3,2,1,0:T(2,128)(2,1)S(1)}) fusion(bf16[2,128,2,256]{3,2,1,0:T(2,128)(2,1)} %param.12, s32[]{:T(128)S(6)} %select_n.80, s32[]{:T(128)S(6)} %select_n.86, ...), kind=kLoop, calls=%fused_computation.32 | loop fusion | bytes 1048592 | tf_op jit(solution)/shard_map/dynamic-slice
  11.7 5.1 %collective-permute-start.2 = (bf16[2,128,256]{2,1,0:T(8,128)(2,1)S(1)}, bf16[2,128,256]{2,1,0:T(8,128)(2,1)S(1)}, u32[]{:S(2)}, u32[]{:S(2)}) collective-permute-start(bf16[2,128,256]{2,1,0:T(8,128)(2,1)S(1)} %bitcast.83), channel_id=1, source_target_pairs={{0,6},{2,0},{4,2},{6,4},{1,7},{3,1},{5,3},{7,5},{8,14},{10,8},{12,... | collective-permute-start | bytes 393224 | tf_op jit(solution)/shard_map/ppermute | solution.py:128
  18.0 2.7 %collective-permute-done.2 = bf16[2,128,256]{2,1,0:T(8,128)(2,1)S(1)} collective-permute-done((bf16[2,128,256]{2,1,0:T(8,128)(2,1)S(1)}, bf16[2,128,256]{2,1,0:T(8,128)(2,1)S(1)}, u32[]{:S(2)}, u32[]{:S(2)}) %collective-permute-start.2) | collective-permute-done | bytes 131104 | tf_op jit(solution)/shard_map/ppermute | solution.py:128
  20.7 4.4 %collective-permute-done = bf16[2,128,256]{2,1,0:T(8,128)(2,1)S(1)} collective-permute-done((bf16[2,128,256]{2,1,0:T(8,128)(2,1)S(1)}, bf16[2,128,256]{2,1,0:T(8,128)(2,1)S(1)}, u32[]{:S(2)}, u32[]{:S(2)}) %collective-permute-start) | collective-permute-done | bytes 131104 | tf_op jit(solution)/shard_map/ppermute | solution.py:128
  25.1 3.3 %collective-permute-done.1 = bf16[2,128,256]{2,1,0:T(8,128)(2,1)S(1)} collective-permute-done((bf16[2,128,256]{2,1,0:T(8,128)(2,1)S(1)}, bf16[2,128,256]{2,1,0:T(8,128)(2,1)S(1)}, u32[]{:S(2)}, u32[]{:S(2)}) %collective-permute-start.1) | collective-permute-done | bytes 131104 | tf_op jit(solution)/shard_map/ppermute | solution.py:128
  28.5 1.6 %collective-permute-start.3 = (bf16[4,2,128,256]{3,2,1,0:T(8,128)(2,1)S(1)}, bf16[4,2,128,256]{3,2,1,0:T(8,128)(2,1)S(1)}, u32[]{:S(2)}, u32[]{:S(2)}) collective-permute-start(bf16[4,2,128,256]{3,2,1,0:T(8,128)(2,1)S(1)} %get-tuple-element.22), channel_id=1, source_target_pairs={{0,8},{8,0},{16,24},{24,16},{1,9},{9,1},{17,25},{25,17},{2,10},{10... | collective-permute-start | bytes 1572872 | tf_op jit(solution)/shard_map/ppermute | solution.py:148
  30.1 1.5 %collective-permute-start.4 = (bf16[4,2,128,256]{3,2,1,0:T(8,128)(2,1)S(1)}, bf16[4,2,128,256]{3,2,1,0:T(8,128)(2,1)S(1)}, u32[]{:S(2)}, u32[]{:S(2)}) collective-permute-start(bf16[4,2,128,256]{3,2,1,0:T(8,128)(2,1)S(1)} %get-tuple-element.22), channel_id=1, source_target_pairs={{0,16},{8,24},{16,0},{24,8},{1,17},{9,25},{17,1},{25,9},{2,18},{10... | collective-permute-start | bytes 1572872 | tf_op jit(solution)/shard_map/ppermute | solution.py:149
  31.6 10.0 %collective-permute-done.3 = bf16[4,2,128,256]{3,2,1,0:T(8,128)(2,1)S(1)} collective-permute-done((bf16[4,2,128,256]{3,2,1,0:T(8,128)(2,1)S(1)}, bf16[4,2,128,256]{3,2,1,0:T(8,128)(2,1)S(1)}, u32[]{:S(2)}, u32[]{:S(2)}) %collective-permute-start.3) | collective-permute-done | bytes 524320 | tf_op jit(solution)/shard_map/ppermute | solution.py:148
  41.6 1.6 %collective-permute-start.6 = (bf16[4,2,64,256]{3,2,1,0:T(8,128)(2,1)S(1)}, bf16[4,2,64,256]{3,2,1,0:T(8,128)(2,1)S(1)}, u32[]{:S(2)}, u32[]{:S(2)}) collective-permute-start(bf16[4,2,64,256]{3,2,1,0:T(8,128)(2,1)S(1)} %slice.51), channel_id=1, source_target_pairs={{0,16},{8,24},{16,0},{24,8},{1,17},{9,25},{17,1},{25,9},{2,18},{10... | collective-permute-start | bytes 786440 | tf_op jit(solution)/shard_map/ppermute | solution.py:152
  43.2 1.6 %collective-permute-start.5 = (bf16[4,2,64,256]{3,2,1,0:T(8,128)(2,1)S(1)}, bf16[4,2,64,256]{3,2,1,0:T(8,128)(2,1)S(1)}, u32[]{:S(2)}, u32[]{:S(2)}) collective-permute-start(bf16[4,2,64,256]{3,2,1,0:T(8,128)(2,1)S(1)} %slice.50), channel_id=1, source_target_pairs={{0,8},{8,0},{16,24},{24,16},{1,9},{9,1},{17,25},{25,17},{2,10},{10... | collective-permute-start | bytes 786440 | tf_op jit(solution)/shard_map/ppermute | solution.py:151
  46.6 1.8 %collective-permute-done.6 = bf16[4,2,64,256]{3,2,1,0:T(8,128)(2,1)S(1)} collective-permute-done((bf16[4,2,64,256]{3,2,1,0:T(8,128)(2,1)S(1)}, bf16[4,2,64,256]{3,2,1,0:T(8,128)(2,1)S(1)}, u32[]{:S(2)}, u32[]{:S(2)}) %collective-permute-start.6) | collective-permute-done | bytes 262176 | tf_op jit(solution)/shard_map/ppermute | solution.py:152
  49.7 1.6 %pad_maximum_fusion.kp_ref.vp_ref = bf16[4,4,2,128,256]{4,3,2,1,0:T(8,128)(2,1)} fusion(bf16[1,4,2,128,256]{4,3,2,1,0:T(8,128)(2,1)S(1)} %maximum_bitcast_fusion, bf16[1,4,2,128,256]{4,3,2,1,0:T(8,128)(2,1)S(1)} %bitcast.78, bf16[1,4,2,128,256]{4,3,2,1,0:T(8,128)(2,1)S(1)} %bitcast.77, bf16[1,4,2,128,256]{4,3,2,1,0:T(8,128)(2,1)S(1)} %get-tuple-element.21), kind=kLoop, calls=%fused_computation.1 | loop fusion | flops 3145728 | bytes 4194304 | tf_op jit(solution)/shard_map/stack | solution.py:153
  51.3 16.7 %shard_map.111 = (bf16[128,2048]{1,0:T(8,128)(2,1)}, bf16[128,1024]{1,0:T(8,128)(2,1)}, bf16[128,1024]{1,0:T(8,128)(2,1)}, bf16[4,4,2,128,256]{4,3,2,1,0:T(8,128)(2,1)}) custom-call(s32[4]{0:T(128)} %gather_fusion, s32[1]{0:T(128)} %bitcast.75.length_ref, s32[1]{0:T(128)} %bitcast.3.pair_ref, bf16[128,2048]{1,0:T(8,128)(2,1)} %bitcast.86, ...), custom_call_target="tpu_custom_call" | custom-call | flops 2013265920 | bytes 6291456 | tf_op jit(solution)/shard_map/pallas_call | solution.py:105
  68.0 1.5 %slice_bitcast_fusion = (bf16[4,2,128,256]{3,2,1,0:T(8,128)(2,1)S(1)}, bf16[4,2,128,256]{3,2,1,0:T(8,128)(2,1)S(1)}, bf16[4,2,128,256]{3,2,1,0:T(8,128)(2,1)S(1)}) fusion(bf16[4,4,2,128,256]{4,3,2,1,0:T(8,128)(2,1)} %get-tuple-element.11), kind=kLoop, calls=%fused_computation.8 | loop fusion | bytes 3145728 | tf_op jit(solution)/shard_map/squeeze | solution.py:164
  69.5 1.5 %collective-permute-start.9 = (bf16[4,2,64,256]{3,2,1,0:T(8,128)(2,1)S(1)}, bf16[4,2,64,256]{3,2,1,0:T(8,128)(2,1)S(1)}, u32[]{:S(2)}, u32[]{:S(2)}) collective-permute-start(bf16[4,2,64,256]{3,2,1,0:T(8,128)(2,1)S(1)} %get-tuple-element.19), channel_id=1, source_target_pairs={{0,8},{8,0},{16,24},{24,16},{1,9},{9,1},{17,25},{25,17},{2,10},{10... | collective-permute-start | bytes 786440 | tf_op jit(solution)/shard_map/ppermute | solution.py:166
  71.6 1.5 %collective-permute-start.8 = (bf16[4,2,128,256]{3,2,1,0:T(8,128)(2,1)S(1)}, bf16[4,2,128,256]{3,2,1,0:T(8,128)(2,1)S(1)}, u32[]{:S(2)}, u32[]{:S(2)}) collective-permute-start(bf16[4,2,128,256]{3,2,1,0:T(8,128)(2,1)S(1)} %get-tuple-element.13), channel_id=1, source_target_pairs={{0,16},{8,24},{16,0},{24,8},{1,17},{9,25},{17,1},{25,9},{2,18},{10... | collective-permute-start | bytes 1572872 | tf_op jit(solution)/shard_map/ppermute | solution.py:167
  73.6 5.2 %collective-permute-done.9 = bf16[4,2,64,256]{3,2,1,0:T(8,128)(2,1)S(1)} collective-permute-done((bf16[4,2,64,256]{3,2,1,0:T(8,128)(2,1)S(1)}, bf16[4,2,64,256]{3,2,1,0:T(8,128)(2,1)S(1)}, u32[]{:S(2)}, u32[]{:S(2)}) %collective-permute-start.9) | collective-permute-done | bytes 262176 | tf_op jit(solution)/shard_map/ppermute | solution.py:166
  78.8 1.3 %collective-permute-start.10 = (bf16[4,2,64,256]{3,2,1,0:T(8,128)(2,1)S(1)}, bf16[4,2,64,256]{3,2,1,0:T(8,128)(2,1)S(1)}, u32[]{:S(2)}, u32[]{:S(2)}) collective-permute-start(bf16[4,2,64,256]{3,2,1,0:T(8,128)(2,1)S(1)} %collective-permute-done.9), channel_id=1, source_target_pairs={{0,16},{8,24},{16,0},{24,8},{1,17},{9,25},{17,1},{25,9},{2,18},{10... | collective-permute-start | bytes 786440 | tf_op jit(solution)/shard_map/ppermute | solution.py:168
  80.9 12.1 %collective-permute-done.10 = bf16[4,2,64,256]{3,2,1,0:T(8,128)(2,1)S(1)} collective-permute-done((bf16[4,2,64,256]{3,2,1,0:T(8,128)(2,1)S(1)}, bf16[4,2,64,256]{3,2,1,0:T(8,128)(2,1)S(1)}, u32[]{:S(2)}, u32[]{:S(2)}) %collective-permute-start.10) | collective-permute-done | bytes 262176 | tf_op jit(solution)/shard_map/ppermute | solution.py:168
  93.0 1.3 %fusion.1 = bf16[4,2,128,256]{3,2,1,0:T(8,128)(2,1)S(1)} fusion(bf16[4,2,128,256]{3,2,1,0:T(8,128)(2,1)S(1)} %collective-permute-done.8, bf16[4,2,128,256]{3,2,1,0:T(8,128)(2,1)S(1)} %collective-permute-done.7, bf16[4,2,64,256]{3,2,1,0:T(8,128)(2,1)S(1)} %collective-permute-done.12, bf16[4,2,64,256]{3,2,1,0:T(8,128)(2,1)S(1)} %collective-permute-done.10, ...), kind=kLoop, calls=%fused_computation.4 | loop fusion | flops 2883584 | bytes 2621440 | tf_op jit(solution)/shard_map/convert_element_type | solution.py:173
  94.4 2.8 %collective-permute-start.15 = (bf16[2,128,256]{2,1,0:T(8,128)(2,1)S(1)}, bf16[2,128,256]{2,1,0:T(8,128)(2,1)S(1)}, u32[]{:S(2)}, u32[]{:S(2)}) collective-permute-start(bf16[2,128,256]{2,1,0:T(8,128)(2,1)S(1)} %get-tuple-element.16), channel_id=1, source_target_pairs={{0,6},{2,0},{4,2},{6,4},{1,7},{3,1},{5,3},{7,5},{8,14},{10,8},{12,... | collective-permute-start | bytes 393224 | tf_op jit(solution)/shard_map/ppermute | solution.py:128
  100.8 6.6 %collective-permute-done.14 = bf16[2,128,256]{2,1,0:T(8,128)(2,1)S(1)} collective-permute-done((bf16[2,128,256]{2,1,0:T(8,128)(2,1)S(1)}, bf16[2,128,256]{2,1,0:T(8,128)(2,1)S(1)}, u32[]{:S(2)}, u32[]{:S(2)}) %collective-permute-start.14) | collective-permute-done | bytes 131104 | tf_op jit(solution)/shard_map/ppermute | solution.py:128
  107.9 1.3 %multiply_add_fusion = f32[2,128,2,256]{3,2,1,0:T(2,128)} fusion(f32[128,2,256]{2,1,0:T(2,128)S(1)} %copy.27, f32[128,2,256]{2,1,0:T(2,128)S(1)} %copy.26, f32[128,2,256]{2,1,0:T(2,128)S(1)} %copy.25, f32[128,2,256]{2,1,0:T(2,128)S(1)} %copy.24, f32[2]{0:T(128)S(1)} %get-tuple-element.35, f32[2]{0:T(128)S(1)} %get-tuple-element.36, ...), kind=kLoop, calls=%fused_computation.7 | loop fusion | flops 917504 | bytes 1572896 | tf_op jit(solution)/shard_map/add | solution.py:186
  (39 shorter events, 9.6 us)
Async XLA Ops:
  0.6 44.8 %copy-start = (s32[1,1,4]{2,1,0:T(1,128)S(1)}, s32[1,1,4]{2,1,0:T(1,128)}, u32[]{:S(2)}) copy-start(s32[1,1,4]{2,1,0:T(1,128)} %param.13) | copy-start | bytes 52
  11.7 9.0 %collective-permute-start.2 = (bf16[2,128,256]{2,1,0:T(8,128)(2,1)S(1)}, bf16[2,128,256]{2,1,0:T(8,128)(2,1)S(1)}, u32[]{:S(2)}, u32[]{:S(2)}) collective-permute-start(bf16[2,128,256]{2,1,0:T(8,128)(2,1)S(1)} %bitcast.83), channel_id=1, source_target_pairs={{0,6},{2,0},{4,2},{6,4},{1,7},{3,1},{5,3},{7,5},{8,14},{10,8},{12,... | collective-permute-start | bytes 393224 | tf_op jit(solution)/shard_map/ppermute | solution.py:128
  16.8 8.3 %collective-permute-start = (bf16[2,128,256]{2,1,0:T(8,128)(2,1)S(1)}, bf16[2,128,256]{2,1,0:T(8,128)(2,1)S(1)}, u32[]{:S(2)}, u32[]{:S(2)}) collective-permute-start(bf16[2,128,256]{2,1,0:T(8,128)(2,1)S(1)} %bitcast.84), channel_id=1, source_target_pairs={{0,2},{2,4},{4,6},{6,0},{1,3},{3,5},{5,7},{7,1},{8,10},{10,12},{12... | collective-permute-start | bytes 393224 | tf_op jit(solution)/shard_map/ppermute | solution.py:128
  16.9 11.5 %collective-permute-start.1 = (bf16[2,128,256]{2,1,0:T(8,128)(2,1)S(1)}, bf16[2,128,256]{2,1,0:T(8,128)(2,1)S(1)}, u32[]{:S(2)}, u32[]{:S(2)}) collective-permute-start(bf16[2,128,256]{2,1,0:T(8,128)(2,1)S(1)} %bitcast.85), channel_id=1, source_target_pairs={{0,4},{2,6},{4,0},{6,2},{1,5},{3,7},{5,1},{7,3},{8,12},{10,14},{12... | collective-permute-start | bytes 393224 | tf_op jit(solution)/shard_map/ppermute | solution.py:128
  28.5 13.1 %collective-permute-start.3 = (bf16[4,2,128,256]{3,2,1,0:T(8,128)(2,1)S(1)}, bf16[4,2,128,256]{3,2,1,0:T(8,128)(2,1)S(1)}, u32[]{:S(2)}, u32[]{:S(2)}) collective-permute-start(bf16[4,2,128,256]{3,2,1,0:T(8,128)(2,1)S(1)} %get-tuple-element.22), channel_id=1, source_target_pairs={{0,8},{8,0},{16,24},{24,16},{1,9},{9,1},{17,25},{25,17},{2,10},{10... | collective-permute-start | bytes 1572872 | tf_op jit(solution)/shard_map/ppermute | solution.py:148
  30.1 13.1 %collective-permute-start.4 = (bf16[4,2,128,256]{3,2,1,0:T(8,128)(2,1)S(1)}, bf16[4,2,128,256]{3,2,1,0:T(8,128)(2,1)S(1)}, u32[]{:S(2)}, u32[]{:S(2)}) collective-permute-start(bf16[4,2,128,256]{3,2,1,0:T(8,128)(2,1)S(1)} %get-tuple-element.22), channel_id=1, source_target_pairs={{0,16},{8,24},{16,0},{24,8},{1,17},{9,25},{17,1},{25,9},{2,18},{10... | collective-permute-start | bytes 1572872 | tf_op jit(solution)/shard_map/ppermute | solution.py:149
  41.6 6.8 %collective-permute-start.6 = (bf16[4,2,64,256]{3,2,1,0:T(8,128)(2,1)S(1)}, bf16[4,2,64,256]{3,2,1,0:T(8,128)(2,1)S(1)}, u32[]{:S(2)}, u32[]{:S(2)}) collective-permute-start(bf16[4,2,64,256]{3,2,1,0:T(8,128)(2,1)S(1)} %slice.51), channel_id=1, source_target_pairs={{0,16},{8,24},{16,0},{24,8},{1,17},{9,25},{17,1},{25,9},{2,18},{10... | collective-permute-start | bytes 786440 | tf_op jit(solution)/shard_map/ppermute | solution.py:152
  43.2 6.4 %collective-permute-start.5 = (bf16[4,2,64,256]{3,2,1,0:T(8,128)(2,1)S(1)}, bf16[4,2,64,256]{3,2,1,0:T(8,128)(2,1)S(1)}, u32[]{:S(2)}, u32[]{:S(2)}) collective-permute-start(bf16[4,2,64,256]{3,2,1,0:T(8,128)(2,1)S(1)} %slice.50), channel_id=1, source_target_pairs={{0,8},{8,0},{16,24},{24,16},{1,9},{9,1},{17,25},{25,17},{2,10},{10... | collective-permute-start | bytes 786440 | tf_op jit(solution)/shard_map/ppermute | solution.py:151
  69.5 9.3 %collective-permute-start.9 = (bf16[4,2,64,256]{3,2,1,0:T(8,128)(2,1)S(1)}, bf16[4,2,64,256]{3,2,1,0:T(8,128)(2,1)S(1)}, u32[]{:S(2)}, u32[]{:S(2)}) collective-permute-start(bf16[4,2,64,256]{3,2,1,0:T(8,128)(2,1)S(1)} %get-tuple-element.19), channel_id=1, source_target_pairs={{0,8},{8,0},{16,24},{24,16},{1,9},{9,1},{17,25},{25,17},{2,10},{10... | collective-permute-start | bytes 786440 | tf_op jit(solution)/shard_map/ppermute | solution.py:166
  71.1 9.2 %collective-permute-start.11 = (bf16[4,2,64,256]{3,2,1,0:T(8,128)(2,1)S(1)}, bf16[4,2,64,256]{3,2,1,0:T(8,128)(2,1)S(1)}, u32[]{:S(2)}, u32[]{:S(2)}) collective-permute-start(bf16[4,2,64,256]{3,2,1,0:T(8,128)(2,1)S(1)} %get-tuple-element.20), channel_id=1, source_target_pairs={{0,16},{8,24},{16,0},{24,8},{1,17},{9,25},{17,1},{25,9},{2,18},{10... | collective-permute-start | bytes 786440 | tf_op jit(solution)/shard_map/ppermute | solution.py:167
  71.6 21.4 %collective-permute-start.8 = (bf16[4,2,128,256]{3,2,1,0:T(8,128)(2,1)S(1)}, bf16[4,2,128,256]{3,2,1,0:T(8,128)(2,1)S(1)}, u32[]{:S(2)}, u32[]{:S(2)}) collective-permute-start(bf16[4,2,128,256]{3,2,1,0:T(8,128)(2,1)S(1)} %get-tuple-element.13), channel_id=1, source_target_pairs={{0,16},{8,24},{16,0},{24,8},{1,17},{9,25},{17,1},{25,9},{2,18},{10... | collective-permute-start | bytes 1572872 | tf_op jit(solution)/shard_map/ppermute | solution.py:167
  73.1 19.9 %collective-permute-start.7 = (bf16[4,2,128,256]{3,2,1,0:T(8,128)(2,1)S(1)}, bf16[4,2,128,256]{3,2,1,0:T(8,128)(2,1)S(1)}, u32[]{:S(2)}, u32[]{:S(2)}) collective-permute-start(bf16[4,2,128,256]{3,2,1,0:T(8,128)(2,1)S(1)} %get-tuple-element.14), channel_id=1, source_target_pairs={{0,8},{8,0},{16,24},{24,16},{1,9},{9,1},{17,25},{25,17},{2,10},{10... | collective-permute-start | bytes 1572872 | tf_op jit(solution)/shard_map/ppermute | solution.py:166
  78.8 14.1 %collective-permute-start.10 = (bf16[4,2,64,256]{3,2,1,0:T(8,128)(2,1)S(1)}, bf16[4,2,64,256]{3,2,1,0:T(8,128)(2,1)S(1)}, u32[]{:S(2)}, u32[]{:S(2)}) collective-permute-start(bf16[4,2,64,256]{3,2,1,0:T(8,128)(2,1)S(1)} %collective-permute-done.9), channel_id=1, source_target_pairs={{0,16},{8,24},{16,0},{24,8},{1,17},{9,25},{17,1},{25,9},{2,18},{10... | collective-permute-start | bytes 786440 | tf_op jit(solution)/shard_map/ppermute | solution.py:168
  80.3 12.7 %collective-permute-start.12 = (bf16[4,2,64,256]{3,2,1,0:T(8,128)(2,1)S(1)}, bf16[4,2,64,256]{3,2,1,0:T(8,128)(2,1)S(1)}, u32[]{:S(2)}, u32[]{:S(2)}) collective-permute-start(bf16[4,2,64,256]{3,2,1,0:T(8,128)(2,1)S(1)} %collective-permute-done.11), channel_id=1, source_target_pairs={{0,8},{8,0},{16,24},{24,16},{1,9},{9,1},{17,25},{25,17},{2,10},{10... | collective-permute-start | bytes 786440 | tf_op jit(solution)/shard_map/ppermute | solution.py:169
  94.4 6.2 %collective-permute-start.15 = (bf16[2,128,256]{2,1,0:T(8,128)(2,1)S(1)}, bf16[2,128,256]{2,1,0:T(8,128)(2,1)S(1)}, u32[]{:S(2)}, u32[]{:S(2)}) collective-permute-start(bf16[2,128,256]{2,1,0:T(8,128)(2,1)S(1)} %get-tuple-element.16), channel_id=1, source_target_pairs={{0,6},{2,0},{4,2},{6,4},{1,7},{3,1},{5,3},{7,5},{8,14},{10,8},{12,... | collective-permute-start | bytes 393224 | tf_op jit(solution)/shard_map/ppermute | solution.py:128
  99.9 7.4 %collective-permute-start.14 = (bf16[2,128,256]{2,1,0:T(8,128)(2,1)S(1)}, bf16[2,128,256]{2,1,0:T(8,128)(2,1)S(1)}, u32[]{:S(2)}, u32[]{:S(2)}) collective-permute-start(bf16[2,128,256]{2,1,0:T(8,128)(2,1)S(1)} %get-tuple-element.17), channel_id=1, source_target_pairs={{0,4},{2,6},{4,0},{6,2},{1,5},{3,7},{5,1},{7,3},{8,12},{10,14},{12... | collective-permute-start | bytes 393224 | tf_op jit(solution)/shard_map/ppermute | solution.py:128
  100.0 7.6 %collective-permute-start.13 = (bf16[2,128,256]{2,1,0:T(8,128)(2,1)S(1)}, bf16[2,128,256]{2,1,0:T(8,128)(2,1)S(1)}, u32[]{:S(2)}, u32[]{:S(2)}) collective-permute-start(bf16[2,128,256]{2,1,0:T(8,128)(2,1)S(1)} %get-tuple-element.18), channel_id=1, source_target_pairs={{0,2},{2,4},{4,6},{6,0},{1,3},{3,5},{5,7},{7,1},{8,10},{10,12},{12... | collective-permute-start | bytes 393224 | tf_op jit(solution)/shard_map/ppermute | solution.py:128

commit v4 on v3

--- a/solution.py
+++ b/solution.py
@@ -11,6 +11,7 @@
 GROUP = 2
 HEAD_DIM = 128
 BLOCK = 128
+HEAD_GROUPS = 2
 
 
 scale_factor = 144.0 ** (-0.5)
@@ -20,8 +21,9 @@
 TN = (((0,), (0,)), ((), ()))
 
 
-def attention_grad_kernel(blocks_ref, length_ref, pair_ref, q_ref, do_ref, kp_ref, vp_ref, kr_ref, vr_ref,
-                          dq_ref, dkr_ref, dvr_ref, dpre_ref):
+def attention_grad_kernel(aliased, blocks_ref, length_ref, pair_ref, q_ref, do_ref, kp_ref, vp_ref, kr_ref, vr_ref,
+                          *refs):
+    dq_ref, dkr_ref, dvr_ref, dpre_ref = refs[3:] if aliased else refs
     resp_rows = q_ref.shape[0]
     n_ctx, chunk_rows, _ = kp_ref.shape
     pre_rows = n_ctx * chunk_rows
@@ -82,16 +84,17 @@
     dpre_ref[:, 1] = dvp.astype(dpre_ref.dtype).reshape(n_ctx, chunk_rows, HEAD_DIM)
 
 
-def attention_grads(blocks, length, pair_index, q, do, panel, kr, vr):
+def attention_grads(blocks, length, pair_index, q, do, panel, kr, vr, first_head, earlier):
     resp_rows, q_width = q.shape
     n_ctx, n_pair, _, chunk_rows, chunk_feats = panel.shape
     kv_width = kr.shape[1]
     pre_rows = n_ctx * chunk_rows
-    heads = kv_width // HEAD_DIM
+    chunk_heads = kv_width // n_pair // HEAD_DIM
     per_chunk = chunk_feats // HEAD_DIM
+    heads = n_pair * per_chunk
 
     def head(g, r):
-        return ((r[0] + n_pair - g // per_chunk) % n_pair) * per_chunk + g % per_chunk
+        return ((r[0] + n_pair - g // per_chunk) % n_pair) * chunk_heads + first_head + g % per_chunk
 
     qspec = pl.BlockSpec((resp_rows, GROUP * HEAD_DIM), lambda g, b, n, r: (0, head(g, r)))
     kspec = pl.BlockSpec((n_ctx, None, None, chunk_rows, HEAD_DIM),
@@ -102,8 +105,15 @@
     dspec = pl.BlockSpec((n_ctx, None, 2, chunk_rows, HEAD_DIM),
                          lambda g, b, n, r: (0, g // per_chunk, 0, 0, g % per_chunk))
     flops = 2 * 6 * resp_rows * GROUP * heads * (pre_rows + resp_rows) * HEAD_DIM
+    in_specs = [qspec, qspec, kspec, vspec, rspec, rspec]
+    operands = [blocks, length, pair_index, q, do, panel, panel, kr, vr]
+    aliases = {}
+    if earlier is not None:
+        in_specs += [pl.BlockSpec(memory_space=pl.ANY)] * 3
+        aliases = {len(operands) + i: i for i in range(3)}
+        operands += list(earlier)
     return pl.pallas_call(
-        attention_grad_kernel,
+        functools.partial(attention_grad_kernel, earlier is not None),
         out_shape=(
             jax.ShapeDtypeStruct((resp_rows, q_width), jnp.bfloat16),
             jax.ShapeDtypeStruct((resp_rows, kv_width), jnp.bfloat16),
@@ -113,15 +123,16 @@
         grid_spec=pltpu.PrefetchScalarGridSpec(
             num_scalar_prefetch=3,
             grid=(heads,),
-            in_specs=[qspec, qspec, kspec, vspec, rspec, rspec],
+            in_specs=in_specs,
             out_specs=[qspec, rspec, rspec, dspec],
         ),
+        input_output_aliases=aliases,
         cost_estimate=pl.CostEstimate(
             flops=flops,
             transcendentals=resp_rows * GROUP * heads * (pre_rows + resp_rows),
-            bytes_accessed=2 * (2 * resp_rows * q_width + 4 * pre_rows * kv_width + 4 * resp_rows * kv_width),
-        ),
-    )(blocks, length, pair_index, q, do, panel, panel, kr, vr)
+            bytes_accessed=2 * heads * HEAD_DIM * (4 * resp_rows * GROUP + 4 * pre_rows + 4 * resp_rows),
+        ),
+    )(*operands)
 
 
 def ring_shift(x, axis, n, d):
@@ -192,20 +203,24 @@
 ):
     n_prompts = prefix_kv.shape[0]
     planes = jnp.transpose(prefix_kv, (0, 2, 1, 3))
-    panel, sources = ctx_gather(pair_gather(planes, pair_prompt))
-    chunk_blocks = panel.shape[3] // BLOCK
-    flags = prefix_blocks[0, 0].reshape(-1, chunk_blocks)[sources].reshape(-1)
-
-    dq, dkr, dvr, dpre = attention_grads(
-        flags, resp_lengths[0, 0].reshape(1), lax.axis_index("pair").reshape(1).astype(jnp.int32),
-        queries[0, 0], d_out[0, 0], panel, resp_keys[0, 0], resp_values[0, 0])
-    d_queries = dq[None, None]
-    d_resp_keys = dkr[None, None]
-    d_resp_values = dvr[None, None]
-
-    ctx_total = ctx_reduce(dpre)
-    d_prefix = pair_reduce(ctx_total, pair_prompt, n_prompts)
-    return (d_queries, d_resp_keys, d_resp_values, d_prefix)
+    chunk_feats = planes.shape[-1]
+    n_groups = HEAD_GROUPS if chunk_feats % (HEAD_GROUPS * HEAD_DIM) == 0 else 1
+    group_feats = chunk_feats // n_groups
+    pair_index = lax.axis_index("pair").reshape(1).astype(jnp.int32)
+    earlier = None
+    parts = []
+    for k in range(n_groups):
+        cols = slice(k * group_feats, (k + 1) * group_feats)
+        panel, sources = ctx_gather(pair_gather(planes[..., cols], pair_prompt))
+        chunk_blocks = panel.shape[3] // BLOCK
+        flags = prefix_blocks[0, 0].reshape(-1, chunk_blocks)[sources].reshape(-1)
+        dq, dkr, dvr, dpre = attention_grads(
+            flags, resp_lengths[0, 0].reshape(1), pair_index, queries[0, 0], d_out[0, 0], panel,
+            resp_keys[0, 0], resp_values[0, 0], k * (group_feats // HEAD_DIM), earlier)
+        earlier = (dq, dkr, dvr)
+        parts.append(pair_reduce(ctx_reduce(dpre), pair_prompt, n_prompts))
+    d_prefix = parts[0] if n_groups == 1 else jnp.concatenate(parts, -1)
+    return (dq[None, None], dkr[None, None], dvr[None, None], d_prefix)
 
 
 def solution(mesh):

time: 110 us -> 107 us (0.973)
  waiting for transfers between devices: 47.5 us -> 27.2 us
  starting transfers between devices: 21.9 us -> 37.4 us
  Pallas kernels: 16.7 us -> 18.9 us
    ppermute x1 -> x2, waiting for transfers between devices: 12.1 us -> 2.2 us  [ctx_reduce(): far_a = lax.ppermute(pass_y, 'ctx', along_y)]
    ppermute x1 -> x2, waiting for transfers between devices: 9.98 us -> 2.74 us  [ctx_gather(): from_x = lax.ppermute(x, 'ctx', along_x)]
    ppermute x6 -> x12, starting transfers between devices: 9.68 us -> 16 us  [ring_shift(): return lax.ppermute(x, axis, [(i, (i + d) % n) for i in range(n)])]
    ppermute x2 -> x4, waiting for transfers between devices: 5.19 us -> 0.62 us  [ctx_reduce(): own_x, pass_y = lax.ppermute((to_x, to_far[..., :half, :]), 'ctx', along_x)]
    ppermute x2 -> x4, starting transfers between devices: 2.09 us -> 5.76 us  [ctx_reduce(): own_x, pass_y = lax.ppermute((to_x, to_far[..., :half, :]), 'ctx', along_x)]
    ppermute x2 -> x4, waiting for transfers between devices: 0.14 us -> 3.37 us  [ctx_reduce(): own_y, pass_x = lax.ppermute((to_y, to_far[..., half:, :]), 'ctx', along_y)]
    ppermute x6 -> x12, waiting for transfers between devices: 17 us -> 14.7 us  [ring_shift(): return lax.ppermute(x, axis, [(i, (i + d) % n) for i in range(n)])]
    pallas_call x1 -> x2, Pallas kernels: 16.7 us -> 18.9 us  [attention_grads(): pl.pallas_call(functools.partial(attention_grad_kernel, earlier is not No...]
  transfers between devices with their start and end apart: 16 -> 32, of which waited for: 10 -> 16; matrix products, arithmetic and copies ran while one was open for 4% -> 7% of each run, Pallas kernels for 0% -> 0%
where the time goes in v4:
time: 107 us
  starting transfers between devices  37.4 us (35%)
  waiting for transfers between devices  27.2 us (25%)
  Pallas kernels  18.9 us (18%)
  between operations  9.49 us (9%)
  other arithmetic  7.79 us (7%)
  local copies, waits for them, and re-layouts  5.79 us (5%)
    pallas_call x2, Pallas kernels, attention_grads(): pl.pallas_call(functools.partial(attention_grad_kernel, earlier is not No...  18.9 us
    ppermute x12, starting transfers between devices, ring_shift(): return lax.ppermute(x, axis, [(i, (i + d) % n) for i in range(n)])  16 us
    ppermute x12, waiting for transfers between devices, ring_shift(): return lax.ppermute(x, axis, [(i, (i + d) % n) for i in range(n)])  14.7 us
    ppermute x4, starting transfers between devices, ctx_reduce(): own_x, pass_y = lax.ppermute((to_x, to_far[..., :half, :]), 'ctx', along_x)  5.76 us
    ppermute x4, waiting for transfers between devices, ctx_reduce(): own_y, pass_x = lax.ppermute((to_y, to_far[..., half:, :]), 'ctx', along_y)  3.37 us
    ppermute x2, starting transfers between devices, ctx_gather(): far_a = lax.ppermute(from_y[..., :half, :], 'ctx', along_x)  3.11 us
    ppermute x4, starting transfers between devices, ctx_reduce(): own_y, pass_x = lax.ppermute((to_y, to_far[..., half:, :]), 'ctx', along_y)  2.81 us
    ppermute x2, waiting for transfers between devices, ctx_gather(): from_x = lax.ppermute(x, 'ctx', along_x)  2.74 us
  transfers between devices with their start and end apart: 32, of which 16 were waited for; matrix products, arithmetic and copies ran while one was open for 7% of the time, Pallas kernels for 0%

profile of v4, /device:TPU:0, one launch (start us, length us, event | category | flops | bytes accessed | tf_op | source)
XLA Modules:
  0.0 106.6 jit_solution(5373193522052192216)
XLA Ops:
  10.9 5.1 %collective-permute-start.9 = (bf16[2,128,128]{2,1,0:T(8,128)(2,1)S(1)}, bf16[2,128,128]{2,1,0:T(8,128)(2,1)S(1)}, u32[]{:S(2)}, u32[]{:S(2)}) collective-permute-start(bf16[2,128,128]{2,1,0:T(8,128)(2,1)S(1)} %get-tuple-element.45), channel_id=1, source_target_pairs={{0,6},{2,0},{4,2},{6,4},{1,7},{3,1},{5,3},{7,5},{8,14},{10,8},{12,... | collective-permute-start | bytes 196616 | tf_op jit(solution)/shard_map/ppermute | solution.py:139
  17.1 1.5 %collective-permute-done.9 = bf16[2,128,128]{2,1,0:T(8,128)(2,1)S(1)} collective-permute-done((bf16[2,128,128]{2,1,0:T(8,128)(2,1)S(1)}, bf16[2,128,128]{2,1,0:T(8,128)(2,1)S(1)}, u32[]{:S(2)}, u32[]{:S(2)}) %collective-permute-start.9) | collective-permute-done | bytes 65568 | tf_op jit(solution)/shard_map/ppermute | solution.py:139
  18.5 4.0 %collective-permute-done.8 = bf16[2,128,128]{2,1,0:T(8,128)(2,1)S(1)} collective-permute-done((bf16[2,128,128]{2,1,0:T(8,128)(2,1)S(1)}, bf16[2,128,128]{2,1,0:T(8,128)(2,1)S(1)}, u32[]{:S(2)}, u32[]{:S(2)}) %collective-permute-start.8) | collective-permute-done | bytes 65568 | tf_op jit(solution)/shard_map/ppermute | solution.py:139
  22.6 1.6 %collective-permute-start.10 = (bf16[4,2,128,128]{3,2,1,0:T(8,128)(2,1)S(1)}, bf16[4,2,128,128]{3,2,1,0:T(8,128)(2,1)S(1)}, u32[]{:S(2)}, u32[]{:S(2)}) collective-permute-start(bf16[4,2,128,128]{3,2,1,0:T(8,128)(2,1)S(1)} %get-tuple-element.39), channel_id=1, source_target_pairs={{0,8},{8,0},{16,24},{24,16},{1,9},{9,1},{17,25},{25,17},{2,10},{10... | collective-permute-start | bytes 786440 | tf_op jit(solution)/shard_map/ppermute | solution.py:159
  24.1 1.5 %collective-permute-start.11 = (bf16[4,2,128,128]{3,2,1,0:T(8,128)(2,1)S(1)}, bf16[4,2,128,128]{3,2,1,0:T(8,128)(2,1)S(1)}, u32[]{:S(2)}, u32[]{:S(2)}) collective-permute-start(bf16[4,2,128,128]{3,2,1,0:T(8,128)(2,1)S(1)} %get-tuple-element.39), channel_id=1, source_target_pairs={{0,16},{8,24},{16,0},{24,8},{1,17},{9,25},{17,1},{25,9},{2,18},{10... | collective-permute-start | bytes 786440 | tf_op jit(solution)/shard_map/ppermute | solution.py:160
  25.7 1.9 %collective-permute-start.2 = (bf16[2,128,128]{2,1,0:T(8,128)(2,1)S(1)}, bf16[2,128,128]{2,1,0:T(8,128)(2,1)S(1)}, u32[]{:S(2)}, u32[]{:S(2)}) collective-permute-start(bf16[2,128,128]{2,1,0:T(8,128)(2,1)S(1)} %get-tuple-element.49), channel_id=1, source_target_pairs={{0,6},{2,0},{4,2},{6,4},{1,7},{3,1},{5,3},{7,5},{8,14},{10,8},{12,... | collective-permute-start | bytes 196616 | tf_op jit(solution)/shard_map/ppermute | solution.py:139
  27.6 1.9 %collective-permute-start = (bf16[2,128,128]{2,1,0:T(8,128)(2,1)S(1)}, bf16[2,128,128]{2,1,0:T(8,128)(2,1)S(1)}, u32[]{:S(2)}, u32[]{:S(2)}) collective-permute-start(bf16[2,128,128]{2,1,0:T(8,128)(2,1)S(1)} %get-tuple-element.51), channel_id=1, source_target_pairs={{0,2},{2,4},{4,6},{6,0},{1,3},{3,5},{5,7},{7,1},{8,10},{10,12},{12... | collective-permute-start | bytes 196616 | tf_op jit(solution)/shard_map/ppermute | solution.py:139
  30.1 3.9 %collective-permute-done.1 = bf16[2,128,128]{2,1,0:T(8,128)(2,1)S(1)} collective-permute-done((bf16[2,128,128]{2,1,0:T(8,128)(2,1)S(1)}, bf16[2,128,128]{2,1,0:T(8,128)(2,1)S(1)}, u32[]{:S(2)}, u32[]{:S(2)}) %collective-permute-start.1) | collective-permute-done | bytes 65568 | tf_op jit(solution)/shard_map/ppermute | solution.py:139
  35.2 1.6 %collective-permute-start.13 = (bf16[4,2,64,128]{3,2,1,0:T(8,128)(2,1)S(1)}, bf16[4,2,64,128]{3,2,1,0:T(8,128)(2,1)S(1)}, u32[]{:S(2)}, u32[]{:S(2)}) collective-permute-start(bf16[4,2,64,128]{3,2,1,0:T(8,128)(2,1)S(1)} %slice.111), channel_id=1, source_target_pairs={{0,16},{8,24},{16,0},{24,8},{1,17},{9,25},{17,1},{25,9},{2,18},{10... | collective-permute-start | bytes 393224 | tf_op jit(solution)/shard_map/ppermute | solution.py:163
  36.8 1.6 %collective-permute-start.12 = (bf16[4,2,64,128]{3,2,1,0:T(8,128)(2,1)S(1)}, bf16[4,2,64,128]{3,2,1,0:T(8,128)(2,1)S(1)}, u32[]{:S(2)}, u32[]{:S(2)}) collective-permute-start(bf16[4,2,64,128]{3,2,1,0:T(8,128)(2,1)S(1)} %slice.110), channel_id=1, source_target_pairs={{0,8},{8,0},{16,24},{24,16},{1,9},{9,1},{17,25},{25,17},{2,10},{10... | collective-permute-start | bytes 393224 | tf_op jit(solution)/shard_map/ppermute | solution.py:162
  40.2 2.7 %collective-permute-done.3 = bf16[4,2,128,128]{3,2,1,0:T(8,128)(2,1)S(1)} collective-permute-done((bf16[4,2,128,128]{3,2,1,0:T(8,128)(2,1)S(1)}, bf16[4,2,128,128]{3,2,1,0:T(8,128)(2,1)S(1)}, u32[]{:S(2)}, u32[]{:S(2)}) %collective-permute-start.3) | collective-permute-done | bytes 262176 | tf_op jit(solution)/shard_map/ppermute | solution.py:159
  43.2 1.6 %collective-permute-start.5 = (bf16[4,2,64,128]{3,2,1,0:T(8,128)(2,1)S(1)}, bf16[4,2,64,128]{3,2,1,0:T(8,128)(2,1)S(1)}, u32[]{:S(2)}, u32[]{:S(2)}) collective-permute-start(bf16[4,2,64,128]{3,2,1,0:T(8,128)(2,1)S(1)} %slice.107), channel_id=1, source_target_pairs={{0,8},{8,0},{16,24},{24,16},{1,9},{9,1},{17,25},{25,17},{2,10},{10... | collective-permute-start | bytes 393224 | tf_op jit(solution)/shard_map/ppermute | solution.py:162
  45.9 2.0 %collective-permute-done.6 = bf16[4,2,64,128]{3,2,1,0:T(8,128)(2,1)S(1)} collective-permute-done((bf16[4,2,64,128]{3,2,1,0:T(8,128)(2,1)S(1)}, bf16[4,2,64,128]{3,2,1,0:T(8,128)(2,1)S(1)}, u32[]{:S(2)}, u32[]{:S(2)}) %collective-permute-start.6) | collective-permute-done | bytes 131104 | tf_op jit(solution)/shard_map/ppermute | solution.py:163
  49.4 9.4 %shard_map.111 = (bf16[128,2048]{1,0:T(8,128)(2,1)}, bf16[128,1024]{1,0:T(8,128)(2,1)}, bf16[128,1024]{1,0:T(8,128)(2,1)}, bf16[4,4,2,128,128]{4,3,2,1,0:T(8,128)(2,1)}) custom-call(s32[4]{0:T(128)} %gather_fusion, s32[1]{0:T(128)} %bitcast.109.length_ref, s32[1]{0:T(128)} %bitcast.3.pair_ref, bf16[128,2048]{1,0:T(8,128)(2,1)} %bitcast.117, ...), custom_call_target="tpu_custom_call" | custom-call | flops 1006632960 | bytes 3670016 | tf_op jit(solution)/shard_map/pallas_call | solution.py:115
  58.8 9.5 %shard_map.112 = (bf16[128,2048]{1,0:T(8,128)(2,1)}, bf16[128,1024]{1,0:T(8,128)(2,1)}, bf16[128,1024]{1,0:T(8,128)(2,1)}, bf16[4,4,2,128,128]{4,3,2,1,0:T(8,128)(2,1)}) custom-call(s32[4]{0:T(128)} %gather_fusion, s32[1]{0:T(128)} %bitcast.110.length_ref, s32[1]{0:T(128)} %bitcast.3.pair_ref, ...), custom_call_target="tpu_custom_call", output_to_operand_aliasing={{0}: (9, {}), {1}: (10, {}), {2}: (11, {})} | custom-call | flops 1006632960 | bytes 3670016 | tf_op jit(solution)/shard_map/pallas_call | solution.py:115
  69.6 1.6 %collective-permute-start.25 = (bf16[4,2,64,128]{3,2,1,0:T(8,128)(2,1)S(1)}, bf16[4,2,64,128]{3,2,1,0:T(8,128)(2,1)S(1)}, u32[]{:S(2)}, u32[]{:S(2)}) collective-permute-start(bf16[4,2,64,128]{3,2,1,0:T(8,128)(2,1)S(1)} %get-tuple-element.36), channel_id=1, source_target_pairs={{0,8},{8,0},{16,24},{24,16},{1,9},{9,1},{17,25},{25,17},{2,10},{10... | collective-permute-start | bytes 393224 | tf_op jit(solution)/shard_map/ppermute | solution.py:177
  71.8 1.9 %collective-permute-start.16 = (bf16[4,2,64,128]{3,2,1,0:T(8,128)(2,1)S(1)}, bf16[4,2,64,128]{3,2,1,0:T(8,128)(2,1)S(1)}, u32[]{:S(2)}, u32[]{:S(2)}) collective-permute-start(bf16[4,2,64,128]{3,2,1,0:T(8,128)(2,1)S(1)} %get-tuple-element.30), channel_id=1, source_target_pairs={{0,8},{8,0},{16,24},{24,16},{1,9},{9,1},{17,25},{25,17},{2,10},{10... | collective-permute-start | bytes 393224 | tf_op jit(solution)/shard_map/ppermute | solution.py:177
  73.9 1.5 %collective-permute-start.23 = (bf16[4,2,128,128]{3,2,1,0:T(8,128)(2,1)S(1)}, bf16[4,2,128,128]{3,2,1,0:T(8,128)(2,1)S(1)}, u32[]{:S(2)}, u32[]{:S(2)}) collective-permute-start(bf16[4,2,128,128]{3,2,1,0:T(8,128)(2,1)S(1)} %get-tuple-element.25), channel_id=1, source_target_pairs={{0,8},{8,0},{16,24},{24,16},{1,9},{9,1},{17,25},{25,17},{2,10},{10... | collective-permute-start | bytes 786440 | tf_op jit(solution)/shard_map/ppermute | solution.py:177
  76.0 1.5 %collective-permute-start.18 = (bf16[4,2,64,128]{3,2,1,0:T(8,128)(2,1)S(1)}, bf16[4,2,64,128]{3,2,1,0:T(8,128)(2,1)S(1)}, u32[]{:S(2)}, u32[]{:S(2)}) collective-permute-start(bf16[4,2,64,128]{3,2,1,0:T(8,128)(2,1)S(1)} %get-tuple-element.31), channel_id=1, source_target_pairs={{0,16},{8,24},{16,0},{24,8},{1,17},{9,25},{17,1},{25,9},{2,18},{10... | collective-permute-start | bytes 393224 | tf_op jit(solution)/shard_map/ppermute | solution.py:178
  78.0 1.6 %collective-permute-start.28 = (bf16[4,2,64,128]{3,2,1,0:T(8,128)(2,1)S(1)}, bf16[4,2,64,128]{3,2,1,0:T(8,128)(2,1)S(1)}, u32[]{:S(2)}, u32[]{:S(2)}) collective-permute-start(bf16[4,2,64,128]{3,2,1,0:T(8,128)(2,1)S(1)} %collective-permute-done.27), channel_id=1, source_target_pairs={{0,8},{8,0},{16,24},{24,16},{1,9},{9,1},{17,25},{25,17},{2,10},{10... | collective-permute-start | bytes 393224 | tf_op jit(solution)/shard_map/ppermute | solution.py:180
  82.1 3.4 %collective-permute-done.18 = bf16[4,2,64,128]{3,2,1,0:T(8,128)(2,1)S(1)} collective-permute-done((bf16[4,2,64,128]{3,2,1,0:T(8,128)(2,1)S(1)}, bf16[4,2,64,128]{3,2,1,0:T(8,128)(2,1)S(1)}, u32[]{:S(2)}, u32[]{:S(2)}) %collective-permute-start.18) | collective-permute-done | bytes 131104 | tf_op jit(solution)/shard_map/ppermute | solution.py:178
  87.7 1.4 %collective-permute-start.17 = (bf16[4,2,64,128]{3,2,1,0:T(8,128)(2,1)S(1)}, bf16[4,2,64,128]{3,2,1,0:T(8,128)(2,1)S(1)}, u32[]{:S(2)}, u32[]{:S(2)}) collective-permute-start(bf16[4,2,64,128]{3,2,1,0:T(8,128)(2,1)S(1)} %collective-permute-done.16), channel_id=1, source_target_pairs={{0,16},{8,24},{16,0},{24,8},{1,17},{9,25},{17,1},{25,9},{2,18},{10... | collective-permute-start | bytes 393224 | tf_op jit(solution)/shard_map/ppermute | solution.py:179
  95.2 3.7 %collective-permute-start.22 = (bf16[2,128,128]{2,1,0:T(8,128)(2,1)S(1)}, bf16[2,128,128]{2,1,0:T(8,128)(2,1)S(1)}, u32[]{:S(2)}, u32[]{:S(2)}) collective-permute-start(bf16[2,128,128]{2,1,0:T(8,128)(2,1)S(1)} %get-tuple-element.27), channel_id=1, source_target_pairs={{0,6},{2,0},{4,2},{6,4},{1,7},{3,1},{5,3},{7,5},{8,14},{10,8},{12,... | collective-permute-start | bytes 196616 | tf_op jit(solution)/shard_map/ppermute | solution.py:139
  100.8 3.2 %collective-permute-done.21 = bf16[2,128,128]{2,1,0:T(8,128)(2,1)S(1)} collective-permute-done((bf16[2,128,128]{2,1,0:T(8,128)(2,1)S(1)}, bf16[2,128,128]{2,1,0:T(8,128)(2,1)S(1)}, u32[]{:S(2)}, u32[]{:S(2)}) %collective-permute-start.21) | collective-permute-done | bytes 65568 | tf_op jit(solution)/shard_map/ppermute | solution.py:139
  (92 shorter events, 27.8 us)
Async XLA Ops:
  10.9 7.6 %collective-permute-start.9 = (bf16[2,128,128]{2,1,0:T(8,128)(2,1)S(1)}, bf16[2,128,128]{2,1,0:T(8,128)(2,1)S(1)}, u32[]{:S(2)}, u32[]{:S(2)}) collective-permute-start(bf16[2,128,128]{2,1,0:T(8,128)(2,1)S(1)} %get-tuple-element.45), channel_id=1, source_target_pairs={{0,6},{2,0},{4,2},{6,4},{1,7},{3,1},{5,3},{7,5},{8,14},{10,8},{12,... | collective-permute-start | bytes 196616 | tf_op jit(solution)/shard_map/ppermute | solution.py:139
  16.0 6.5 %collective-permute-start.8 = (bf16[2,128,128]{2,1,0:T(8,128)(2,1)S(1)}, bf16[2,128,128]{2,1,0:T(8,128)(2,1)S(1)}, u32[]{:S(2)}, u32[]{:S(2)}) collective-permute-start(bf16[2,128,128]{2,1,0:T(8,128)(2,1)S(1)} %get-tuple-element.46), channel_id=1, source_target_pairs={{0,4},{2,6},{4,0},{6,2},{1,5},{3,7},{5,1},{7,3},{8,12},{10,14},{12... | collective-permute-start | bytes 196616 | tf_op jit(solution)/shard_map/ppermute | solution.py:139
  16.0 6.5 %collective-permute-start.7 = (bf16[2,128,128]{2,1,0:T(8,128)(2,1)S(1)}, bf16[2,128,128]{2,1,0:T(8,128)(2,1)S(1)}, u32[]{:S(2)}, u32[]{:S(2)}) collective-permute-start(bf16[2,128,128]{2,1,0:T(8,128)(2,1)S(1)} %get-tuple-element.47), channel_id=1, source_target_pairs={{0,2},{2,4},{4,6},{6,0},{1,3},{3,5},{5,7},{7,1},{8,10},{10,12},{12... | collective-permute-start | bytes 196616 | tf_op jit(solution)/shard_map/ppermute | solution.py:139
  22.6 12.6 %collective-permute-start.10 = (bf16[4,2,128,128]{3,2,1,0:T(8,128)(2,1)S(1)}, bf16[4,2,128,128]{3,2,1,0:T(8,128)(2,1)S(1)}, u32[]{:S(2)}, u32[]{:S(2)}) collective-permute-start(bf16[4,2,128,128]{3,2,1,0:T(8,128)(2,1)S(1)} %get-tuple-element.39), channel_id=1, source_target_pairs={{0,8},{8,0},{16,24},{24,16},{1,9},{9,1},{17,25},{25,17},{2,10},{10... | collective-permute-start | bytes 786440 | tf_op jit(solution)/shard_map/ppermute | solution.py:159
  24.1 12.6 %collective-permute-start.11 = (bf16[4,2,128,128]{3,2,1,0:T(8,128)(2,1)S(1)}, bf16[4,2,128,128]{3,2,1,0:T(8,128)(2,1)S(1)}, u32[]{:S(2)}, u32[]{:S(2)}) collective-permute-start(bf16[4,2,128,128]{3,2,1,0:T(8,128)(2,1)S(1)} %get-tuple-element.39), channel_id=1, source_target_pairs={{0,16},{8,24},{16,0},{24,8},{1,17},{9,25},{17,1},{25,9},{2,18},{10... | collective-permute-start | bytes 786440 | tf_op jit(solution)/shard_map/ppermute | solution.py:160
  27.6 6.4 %collective-permute-start.1 = (bf16[2,128,128]{2,1,0:T(8,128)(2,1)S(1)}, bf16[2,128,128]{2,1,0:T(8,128)(2,1)S(1)}, u32[]{:S(2)}, u32[]{:S(2)}) collective-permute-start(bf16[2,128,128]{2,1,0:T(8,128)(2,1)S(1)} %get-tuple-element.50), channel_id=1, source_target_pairs={{0,4},{2,6},{4,0},{6,2},{1,5},{3,7},{5,1},{7,3},{8,12},{10,14},{12... | collective-permute-start | bytes 196616 | tf_op jit(solution)/shard_map/ppermute | solution.py:139
  27.6 6.4 %collective-permute-start = (bf16[2,128,128]{2,1,0:T(8,128)(2,1)S(1)}, bf16[2,128,128]{2,1,0:T(8,128)(2,1)S(1)}, u32[]{:S(2)}, u32[]{:S(2)}) collective-permute-start(bf16[2,128,128]{2,1,0:T(8,128)(2,1)S(1)} %get-tuple-element.51), channel_id=1, source_target_pairs={{0,2},{2,4},{4,6},{6,0},{1,3},{3,5},{5,7},{7,1},{8,10},{10,12},{12... | collective-permute-start | bytes 196616 | tf_op jit(solution)/shard_map/ppermute | solution.py:139
  34.1 8.8 %collective-permute-start.3 = (bf16[4,2,128,128]{3,2,1,0:T(8,128)(2,1)S(1)}, bf16[4,2,128,128]{3,2,1,0:T(8,128)(2,1)S(1)}, u32[]{:S(2)}, u32[]{:S(2)}) collective-permute-start(bf16[4,2,128,128]{3,2,1,0:T(8,128)(2,1)S(1)} %get-tuple-element.43), channel_id=1, source_target_pairs={{0,8},{8,0},{16,24},{24,16},{1,9},{9,1},{17,25},{25,17},{2,10},{10... | collective-permute-start | bytes 786440 | tf_op jit(solution)/shard_map/ppermute | solution.py:159
  34.7 8.6 %collective-permute-start.4 = (bf16[4,2,128,128]{3,2,1,0:T(8,128)(2,1)S(1)}, bf16[4,2,128,128]{3,2,1,0:T(8,128)(2,1)S(1)}, u32[]{:S(2)}, u32[]{:S(2)}) collective-permute-start(bf16[4,2,128,128]{3,2,1,0:T(8,128)(2,1)S(1)} %get-tuple-element.43), channel_id=1, source_target_pairs={{0,16},{8,24},{16,0},{24,8},{1,17},{9,25},{17,1},{25,9},{2,18},{10... | collective-permute-start | bytes 786440 | tf_op jit(solution)/shard_map/ppermute | solution.py:160
  35.2 9.6 %collective-permute-start.13 = (bf16[4,2,64,128]{3,2,1,0:T(8,128)(2,1)S(1)}, bf16[4,2,64,128]{3,2,1,0:T(8,128)(2,1)S(1)}, u32[]{:S(2)}, u32[]{:S(2)}) collective-permute-start(bf16[4,2,64,128]{3,2,1,0:T(8,128)(2,1)S(1)} %slice.111), channel_id=1, source_target_pairs={{0,16},{8,24},{16,0},{24,8},{1,17},{9,25},{17,1},{25,9},{2,18},{10... | collective-permute-start | bytes 393224 | tf_op jit(solution)/shard_map/ppermute | solution.py:163
  36.8 8.0 %collective-permute-start.12 = (bf16[4,2,64,128]{3,2,1,0:T(8,128)(2,1)S(1)}, bf16[4,2,64,128]{3,2,1,0:T(8,128)(2,1)S(1)}, u32[]{:S(2)}, u32[]{:S(2)}) collective-permute-start(bf16[4,2,64,128]{3,2,1,0:T(8,128)(2,1)S(1)} %slice.110), channel_id=1, source_target_pairs={{0,8},{8,0},{16,24},{24,16},{1,9},{9,1},{17,25},{25,17},{2,10},{10... | collective-permute-start | bytes 393224 | tf_op jit(solution)/shard_map/ppermute | solution.py:162
  69.6 6.4 %collective-permute-start.25 = (bf16[4,2,64,128]{3,2,1,0:T(8,128)(2,1)S(1)}, bf16[4,2,64,128]{3,2,1,0:T(8,128)(2,1)S(1)}, u32[]{:S(2)}, u32[]{:S(2)}) collective-permute-start(bf16[4,2,64,128]{3,2,1,0:T(8,128)(2,1)S(1)} %get-tuple-element.36), channel_id=1, source_target_pairs={{0,8},{8,0},{16,24},{24,16},{1,9},{9,1},{17,25},{25,17},{2,10},{10... | collective-permute-start | bytes 393224 | tf_op jit(solution)/shard_map/ppermute | solution.py:177
  71.2 6.4 %collective-permute-start.27 = (bf16[4,2,64,128]{3,2,1,0:T(8,128)(2,1)S(1)}, bf16[4,2,64,128]{3,2,1,0:T(8,128)(2,1)S(1)}, u32[]{:S(2)}, u32[]{:S(2)}) collective-permute-start(bf16[4,2,64,128]{3,2,1,0:T(8,128)(2,1)S(1)} %get-tuple-element.37), channel_id=1, source_target_pairs={{0,16},{8,24},{16,0},{24,8},{1,17},{9,25},{17,1},{25,9},{2,18},{10... | collective-permute-start | bytes 393224 | tf_op jit(solution)/shard_map/ppermute | solution.py:178
  71.8 6.3 %collective-permute-start.16 = (bf16[4,2,64,128]{3,2,1,0:T(8,128)(2,1)S(1)}, bf16[4,2,64,128]{3,2,1,0:T(8,128)(2,1)S(1)}, u32[]{:S(2)}, u32[]{:S(2)}) collective-permute-start(bf16[4,2,64,128]{3,2,1,0:T(8,128)(2,1)S(1)} %get-tuple-element.30), channel_id=1, source_target_pairs={{0,8},{8,0},{16,24},{24,16},{1,9},{9,1},{17,25},{25,17},{2,10},{10... | collective-permute-start | bytes 393224 | tf_op jit(solution)/shard_map/ppermute | solution.py:177
  73.7 15.4 %collective-permute-start.24 = (bf16[4,2,128,128]{3,2,1,0:T(8,128)(2,1)S(1)}, bf16[4,2,128,128]{3,2,1,0:T(8,128)(2,1)S(1)}, u32[]{:S(2)}, u32[]{:S(2)}) collective-permute-start(bf16[4,2,128,128]{3,2,1,0:T(8,128)(2,1)S(1)} %get-tuple-element.24), channel_id=1, source_target_pairs={{0,16},{8,24},{16,0},{24,8},{1,17},{9,25},{17,1},{25,9},{2,18},{10... | collective-permute-start | bytes 786440 | tf_op jit(solution)/shard_map/ppermute | solution.py:178
  73.9 15.6 %collective-permute-start.23 = (bf16[4,2,128,128]{3,2,1,0:T(8,128)(2,1)S(1)}, bf16[4,2,128,128]{3,2,1,0:T(8,128)(2,1)S(1)}, u32[]{:S(2)}, u32[]{:S(2)}) collective-permute-start(bf16[4,2,128,128]{3,2,1,0:T(8,128)(2,1)S(1)} %get-tuple-element.25), channel_id=1, source_target_pairs={{0,8},{8,0},{16,24},{24,16},{1,9},{9,1},{17,25},{25,17},{2,10},{10... | collective-permute-start | bytes 786440 | tf_op jit(solution)/shard_map/ppermute | solution.py:177
  76.0 9.5 %collective-permute-start.18 = (bf16[4,2,64,128]{3,2,1,0:T(8,128)(2,1)S(1)}, bf16[4,2,64,128]{3,2,1,0:T(8,128)(2,1)S(1)}, u32[]{:S(2)}, u32[]{:S(2)}) collective-permute-start(bf16[4,2,64,128]{3,2,1,0:T(8,128)(2,1)S(1)} %get-tuple-element.31), channel_id=1, source_target_pairs={{0,16},{8,24},{16,0},{24,8},{1,17},{9,25},{17,1},{25,9},{2,18},{10... | collective-permute-start | bytes 393224 | tf_op jit(solution)/shard_map/ppermute | solution.py:178
  77.5 9.3 %collective-permute-start.26 = (bf16[4,2,64,128]{3,2,1,0:T(8,128)(2,1)S(1)}, bf16[4,2,64,128]{3,2,1,0:T(8,128)(2,1)S(1)}, u32[]{:S(2)}, u32[]{:S(2)}) collective-permute-start(bf16[4,2,64,128]{3,2,1,0:T(8,128)(2,1)S(1)} %collective-permute-done.25), channel_id=1, source_target_pairs={{0,16},{8,24},{16,0},{24,8},{1,17},{9,25},{17,1},{25,9},{2,18},{10... | collective-permute-start | bytes 393224 | tf_op jit(solution)/shard_map/ppermute | solution.py:179
  78.0 9.7 %collective-permute-start.28 = (bf16[4,2,64,128]{3,2,1,0:T(8,128)(2,1)S(1)}, bf16[4,2,64,128]{3,2,1,0:T(8,128)(2,1)S(1)}, u32[]{:S(2)}, u32[]{:S(2)}) collective-permute-start(bf16[4,2,64,128]{3,2,1,0:T(8,128)(2,1)S(1)} %collective-permute-done.27), channel_id=1, source_target_pairs={{0,8},{8,0},{16,24},{24,16},{1,9},{9,1},{17,25},{25,17},{2,10},{10... | collective-permute-start | bytes 393224 | tf_op jit(solution)/shard_map/ppermute | solution.py:180
  85.5 9.4 %collective-permute-start.15 = (bf16[4,2,128,128]{3,2,1,0:T(8,128)(2,1)S(1)}, bf16[4,2,128,128]{3,2,1,0:T(8,128)(2,1)S(1)}, u32[]{:S(2)}, u32[]{:S(2)}) collective-permute-start(bf16[4,2,128,128]{3,2,1,0:T(8,128)(2,1)S(1)} %get-tuple-element.21), channel_id=1, source_target_pairs={{0,16},{8,24},{16,0},{24,8},{1,17},{9,25},{17,1},{25,9},{2,18},{10... | collective-permute-start | bytes 786440 | tf_op jit(solution)/shard_map/ppermute | solution.py:178
  86.9 8.0 %collective-permute-start.14 = (bf16[4,2,128,128]{3,2,1,0:T(8,128)(2,1)S(1)}, bf16[4,2,128,128]{3,2,1,0:T(8,128)(2,1)S(1)}, u32[]{:S(2)}, u32[]{:S(2)}) collective-permute-start(bf16[4,2,128,128]{3,2,1,0:T(8,128)(2,1)S(1)} %get-tuple-element.22), channel_id=1, source_target_pairs={{0,8},{8,0},{16,24},{24,16},{1,9},{9,1},{17,25},{25,17},{2,10},{10... | collective-permute-start | bytes 786440 | tf_op jit(solution)/shard_map/ppermute | solution.py:177
  90.8 8.1 %collective-permute-start.31 = (bf16[2,128,128]{2,1,0:T(8,128)(2,1)S(1)}, bf16[2,128,128]{2,1,0:T(8,128)(2,1)S(1)}, u32[]{:S(2)}, u32[]{:S(2)}) collective-permute-start(bf16[2,128,128]{2,1,0:T(8,128)(2,1)S(1)} %get-tuple-element.33), channel_id=1, source_target_pairs={{0,6},{2,0},{4,2},{6,4},{1,7},{3,1},{5,3},{7,5},{8,14},{10,8},{12,... | collective-permute-start | bytes 196616 | tf_op jit(solution)/shard_map/ppermute | solution.py:139
  93.3 6.2 %collective-permute-start.30 = (bf16[2,128,128]{2,1,0:T(8,128)(2,1)S(1)}, bf16[2,128,128]{2,1,0:T(8,128)(2,1)S(1)}, u32[]{:S(2)}, u32[]{:S(2)}) collective-permute-start(bf16[2,128,128]{2,1,0:T(8,128)(2,1)S(1)} %get-tuple-element.34), channel_id=1, source_target_pairs={{0,4},{2,6},{4,0},{6,2},{1,5},{3,7},{5,1},{7,3},{8,12},{10,14},{12... | collective-permute-start | bytes 196616 | tf_op jit(solution)/shard_map/ppermute | solution.py:139
  94.7 6.1 %collective-permute-start.29 = (bf16[2,128,128]{2,1,0:T(8,128)(2,1)S(1)}, bf16[2,128,128]{2,1,0:T(8,128)(2,1)S(1)}, u32[]{:S(2)}, u32[]{:S(2)}) collective-permute-start(bf16[2,128,128]{2,1,0:T(8,128)(2,1)S(1)} %get-tuple-element.35), channel_id=1, source_target_pairs={{0,2},{2,4},{4,6},{6,0},{1,3},{3,5},{5,7},{7,1},{8,10},{10,12},{12... | collective-permute-start | bytes 196616 | tf_op jit(solution)/shard_map/ppermute | solution.py:139
  (11 other events, 84.9 us)

commit v5 on v4

--- a/solution.py
+++ b/solution.py
@@ -21,22 +21,28 @@
 TN = (((0,), (0,)), ((), ()))
 
 
-def attention_grad_kernel(aliased, blocks_ref, length_ref, pair_ref, q_ref, do_ref, kp_ref, vp_ref, kr_ref, vr_ref,
-                          *refs):
-    dq_ref, dkr_ref, dvr_ref, dpre_ref = refs[3:] if aliased else refs
+def attention_grad_kernel(layout, blocks_ref, length_ref, place_ref, q_ref, do_ref, *refs):
+    n_in, n_slots, slot_rows, xor_slots, out_ranges, aliased = layout
+    kp_refs, vp_refs = refs[:n_in], refs[n_in:2 * n_in]
+    kr_ref, vr_ref = refs[2 * n_in:2 * n_in + 2]
+    outs = refs[2 * n_in + 2 + (3 if aliased else 0):]
+    dq_ref, dkr_ref, dvr_ref = outs[:3]
+    piece_refs = outs[3:]
     resp_rows = q_ref.shape[0]
-    n_ctx, chunk_rows, _ = kp_ref.shape
-    pre_rows = n_ctx * chunk_rows
-    n_blocks = pre_rows // BLOCK
-    kp = kp_ref[...].reshape(pre_rows, HEAD_DIM)
-    vp = vp_ref[...].reshape(pre_rows, HEAD_DIM)
+    kp = jnp.concatenate([r[...] for r in kp_refs], 0)
+    vp = jnp.concatenate([r[...] for r in vp_refs], 0)
+    pre_rows = kp.shape[0]
     kr = kr_ref[...]
     vr = vr_ref[...]
 
+    slot_blocks = slot_rows // BLOCK
+    c = place_ref[1]
     col_block = lax.broadcasted_iota(jnp.int32, (1, pre_rows), 1) // BLOCK
     flag = jnp.zeros((1, pre_rows), jnp.int32)
-    for b in range(n_blocks):
-        flag = jnp.where(col_block == b, blocks_ref[b], flag)
+    for b in range(n_slots * slot_blocks):
+        slot, sub = b // slot_blocks, b % slot_blocks
+        source = jnp.bitwise_xor(c, slot) if xor_slots else slot
+        flag = jnp.where(col_block == b, blocks_ref[source * slot_blocks + sub], flag)
     pre_ok = flag > 0
     row_i = lax.broadcasted_iota(jnp.int32, (resp_rows, resp_rows), 0)
     col_i = lax.broadcasted_iota(jnp.int32, (resp_rows, resp_rows), 1)
@@ -80,51 +86,63 @@
         dvr = dvr + lax.dot_general(pr, doj, TN, preferred_element_type=jnp.float32)
     dkr_ref[...] = (dkr * scale_factor).astype(dkr_ref.dtype)
     dvr_ref[...] = dvr.astype(dvr_ref.dtype)
-    dpre_ref[:, 0] = (dkp * scale_factor).astype(dpre_ref.dtype).reshape(n_ctx, chunk_rows, HEAD_DIM)
-    dpre_ref[:, 1] = dvp.astype(dpre_ref.dtype).reshape(n_ctx, chunk_rows, HEAD_DIM)
-
-
-def attention_grads(blocks, length, pair_index, q, do, panel, kr, vr, first_head, earlier):
+    dkp = (dkp * scale_factor).astype(jnp.bfloat16)
+    dvp = dvp.astype(jnp.bfloat16)
+    for ref, ranges in zip(piece_refs, out_ranges):
+        at = 0
+        for start, rows in ranges:
+            ref[0, at:at + rows] = dkp[start:start + rows]
+            ref[1, at:at + rows] = dvp[start:start + rows]
+            at += rows
+
+
+def attention_grads(blocks, length, place, q, do, pieces, xor_slots, out_ranges, kr, vr, first_head, earlier):
     resp_rows, q_width = q.shape
-    n_ctx, n_pair, _, chunk_rows, chunk_feats = panel.shape
+    n_pair, _, _, chunk_feats = pieces[0].shape
     kv_width = kr.shape[1]
-    pre_rows = n_ctx * chunk_rows
+    pre_rows = sum(p.shape[2] for p in pieces)
     chunk_heads = kv_width // n_pair // HEAD_DIM
     per_chunk = chunk_feats // HEAD_DIM
     heads = n_pair * per_chunk
+    n_slots = lax.axis_size("ctx")
+    slot_rows = pre_rows // n_slots
 
     def head(g, r):
         return ((r[0] + n_pair - g // per_chunk) % n_pair) * chunk_heads + first_head + g % per_chunk
 
+    def piece_spec(rows, kv):
+        return pl.BlockSpec((None, None, rows, HEAD_DIM), lambda g, b, n, r: (g // per_chunk, kv, 0, g % per_chunk))
+
     qspec = pl.BlockSpec((resp_rows, GROUP * HEAD_DIM), lambda g, b, n, r: (0, head(g, r)))
-    kspec = pl.BlockSpec((n_ctx, None, None, chunk_rows, HEAD_DIM),
-                         lambda g, b, n, r: (0, g // per_chunk, 0, 0, g % per_chunk))
-    vspec = pl.BlockSpec((n_ctx, None, None, chunk_rows, HEAD_DIM),
-                         lambda g, b, n, r: (0, g // per_chunk, 1, 0, g % per_chunk))
     rspec = pl.BlockSpec((resp_rows, HEAD_DIM), lambda g, b, n, r: (0, head(g, r)))
-    dspec = pl.BlockSpec((n_ctx, None, 2, chunk_rows, HEAD_DIM),
-                         lambda g, b, n, r: (0, g // per_chunk, 0, 0, g % per_chunk))
-    flops = 2 * 6 * resp_rows * GROUP * heads * (pre_rows + resp_rows) * HEAD_DIM
-    in_specs = [qspec, qspec, kspec, vspec, rspec, rspec]
-    operands = [blocks, length, pair_index, q, do, panel, panel, kr, vr]
+    in_specs = [qspec, qspec]
+    in_specs += [piece_spec(p.shape[2], 0) for p in pieces] + [piece_spec(p.shape[2], 1) for p in pieces]
+    in_specs += [rspec, rspec]
+    operands = [blocks, length, place, q, do] + list(pieces) + list(pieces) + [kr, vr]
     aliases = {}
     if earlier is not None:
         in_specs += [pl.BlockSpec(memory_space=pl.ANY)] * 3
         aliases = {len(operands) + i: i for i in range(3)}
         operands += list(earlier)
+    out_rows = [sum(rows for _, rows in ranges) for ranges in out_ranges]
+    out_specs = [qspec, rspec, rspec] + [
+        pl.BlockSpec((None, 2, rows, HEAD_DIM), lambda g, b, n, r: (g // per_chunk, 0, 0, g % per_chunk))
+        for rows in out_rows]
+    out_shape = [
+        jax.ShapeDtypeStruct((resp_rows, q_width), jnp.bfloat16),
+        jax.ShapeDtypeStruct((resp_rows, kv_width), jnp.bfloat16),
+        jax.ShapeDtypeStruct((resp_rows, kv_width), jnp.bfloat16),
+    ] + [jax.ShapeDtypeStruct((n_pair, 2, rows, chunk_feats), jnp.bfloat16) for rows in out_rows]
+    layout = (len(pieces), n_slots, slot_rows, xor_slots, tuple(tuple(r) for r in out_ranges), earlier is not None)
+    flops = 2 * 6 * resp_rows * GROUP * heads * (pre_rows + resp_rows) * HEAD_DIM
     return pl.pallas_call(
-        functools.partial(attention_grad_kernel, earlier is not None),
-        out_shape=(
-            jax.ShapeDtypeStruct((resp_rows, q_width), jnp.bfloat16),
-            jax.ShapeDtypeStruct((resp_rows, kv_width), jnp.bfloat16),
-            jax.ShapeDtypeStruct((resp_rows, kv_width), jnp.bfloat16),
-            jax.ShapeDtypeStruct(panel.shape, jnp.bfloat16),
-        ),
+        functools.partial(attention_grad_kernel, layout),
+        out_shape=tuple(out_shape),
         grid_spec=pltpu.PrefetchScalarGridSpec(
             num_scalar_prefetch=3,
             grid=(heads,),
             in_specs=in_specs,
-            out_specs=[qspec, rspec, rspec, dspec],
+            out_specs=out_specs,
         ),
         input_output_aliases=aliases,
         cost_estimate=pl.CostEstimate(
@@ -149,38 +167,51 @@
     return jnp.stack(held)
 
 
+def tree_ctx():
+    return lax.axis_size("ctx") == 4
+
+
 def ctx_gather(x):
     n = lax.axis_size("ctx")
-    if n != 4:
-        return lax.all_gather(x, "ctx", axis=0, tiled=False), jnp.arange(n, dtype=jnp.int32)
-    c = lax.axis_index("ctx")
+    if not tree_ctx():
+        got = lax.all_gather(x, "ctx", axis=0, tiled=False)
+        return [got[j] for j in range(n)]
     along_x = [(i, i ^ 1) for i in range(n)]
     along_y = [(i, i ^ 2) for i in range(n)]
     from_x = lax.ppermute(x, "ctx", along_x)
     from_y = lax.ppermute(x, "ctx", along_y)
-    half = x.shape[-2] // 2
-    far_a = lax.ppermute(from_y[..., :half, :], "ctx", along_x)
-    far_b = lax.ppermute(from_x[..., half:, :], "ctx", along_y)
-    held = jnp.stack([x, from_x, from_y, jnp.concatenate([far_a, far_b], -2)])
-    return held, jnp.bitwise_xor(jnp.arange(n, dtype=jnp.int32), c)
+    half = x.shape[2] // 2
+    far_a = lax.ppermute(from_y[:, :, :half], "ctx", along_x)
+    far_b = lax.ppermute(from_x[:, :, half:], "ctx", along_y)
+    return [x, from_x, from_y, far_a, far_b]
+
+
+def ctx_out_ranges(slot_rows):
+    n = lax.axis_size("ctx")
+    if not tree_ctx():
+        return [[(j * slot_rows, slot_rows)] for j in range(n)]
+    half = slot_rows // 2
+    return [[(0, slot_rows)],
+            [(slot_rows, slot_rows), (3 * slot_rows, half)],
+            [(2 * slot_rows, slot_rows), (3 * slot_rows + half, half)]]
 
 
 def ctx_reduce(pieces):
+    if not tree_ctx():
+        got = lax.all_to_all(jnp.stack(pieces), "ctx", split_axis=0, concat_axis=0, tiled=True)
+        return jnp.sum(got.astype(jnp.float32), axis=0).astype(jnp.bfloat16)
     n = lax.axis_size("ctx")
-    if n != 4:
-        got = lax.all_to_all(pieces, "ctx", split_axis=0, concat_axis=0, tiled=True)
-        return jnp.sum(got.astype(jnp.float32), axis=0).astype(jnp.bfloat16)
     along_x = [(i, i ^ 1) for i in range(n)]
     along_y = [(i, i ^ 2) for i in range(n)]
-    mine, to_x, to_y, to_far = pieces[0], pieces[1], pieces[2], pieces[3]
-    half = to_far.shape[-2] // 2
-    own_x, pass_y = lax.ppermute((to_x, to_far[..., :half, :]), "ctx", along_x)
-    own_y, pass_x = lax.ppermute((to_y, to_far[..., half:, :]), "ctx", along_y)
-    far_a = lax.ppermute(pass_y, "ctx", along_y)
-    far_b = lax.ppermute(pass_x, "ctx", along_x)
-    far = jnp.concatenate([far_a, far_b], -2)
-    total = (mine.astype(jnp.float32) + own_x.astype(jnp.float32)) + (
-        own_y.astype(jnp.float32) + far.astype(jnp.float32))
+    mine, send_x, send_y = pieces
+    rows = mine.shape[2]
+    got_x = lax.ppermute(send_x, "ctx", along_x)
+    got_y = lax.ppermute(send_y, "ctx", along_y)
+    far_a = lax.ppermute(got_x[:, :, rows:], "ctx", along_y)
+    far_b = lax.ppermute(got_y[:, :, rows:], "ctx", along_x)
+    far = jnp.concatenate([far_a, far_b], 2)
+    total = (mine.astype(jnp.float32) + got_x[:, :, :rows].astype(jnp.float32)) + (
+        got_y[:, :, :rows].astype(jnp.float32) + far.astype(jnp.float32))
     return total.astype(jnp.bfloat16)
 
 
@@ -203,22 +234,23 @@
 ):
     n_prompts = prefix_kv.shape[0]
     planes = jnp.transpose(prefix_kv, (0, 2, 1, 3))
+    slot_rows = planes.shape[2]
     chunk_feats = planes.shape[-1]
     n_groups = HEAD_GROUPS if chunk_feats % (HEAD_GROUPS * HEAD_DIM) == 0 else 1
     group_feats = chunk_feats // n_groups
-    pair_index = lax.axis_index("pair").reshape(1).astype(jnp.int32)
+    place = jnp.stack([lax.axis_index("pair"), lax.axis_index("ctx")]).astype(jnp.int32)
     earlier = None
     parts = []
     for k in range(n_groups):
         cols = slice(k * group_feats, (k + 1) * group_feats)
-        panel, sources = ctx_gather(pair_gather(planes[..., cols], pair_prompt))
-        chunk_blocks = panel.shape[3] // BLOCK
-        flags = prefix_blocks[0, 0].reshape(-1, chunk_blocks)[sources].reshape(-1)
-        dq, dkr, dvr, dpre = attention_grads(
-            flags, resp_lengths[0, 0].reshape(1), pair_index, queries[0, 0], d_out[0, 0], panel,
-            resp_keys[0, 0], resp_values[0, 0], k * (group_feats // HEAD_DIM), earlier)
-        earlier = (dq, dkr, dvr)
-        parts.append(pair_reduce(ctx_reduce(dpre), pair_prompt, n_prompts))
+        pieces = ctx_gather(pair_gather(planes[..., cols], pair_prompt))
+        outs = attention_grads(
+            prefix_blocks[0, 0], resp_lengths[0, 0].reshape(1), place, queries[0, 0], d_out[0, 0], pieces,
+            tree_ctx(), ctx_out_ranges(slot_rows), resp_keys[0, 0], resp_values[0, 0],
+            k * (group_feats // HEAD_DIM), earlier)
+        earlier = outs[:3]
+        parts.append(pair_reduce(ctx_reduce(list(outs[3:])), pair_prompt, n_prompts))
+    dq, dkr, dvr = earlier
     d_prefix = parts[0] if n_groups == 1 else jnp.concatenate(parts, -1)
     return (dq[None, None], dkr[None, None], dvr[None, None], d_prefix)
 

time: 107 us -> 100 us (0.935)
  other arithmetic: 7.79 us -> 5.14 us
  waiting for transfers between devices: 27.2 us -> 25.6 us
  starting transfers between devices: 37.4 us -> 35.9 us
    ppermute x12, waiting for transfers between devices: 14.7 us -> 7.99 us  [ring_shift(): return lax.ppermute(x, axis, [(i, (i + d) % n) for i in range(n)])]
    ppermute x16 -> x12, waiting for transfers between devices: 9.55 us -> 14.6 us  [the longest x2 11.2 us: ctx_reduce(): got_x = lax.ppermute(send_x, 'ctx', along_x)]
    ppermute x16 -> x12, starting transfers between devices: 17.3 us -> 12.5 us  [the longest x2 3.17 us: ctx_gather(): far_b = lax.ppermute(from_x[:, :, half:], 'ctx', along_y)]
    ppermute x2, waiting for transfers between devices: 0.23 us -> 2.99 us  [ctx_gather(): from_y = lax.ppermute(x, 'ctx', along_y)]
    ppermute x2, waiting for transfers between devices: 2.74 us -> 0.01 us  [ctx_gather(): from_x = lax.ppermute(x, 'ctx', along_x)]
    another operation x6 -> x3, other arithmetic: 2.37 us -> 0.66 us  [the longest x1 0.59 us: shards(): jnp.stack([lax.axis_index('pair'), lax.axis_index('ctx')]).astype(jnp.int32)]
    unnamed x7 -> x31, local copies, waits for them, and re-layouts: 1.64 us -> 3.03 us
    squeeze x2 -> x0, local copies, waits for them, and re-layouts: 1.33 us -> none  [ctx_reduce(): mine, to_x, to_y, to_far = (pieces[0], pieces[1], pieces[2], pieces[3])]
  transfers between devices with their start and end apart: 32 -> 28, of which waited for: 16 -> 13; matrix products, arithmetic and copies ran while one was open for 7% -> 4% of each run, Pallas kernels for 0% -> 9%
where the time goes in v5:
time: 100 us; the launch traced here: 99.5 us
  starting transfers between devices  35.9 us (36%)
  waiting for transfers between devices  25.6 us (26%)
  Pallas kernels  18.9 us (19%)
  between operations  9.31 us (9%)
  other arithmetic  5.14 us (5%)
  local copies, waits for them, and re-layouts  4.73 us (5%)
    pallas_call x2, Pallas kernels, attention_grads(): pl.pallas_call(functools.partial(attention_grad_kernel, layout), out_shap...  18.9 us
    ppermute x12, starting transfers between devices, ring_shift(): return lax.ppermute(x, axis, [(i, (i + d) % n) for i in range(n)])  17.2 us
    ppermute x2, waiting for transfers between devices, ctx_reduce(): got_x = lax.ppermute(send_x, 'ctx', along_x)  11.2 us
    ppermute x12, waiting for transfers between devices, ring_shift(): return lax.ppermute(x, axis, [(i, (i + d) % n) for i in range(n)])  7.99 us
    ppermute x2, starting transfers between devices, ctx_gather(): from_y = lax.ppermute(x, 'ctx', along_y)  3.17 us
    ppermute x2, starting transfers between devices, ctx_gather(): far_b = lax.ppermute(from_x[:, :, half:], 'ctx', along_y)  3.17 us
    ppermute x2, starting transfers between devices, ctx_gather(): far_a = lax.ppermute(from_y[:, :, :half], 'ctx', along_x)  3.11 us
    unnamed x31, local copies, waits for them, and re-layouts  3.03 us
  transfers between devices with their start and end apart: 28, of which 13 were waited for; matrix products, arithmetic and copies ran while one was open for 4% of the time, Pallas kernels for 9%

profile of v5, /device:TPU:0, one launch (start us, length us, event | category | flops | bytes accessed | tf_op | source)
XLA Modules:
  0.0 99.5 jit_solution(14993248707438279302)
XLA Ops:
  10.7 5.1 %collective-permute-start.9 = (bf16[2,128,128]{2,1,0:T(8,128)(2,1)S(1)}, bf16[2,128,128]{2,1,0:T(8,128)(2,1)S(1)}, u32[]{:S(2)}, u32[]{:S(2)}) collective-permute-start(bf16[2,128,128]{2,1,0:T(8,128)(2,1)S(1)} %get-tuple-element.39), channel_id=1, source_target_pairs={{0,6},{2,0},{4,2},{6,4},{1,7},{3,1},{5,3},{7,5},{8,14},{10,8},{12,... | collective-permute-start | bytes 196616 | tf_op jit(solution)/shard_map/ppermute | solution.py:157
  16.8 2.9 %collective-permute-start.2 = (bf16[2,128,128]{2,1,0:T(8,128)(2,1)S(1)}, bf16[2,128,128]{2,1,0:T(8,128)(2,1)S(1)}, u32[]{:S(2)}, u32[]{:S(2)}) collective-permute-start(bf16[2,128,128]{2,1,0:T(8,128)(2,1)S(1)} %get-tuple-element.43), channel_id=1, source_target_pairs={{0,6},{2,0},{4,2},{6,4},{1,7},{3,1},{5,3},{7,5},{8,14},{10,8},{12,... | collective-permute-start | bytes 196616 | tf_op jit(solution)/shard_map/ppermute | solution.py:157
  20.8 2.5 %collective-permute-done.8 = bf16[2,128,128]{2,1,0:T(8,128)(2,1)S(1)} collective-permute-done((bf16[2,128,128]{2,1,0:T(8,128)(2,1)S(1)}, bf16[2,128,128]{2,1,0:T(8,128)(2,1)S(1)}, u32[]{:S(2)}, u32[]{:S(2)}) %collective-permute-start.8) | collective-permute-done | bytes 65568 | tf_op jit(solution)/shard_map/ppermute | solution.py:157
  23.3 1.6 %collective-permute-start.11 = (bf16[4,2,128,128]{3,2,1,0:T(8,128)(2,1)S(1)}, bf16[4,2,128,128]{3,2,1,0:T(8,128)(2,1)S(1)}, u32[]{:S(2)}, u32[]{:S(2)}) collective-permute-start(bf16[4,2,128,128]{3,2,1,0:T(8,128)(2,1)S(1)} %pad_maximum_fusion.2.refs_0_.refs_5_), channel_id=1, source_target_pairs={{0,16},{8,24},{16,0},{24,8},{1,17},{9,25},{17,1},{25,9},{2,18},{10... | collective-permute-start | bytes 786440 | tf_op jit(solution)/shard_map/ppermute | solution.py:182
  24.9 1.5 %collective-permute-start.10 = (bf16[4,2,128,128]{3,2,1,0:T(8,128)(2,1)S(1)}, bf16[4,2,128,128]{3,2,1,0:T(8,128)(2,1)S(1)}, u32[]{:S(2)}, u32[]{:S(2)}) collective-permute-start(bf16[4,2,128,128]{3,2,1,0:T(8,128)(2,1)S(1)} %pad_maximum_fusion.2.refs_0_.refs_5_), channel_id=1, source_target_pairs={{0,8},{8,0},{16,24},{24,16},{1,9},{9,1},{17,25},{25,17},{2,10},{10... | collective-permute-start | bytes 786440 | tf_op jit(solution)/shard_map/ppermute | solution.py:181
  26.4 1.5 %collective-permute-done.1 = bf16[2,128,128]{2,1,0:T(8,128)(2,1)S(1)} collective-permute-done((bf16[2,128,128]{2,1,0:T(8,128)(2,1)S(1)}, bf16[2,128,128]{2,1,0:T(8,128)(2,1)S(1)}, u32[]{:S(2)}, u32[]{:S(2)}) %collective-permute-start.1) | collective-permute-done | bytes 65568 | tf_op jit(solution)/shard_map/ppermute | solution.py:157
  28.0 1.6 %collective-permute-start.4 = (bf16[4,2,128,128]{3,2,1,0:T(8,128)(2,1)S(1)}, bf16[4,2,128,128]{3,2,1,0:T(8,128)(2,1)S(1)}, u32[]{:S(2)}, u32[]{:S(2)}) collective-permute-start(bf16[4,2,128,128]{3,2,1,0:T(8,128)(2,1)S(1)} %pad_maximum_fusion.1.refs_0_.refs_5_), channel_id=1, source_target_pairs={{0,16},{8,24},{16,0},{24,8},{1,17},{9,25},{17,1},{25,9},{2,18},{10... | collective-permute-start | bytes 786440 | tf_op jit(solution)/shard_map/ppermute | solution.py:182
  29.6 1.5 %collective-permute-start.3 = (bf16[4,2,128,128]{3,2,1,0:T(8,128)(2,1)S(1)}, bf16[4,2,128,128]{3,2,1,0:T(8,128)(2,1)S(1)}, u32[]{:S(2)}, u32[]{:S(2)}) collective-permute-start(bf16[4,2,128,128]{3,2,1,0:T(8,128)(2,1)S(1)} %pad_maximum_fusion.1.refs_0_.refs_5_), channel_id=1, source_target_pairs={{0,8},{8,0},{16,24},{24,16},{1,9},{9,1},{17,25},{25,17},{2,10},{10... | collective-permute-start | bytes 786440 | tf_op jit(solution)/shard_map/ppermute | solution.py:181
  31.6 1.6 %collective-permute-start.12 = (bf16[4,2,64,128]{3,2,1,0:T(8,128)(2,1)S(1)}, bf16[4,2,64,128]{3,2,1,0:T(8,128)(2,1)S(1)}, u32[]{:S(2)}, u32[]{:S(2)}) collective-permute-start(bf16[4,2,64,128]{3,2,1,0:T(8,128)(2,1)S(1)} %slice.92), channel_id=1, source_target_pairs={{0,8},{8,0},{16,24},{24,16},{1,9},{9,1},{17,25},{25,17},{2,10},{10... | collective-permute-start | bytes 393224 | tf_op jit(solution)/shard_map/ppermute | solution.py:184
  33.2 1.6 %collective-permute-start.13 = (bf16[4,2,64,128]{3,2,1,0:T(8,128)(2,1)S(1)}, bf16[4,2,64,128]{3,2,1,0:T(8,128)(2,1)S(1)}, u32[]{:S(2)}, u32[]{:S(2)}) collective-permute-start(bf16[4,2,64,128]{3,2,1,0:T(8,128)(2,1)S(1)} %slice.93), channel_id=1, source_target_pairs={{0,16},{8,24},{16,0},{24,8},{1,17},{9,25},{17,1},{25,9},{2,18},{10... | collective-permute-start | bytes 393224 | tf_op jit(solution)/shard_map/ppermute | solution.py:185
  34.8 2.4 %collective-permute-done.4.refs_2_.refs_7_ = bf16[4,2,128,128]{3,2,1,0:T(8,128)(2,1)S(1)} collective-permute-done((bf16[4,2,128,128]{3,2,1,0:T(8,128)(2,1)S(1)}, bf16[4,2,128,128]{3,2,1,0:T(8,128)(2,1)S(1)}, u32[]{:S(2)}, u32[]{:S(2)}) %collective-permute-start.4) | collective-permute-done | bytes 262176 | tf_op jit(solution)/shard_map/ppermute | solution.py:182
  37.3 1.6 %collective-permute-start.5 = (bf16[4,2,64,128]{3,2,1,0:T(8,128)(2,1)S(1)}, bf16[4,2,64,128]{3,2,1,0:T(8,128)(2,1)S(1)}, u32[]{:S(2)}, u32[]{:S(2)}) collective-permute-start(bf16[4,2,64,128]{3,2,1,0:T(8,128)(2,1)S(1)} %slice.89), channel_id=1, source_target_pairs={{0,8},{8,0},{16,24},{24,16},{1,9},{9,1},{17,25},{25,17},{2,10},{10... | collective-permute-start | bytes 393224 | tf_op jit(solution)/shard_map/ppermute | solution.py:184
  38.8 1.6 %collective-permute-start.6 = (bf16[4,2,64,128]{3,2,1,0:T(8,128)(2,1)S(1)}, bf16[4,2,64,128]{3,2,1,0:T(8,128)(2,1)S(1)}, u32[]{:S(2)}, u32[]{:S(2)}) collective-permute-start(bf16[4,2,64,128]{3,2,1,0:T(8,128)(2,1)S(1)} %slice.90), channel_id=1, source_target_pairs={{0,16},{8,24},{16,0},{24,8},{1,17},{9,25},{17,1},{25,9},{2,18},{10... | collective-permute-start | bytes 393224 | tf_op jit(solution)/shard_map/ppermute | solution.py:185
  42.4 9.4 %shard_map.111 = (bf16[128,2048]{1,0:T(8,128)(2,1)}, bf16[128,1024]{1,0:T(8,128)(2,1)}, bf16[128,1024]{1,0:T(8,128)(2,1)}, bf16[4,2,128,128]{3,2,1,0:T(8,128)(2,...) custom-call(s32[4]{0:T(128)} %bitcast.98, s32[1]{0:T(128)} %bitcast.78.length_ref, ...), custom_call_target="tpu_custom_call" | custom-call | flops 1006632960 | bytes 3670016 | tf_op jit(solution)/shard_map/pallas_call | solution.py:138
  52.5 9.5 %shard_map.112 = (bf16[128,2048]{1,0:T(8,128)(2,1)}, bf16[128,1024]{1,0:T(8,128)(2,1)}, bf16[128,1024]{1,0:T(8,128)(2,1)}, bf16[4,2,128,128]{3,2,1,0:T(8,128)(2,...) custom-call(s32[4]{0:T(128)} %bitcast.99, ...), custom_call_target="tpu_custom_call", output_to_operand_aliasing={{0}: (17, {}), {1}: (18, {}), {2}: (19, {})} | custom-call | flops 1006632960 | bytes 3670016 | tf_op jit(solution)/shard_map/pallas_call | solution.py:138
  64.6 1.5 %collective-permute-start.15 = (bf16[4,2,192,128]{3,2,1,0:T(8,128)(2,1)S(1)}, bf16[4,2,192,128]{3,2,1,0:T(8,128)(2,1)S(1)}, u32[]{:S(2)}, u32[]{:S(2)}) collective-permute-start(bf16[4,2,192,128]{3,2,1,0:T(8,128)(2,1)S(1)} %copy-done.11), channel_id=1, source_target_pairs={{0,16},{8,24},{16,0},{24,8},{1,17},{9,25},{17,1},{25,9},{2,18},{10... | collective-permute-start | bytes 1179656 | tf_op jit(solution)/shard_map/ppermute | solution.py:209
  66.2 8.2 %collective-permute-done.21 = bf16[4,2,192,128]{3,2,1,0:T(8,128)(2,1)S(1)} collective-permute-done((bf16[4,2,192,128]{3,2,1,0:T(8,128)(2,1)}, bf16[4,2,192,128]{3,2,1,0:T(8,128)(2,1)S(1)}, u32[]{:S(2)}, u32[]{:S(2)}) %collective-permute-start.21) | collective-permute-done | bytes 393248 | tf_op jit(solution)/shard_map/ppermute | solution.py:208
  79.0 3.0 %collective-permute-done.14 = bf16[4,2,192,128]{3,2,1,0:T(8,128)(2,1)S(1)} collective-permute-done((bf16[4,2,192,128]{3,2,1,0:T(8,128)(2,1)S(1)}, bf16[4,2,192,128]{3,2,1,0:T(8,128)(2,1)S(1)}, u32[]{:S(2)}, u32[]{:S(2)}) %collective-permute-start.14) | collective-permute-done | bytes 393248 | tf_op jit(solution)/shard_map/ppermute | solution.py:208
  82.2 1.9 %collective-permute-done.15 = bf16[4,2,192,128]{3,2,1,0:T(8,128)(2,1)S(1)} collective-permute-done((bf16[4,2,192,128]{3,2,1,0:T(8,128)(2,1)S(1)}, bf16[4,2,192,128]{3,2,1,0:T(8,128)(2,1)S(1)}, u32[]{:S(2)}, u32[]{:S(2)}) %collective-permute-start.15) | collective-permute-done | bytes 393248 | tf_op jit(solution)/shard_map/ppermute | solution.py:209
  85.8 1.6 %collective-permute-start.26 = (bf16[2,128,128]{2,1,0:T(8,128)(2,1)S(1)}, bf16[2,128,128]{2,1,0:T(8,128)(2,1)S(1)}, u32[]{:S(2)}, u32[]{:S(2)}) collective-permute-start(bf16[2,128,128]{2,1,0:T(8,128)(2,1)S(1)} %get-tuple-element.34), channel_id=1, source_target_pairs={{0,4},{2,6},{4,0},{6,2},{1,5},{3,7},{5,1},{7,3},{8,12},{10,14},{12... | collective-permute-start | bytes 196616 | tf_op jit(solution)/shard_map/ppermute | solution.py:157
  87.5 1.9 %collective-permute-start.25 = (bf16[2,128,128]{2,1,0:T(8,128)(2,1)S(1)}, bf16[2,128,128]{2,1,0:T(8,128)(2,1)S(1)}, u32[]{:S(2)}, u32[]{:S(2)}) collective-permute-start(bf16[2,128,128]{2,1,0:T(8,128)(2,1)S(1)} %get-tuple-element.35), channel_id=1, source_target_pairs={{0,2},{2,4},{4,6},{6,0},{1,3},{3,5},{5,7},{7,1},{8,10},{10,12},{12... | collective-permute-start | bytes 196616 | tf_op jit(solution)/shard_map/ppermute | solution.py:157
  89.7 1.9 %collective-permute-start.20 = (bf16[2,128,128]{2,1,0:T(8,128)(2,1)S(1)}, bf16[2,128,128]{2,1,0:T(8,128)(2,1)S(1)}, u32[]{:S(2)}, u32[]{:S(2)}) collective-permute-start(bf16[2,128,128]{2,1,0:T(8,128)(2,1)S(1)} %get-tuple-element.29), channel_id=1, source_target_pairs={{0,6},{2,0},{4,2},{6,4},{1,7},{3,1},{5,3},{7,5},{8,14},{10,8},{12,... | collective-permute-start | bytes 196616 | tf_op jit(solution)/shard_map/ppermute | solution.py:157
  91.7 1.5 %collective-permute-start.18 = (bf16[2,128,128]{2,1,0:T(8,128)(2,1)S(1)}, bf16[2,128,128]{2,1,0:T(8,128)(2,1)S(1)}, u32[]{:S(2)}, u32[]{:S(2)}) collective-permute-start(bf16[2,128,128]{2,1,0:T(8,128)(2,1)S(1)} %get-tuple-element.31), channel_id=1, source_target_pairs={{0,2},{2,4},{4,6},{6,0},{1,3},{3,5},{5,7},{7,1},{8,10},{10,12},{12... | collective-permute-start | bytes 196616 | tf_op jit(solution)/shard_map/ppermute | solution.py:157
  94.6 2.6 %collective-permute-done.19 = bf16[2,128,128]{2,1,0:T(8,128)(2,1)S(1)} collective-permute-done((bf16[2,128,128]{2,1,0:T(8,128)(2,1)S(1)}, bf16[2,128,128]{2,1,0:T(8,128)(2,1)S(1)}, u32[]{:S(2)}, u32[]{:S(2)}) %collective-permute-start.19) | collective-permute-done | bytes 65568 | tf_op jit(solution)/shard_map/ppermute | solution.py:157
  (102 shorter events, 20.3 us)
Async XLA Ops:
  10.7 10.1 %collective-permute-start.9 = (bf16[2,128,128]{2,1,0:T(8,128)(2,1)S(1)}, bf16[2,128,128]{2,1,0:T(8,128)(2,1)S(1)}, u32[]{:S(2)}, u32[]{:S(2)}) collective-permute-start(bf16[2,128,128]{2,1,0:T(8,128)(2,1)S(1)} %get-tuple-element.39), channel_id=1, source_target_pairs={{0,6},{2,0},{4,2},{6,4},{1,7},{3,1},{5,3},{7,5},{8,14},{10,8},{12,... | collective-permute-start | bytes 196616 | tf_op jit(solution)/shard_map/ppermute | solution.py:157
  15.8 7.5 %collective-permute-start.8 = (bf16[2,128,128]{2,1,0:T(8,128)(2,1)S(1)}, bf16[2,128,128]{2,1,0:T(8,128)(2,1)S(1)}, u32[]{:S(2)}, u32[]{:S(2)}) collective-permute-start(bf16[2,128,128]{2,1,0:T(8,128)(2,1)S(1)} %get-tuple-element.40), channel_id=1, source_target_pairs={{0,4},{2,6},{4,0},{6,2},{1,5},{3,7},{5,1},{7,3},{8,12},{10,14},{12... | collective-permute-start | bytes 196616 | tf_op jit(solution)/shard_map/ppermute | solution.py:157
  15.8 7.5 %collective-permute-start.7 = (bf16[2,128,128]{2,1,0:T(8,128)(2,1)S(1)}, bf16[2,128,128]{2,1,0:T(8,128)(2,1)S(1)}, u32[]{:S(2)}, u32[]{:S(2)}) collective-permute-start(bf16[2,128,128]{2,1,0:T(8,128)(2,1)S(1)} %get-tuple-element.41), channel_id=1, source_target_pairs={{0,2},{2,4},{4,6},{6,0},{1,3},{3,5},{5,7},{7,1},{8,10},{10,12},{12... | collective-permute-start | bytes 196616 | tf_op jit(solution)/shard_map/ppermute | solution.py:157
  16.8 9.6 %collective-permute-start.2 = (bf16[2,128,128]{2,1,0:T(8,128)(2,1)S(1)}, bf16[2,128,128]{2,1,0:T(8,128)(2,1)S(1)}, u32[]{:S(2)}, u32[]{:S(2)}) collective-permute-start(bf16[2,128,128]{2,1,0:T(8,128)(2,1)S(1)} %get-tuple-element.43), channel_id=1, source_target_pairs={{0,6},{2,0},{4,2},{6,4},{1,7},{3,1},{5,3},{7,5},{8,14},{10,8},{12,... | collective-permute-start | bytes 196616 | tf_op jit(solution)/shard_map/ppermute | solution.py:157
  19.7 8.2 %collective-permute-start.1 = (bf16[2,128,128]{2,1,0:T(8,128)(2,1)S(1)}, bf16[2,128,128]{2,1,0:T(8,128)(2,1)S(1)}, u32[]{:S(2)}, u32[]{:S(2)}) collective-permute-start(bf16[2,128,128]{2,1,0:T(8,128)(2,1)S(1)} %get-tuple-element.44), channel_id=1, source_target_pairs={{0,4},{2,6},{4,0},{6,2},{1,5},{3,7},{5,1},{7,3},{8,12},{10,14},{12... | collective-permute-start | bytes 196616 | tf_op jit(solution)/shard_map/ppermute | solution.py:157
  20.8 7.1 %collective-permute-start = (bf16[2,128,128]{2,1,0:T(8,128)(2,1)S(1)}, bf16[2,128,128]{2,1,0:T(8,128)(2,1)S(1)}, u32[]{:S(2)}, u32[]{:S(2)}) collective-permute-start(bf16[2,128,128]{2,1,0:T(8,128)(2,1)S(1)} %get-tuple-element.45), channel_id=1, source_target_pairs={{0,2},{2,4},{4,6},{6,0},{1,3},{3,5},{5,7},{7,1},{8,10},{10,12},{12... | collective-permute-start | bytes 196616 | tf_op jit(solution)/shard_map/ppermute | solution.py:157
  23.3 8.3 %collective-permute-start.11 = (bf16[4,2,128,128]{3,2,1,0:T(8,128)(2,1)S(1)}, bf16[4,2,128,128]{3,2,1,0:T(8,128)(2,1)S(1)}, u32[]{:S(2)}, u32[]{:S(2)}) collective-permute-start(bf16[4,2,128,128]{3,2,1,0:T(8,128)(2,1)S(1)} %pad_maximum_fusion.2.refs_0_.refs_5_), channel_id=1, source_target_pairs={{0,16},{8,24},{16,0},{24,8},{1,17},{9,25},{17,1},{25,9},{2,18},{10... | collective-permute-start | bytes 786440 | tf_op jit(solution)/shard_map/ppermute | solution.py:182
  24.9 8.2 %collective-permute-start.10 = (bf16[4,2,128,128]{3,2,1,0:T(8,128)(2,1)S(1)}, bf16[4,2,128,128]{3,2,1,0:T(8,128)(2,1)S(1)}, u32[]{:S(2)}, u32[]{:S(2)}) collective-permute-start(bf16[4,2,128,128]{3,2,1,0:T(8,128)(2,1)S(1)} %pad_maximum_fusion.2.refs_0_.refs_5_), channel_id=1, source_target_pairs={{0,8},{8,0},{16,24},{24,16},{1,9},{9,1},{17,25},{25,17},{2,10},{10... | collective-permute-start | bytes 786440 | tf_op jit(solution)/shard_map/ppermute | solution.py:181
  28.0 9.3 %collective-permute-start.4 = (bf16[4,2,128,128]{3,2,1,0:T(8,128)(2,1)S(1)}, bf16[4,2,128,128]{3,2,1,0:T(8,128)(2,1)S(1)}, u32[]{:S(2)}, u32[]{:S(2)}) collective-permute-start(bf16[4,2,128,128]{3,2,1,0:T(8,128)(2,1)S(1)} %pad_maximum_fusion.1.refs_0_.refs_5_), channel_id=1, source_target_pairs={{0,16},{8,24},{16,0},{24,8},{1,17},{9,25},{17,1},{25,9},{2,18},{10... | collective-permute-start | bytes 786440 | tf_op jit(solution)/shard_map/ppermute | solution.py:182
  29.6 9.3 %collective-permute-start.3 = (bf16[4,2,128,128]{3,2,1,0:T(8,128)(2,1)S(1)}, bf16[4,2,128,128]{3,2,1,0:T(8,128)(2,1)S(1)}, u32[]{:S(2)}, u32[]{:S(2)}) collective-permute-start(bf16[4,2,128,128]{3,2,1,0:T(8,128)(2,1)S(1)} %pad_maximum_fusion.1.refs_0_.refs_5_), channel_id=1, source_target_pairs={{0,8},{8,0},{16,24},{24,16},{1,9},{9,1},{17,25},{25,17},{2,10},{10... | collective-permute-start | bytes 786440 | tf_op jit(solution)/shard_map/ppermute | solution.py:181
  31.6 10.1 %collective-permute-start.12 = (bf16[4,2,64,128]{3,2,1,0:T(8,128)(2,1)S(1)}, bf16[4,2,64,128]{3,2,1,0:T(8,128)(2,1)S(1)}, u32[]{:S(2)}, u32[]{:S(2)}) collective-permute-start(bf16[4,2,64,128]{3,2,1,0:T(8,128)(2,1)S(1)} %slice.92), channel_id=1, source_target_pairs={{0,8},{8,0},{16,24},{24,16},{1,9},{9,1},{17,25},{25,17},{2,10},{10... | collective-permute-start | bytes 393224 | tf_op jit(solution)/shard_map/ppermute | solution.py:184
  33.2 8.5 %collective-permute-start.13 = (bf16[4,2,64,128]{3,2,1,0:T(8,128)(2,1)S(1)}, bf16[4,2,64,128]{3,2,1,0:T(8,128)(2,1)S(1)}, u32[]{:S(2)}, u32[]{:S(2)}) collective-permute-start(bf16[4,2,64,128]{3,2,1,0:T(8,128)(2,1)S(1)} %slice.93), channel_id=1, source_target_pairs={{0,16},{8,24},{16,0},{24,8},{1,17},{9,25},{17,1},{25,9},{2,18},{10... | collective-permute-start | bytes 393224 | tf_op jit(solution)/shard_map/ppermute | solution.py:185
  37.3 14.5 %collective-permute-start.5 = (bf16[4,2,64,128]{3,2,1,0:T(8,128)(2,1)S(1)}, bf16[4,2,64,128]{3,2,1,0:T(8,128)(2,1)S(1)}, u32[]{:S(2)}, u32[]{:S(2)}) collective-permute-start(bf16[4,2,64,128]{3,2,1,0:T(8,128)(2,1)S(1)} %slice.89), channel_id=1, source_target_pairs={{0,8},{8,0},{16,24},{24,16},{1,9},{9,1},{17,25},{25,17},{2,10},{10... | collective-permute-start | bytes 393224 | tf_op jit(solution)/shard_map/ppermute | solution.py:184
  38.8 13.0 %collective-permute-start.6 = (bf16[4,2,64,128]{3,2,1,0:T(8,128)(2,1)S(1)}, bf16[4,2,64,128]{3,2,1,0:T(8,128)(2,1)S(1)}, u32[]{:S(2)}, u32[]{:S(2)}) collective-permute-start(bf16[4,2,64,128]{3,2,1,0:T(8,128)(2,1)S(1)} %slice.90), channel_id=1, source_target_pairs={{0,16},{8,24},{16,0},{24,8},{1,17},{9,25},{17,1},{25,9},{2,18},{10... | collective-permute-start | bytes 393224 | tf_op jit(solution)/shard_map/ppermute | solution.py:185
  62.0 12.3 %collective-permute-start.21 = (bf16[4,2,192,128]{3,2,1,0:T(8,128)(2,1)}, bf16[4,2,192,128]{3,2,1,0:T(8,128)(2,1)S(1)}, u32[]{:S(2)}, u32[]{:S(2)}) collective-permute-start(bf16[4,2,192,128]{3,2,1,0:T(8,128)(2,1)} %get-tuple-element.26), channel_id=1, source_target_pairs={{0,8},{8,0},{16,24},{24,16},{1,9},{9,1},{17,25},{25,17},{2,10},{10... | collective-permute-start | bytes 1179656 | tf_op jit(solution)/shard_map/ppermute | solution.py:208
  63.5 12.3 %collective-permute-start.22 = (bf16[4,2,192,128]{3,2,1,0:T(8,128)(2,1)}, bf16[4,2,192,128]{3,2,1,0:T(8,128)(2,1)S(1)}, u32[]{:S(2)}, u32[]{:S(2)}) collective-permute-start(bf16[4,2,192,128]{3,2,1,0:T(8,128)(2,1)} %get-tuple-element.27), channel_id=1, source_target_pairs={{0,16},{8,24},{16,0},{24,8},{1,17},{9,25},{17,1},{25,9},{2,18},{10... | collective-permute-start | bytes 1179656 | tf_op jit(solution)/shard_map/ppermute | solution.py:209
  64.1 18.0 %collective-permute-start.14 = (bf16[4,2,192,128]{3,2,1,0:T(8,128)(2,1)S(1)}, bf16[4,2,192,128]{3,2,1,0:T(8,128)(2,1)S(1)}, u32[]{:S(2)}, u32[]{:S(2)}) collective-permute-start(bf16[4,2,192,128]{3,2,1,0:T(8,128)(2,1)S(1)} %copy-done.12), channel_id=1, source_target_pairs={{0,8},{8,0},{16,24},{24,16},{1,9},{9,1},{17,25},{25,17},{2,10},{10... | collective-permute-start | bytes 1179656 | tf_op jit(solution)/shard_map/ppermute | solution.py:208
  64.6 19.4 %collective-permute-start.15 = (bf16[4,2,192,128]{3,2,1,0:T(8,128)(2,1)S(1)}, bf16[4,2,192,128]{3,2,1,0:T(8,128)(2,1)S(1)}, u32[]{:S(2)}, u32[]{:S(2)}) collective-permute-start(bf16[4,2,192,128]{3,2,1,0:T(8,128)(2,1)S(1)} %copy-done.11), channel_id=1, source_target_pairs={{0,16},{8,24},{16,0},{24,8},{1,17},{9,25},{17,1},{25,9},{2,18},{10... | collective-permute-start | bytes 1179656 | tf_op jit(solution)/shard_map/ppermute | solution.py:209
  74.4 11.1 %collective-permute-start.23 = (bf16[4,2,64,128]{3,2,1,0:T(8,128)(2,1)S(1)}, bf16[4,2,64,128]{3,2,1,0:T(8,128)(2,1)S(1)}, u32[]{:S(2)}, u32[]{:S(2)}) collective-permute-start(bf16[4,2,64,128]{3,2,1,0:T(8,128)(2,1)S(1)} %slice.104), channel_id=1, source_target_pairs={{0,16},{8,24},{16,0},{24,8},{1,17},{9,25},{17,1},{25,9},{2,18},{10... | collective-permute-start | bytes 393224 | tf_op jit(solution)/shard_map/ppermute | solution.py:210
  75.8 9.7 %collective-permute-start.24 = (bf16[4,2,64,128]{3,2,1,0:T(8,128)(2,1)S(1)}, bf16[4,2,64,128]{3,2,1,0:T(8,128)(2,1)S(1)}, u32[]{:S(2)}, u32[]{:S(2)}) collective-permute-start(bf16[4,2,64,128]{3,2,1,0:T(8,128)(2,1)S(1)} %slice.105), channel_id=1, source_target_pairs={{0,8},{8,0},{16,24},{24,16},{1,9},{9,1},{17,25},{25,17},{2,10},{10... | collective-permute-start | bytes 393224 | tf_op jit(solution)/shard_map/ppermute | solution.py:211
  82.1 7.4 %collective-permute-start.16 = (bf16[4,2,64,128]{3,2,1,0:T(8,128)(2,1)S(1)}, bf16[4,2,64,128]{3,2,1,0:T(8,128)(2,1)S(1)}, u32[]{:S(2)}, u32[]{:S(2)}) collective-permute-start(bf16[4,2,64,128]{3,2,1,0:T(8,128)(2,1)S(1)} %slice.96), channel_id=1, source_target_pairs={{0,16},{8,24},{16,0},{24,8},{1,17},{9,25},{17,1},{25,9},{2,18},{10... | collective-permute-start | bytes 393224 | tf_op jit(solution)/shard_map/ppermute | solution.py:210
  85.8 8.1 %collective-permute-start.26 = (bf16[2,128,128]{2,1,0:T(8,128)(2,1)S(1)}, bf16[2,128,128]{2,1,0:T(8,128)(2,1)S(1)}, u32[]{:S(2)}, u32[]{:S(2)}) collective-permute-start(bf16[2,128,128]{2,1,0:T(8,128)(2,1)S(1)} %get-tuple-element.34), channel_id=1, source_target_pairs={{0,4},{2,6},{4,0},{6,2},{1,5},{3,7},{5,1},{7,3},{8,12},{10,14},{12... | collective-permute-start | bytes 196616 | tf_op jit(solution)/shard_map/ppermute | solution.py:157
  87.5 6.5 %collective-permute-start.25 = (bf16[2,128,128]{2,1,0:T(8,128)(2,1)S(1)}, bf16[2,128,128]{2,1,0:T(8,128)(2,1)S(1)}, u32[]{:S(2)}, u32[]{:S(2)}) collective-permute-start(bf16[2,128,128]{2,1,0:T(8,128)(2,1)S(1)} %get-tuple-element.35), channel_id=1, source_target_pairs={{0,2},{2,4},{4,6},{6,0},{1,3},{3,5},{5,7},{7,1},{8,10},{10,12},{12... | collective-permute-start | bytes 196616 | tf_op jit(solution)/shard_map/ppermute | solution.py:157
  91.7 6.1 %collective-permute-start.18 = (bf16[2,128,128]{2,1,0:T(8,128)(2,1)S(1)}, bf16[2,128,128]{2,1,0:T(8,128)(2,1)S(1)}, u32[]{:S(2)}, u32[]{:S(2)}) collective-permute-start(bf16[2,128,128]{2,1,0:T(8,128)(2,1)S(1)} %get-tuple-element.31), channel_id=1, source_target_pairs={{0,2},{2,4},{4,6},{6,0},{1,3},{3,5},{5,7},{7,1},{8,10},{10,12},{12... | collective-permute-start | bytes 196616 | tf_op jit(solution)/shard_map/ppermute | solution.py:157
  (19 other events, 88.9 us)

commit v6 on v5

--- a/solution.py
+++ b/solution.py
@@ -229,6 +229,11 @@
     return out
 
 
+def in_group(width, kv_heads, chunk_heads, group_heads, k):
+    head = jnp.arange(width) // (width // kv_heads)
+    return ((head % chunk_heads) // group_heads == k)[None]
+
+
 def shards(
     queries, resp_keys, resp_values, d_out, prefix_kv, prefix_blocks, resp_lengths, pair_prompt
 ):
@@ -239,6 +244,9 @@
     n_groups = HEAD_GROUPS if chunk_feats % (HEAD_GROUPS * HEAD_DIM) == 0 else 1
     group_feats = chunk_feats // n_groups
     place = jnp.stack([lax.axis_index("pair"), lax.axis_index("ctx")]).astype(jnp.int32)
+    kv_heads = resp_keys.shape[-1] // HEAD_DIM
+    chunk_heads = chunk_feats // HEAD_DIM
+    group_heads = group_feats // HEAD_DIM
     earlier = None
     parts = []
     for k in range(n_groups):
@@ -247,8 +255,12 @@
         outs = attention_grads(
             prefix_blocks[0, 0], resp_lengths[0, 0].reshape(1), place, queries[0, 0], d_out[0, 0], pieces,
             tree_ctx(), ctx_out_ranges(slot_rows), resp_keys[0, 0], resp_values[0, 0],
-            k * (group_feats // HEAD_DIM), earlier)
-        earlier = outs[:3]
+            k * (group_feats // HEAD_DIM), None)
+        if earlier is None:
+            earlier = outs[:3]
+        else:
+            earlier = tuple(jnp.where(in_group(o.shape[1], kv_heads, chunk_heads, group_heads, k), o, e)
+                            for o, e in zip(outs[:3], earlier))
         parts.append(pair_reduce(ctx_reduce(list(outs[3:])), pair_prompt, n_prompts))
     dq, dkr, dvr = earlier
     d_prefix = parts[0] if n_groups == 1 else jnp.concatenate(parts, -1)

time: 100 us -> 92.3 us (0.923)
  waiting for transfers between devices: 25.6 us -> 10.6 us
  starting transfers between devices: 35.9 us -> 40.3 us
  other arithmetic: 5.14 us -> 8.03 us
    ppermute x2, waiting for transfers between devices: 11.2 us -> 2.65 us  [ctx_reduce(): got_x = lax.ppermute(send_x, 'ctx', along_x)]
    ppermute x12, starting transfers between devices: 17.2 us -> 21.4 us  [ring_shift(): return lax.ppermute(x, axis, [(i, (i + d) % n) for i in range(n)])]
    ppermute x12, waiting for transfers between devices: 7.99 us -> 5.16 us  [ring_shift(): return lax.ppermute(x, axis, [(i, (i + d) % n) for i in range(n)])]
    broadcast_in_dim x0 -> x2, other arithmetic: none -> 2.79 us  [shards(): return (dq[None, None], dkr[None, None], dvr[None, None], d_prefix)]
    ppermute x2, waiting for transfers between devices: 2.7 us -> 0.01 us  [ctx_reduce(): got_y = lax.ppermute(send_y, 'ctx', along_y)]
    ppermute x2, starting transfers between devices: 3.17 us -> 1.59 us  [ctx_gather(): far_b = lax.ppermute(from_x[:, :, half:], 'ctx', along_y)]
    ppermute x2, starting transfers between devices: 0.69 us -> 2.2 us  [ctx_reduce(): far_a = lax.ppermute(got_x[:, :, rows:], 'ctx', along_y)]
    ppermute x2, starting transfers between devices: 3.11 us -> 2.02 us  [ctx_gather(): far_a = lax.ppermute(from_y[:, :, :half], 'ctx', along_x)]
  transfers between devices with their start and end apart: 28 -> 28, of which waited for: 13 -> 6; matrix products, arithmetic and copies ran while one was open for 4% -> 8% of each run, Pallas kernels for 9% -> 21%
where the time goes in v6:
time: 92.3 us; the launch traced here: 91.8 us
  starting transfers between devices  40.3 us (44%)
  Pallas kernels  18.9 us (20%)
  waiting for transfers between devices  10.6 us (11%)
  between operations  9.31 us (10%)
  other arithmetic  8.03 us (9%)
  local copies, waits for them, and re-layouts  4.7 us (5%)
    ppermute x12, starting transfers between devices, ring_shift(): return lax.ppermute(x, axis, [(i, (i + d) % n) for i in range(n)])  21.4 us
    pallas_call x2, Pallas kernels, attention_grads(): pl.pallas_call(functools.partial(attention_grad_kernel, layout), out_shap...  18.9 us
    ppermute x12, waiting for transfers between devices, ring_shift(): return lax.ppermute(x, axis, [(i, (i + d) % n) for i in range(n)])  5.16 us
    ppermute x2, starting transfers between devices, ctx_gather(): from_y = lax.ppermute(x, 'ctx', along_y)  3.44 us
    unnamed x37, local copies, waits for them, and re-layouts  3.03 us
    ppermute x2, starting transfers between devices, ctx_gather(): from_x = lax.ppermute(x, 'ctx', along_x)  2.98 us
    broadcast_in_dim x2, other arithmetic, shards(): return (dq[None, None], dkr[None, None], dvr[None, None], d_prefix)  2.79 us
    ppermute x2, waiting for transfers between devices, ctx_reduce(): got_x = lax.ppermute(send_x, 'ctx', along_x)  2.65 us
  transfers between devices with their start and end apart: 28, of which 6 were waited for; matrix products, arithmetic and copies ran while one was open for 8% of the time, Pallas kernels for 21%

profile of v6, /device:TPU:0, one launch (start us, length us, event | category | flops | bytes accessed | tf_op | source)
XLA Modules:
  0.0 91.8 jit_solution(16476155676460317762)
XLA Ops:
  10.6 3.1 %collective-permute-start = (bf16[2,128,128]{2,1,0:T(8,128)(2,1)S(1)}, bf16[2,128,128]{2,1,0:T(8,128)(2,1)S(1)}, u32[]{:S(2)}, u32[]{:S(2)}) collective-permute-start(bf16[2,128,128]{2,1,0:T(8,128)(2,1)S(1)} %get-tuple-element.45), channel_id=1, source_target_pairs={{0,2},{2,4},{4,6},{6,0},{1,3},{3,5},{5,7},{7,1},{8,10},{10,12},{12... | collective-permute-start | bytes 196616 | tf_op jit(solution)/shard_map/ppermute | solution.py:157
  13.7 2.6 %collective-permute-start.1 = (bf16[2,128,128]{2,1,0:T(8,128)(2,1)S(1)}, bf16[2,128,128]{2,1,0:T(8,128)(2,1)S(1)}, u32[]{:S(2)}, u32[]{:S(2)}) collective-permute-start(bf16[2,128,128]{2,1,0:T(8,128)(2,1)S(1)} %get-tuple-element.44), channel_id=1, source_target_pairs={{0,4},{2,6},{4,0},{6,2},{1,5},{3,7},{5,1},{7,3},{8,12},{10,14},{12... | collective-permute-start | bytes 196616 | tf_op jit(solution)/shard_map/ppermute | solution.py:157
  16.3 1.3 %collective-permute-start.2 = (bf16[2,128,128]{2,1,0:T(8,128)(2,1)S(1)}, bf16[2,128,128]{2,1,0:T(8,128)(2,1)S(1)}, u32[]{:S(2)}, u32[]{:S(2)}) collective-permute-start(bf16[2,128,128]{2,1,0:T(8,128)(2,1)S(1)} %get-tuple-element.43), channel_id=1, source_target_pairs={{0,6},{2,0},{4,2},{6,4},{1,7},{3,1},{5,3},{7,5},{8,14},{10,8},{12,... | collective-permute-start | bytes 196616 | tf_op jit(solution)/shard_map/ppermute | solution.py:157
  18.7 2.9 %collective-permute-start.9 = (bf16[2,128,128]{2,1,0:T(8,128)(2,1)S(1)}, bf16[2,128,128]{2,1,0:T(8,128)(2,1)S(1)}, u32[]{:S(2)}, u32[]{:S(2)}) collective-permute-start(bf16[2,128,128]{2,1,0:T(8,128)(2,1)S(1)} %get-tuple-element.39), channel_id=1, source_target_pairs={{0,6},{2,0},{4,2},{6,4},{1,7},{3,1},{5,3},{7,5},{8,14},{10,8},{12,... | collective-permute-start | bytes 196616 | tf_op jit(solution)/shard_map/ppermute | solution.py:157
  21.7 1.6 %collective-permute-start.4 = (bf16[4,2,128,128]{3,2,1,0:T(8,128)(2,1)S(1)}, bf16[4,2,128,128]{3,2,1,0:T(8,128)(2,1)S(1)}, u32[]{:S(2)}, u32[]{:S(2)}) collective-permute-start(bf16[4,2,128,128]{3,2,1,0:T(8,128)(2,1)S(1)} %pad_maximum_fusion.1.refs_0_.refs_5_), channel_id=1, source_target_pairs={{0,16},{8,24},{16,0},{24,8},{1,17},{9,25},{17,1},{25,9},{2,18},{10... | collective-permute-start | bytes 786440 | tf_op jit(solution)/shard_map/ppermute | solution.py:182
  23.3 1.5 %collective-permute-start.3 = (bf16[4,2,128,128]{3,2,1,0:T(8,128)(2,1)S(1)}, bf16[4,2,128,128]{3,2,1,0:T(8,128)(2,1)S(1)}, u32[]{:S(2)}, u32[]{:S(2)}) collective-permute-start(bf16[4,2,128,128]{3,2,1,0:T(8,128)(2,1)S(1)} %pad_maximum_fusion.1.refs_0_.refs_5_), channel_id=1, source_target_pairs={{0,8},{8,0},{16,24},{24,16},{1,9},{9,1},{17,25},{25,17},{2,10},{10... | collective-permute-start | bytes 786440 | tf_op jit(solution)/shard_map/ppermute | solution.py:181
  24.8 1.6 %collective-permute-done.8 = bf16[2,128,128]{2,1,0:T(8,128)(2,1)S(1)} collective-permute-done((bf16[2,128,128]{2,1,0:T(8,128)(2,1)S(1)}, bf16[2,128,128]{2,1,0:T(8,128)(2,1)S(1)}, u32[]{:S(2)}, u32[]{:S(2)}) %collective-permute-start.8) | collective-permute-done | bytes 65568 | tf_op jit(solution)/shard_map/ppermute | solution.py:157
  26.5 1.9 %collective-permute-start.11 = (bf16[4,2,128,128]{3,2,1,0:T(8,128)(2,1)S(1)}, bf16[4,2,128,128]{3,2,1,0:T(8,128)(2,1)S(1)}, u32[]{:S(2)}, u32[]{:S(2)}) collective-permute-start(bf16[4,2,128,128]{3,2,1,0:T(8,128)(2,1)S(1)} %pad_maximum_fusion.2.refs_0_.refs_5_), channel_id=1, source_target_pairs={{0,16},{8,24},{16,0},{24,8},{1,17},{9,25},{17,1},{25,9},{2,18},{10... | collective-permute-start | bytes 786440 | tf_op jit(solution)/shard_map/ppermute | solution.py:182
  28.3 1.5 %collective-permute-start.10 = (bf16[4,2,128,128]{3,2,1,0:T(8,128)(2,1)S(1)}, bf16[4,2,128,128]{3,2,1,0:T(8,128)(2,1)S(1)}, u32[]{:S(2)}, u32[]{:S(2)}) collective-permute-start(bf16[4,2,128,128]{3,2,1,0:T(8,128)(2,1)S(1)} %pad_maximum_fusion.2.refs_0_.refs_5_), channel_id=1, source_target_pairs={{0,8},{8,0},{16,24},{24,16},{1,9},{9,1},{17,25},{25,17},{2,10},{10... | collective-permute-start | bytes 786440 | tf_op jit(solution)/shard_map/ppermute | solution.py:181
  29.8 1.3 %compare_convert_fusion = (f32[2]{0:T(128)S(1)}, f32[2]{0:T(128)S(1)}) fusion(s32[]{:T(128)} %bitcast.37, s32[]{:T(128)} %bitcast.34), kind=kLoop, calls=%fused_computation.59 | loop fusion | flops 8 | bytes 24 | tf_op jit(solution)/shard_map/convert_element_type | solution.py:226
  33.4 2.3 %collective-permute-done.11.refs_2_.refs_7_ = bf16[4,2,128,128]{3,2,1,0:T(8,128)(2,1)S(1)} collective-permute-done((bf16[4,2,128,128]{3,2,1,0:T(8,128)(2,1)S(1)}, bf16[4,2,128,128]{3,2,1,0:T(8,128)(2,1)S(1)}, u32[]{:S(2)}, u32[]{:S(2)}) %collective-permute-start.11) | collective-permute-done | bytes 262176 | tf_op jit(solution)/shard_map/ppermute | solution.py:182
  35.7 1.4 %collective-permute-start.12 = (bf16[4,2,64,128]{3,2,1,0:T(8,128)(2,1)S(1)}, bf16[4,2,64,128]{3,2,1,0:T(8,128)(2,1)S(1)}, u32[]{:S(2)}, u32[]{:S(2)}) collective-permute-start(bf16[4,2,64,128]{3,2,1,0:T(8,128)(2,1)S(1)} %slice.92), channel_id=1, source_target_pairs={{0,8},{8,0},{16,24},{24,16},{1,9},{9,1},{17,25},{25,17},{2,10},{10... | collective-permute-start | bytes 393224 | tf_op jit(solution)/shard_map/ppermute | solution.py:184
  40.8 9.4 %shard_map.111 = (bf16[128,2048]{1,0:T(8,128)(2,1)}, bf16[128,1024]{1,0:T(8,128)(2,1)}, bf16[128,1024]{1,0:T(8,128)(2,1)}, bf16[4,2,128,128]{3,2,1,0:T(8,128)(2,...) custom-call(s32[4]{0:T(128)} %bitcast.98, s32[1]{0:T(128)} %bitcast.81.length_ref, ...), custom_call_target="tpu_custom_call" | custom-call | flops 1006632960 | bytes 3670016 | tf_op jit(solution)/shard_map/pallas_call | solution.py:138
  53.3 9.5 %shard_map.112 = (bf16[128,2048]{1,0:T(8,128)(2,1)}, bf16[128,1024]{1,0:T(8,128)(2,1)}, bf16[128,1024]{1,0:T(8,128)(2,1)}, bf16[4,2,128,128]{3,2,1,0:T(8,128)(2,...) custom-call(s32[4]{0:T(128)} %bitcast.99, s32[1]{0:T(128)} %bitcast.82.length_ref, ...), custom_call_target="tpu_custom_call" | custom-call | flops 1006632960 | bytes 3670016 | tf_op jit(solution)/shard_map/pallas_call | solution.py:138
  64.6 1.9 %select_bitcast_fusion = bf16[1,1,128,2048]{3,2,1,0:T(8,128)(2,1)} fusion(bf16[128,2048]{1,0:T(8,128)(2,1)S(1)} %copy-done, bf16[128,2048]{1,0:T(8,128)(2,1)} %get-tuple-element.17, pred[2048]{0:T(1024)(128)(4,1)S(1)} %fusion.1), kind=kLoop, calls=%fused_computation.3 | loop fusion | flops 262144 | bytes 1574912 | tf_op jit(solution)/shard_map/broadcast_in_dim | solution.py:267
  67.5 1.6 %collective-permute-start.24 = (bf16[4,2,64,128]{3,2,1,0:T(8,128)(2,1)S(1)}, bf16[4,2,64,128]{3,2,1,0:T(8,128)(2,1)S(1)}, u32[]{:S(2)}, u32[]{:S(2)}) collective-permute-start(bf16[4,2,64,128]{3,2,1,0:T(8,128)(2,1)S(1)} %slice.105), channel_id=1, source_target_pairs={{0,8},{8,0},{16,24},{24,16},{1,9},{9,1},{17,25},{25,17},{2,10},{10... | collective-permute-start | bytes 393224 | tf_op jit(solution)/shard_map/ppermute | solution.py:211
  69.9 2.6 %collective-permute-done.14 = bf16[4,2,192,128]{3,2,1,0:T(8,128)(2,1)S(1)} collective-permute-done((bf16[4,2,192,128]{3,2,1,0:T(8,128)(2,1)}, bf16[4,2,192,128]{3,2,1,0:T(8,128)(2,1)S(1)}, u32[]{:S(2)}, u32[]{:S(2)}) %collective-permute-start.14) | collective-permute-done | bytes 393248 | tf_op jit(solution)/shard_map/ppermute | solution.py:208
  72.6 1.3 %collective-permute-start.16 = (bf16[4,2,64,128]{3,2,1,0:T(8,128)(2,1)S(1)}, bf16[4,2,64,128]{3,2,1,0:T(8,128)(2,1)S(1)}, u32[]{:S(2)}, u32[]{:S(2)}) collective-permute-start(bf16[4,2,64,128]{3,2,1,0:T(8,128)(2,1)S(1)} %slice.96), channel_id=1, source_target_pairs={{0,16},{8,24},{16,0},{24,8},{1,17},{9,25},{17,1},{25,9},{2,18},{10... | collective-permute-start | bytes 393224 | tf_op jit(solution)/shard_map/ppermute | solution.py:210
  75.1 4.0 %collective-permute-start.25 = (bf16[2,128,128]{2,1,0:T(8,128)(2,1)S(1)}, bf16[2,128,128]{2,1,0:T(8,128)(2,1)S(1)}, u32[]{:S(2)}, u32[]{:S(2)}) collective-permute-start(bf16[2,128,128]{2,1,0:T(8,128)(2,1)S(1)} %get-tuple-element.35), channel_id=1, source_target_pairs={{0,2},{2,4},{4,6},{6,0},{1,3},{3,5},{5,7},{7,1},{8,10},{10,12},{12... | collective-permute-start | bytes 196616 | tf_op jit(solution)/shard_map/ppermute | solution.py:157
  80.1 1.5 %collective-permute-start.27 = (bf16[2,128,128]{2,1,0:T(8,128)(2,1)S(1)}, bf16[2,128,128]{2,1,0:T(8,128)(2,1)S(1)}, u32[]{:S(2)}, u32[]{:S(2)}) collective-permute-start(bf16[2,128,128]{2,1,0:T(8,128)(2,1)S(1)} %get-tuple-element.33), channel_id=1, source_target_pairs={{0,6},{2,0},{4,2},{6,4},{1,7},{3,1},{5,3},{7,5},{8,14},{10,8},{12,... | collective-permute-start | bytes 196616 | tf_op jit(solution)/shard_map/ppermute | solution.py:157
  81.9 1.4 %collective-permute-start.18 = (bf16[2,128,128]{2,1,0:T(8,128)(2,1)S(1)}, bf16[2,128,128]{2,1,0:T(8,128)(2,1)S(1)}, u32[]{:S(2)}, u32[]{:S(2)}) collective-permute-start(bf16[2,128,128]{2,1,0:T(8,128)(2,1)S(1)} %get-tuple-element.31), channel_id=1, source_target_pairs={{0,2},{2,4},{4,6},{6,0},{1,3},{3,5},{5,7},{7,1},{8,10},{10,12},{12... | collective-permute-start | bytes 196616 | tf_op jit(solution)/shard_map/ppermute | solution.py:157
  83.3 1.5 %collective-permute-start.19 = (bf16[2,128,128]{2,1,0:T(8,128)(2,1)S(1)}, bf16[2,128,128]{2,1,0:T(8,128)(2,1)S(1)}, u32[]{:S(2)}, u32[]{:S(2)}) collective-permute-start(bf16[2,128,128]{2,1,0:T(8,128)(2,1)S(1)} %get-tuple-element.30), channel_id=1, source_target_pairs={{0,4},{2,6},{4,0},{6,2},{1,5},{3,7},{5,1},{7,3},{8,12},{10,14},{12... | collective-permute-start | bytes 196616 | tf_op jit(solution)/shard_map/ppermute | solution.py:157
  86.0 2.0 %collective-permute-done.18 = bf16[2,128,128]{2,1,0:T(8,128)(2,1)S(1)} collective-permute-done((bf16[2,128,128]{2,1,0:T(8,128)(2,1)S(1)}, bf16[2,128,128]{2,1,0:T(8,128)(2,1)S(1)}, u32[]{:S(2)}, u32[]{:S(2)}) %collective-permute-start.18) | collective-permute-done | bytes 65568 | tf_op jit(solution)/shard_map/ppermute | solution.py:157
  88.0 1.5 %collective-permute-done.19 = bf16[2,128,128]{2,1,0:T(8,128)(2,1)S(1)} collective-permute-done((bf16[2,128,128]{2,1,0:T(8,128)(2,1)S(1)}, bf16[2,128,128]{2,1,0:T(8,128)(2,1)S(1)}, u32[]{:S(2)}, u32[]{:S(2)}) %collective-permute-start.19) | collective-permute-done | bytes 65568 | tf_op jit(solution)/shard_map/ppermute | solution.py:157
  (112 shorter events, 21.2 us)
Async XLA Ops:
  10.6 8.1 %collective-permute-start = (bf16[2,128,128]{2,1,0:T(8,128)(2,1)S(1)}, bf16[2,128,128]{2,1,0:T(8,128)(2,1)S(1)}, u32[]{:S(2)}, u32[]{:S(2)}) collective-permute-start(bf16[2,128,128]{2,1,0:T(8,128)(2,1)S(1)} %get-tuple-element.45), channel_id=1, source_target_pairs={{0,2},{2,4},{4,6},{6,0},{1,3},{3,5},{5,7},{7,1},{8,10},{10,12},{12... | collective-permute-start | bytes 196616 | tf_op jit(solution)/shard_map/ppermute | solution.py:157
  13.7 7.9 %collective-permute-start.1 = (bf16[2,128,128]{2,1,0:T(8,128)(2,1)S(1)}, bf16[2,128,128]{2,1,0:T(8,128)(2,1)S(1)}, u32[]{:S(2)}, u32[]{:S(2)}) collective-permute-start(bf16[2,128,128]{2,1,0:T(8,128)(2,1)S(1)} %get-tuple-element.44), channel_id=1, source_target_pairs={{0,4},{2,6},{4,0},{6,2},{1,5},{3,7},{5,1},{7,3},{8,12},{10,14},{12... | collective-permute-start | bytes 196616 | tf_op jit(solution)/shard_map/ppermute | solution.py:157
  17.7 7.1 %collective-permute-start.7 = (bf16[2,128,128]{2,1,0:T(8,128)(2,1)S(1)}, bf16[2,128,128]{2,1,0:T(8,128)(2,1)S(1)}, u32[]{:S(2)}, u32[]{:S(2)}) collective-permute-start(bf16[2,128,128]{2,1,0:T(8,128)(2,1)S(1)} %get-tuple-element.41), channel_id=1, source_target_pairs={{0,2},{2,4},{4,6},{6,0},{1,3},{3,5},{5,7},{7,1},{8,10},{10,12},{12... | collective-permute-start | bytes 196616 | tf_op jit(solution)/shard_map/ppermute | solution.py:157
  18.4 8.0 %collective-permute-start.8 = (bf16[2,128,128]{2,1,0:T(8,128)(2,1)S(1)}, bf16[2,128,128]{2,1,0:T(8,128)(2,1)S(1)}, u32[]{:S(2)}, u32[]{:S(2)}) collective-permute-start(bf16[2,128,128]{2,1,0:T(8,128)(2,1)S(1)} %get-tuple-element.40), channel_id=1, source_target_pairs={{0,4},{2,6},{4,0},{6,2},{1,5},{3,7},{5,1},{7,3},{8,12},{10,14},{12... | collective-permute-start | bytes 196616 | tf_op jit(solution)/shard_map/ppermute | solution.py:157
  18.7 7.7 %collective-permute-start.9 = (bf16[2,128,128]{2,1,0:T(8,128)(2,1)S(1)}, bf16[2,128,128]{2,1,0:T(8,128)(2,1)S(1)}, u32[]{:S(2)}, u32[]{:S(2)}) collective-permute-start(bf16[2,128,128]{2,1,0:T(8,128)(2,1)S(1)} %get-tuple-element.39), channel_id=1, source_target_pairs={{0,6},{2,0},{4,2},{6,4},{1,7},{3,1},{5,3},{7,5},{8,14},{10,8},{12,... | collective-permute-start | bytes 196616 | tf_op jit(solution)/shard_map/ppermute | solution.py:157
  21.7 9.5 %collective-permute-start.4 = (bf16[4,2,128,128]{3,2,1,0:T(8,128)(2,1)S(1)}, bf16[4,2,128,128]{3,2,1,0:T(8,128)(2,1)S(1)}, u32[]{:S(2)}, u32[]{:S(2)}) collective-permute-start(bf16[4,2,128,128]{3,2,1,0:T(8,128)(2,1)S(1)} %pad_maximum_fusion.1.refs_0_.refs_5_), channel_id=1, source_target_pairs={{0,16},{8,24},{16,0},{24,8},{1,17},{9,25},{17,1},{25,9},{2,18},{10... | collective-permute-start | bytes 786440 | tf_op jit(solution)/shard_map/ppermute | solution.py:182
  23.3 8.5 %collective-permute-start.3 = (bf16[4,2,128,128]{3,2,1,0:T(8,128)(2,1)S(1)}, bf16[4,2,128,128]{3,2,1,0:T(8,128)(2,1)S(1)}, u32[]{:S(2)}, u32[]{:S(2)}) collective-permute-start(bf16[4,2,128,128]{3,2,1,0:T(8,128)(2,1)S(1)} %pad_maximum_fusion.1.refs_0_.refs_5_), channel_id=1, source_target_pairs={{0,8},{8,0},{16,24},{24,16},{1,9},{9,1},{17,25},{25,17},{2,10},{10... | collective-permute-start | bytes 786440 | tf_op jit(solution)/shard_map/ppermute | solution.py:181
  26.5 9.3 %collective-permute-start.11 = (bf16[4,2,128,128]{3,2,1,0:T(8,128)(2,1)S(1)}, bf16[4,2,128,128]{3,2,1,0:T(8,128)(2,1)S(1)}, u32[]{:S(2)}, u32[]{:S(2)}) collective-permute-start(bf16[4,2,128,128]{3,2,1,0:T(8,128)(2,1)S(1)} %pad_maximum_fusion.2.refs_0_.refs_5_), channel_id=1, source_target_pairs={{0,16},{8,24},{16,0},{24,8},{1,17},{9,25},{17,1},{25,9},{2,18},{10... | collective-permute-start | bytes 786440 | tf_op jit(solution)/shard_map/ppermute | solution.py:182
  28.3 9.2 %collective-permute-start.10 = (bf16[4,2,128,128]{3,2,1,0:T(8,128)(2,1)S(1)}, bf16[4,2,128,128]{3,2,1,0:T(8,128)(2,1)S(1)}, u32[]{:S(2)}, u32[]{:S(2)}) collective-permute-start(bf16[4,2,128,128]{3,2,1,0:T(8,128)(2,1)S(1)} %pad_maximum_fusion.2.refs_0_.refs_5_), channel_id=1, source_target_pairs={{0,8},{8,0},{16,24},{24,16},{1,9},{9,1},{17,25},{25,17},{2,10},{10... | collective-permute-start | bytes 786440 | tf_op jit(solution)/shard_map/ppermute | solution.py:181
  31.2 8.9 %collective-permute-start.5 = (bf16[4,2,64,128]{3,2,1,0:T(8,128)(2,1)S(1)}, bf16[4,2,64,128]{3,2,1,0:T(8,128)(2,1)S(1)}, u32[]{:S(2)}, u32[]{:S(2)}) collective-permute-start(bf16[4,2,64,128]{3,2,1,0:T(8,128)(2,1)S(1)} %slice.89), channel_id=1, source_target_pairs={{0,8},{8,0},{16,24},{24,16},{1,9},{9,1},{17,25},{25,17},{2,10},{10... | collective-permute-start | bytes 393224 | tf_op jit(solution)/shard_map/ppermute | solution.py:184
  31.8 8.3 %collective-permute-start.6 = (bf16[4,2,64,128]{3,2,1,0:T(8,128)(2,1)S(1)}, bf16[4,2,64,128]{3,2,1,0:T(8,128)(2,1)S(1)}, u32[]{:S(2)}, u32[]{:S(2)}) collective-permute-start(bf16[4,2,64,128]{3,2,1,0:T(8,128)(2,1)S(1)} %slice.90), channel_id=1, source_target_pairs={{0,16},{8,24},{16,0},{24,8},{1,17},{9,25},{17,1},{25,9},{2,18},{10... | collective-permute-start | bytes 393224 | tf_op jit(solution)/shard_map/ppermute | solution.py:185
  35.7 16.8 %collective-permute-start.12 = (bf16[4,2,64,128]{3,2,1,0:T(8,128)(2,1)S(1)}, bf16[4,2,64,128]{3,2,1,0:T(8,128)(2,1)S(1)}, u32[]{:S(2)}, u32[]{:S(2)}) collective-permute-start(bf16[4,2,64,128]{3,2,1,0:T(8,128)(2,1)S(1)} %slice.92), channel_id=1, source_target_pairs={{0,8},{8,0},{16,24},{24,16},{1,9},{9,1},{17,25},{25,17},{2,10},{10... | collective-permute-start | bytes 393224 | tf_op jit(solution)/shard_map/ppermute | solution.py:184
  37.6 15.0 %collective-permute-start.13 = (bf16[4,2,64,128]{3,2,1,0:T(8,128)(2,1)S(1)}, bf16[4,2,64,128]{3,2,1,0:T(8,128)(2,1)S(1)}, u32[]{:S(2)}, u32[]{:S(2)}) collective-permute-start(bf16[4,2,64,128]{3,2,1,0:T(8,128)(2,1)S(1)} %slice.93), channel_id=1, source_target_pairs={{0,16},{8,24},{16,0},{24,8},{1,17},{9,25},{17,1},{25,9},{2,18},{10... | collective-permute-start | bytes 393224 | tf_op jit(solution)/shard_map/ppermute | solution.py:185
  50.2 16.4 %collective-permute-start.21 = (bf16[4,2,192,128]{3,2,1,0:T(8,128)(2,1)}, bf16[4,2,192,128]{3,2,1,0:T(8,128)(2,1)S(1)}, u32[]{:S(2)}, u32[]{:S(2)}) collective-permute-start(bf16[4,2,192,128]{3,2,1,0:T(8,128)(2,1)} %get-tuple-element.26), channel_id=1, source_target_pairs={{0,8},{8,0},{16,24},{24,16},{1,9},{9,1},{17,25},{25,17},{2,10},{10... | collective-permute-start | bytes 1179656 | tf_op jit(solution)/shard_map/ppermute | solution.py:208
  51.4 16.1 %collective-permute-start.22 = (bf16[4,2,192,128]{3,2,1,0:T(8,128)(2,1)}, bf16[4,2,192,128]{3,2,1,0:T(8,128)(2,1)S(1)}, u32[]{:S(2)}, u32[]{:S(2)}) collective-permute-start(bf16[4,2,192,128]{3,2,1,0:T(8,128)(2,1)} %get-tuple-element.27), channel_id=1, source_target_pairs={{0,16},{8,24},{16,0},{24,8},{1,17},{9,25},{17,1},{25,9},{2,18},{10... | collective-permute-start | bytes 1179656 | tf_op jit(solution)/shard_map/ppermute | solution.py:209
  62.8 9.8 %collective-permute-start.14 = (bf16[4,2,192,128]{3,2,1,0:T(8,128)(2,1)}, bf16[4,2,192,128]{3,2,1,0:T(8,128)(2,1)S(1)}, u32[]{:S(2)}, u32[]{:S(2)}) collective-permute-start(bf16[4,2,192,128]{3,2,1,0:T(8,128)(2,1)} %get-tuple-element.23), channel_id=1, source_target_pairs={{0,8},{8,0},{16,24},{24,16},{1,9},{9,1},{17,25},{25,17},{2,10},{10... | collective-permute-start | bytes 1179656 | tf_op jit(solution)/shard_map/ppermute | solution.py:208
  63.4 10.5 %collective-permute-start.15 = (bf16[4,2,192,128]{3,2,1,0:T(8,128)(2,1)}, bf16[4,2,192,128]{3,2,1,0:T(8,128)(2,1)S(1)}, u32[]{:S(2)}, u32[]{:S(2)}) collective-permute-start(bf16[4,2,192,128]{3,2,1,0:T(8,128)(2,1)} %get-tuple-element.24), channel_id=1, source_target_pairs={{0,16},{8,24},{16,0},{24,8},{1,17},{9,25},{17,1},{25,9},{2,18},{10... | collective-permute-start | bytes 1179656 | tf_op jit(solution)/shard_map/ppermute | solution.py:209
  66.6 8.3 %collective-permute-start.23 = (bf16[4,2,64,128]{3,2,1,0:T(8,128)(2,1)S(1)}, bf16[4,2,64,128]{3,2,1,0:T(8,128)(2,1)S(1)}, u32[]{:S(2)}, u32[]{:S(2)}) collective-permute-start(bf16[4,2,64,128]{3,2,1,0:T(8,128)(2,1)S(1)} %slice.104), channel_id=1, source_target_pairs={{0,16},{8,24},{16,0},{24,8},{1,17},{9,25},{17,1},{25,9},{2,18},{10... | collective-permute-start | bytes 393224 | tf_op jit(solution)/shard_map/ppermute | solution.py:210
  67.5 7.4 %collective-permute-start.24 = (bf16[4,2,64,128]{3,2,1,0:T(8,128)(2,1)S(1)}, bf16[4,2,64,128]{3,2,1,0:T(8,128)(2,1)S(1)}, u32[]{:S(2)}, u32[]{:S(2)}) collective-permute-start(bf16[4,2,64,128]{3,2,1,0:T(8,128)(2,1)S(1)} %slice.105), channel_id=1, source_target_pairs={{0,8},{8,0},{16,24},{24,16},{1,9},{9,1},{17,25},{25,17},{2,10},{10... | collective-permute-start | bytes 393224 | tf_op jit(solution)/shard_map/ppermute | solution.py:211
  72.6 9.0 %collective-permute-start.16 = (bf16[4,2,64,128]{3,2,1,0:T(8,128)(2,1)S(1)}, bf16[4,2,64,128]{3,2,1,0:T(8,128)(2,1)S(1)}, u32[]{:S(2)}, u32[]{:S(2)}) collective-permute-start(bf16[4,2,64,128]{3,2,1,0:T(8,128)(2,1)S(1)} %slice.96), channel_id=1, source_target_pairs={{0,16},{8,24},{16,0},{24,8},{1,17},{9,25},{17,1},{25,9},{2,18},{10... | collective-permute-start | bytes 393224 | tf_op jit(solution)/shard_map/ppermute | solution.py:210
  73.9 7.7 %collective-permute-start.17 = (bf16[4,2,64,128]{3,2,1,0:T(8,128)(2,1)S(1)}, bf16[4,2,64,128]{3,2,1,0:T(8,128)(2,1)S(1)}, u32[]{:S(2)}, u32[]{:S(2)}) collective-permute-start(bf16[4,2,64,128]{3,2,1,0:T(8,128)(2,1)S(1)} %slice.97), channel_id=1, source_target_pairs={{0,8},{8,0},{16,24},{24,16},{1,9},{9,1},{17,25},{25,17},{2,10},{10... | collective-permute-start | bytes 393224 | tf_op jit(solution)/shard_map/ppermute | solution.py:211
  75.1 9.8 %collective-permute-start.25 = (bf16[2,128,128]{2,1,0:T(8,128)(2,1)S(1)}, bf16[2,128,128]{2,1,0:T(8,128)(2,1)S(1)}, u32[]{:S(2)}, u32[]{:S(2)}) collective-permute-start(bf16[2,128,128]{2,1,0:T(8,128)(2,1)S(1)} %get-tuple-element.35), channel_id=1, source_target_pairs={{0,2},{2,4},{4,6},{6,0},{1,3},{3,5},{5,7},{7,1},{8,10},{10,12},{12... | collective-permute-start | bytes 196616 | tf_op jit(solution)/shard_map/ppermute | solution.py:157
  79.1 6.8 %collective-permute-start.26 = (bf16[2,128,128]{2,1,0:T(8,128)(2,1)S(1)}, bf16[2,128,128]{2,1,0:T(8,128)(2,1)S(1)}, u32[]{:S(2)}, u32[]{:S(2)}) collective-permute-start(bf16[2,128,128]{2,1,0:T(8,128)(2,1)S(1)} %get-tuple-element.34), channel_id=1, source_target_pairs={{0,4},{2,6},{4,0},{6,2},{1,5},{3,7},{5,1},{7,3},{8,12},{10,14},{12... | collective-permute-start | bytes 196616 | tf_op jit(solution)/shard_map/ppermute | solution.py:157
  83.3 6.2 %collective-permute-start.19 = (bf16[2,128,128]{2,1,0:T(8,128)(2,1)S(1)}, bf16[2,128,128]{2,1,0:T(8,128)(2,1)S(1)}, u32[]{:S(2)}, u32[]{:S(2)}) collective-permute-start(bf16[2,128,128]{2,1,0:T(8,128)(2,1)S(1)} %get-tuple-element.30), channel_id=1, source_target_pairs={{0,4},{2,6},{4,0},{6,2},{1,5},{3,7},{5,1},{7,3},{8,12},{10,14},{12... | collective-permute-start | bytes 196616 | tf_op jit(solution)/shard_map/ppermute | solution.py:157
  (22 other events, 92.1 us)

commit v7 on v6

--- a/solution.py
+++ b/solution.py
@@ -44,46 +44,44 @@
         source = jnp.bitwise_xor(c, slot) if xor_slots else slot
         flag = jnp.where(col_block == b, blocks_ref[source * slot_blocks + sub], flag)
     pre_ok = flag > 0
-    row_i = lax.broadcasted_iota(jnp.int32, (resp_rows, resp_rows), 0)
-    col_i = lax.broadcasted_iota(jnp.int32, (resp_rows, resp_rows), 1)
+    rows = GROUP * resp_rows
+    row_i = lax.broadcasted_iota(jnp.int32, (rows, resp_rows), 0) % resp_rows
+    col_i = lax.broadcasted_iota(jnp.int32, (rows, resp_rows), 1)
     causal = row_i >= col_i
-    live = lax.broadcasted_iota(jnp.int32, (resp_rows, 1), 0) < length_ref[0]
-
-    dkp = jnp.zeros((pre_rows, HEAD_DIM), jnp.float32)
-    dvp = jnp.zeros((pre_rows, HEAD_DIM), jnp.float32)
-    dkr = jnp.zeros((resp_rows, HEAD_DIM), jnp.float32)
-    dvr = jnp.zeros((resp_rows, HEAD_DIM), jnp.float32)
-    for j in range(GROUP):
-        cols = slice(j * HEAD_DIM, (j + 1) * HEAD_DIM)
-        qj = q_ref[:, cols]
-        doj = jnp.where(live, do_ref[:, cols], jnp.zeros_like(do_ref[:, cols]))
-        sp = lax.dot_general(qj, kp, NT, preferred_element_type=jnp.float32) * scale_factor
-        sr = lax.dot_general(qj, kr, NT, preferred_element_type=jnp.float32) * scale_factor
-        sp = jnp.where(pre_ok, sp, neg_big)
-        sr = jnp.where(causal, sr, neg_big)
-        peak = jnp.maximum(jnp.max(sp, axis=-1, keepdims=True), jnp.max(sr, axis=-1, keepdims=True))
-        ep = jnp.exp(sp - peak)
-        er = jnp.exp(sr - peak)
-        total = jnp.sum(ep, axis=-1, keepdims=True) + jnp.sum(er, axis=-1, keepdims=True)
-        wp = ep / total
-        wr = er / total
-        pp = wp.astype(jnp.bfloat16)
-        pr = wr.astype(jnp.bfloat16)
-        att = jnp.dot(pp, vp, preferred_element_type=jnp.float32) + jnp.dot(
-            pr, vr, preferred_element_type=jnp.float32)
-        att = att.astype(jnp.bfloat16).astype(jnp.float32)
-        delta = jnp.sum(doj.astype(jnp.float32) * att, axis=-1, keepdims=True)
-        dpp = lax.dot_general(doj, vp, NT, preferred_element_type=jnp.float32)
-        dpr = lax.dot_general(doj, vr, NT, preferred_element_type=jnp.float32)
-        dsp = (wp * (dpp - delta)).astype(jnp.bfloat16)
-        dsr = (wr * (dpr - delta)).astype(jnp.bfloat16)
-        dq = (jnp.dot(dsp, kp, preferred_element_type=jnp.float32) + jnp.dot(
-            dsr, kr, preferred_element_type=jnp.float32)) * scale_factor
-        dq_ref[:, cols] = dq.astype(dq_ref.dtype)
-        dkp = dkp + lax.dot_general(dsp, qj, TN, preferred_element_type=jnp.float32)
-        dkr = dkr + lax.dot_general(dsr, qj, TN, preferred_element_type=jnp.float32)
-        dvp = dvp + lax.dot_general(pp, doj, TN, preferred_element_type=jnp.float32)
-        dvr = dvr + lax.dot_general(pr, doj, TN, preferred_element_type=jnp.float32)
+    live = lax.broadcasted_iota(jnp.int32, (rows, 1), 0) % resp_rows < length_ref[0]
+    heads = [slice(j * HEAD_DIM, (j + 1) * HEAD_DIM) for j in range(GROUP)]
+    q2 = jnp.concatenate([q_ref[:, cols] for cols in heads], 0)
+    do2 = jnp.concatenate([do_ref[:, cols] for cols in heads], 0)
+    do2 = jnp.where(live, do2, jnp.zeros_like(do2))
+
+    sp = lax.dot_general(q2, kp, NT, preferred_element_type=jnp.float32) * scale_factor
+    sr = lax.dot_general(q2, kr, NT, preferred_element_type=jnp.float32) * scale_factor
+    sp = jnp.where(pre_ok, sp, neg_big)
+    sr = jnp.where(causal, sr, neg_big)
+    peak = jnp.maximum(jnp.max(sp, axis=-1, keepdims=True), jnp.max(sr, axis=-1, keepdims=True))
+    ep = jnp.exp(sp - peak)
+    er = jnp.exp(sr - peak)
+    inv = 1.0 / (jnp.sum(ep, axis=-1, keepdims=True) + jnp.sum(er, axis=-1, keepdims=True))
+    wp = ep * inv
+    wr = er * inv
+    pp = wp.astype(jnp.bfloat16)
+    pr = wr.astype(jnp.bfloat16)
+    att = jnp.dot(pp, vp, preferred_element_type=jnp.float32) + jnp.dot(pr, vr, preferred_element_type=jnp.float32)
+    att = att.astype(jnp.bfloat16).astype(jnp.float32)
+    delta = jnp.sum(do2.astype(jnp.float32) * att, axis=-1, keepdims=True)
+    dpp = lax.dot_general(do2, vp, NT, preferred_element_type=jnp.float32)
+    dpr = lax.dot_general(do2, vr, NT, preferred_element_type=jnp.float32)
+    dsp = (wp * (dpp - delta)).astype(jnp.bfloat16)
+    dsr = (wr * (dpr - delta)).astype(jnp.bfloat16)
+    dq = (jnp.dot(dsp, kp, preferred_element_type=jnp.float32) + jnp.dot(
+        dsr, kr, preferred_element_type=jnp.float32)) * scale_factor
+    dq = dq.astype(dq_ref.dtype)
+    for j, cols in enumerate(heads):
+        dq_ref[:, cols] = dq[j * resp_rows:(j + 1) * resp_rows]
+    dkp = lax.dot_general(dsp, q2, TN, preferred_element_type=jnp.float32)
+    dkr = lax.dot_general(dsr, q2, TN, preferred_element_type=jnp.float32)
+    dvp = lax.dot_general(pp, do2, TN, preferred_element_type=jnp.float32)
+    dvr = lax.dot_general(pr, do2, TN, preferred_element_type=jnp.float32)
     dkr_ref[...] = (dkr * scale_factor).astype(dkr_ref.dtype)
     dvr_ref[...] = dvr.astype(dvr_ref.dtype)
     dkp = (dkp * scale_factor).astype(jnp.bfloat16)

time: 92.3 us -> 88.3 us (0.957)
  Pallas kernels: 18.9 us -> 14.9 us
    pallas_call x2, Pallas kernels: 18.9 us -> 14.9 us  [attention_grads(): pl.pallas_call(functools.partial(attention_grad_kernel, layout), out_shap...]
  transfers between devices with their start and end apart: 28 -> 28, of which waited for: 6 -> 6; matrix products, arithmetic and copies ran while one was open for 8% -> 8% of each run, Pallas kernels for 21% -> 17%
where the time goes in v7:
time: 88.3 us; the launch traced here: 87.8 us
  starting transfers between devices  40.3 us (46%)
  Pallas kernels  14.9 us (17%)
  waiting for transfers between devices  10.6 us (12%)
  between operations  9.31 us (11%)
  other arithmetic  8.03 us (9%)
  local copies, waits for them, and re-layouts  4.7 us (5%)
    ppermute x12, starting transfers between devices, ring_shift(): return lax.ppermute(x, axis, [(i, (i + d) % n) for i in range(n)])  21.4 us
    pallas_call x2, Pallas kernels, attention_grads(): pl.pallas_call(functools.partial(attention_grad_kernel, layout), out_shap...  14.9 us
    ppermute x12, waiting for transfers between devices, ring_shift(): return lax.ppermute(x, axis, [(i, (i + d) % n) for i in range(n)])  5.15 us
    ppermute x2, starting transfers between devices, ctx_gather(): from_y = lax.ppermute(x, 'ctx', along_y)  3.44 us
    unnamed x37, local copies, waits for them, and re-layouts  3.03 us
    ppermute x2, starting transfers between devices, ctx_gather(): from_x = lax.ppermute(x, 'ctx', along_x)  2.98 us
    broadcast_in_dim x2, other arithmetic, shards(): return (dq[None, None], dkr[None, None], dvr[None, None], d_prefix)  2.79 us
    ppermute x2, waiting for transfers between devices, ctx_reduce(): got_x = lax.ppermute(send_x, 'ctx', along_x)  2.65 us
  transfers between devices with their start and end apart: 28, of which 6 were waited for; matrix products, arithmetic and copies ran while one was open for 8% of the time, Pallas kernels for 17%

profile of v7, /device:TPU:0, one launch (start us, length us, event | category | flops | bytes accessed | tf_op | source)
XLA Modules:
  0.0 87.8 jit_solution(8685848538364416273)
XLA Ops:
  10.6 3.1 %collective-permute-start = (bf16[2,128,128]{2,1,0:T(8,128)(2,1)S(1)}, bf16[2,128,128]{2,1,0:T(8,128)(2,1)S(1)}, u32[]{:S(2)}, u32[]{:S(2)}) collective-permute-start(bf16[2,128,128]{2,1,0:T(8,128)(2,1)S(1)} %get-tuple-element.45), channel_id=1, source_target_pairs={{0,2},{2,4},{4,6},{6,0},{1,3},{3,5},{5,7},{7,1},{8,10},{10,12},{12... | collective-permute-start | bytes 196616 | tf_op jit(solution)/shard_map/ppermute | solution.py:155
  13.7 2.6 %collective-permute-start.1 = (bf16[2,128,128]{2,1,0:T(8,128)(2,1)S(1)}, bf16[2,128,128]{2,1,0:T(8,128)(2,1)S(1)}, u32[]{:S(2)}, u32[]{:S(2)}) collective-permute-start(bf16[2,128,128]{2,1,0:T(8,128)(2,1)S(1)} %get-tuple-element.44), channel_id=1, source_target_pairs={{0,4},{2,6},{4,0},{6,2},{1,5},{3,7},{5,1},{7,3},{8,12},{10,14},{12... | collective-permute-start | bytes 196616 | tf_op jit(solution)/shard_map/ppermute | solution.py:155
  16.3 1.3 %collective-permute-start.2 = (bf16[2,128,128]{2,1,0:T(8,128)(2,1)S(1)}, bf16[2,128,128]{2,1,0:T(8,128)(2,1)S(1)}, u32[]{:S(2)}, u32[]{:S(2)}) collective-permute-start(bf16[2,128,128]{2,1,0:T(8,128)(2,1)S(1)} %get-tuple-element.43), channel_id=1, source_target_pairs={{0,6},{2,0},{4,2},{6,4},{1,7},{3,1},{5,3},{7,5},{8,14},{10,8},{12,... | collective-permute-start | bytes 196616 | tf_op jit(solution)/shard_map/ppermute | solution.py:155
  18.7 2.9 %collective-permute-start.9 = (bf16[2,128,128]{2,1,0:T(8,128)(2,1)S(1)}, bf16[2,128,128]{2,1,0:T(8,128)(2,1)S(1)}, u32[]{:S(2)}, u32[]{:S(2)}) collective-permute-start(bf16[2,128,128]{2,1,0:T(8,128)(2,1)S(1)} %get-tuple-element.39), channel_id=1, source_target_pairs={{0,6},{2,0},{4,2},{6,4},{1,7},{3,1},{5,3},{7,5},{8,14},{10,8},{12,... | collective-permute-start | bytes 196616 | tf_op jit(solution)/shard_map/ppermute | solution.py:155
  21.7 1.6 %collective-permute-start.4 = (bf16[4,2,128,128]{3,2,1,0:T(8,128)(2,1)S(1)}, bf16[4,2,128,128]{3,2,1,0:T(8,128)(2,1)S(1)}, u32[]{:S(2)}, u32[]{:S(2)}) collective-permute-start(bf16[4,2,128,128]{3,2,1,0:T(8,128)(2,1)S(1)} %pad_maximum_fusion.1.refs_0_.refs_5_), channel_id=1, source_target_pairs={{0,16},{8,24},{16,0},{24,8},{1,17},{9,25},{17,1},{25,9},{2,18},{10... | collective-permute-start | bytes 786440 | tf_op jit(solution)/shard_map/ppermute | solution.py:180
  23.3 1.5 %collective-permute-start.3 = (bf16[4,2,128,128]{3,2,1,0:T(8,128)(2,1)S(1)}, bf16[4,2,128,128]{3,2,1,0:T(8,128)(2,1)S(1)}, u32[]{:S(2)}, u32[]{:S(2)}) collective-permute-start(bf16[4,2,128,128]{3,2,1,0:T(8,128)(2,1)S(1)} %pad_maximum_fusion.1.refs_0_.refs_5_), channel_id=1, source_target_pairs={{0,8},{8,0},{16,24},{24,16},{1,9},{9,1},{17,25},{25,17},{2,10},{10... | collective-permute-start | bytes 786440 | tf_op jit(solution)/shard_map/ppermute | solution.py:179
  24.8 1.6 %collective-permute-done.8 = bf16[2,128,128]{2,1,0:T(8,128)(2,1)S(1)} collective-permute-done((bf16[2,128,128]{2,1,0:T(8,128)(2,1)S(1)}, bf16[2,128,128]{2,1,0:T(8,128)(2,1)S(1)}, u32[]{:S(2)}, u32[]{:S(2)}) %collective-permute-start.8) | collective-permute-done | bytes 65568 | tf_op jit(solution)/shard_map/ppermute | solution.py:155
  26.5 1.9 %collective-permute-start.11 = (bf16[4,2,128,128]{3,2,1,0:T(8,128)(2,1)S(1)}, bf16[4,2,128,128]{3,2,1,0:T(8,128)(2,1)S(1)}, u32[]{:S(2)}, u32[]{:S(2)}) collective-permute-start(bf16[4,2,128,128]{3,2,1,0:T(8,128)(2,1)S(1)} %pad_maximum_fusion.2.refs_0_.refs_5_), channel_id=1, source_target_pairs={{0,16},{8,24},{16,0},{24,8},{1,17},{9,25},{17,1},{25,9},{2,18},{10... | collective-permute-start | bytes 786440 | tf_op jit(solution)/shard_map/ppermute | solution.py:180
  28.3 1.5 %collective-permute-start.10 = (bf16[4,2,128,128]{3,2,1,0:T(8,128)(2,1)S(1)}, bf16[4,2,128,128]{3,2,1,0:T(8,128)(2,1)S(1)}, u32[]{:S(2)}, u32[]{:S(2)}) collective-permute-start(bf16[4,2,128,128]{3,2,1,0:T(8,128)(2,1)S(1)} %pad_maximum_fusion.2.refs_0_.refs_5_), channel_id=1, source_target_pairs={{0,8},{8,0},{16,24},{24,16},{1,9},{9,1},{17,25},{25,17},{2,10},{10... | collective-permute-start | bytes 786440 | tf_op jit(solution)/shard_map/ppermute | solution.py:179
  29.8 1.3 %compare_convert_fusion = (f32[2]{0:T(128)S(1)}, f32[2]{0:T(128)S(1)}) fusion(s32[]{:T(128)} %bitcast.37, s32[]{:T(128)} %bitcast.34), kind=kLoop, calls=%fused_computation.59 | loop fusion | flops 8 | bytes 24 | tf_op jit(solution)/shard_map/convert_element_type | solution.py:224
  33.4 2.3 %collective-permute-done.11.refs_2_.refs_7_ = bf16[4,2,128,128]{3,2,1,0:T(8,128)(2,1)S(1)} collective-permute-done((bf16[4,2,128,128]{3,2,1,0:T(8,128)(2,1)S(1)}, bf16[4,2,128,128]{3,2,1,0:T(8,128)(2,1)S(1)}, u32[]{:S(2)}, u32[]{:S(2)}) %collective-permute-start.11) | collective-permute-done | bytes 262176 | tf_op jit(solution)/shard_map/ppermute | solution.py:180
  35.7 1.4 %collective-permute-start.12 = (bf16[4,2,64,128]{3,2,1,0:T(8,128)(2,1)S(1)}, bf16[4,2,64,128]{3,2,1,0:T(8,128)(2,1)S(1)}, u32[]{:S(2)}, u32[]{:S(2)}) collective-permute-start(bf16[4,2,64,128]{3,2,1,0:T(8,128)(2,1)S(1)} %slice.92), channel_id=1, source_target_pairs={{0,8},{8,0},{16,24},{24,16},{1,9},{9,1},{17,25},{25,17},{2,10},{10... | collective-permute-start | bytes 393224 | tf_op jit(solution)/shard_map/ppermute | solution.py:182
  40.8 7.4 %shard_map.111 = (bf16[128,2048]{1,0:T(8,128)(2,1)}, bf16[128,1024]{1,0:T(8,128)(2,1)}, bf16[128,1024]{1,0:T(8,128)(2,1)}, bf16[4,2,128,128]{3,2,1,0:T(8,128)(2,...) custom-call(s32[4]{0:T(128)} %bitcast.98, s32[1]{0:T(128)} %bitcast.81.length_ref, ...), custom_call_target="tpu_custom_call" | custom-call | flops 1006632960 | bytes 3670016 | tf_op jit(solution)/shard_map/pallas_call | solution.py:136
  51.3 7.5 %shard_map.112 = (bf16[128,2048]{1,0:T(8,128)(2,1)}, bf16[128,1024]{1,0:T(8,128)(2,1)}, bf16[128,1024]{1,0:T(8,128)(2,1)}, bf16[4,2,128,128]{3,2,1,0:T(8,128)(2,...) custom-call(s32[4]{0:T(128)} %bitcast.99, s32[1]{0:T(128)} %bitcast.82.length_ref, ...), custom_call_target="tpu_custom_call" | custom-call | flops 1006632960 | bytes 3670016 | tf_op jit(solution)/shard_map/pallas_call | solution.py:136
  60.6 1.9 %select_bitcast_fusion = bf16[1,1,128,2048]{3,2,1,0:T(8,128)(2,1)} fusion(bf16[128,2048]{1,0:T(8,128)(2,1)S(1)} %copy-done, bf16[128,2048]{1,0:T(8,128)(2,1)} %get-tuple-element.17, pred[2048]{0:T(1024)(128)(4,1)S(1)} %fusion.1), kind=kLoop, calls=%fused_computation.3 | loop fusion | flops 262144 | bytes 1574912 | tf_op jit(solution)/shard_map/broadcast_in_dim | solution.py:265
  63.5 1.6 %collective-permute-start.24 = (bf16[4,2,64,128]{3,2,1,0:T(8,128)(2,1)S(1)}, bf16[4,2,64,128]{3,2,1,0:T(8,128)(2,1)S(1)}, u32[]{:S(2)}, u32[]{:S(2)}) collective-permute-start(bf16[4,2,64,128]{3,2,1,0:T(8,128)(2,1)S(1)} %slice.105), channel_id=1, source_target_pairs={{0,8},{8,0},{16,24},{24,16},{1,9},{9,1},{17,25},{25,17},{2,10},{10... | collective-permute-start | bytes 393224 | tf_op jit(solution)/shard_map/ppermute | solution.py:209
  65.9 2.6 %collective-permute-done.14 = bf16[4,2,192,128]{3,2,1,0:T(8,128)(2,1)S(1)} collective-permute-done((bf16[4,2,192,128]{3,2,1,0:T(8,128)(2,1)}, bf16[4,2,192,128]{3,2,1,0:T(8,128)(2,1)S(1)}, u32[]{:S(2)}, u32[]{:S(2)}) %collective-permute-start.14) | collective-permute-done | bytes 393248 | tf_op jit(solution)/shard_map/ppermute | solution.py:206
  68.6 1.3 %collective-permute-start.16 = (bf16[4,2,64,128]{3,2,1,0:T(8,128)(2,1)S(1)}, bf16[4,2,64,128]{3,2,1,0:T(8,128)(2,1)S(1)}, u32[]{:S(2)}, u32[]{:S(2)}) collective-permute-start(bf16[4,2,64,128]{3,2,1,0:T(8,128)(2,1)S(1)} %slice.96), channel_id=1, source_target_pairs={{0,16},{8,24},{16,0},{24,8},{1,17},{9,25},{17,1},{25,9},{2,18},{10... | collective-permute-start | bytes 393224 | tf_op jit(solution)/shard_map/ppermute | solution.py:208
  71.1 4.0 %collective-permute-start.25 = (bf16[2,128,128]{2,1,0:T(8,128)(2,1)S(1)}, bf16[2,128,128]{2,1,0:T(8,128)(2,1)S(1)}, u32[]{:S(2)}, u32[]{:S(2)}) collective-permute-start(bf16[2,128,128]{2,1,0:T(8,128)(2,1)S(1)} %get-tuple-element.35), channel_id=1, source_target_pairs={{0,2},{2,4},{4,6},{6,0},{1,3},{3,5},{5,7},{7,1},{8,10},{10,12},{12... | collective-permute-start | bytes 196616 | tf_op jit(solution)/shard_map/ppermute | solution.py:155
  76.1 1.5 %collective-permute-start.27 = (bf16[2,128,128]{2,1,0:T(8,128)(2,1)S(1)}, bf16[2,128,128]{2,1,0:T(8,128)(2,1)S(1)}, u32[]{:S(2)}, u32[]{:S(2)}) collective-permute-start(bf16[2,128,128]{2,1,0:T(8,128)(2,1)S(1)} %get-tuple-element.33), channel_id=1, source_target_pairs={{0,6},{2,0},{4,2},{6,4},{1,7},{3,1},{5,3},{7,5},{8,14},{10,8},{12,... | collective-permute-start | bytes 196616 | tf_op jit(solution)/shard_map/ppermute | solution.py:155
  77.9 1.4 %collective-permute-start.18 = (bf16[2,128,128]{2,1,0:T(8,128)(2,1)S(1)}, bf16[2,128,128]{2,1,0:T(8,128)(2,1)S(1)}, u32[]{:S(2)}, u32[]{:S(2)}) collective-permute-start(bf16[2,128,128]{2,1,0:T(8,128)(2,1)S(1)} %get-tuple-element.31), channel_id=1, source_target_pairs={{0,2},{2,4},{4,6},{6,0},{1,3},{3,5},{5,7},{7,1},{8,10},{10,12},{12... | collective-permute-start | bytes 196616 | tf_op jit(solution)/shard_map/ppermute | solution.py:155
  79.3 1.5 %collective-permute-start.19 = (bf16[2,128,128]{2,1,0:T(8,128)(2,1)S(1)}, bf16[2,128,128]{2,1,0:T(8,128)(2,1)S(1)}, u32[]{:S(2)}, u32[]{:S(2)}) collective-permute-start(bf16[2,128,128]{2,1,0:T(8,128)(2,1)S(1)} %get-tuple-element.30), channel_id=1, source_target_pairs={{0,4},{2,6},{4,0},{6,2},{1,5},{3,7},{5,1},{7,3},{8,12},{10,14},{12... | collective-permute-start | bytes 196616 | tf_op jit(solution)/shard_map/ppermute | solution.py:155
  82.0 2.0 %collective-permute-done.18 = bf16[2,128,128]{2,1,0:T(8,128)(2,1)S(1)} collective-permute-done((bf16[2,128,128]{2,1,0:T(8,128)(2,1)S(1)}, bf16[2,128,128]{2,1,0:T(8,128)(2,1)S(1)}, u32[]{:S(2)}, u32[]{:S(2)}) %collective-permute-start.18) | collective-permute-done | bytes 65568 | tf_op jit(solution)/shard_map/ppermute | solution.py:155
  84.0 1.5 %collective-permute-done.19 = bf16[2,128,128]{2,1,0:T(8,128)(2,1)S(1)} collective-permute-done((bf16[2,128,128]{2,1,0:T(8,128)(2,1)S(1)}, bf16[2,128,128]{2,1,0:T(8,128)(2,1)S(1)}, u32[]{:S(2)}, u32[]{:S(2)}) %collective-permute-start.19) | collective-permute-done | bytes 65568 | tf_op jit(solution)/shard_map/ppermute | solution.py:155
  (112 shorter events, 21.2 us)
Async XLA Ops:
  10.6 8.1 %collective-permute-start = (bf16[2,128,128]{2,1,0:T(8,128)(2,1)S(1)}, bf16[2,128,128]{2,1,0:T(8,128)(2,1)S(1)}, u32[]{:S(2)}, u32[]{:S(2)}) collective-permute-start(bf16[2,128,128]{2,1,0:T(8,128)(2,1)S(1)} %get-tuple-element.45), channel_id=1, source_target_pairs={{0,2},{2,4},{4,6},{6,0},{1,3},{3,5},{5,7},{7,1},{8,10},{10,12},{12... | collective-permute-start | bytes 196616 | tf_op jit(solution)/shard_map/ppermute | solution.py:155
  13.7 7.9 %collective-permute-start.1 = (bf16[2,128,128]{2,1,0:T(8,128)(2,1)S(1)}, bf16[2,128,128]{2,1,0:T(8,128)(2,1)S(1)}, u32[]{:S(2)}, u32[]{:S(2)}) collective-permute-start(bf16[2,128,128]{2,1,0:T(8,128)(2,1)S(1)} %get-tuple-element.44), channel_id=1, source_target_pairs={{0,4},{2,6},{4,0},{6,2},{1,5},{3,7},{5,1},{7,3},{8,12},{10,14},{12... | collective-permute-start | bytes 196616 | tf_op jit(solution)/shard_map/ppermute | solution.py:155
  17.7 7.1 %collective-permute-start.7 = (bf16[2,128,128]{2,1,0:T(8,128)(2,1)S(1)}, bf16[2,128,128]{2,1,0:T(8,128)(2,1)S(1)}, u32[]{:S(2)}, u32[]{:S(2)}) collective-permute-start(bf16[2,128,128]{2,1,0:T(8,128)(2,1)S(1)} %get-tuple-element.41), channel_id=1, source_target_pairs={{0,2},{2,4},{4,6},{6,0},{1,3},{3,5},{5,7},{7,1},{8,10},{10,12},{12... | collective-permute-start | bytes 196616 | tf_op jit(solution)/shard_map/ppermute | solution.py:155
  18.4 8.0 %collective-permute-start.8 = (bf16[2,128,128]{2,1,0:T(8,128)(2,1)S(1)}, bf16[2,128,128]{2,1,0:T(8,128)(2,1)S(1)}, u32[]{:S(2)}, u32[]{:S(2)}) collective-permute-start(bf16[2,128,128]{2,1,0:T(8,128)(2,1)S(1)} %get-tuple-element.40), channel_id=1, source_target_pairs={{0,4},{2,6},{4,0},{6,2},{1,5},{3,7},{5,1},{7,3},{8,12},{10,14},{12... | collective-permute-start | bytes 196616 | tf_op jit(solution)/shard_map/ppermute | solution.py:155
  18.7 7.7 %collective-permute-start.9 = (bf16[2,128,128]{2,1,0:T(8,128)(2,1)S(1)}, bf16[2,128,128]{2,1,0:T(8,128)(2,1)S(1)}, u32[]{:S(2)}, u32[]{:S(2)}) collective-permute-start(bf16[2,128,128]{2,1,0:T(8,128)(2,1)S(1)} %get-tuple-element.39), channel_id=1, source_target_pairs={{0,6},{2,0},{4,2},{6,4},{1,7},{3,1},{5,3},{7,5},{8,14},{10,8},{12,... | collective-permute-start | bytes 196616 | tf_op jit(solution)/shard_map/ppermute | solution.py:155
  21.7 9.5 %collective-permute-start.4 = (bf16[4,2,128,128]{3,2,1,0:T(8,128)(2,1)S(1)}, bf16[4,2,128,128]{3,2,1,0:T(8,128)(2,1)S(1)}, u32[]{:S(2)}, u32[]{:S(2)}) collective-permute-start(bf16[4,2,128,128]{3,2,1,0:T(8,128)(2,1)S(1)} %pad_maximum_fusion.1.refs_0_.refs_5_), channel_id=1, source_target_pairs={{0,16},{8,24},{16,0},{24,8},{1,17},{9,25},{17,1},{25,9},{2,18},{10... | collective-permute-start | bytes 786440 | tf_op jit(solution)/shard_map/ppermute | solution.py:180
  23.3 8.5 %collective-permute-start.3 = (bf16[4,2,128,128]{3,2,1,0:T(8,128)(2,1)S(1)}, bf16[4,2,128,128]{3,2,1,0:T(8,128)(2,1)S(1)}, u32[]{:S(2)}, u32[]{:S(2)}) collective-permute-start(bf16[4,2,128,128]{3,2,1,0:T(8,128)(2,1)S(1)} %pad_maximum_fusion.1.refs_0_.refs_5_), channel_id=1, source_target_pairs={{0,8},{8,0},{16,24},{24,16},{1,9},{9,1},{17,25},{25,17},{2,10},{10... | collective-permute-start | bytes 786440 | tf_op jit(solution)/shard_map/ppermute | solution.py:179
  26.5 9.3 %collective-permute-start.11 = (bf16[4,2,128,128]{3,2,1,0:T(8,128)(2,1)S(1)}, bf16[4,2,128,128]{3,2,1,0:T(8,128)(2,1)S(1)}, u32[]{:S(2)}, u32[]{:S(2)}) collective-permute-start(bf16[4,2,128,128]{3,2,1,0:T(8,128)(2,1)S(1)} %pad_maximum_fusion.2.refs_0_.refs_5_), channel_id=1, source_target_pairs={{0,16},{8,24},{16,0},{24,8},{1,17},{9,25},{17,1},{25,9},{2,18},{10... | collective-permute-start | bytes 786440 | tf_op jit(solution)/shard_map/ppermute | solution.py:180
  28.3 9.2 %collective-permute-start.10 = (bf16[4,2,128,128]{3,2,1,0:T(8,128)(2,1)S(1)}, bf16[4,2,128,128]{3,2,1,0:T(8,128)(2,1)S(1)}, u32[]{:S(2)}, u32[]{:S(2)}) collective-permute-start(bf16[4,2,128,128]{3,2,1,0:T(8,128)(2,1)S(1)} %pad_maximum_fusion.2.refs_0_.refs_5_), channel_id=1, source_target_pairs={{0,8},{8,0},{16,24},{24,16},{1,9},{9,1},{17,25},{25,17},{2,10},{10... | collective-permute-start | bytes 786440 | tf_op jit(solution)/shard_map/ppermute | solution.py:179
  31.2 8.9 %collective-permute-start.5 = (bf16[4,2,64,128]{3,2,1,0:T(8,128)(2,1)S(1)}, bf16[4,2,64,128]{3,2,1,0:T(8,128)(2,1)S(1)}, u32[]{:S(2)}, u32[]{:S(2)}) collective-permute-start(bf16[4,2,64,128]{3,2,1,0:T(8,128)(2,1)S(1)} %slice.89), channel_id=1, source_target_pairs={{0,8},{8,0},{16,24},{24,16},{1,9},{9,1},{17,25},{25,17},{2,10},{10... | collective-permute-start | bytes 393224 | tf_op jit(solution)/shard_map/ppermute | solution.py:182
  31.8 8.3 %collective-permute-start.6 = (bf16[4,2,64,128]{3,2,1,0:T(8,128)(2,1)S(1)}, bf16[4,2,64,128]{3,2,1,0:T(8,128)(2,1)S(1)}, u32[]{:S(2)}, u32[]{:S(2)}) collective-permute-start(bf16[4,2,64,128]{3,2,1,0:T(8,128)(2,1)S(1)} %slice.90), channel_id=1, source_target_pairs={{0,16},{8,24},{16,0},{24,8},{1,17},{9,25},{17,1},{25,9},{2,18},{10... | collective-permute-start | bytes 393224 | tf_op jit(solution)/shard_map/ppermute | solution.py:183
  35.7 14.8 %collective-permute-start.12 = (bf16[4,2,64,128]{3,2,1,0:T(8,128)(2,1)S(1)}, bf16[4,2,64,128]{3,2,1,0:T(8,128)(2,1)S(1)}, u32[]{:S(2)}, u32[]{:S(2)}) collective-permute-start(bf16[4,2,64,128]{3,2,1,0:T(8,128)(2,1)S(1)} %slice.92), channel_id=1, source_target_pairs={{0,8},{8,0},{16,24},{24,16},{1,9},{9,1},{17,25},{25,17},{2,10},{10... | collective-permute-start | bytes 393224 | tf_op jit(solution)/shard_map/ppermute | solution.py:182
  37.6 13.0 %collective-permute-start.13 = (bf16[4,2,64,128]{3,2,1,0:T(8,128)(2,1)S(1)}, bf16[4,2,64,128]{3,2,1,0:T(8,128)(2,1)S(1)}, u32[]{:S(2)}, u32[]{:S(2)}) collective-permute-start(bf16[4,2,64,128]{3,2,1,0:T(8,128)(2,1)S(1)} %slice.93), channel_id=1, source_target_pairs={{0,16},{8,24},{16,0},{24,8},{1,17},{9,25},{17,1},{25,9},{2,18},{10... | collective-permute-start | bytes 393224 | tf_op jit(solution)/shard_map/ppermute | solution.py:183
  48.2 14.4 %collective-permute-start.21 = (bf16[4,2,192,128]{3,2,1,0:T(8,128)(2,1)}, bf16[4,2,192,128]{3,2,1,0:T(8,128)(2,1)S(1)}, u32[]{:S(2)}, u32[]{:S(2)}) collective-permute-start(bf16[4,2,192,128]{3,2,1,0:T(8,128)(2,1)} %get-tuple-element.26), channel_id=1, source_target_pairs={{0,8},{8,0},{16,24},{24,16},{1,9},{9,1},{17,25},{25,17},{2,10},{10... | collective-permute-start | bytes 1179656 | tf_op jit(solution)/shard_map/ppermute | solution.py:206
  49.4 14.1 %collective-permute-start.22 = (bf16[4,2,192,128]{3,2,1,0:T(8,128)(2,1)}, bf16[4,2,192,128]{3,2,1,0:T(8,128)(2,1)S(1)}, u32[]{:S(2)}, u32[]{:S(2)}) collective-permute-start(bf16[4,2,192,128]{3,2,1,0:T(8,128)(2,1)} %get-tuple-element.27), channel_id=1, source_target_pairs={{0,16},{8,24},{16,0},{24,8},{1,17},{9,25},{17,1},{25,9},{2,18},{10... | collective-permute-start | bytes 1179656 | tf_op jit(solution)/shard_map/ppermute | solution.py:207
  58.8 9.8 %collective-permute-start.14 = (bf16[4,2,192,128]{3,2,1,0:T(8,128)(2,1)}, bf16[4,2,192,128]{3,2,1,0:T(8,128)(2,1)S(1)}, u32[]{:S(2)}, u32[]{:S(2)}) collective-permute-start(bf16[4,2,192,128]{3,2,1,0:T(8,128)(2,1)} %get-tuple-element.23), channel_id=1, source_target_pairs={{0,8},{8,0},{16,24},{24,16},{1,9},{9,1},{17,25},{25,17},{2,10},{10... | collective-permute-start | bytes 1179656 | tf_op jit(solution)/shard_map/ppermute | solution.py:206
  59.4 10.5 %collective-permute-start.15 = (bf16[4,2,192,128]{3,2,1,0:T(8,128)(2,1)}, bf16[4,2,192,128]{3,2,1,0:T(8,128)(2,1)S(1)}, u32[]{:S(2)}, u32[]{:S(2)}) collective-permute-start(bf16[4,2,192,128]{3,2,1,0:T(8,128)(2,1)} %get-tuple-element.24), channel_id=1, source_target_pairs={{0,16},{8,24},{16,0},{24,8},{1,17},{9,25},{17,1},{25,9},{2,18},{10... | collective-permute-start | bytes 1179656 | tf_op jit(solution)/shard_map/ppermute | solution.py:207
  62.6 8.3 %collective-permute-start.23 = (bf16[4,2,64,128]{3,2,1,0:T(8,128)(2,1)S(1)}, bf16[4,2,64,128]{3,2,1,0:T(8,128)(2,1)S(1)}, u32[]{:S(2)}, u32[]{:S(2)}) collective-permute-start(bf16[4,2,64,128]{3,2,1,0:T(8,128)(2,1)S(1)} %slice.104), channel_id=1, source_target_pairs={{0,16},{8,24},{16,0},{24,8},{1,17},{9,25},{17,1},{25,9},{2,18},{10... | collective-permute-start | bytes 393224 | tf_op jit(solution)/shard_map/ppermute | solution.py:208
  63.5 7.4 %collective-permute-start.24 = (bf16[4,2,64,128]{3,2,1,0:T(8,128)(2,1)S(1)}, bf16[4,2,64,128]{3,2,1,0:T(8,128)(2,1)S(1)}, u32[]{:S(2)}, u32[]{:S(2)}) collective-permute-start(bf16[4,2,64,128]{3,2,1,0:T(8,128)(2,1)S(1)} %slice.105), channel_id=1, source_target_pairs={{0,8},{8,0},{16,24},{24,16},{1,9},{9,1},{17,25},{25,17},{2,10},{10... | collective-permute-start | bytes 393224 | tf_op jit(solution)/shard_map/ppermute | solution.py:209
  68.6 9.0 %collective-permute-start.16 = (bf16[4,2,64,128]{3,2,1,0:T(8,128)(2,1)S(1)}, bf16[4,2,64,128]{3,2,1,0:T(8,128)(2,1)S(1)}, u32[]{:S(2)}, u32[]{:S(2)}) collective-permute-start(bf16[4,2,64,128]{3,2,1,0:T(8,128)(2,1)S(1)} %slice.96), channel_id=1, source_target_pairs={{0,16},{8,24},{16,0},{24,8},{1,17},{9,25},{17,1},{25,9},{2,18},{10... | collective-permute-start | bytes 393224 | tf_op jit(solution)/shard_map/ppermute | solution.py:208
  69.9 7.7 %collective-permute-start.17 = (bf16[4,2,64,128]{3,2,1,0:T(8,128)(2,1)S(1)}, bf16[4,2,64,128]{3,2,1,0:T(8,128)(2,1)S(1)}, u32[]{:S(2)}, u32[]{:S(2)}) collective-permute-start(bf16[4,2,64,128]{3,2,1,0:T(8,128)(2,1)S(1)} %slice.97), channel_id=1, source_target_pairs={{0,8},{8,0},{16,24},{24,16},{1,9},{9,1},{17,25},{25,17},{2,10},{10... | collective-permute-start | bytes 393224 | tf_op jit(solution)/shard_map/ppermute | solution.py:209
  71.1 9.8 %collective-permute-start.25 = (bf16[2,128,128]{2,1,0:T(8,128)(2,1)S(1)}, bf16[2,128,128]{2,1,0:T(8,128)(2,1)S(1)}, u32[]{:S(2)}, u32[]{:S(2)}) collective-permute-start(bf16[2,128,128]{2,1,0:T(8,128)(2,1)S(1)} %get-tuple-element.35), channel_id=1, source_target_pairs={{0,2},{2,4},{4,6},{6,0},{1,3},{3,5},{5,7},{7,1},{8,10},{10,12},{12... | collective-permute-start | bytes 196616 | tf_op jit(solution)/shard_map/ppermute | solution.py:155
  75.1 6.8 %collective-permute-start.26 = (bf16[2,128,128]{2,1,0:T(8,128)(2,1)S(1)}, bf16[2,128,128]{2,1,0:T(8,128)(2,1)S(1)}, u32[]{:S(2)}, u32[]{:S(2)}) collective-permute-start(bf16[2,128,128]{2,1,0:T(8,128)(2,1)S(1)} %get-tuple-element.34), channel_id=1, source_target_pairs={{0,4},{2,6},{4,0},{6,2},{1,5},{3,7},{5,1},{7,3},{8,12},{10,14},{12... | collective-permute-start | bytes 196616 | tf_op jit(solution)/shard_map/ppermute | solution.py:155
  79.3 6.2 %collective-permute-start.19 = (bf16[2,128,128]{2,1,0:T(8,128)(2,1)S(1)}, bf16[2,128,128]{2,1,0:T(8,128)(2,1)S(1)}, u32[]{:S(2)}, u32[]{:S(2)}) collective-permute-start(bf16[2,128,128]{2,1,0:T(8,128)(2,1)S(1)} %get-tuple-element.30), channel_id=1, source_target_pairs={{0,4},{2,6},{4,0},{6,2},{1,5},{3,7},{5,1},{7,3},{8,12},{10,14},{12... | collective-permute-start | bytes 196616 | tf_op jit(solution)/shard_map/ppermute | solution.py:155
  (22 other events, 88.1 us)

commit v8 on v7

--- a/solution.py
+++ b/solution.py
@@ -259,9 +259,9 @@
         else:
             earlier = tuple(jnp.where(in_group(o.shape[1], kv_heads, chunk_heads, group_heads, k), o, e)
                             for o, e in zip(outs[:3], earlier))
-        parts.append(pair_reduce(ctx_reduce(list(outs[3:])), pair_prompt, n_prompts))
+        parts.append(ctx_reduce(list(outs[3:])))
     dq, dkr, dvr = earlier
-    d_prefix = parts[0] if n_groups == 1 else jnp.concatenate(parts, -1)
+    d_prefix = pair_reduce(parts[0] if n_groups == 1 else jnp.concatenate(parts, -1), pair_prompt, n_prompts)
     return (dq[None, None], dkr[None, None], dvr[None, None], d_prefix)
 
 

time: 88.3 us -> 92.6 us (1.049)
  waiting for transfers between devices: 10.6 us -> 21.3 us
  starting transfers between devices: 40.3 us -> 34.2 us
    ppermute x12 -> x9, starting transfers between devices: 21.4 us -> 17.4 us  [ring_shift(): return lax.ppermute(x, axis, [(i, (i + d) % n) for i in range(n)])]
    ppermute x2, waiting for transfers between devices: 0.01 us -> 3.7 us  [ctx_gather(): far_a = lax.ppermute(from_y[:, :, :half], 'ctx', along_x)]
    ppermute x2, waiting for transfers between devices: 0.01 us -> 3.08 us  [ctx_reduce(): far_a = lax.ppermute(got_x[:, :, rows:], 'ctx', along_y)]
    ppermute x12 -> x9, waiting for transfers between devices: 5.15 us -> 8.13 us  [ring_shift(): return lax.ppermute(x, axis, [(i, (i + d) % n) for i in range(n)])]
    ppermute x2, waiting for transfers between devices: 0.01 us -> 1.87 us  [ctx_gather(): far_b = lax.ppermute(from_x[:, :, half:], 'ctx', along_y)]
    ppermute x2, waiting for transfers between devices: 2.33 us -> 0.67 us  [ctx_gather(): from_y = lax.ppermute(x, 'ctx', along_y)]
    ppermute x2, starting transfers between devices: 3.44 us -> 2.2 us  [ctx_gather(): from_y = lax.ppermute(x, 'ctx', along_y)]
    ppermute x2, starting transfers between devices: 2.43 us -> 1.37 us  [ctx_reduce(): got_y = lax.ppermute(send_y, 'ctx', along_y)]
  transfers between devices with their start and end apart: 28 -> 25, of which waited for: 6 -> 14; matrix products, arithmetic and copies ran while one was open for 8% -> 7% of each run, Pallas kernels for 17% -> 16%
where the time goes in v8:
time: 92.6 us; the launch traced here: 92.1 us
  starting transfers between devices  34.2 us (37%)
  waiting for transfers between devices  21.3 us (23%)
  Pallas kernels  14.7 us (16%)
  between operations  9.51 us (10%)
  other arithmetic  7.64 us (8%)
  local copies, waits for them, and re-layouts  4.64 us (5%)
    ppermute x9, starting transfers between devices, ring_shift(): return lax.ppermute(x, axis, [(i, (i + d) % n) for i in range(n)])  17.4 us
    pallas_call x2, Pallas kernels, attention_grads(): pl.pallas_call(functools.partial(attention_grad_kernel, layout), out_shap...  14.7 us
    ppermute x9, waiting for transfers between devices, ring_shift(): return lax.ppermute(x, axis, [(i, (i + d) % n) for i in range(n)])  8.13 us
    ppermute x2, waiting for transfers between devices, ctx_gather(): far_a = lax.ppermute(from_y[:, :, :half], 'ctx', along_x)  3.7 us
    ppermute x2, waiting for transfers between devices, ctx_reduce(): got_x = lax.ppermute(send_x, 'ctx', along_x)  3.28 us
    ppermute x2, waiting for transfers between devices, ctx_reduce(): far_a = lax.ppermute(got_x[:, :, rows:], 'ctx', along_y)  3.08 us
    unnamed x37, local copies, waits for them, and re-layouts  2.98 us
    broadcast_in_dim x2, other arithmetic, shards(): return (dq[None, None], dkr[None, None], dvr[None, None], d_prefix)  2.73 us
  transfers between devices with their start and end apart: 25, of which 14 were waited for; matrix products, arithmetic and copies ran while one was open for 7% of the time, Pallas kernels for 16%

profile of v8, /device:TPU:0, one launch (start us, length us, event | category | flops | bytes accessed | tf_op | source)
XLA Modules:
  0.0 92.1 jit_solution(3444915033076686710)
XLA Ops:
  10.9 3.1 %collective-permute-start = (bf16[2,128,128]{2,1,0:T(8,128)(2,1)S(1)}, bf16[2,128,128]{2,1,0:T(8,128)(2,1)S(1)}, u32[]{:S(2)}, u32[]{:S(2)}) collective-permute-start(bf16[2,128,128]{2,1,0:T(8,128)(2,1)S(1)} %get-tuple-element.41), channel_id=1, source_target_pairs={{0,2},{2,4},{4,6},{6,0},{1,3},{3,5},{5,7},{7,1},{8,10},{10,12},{12... | collective-permute-start | bytes 196616 | tf_op jit(solution)/shard_map/ppermute | solution.py:155
  14.0 2.6 %collective-permute-start.1 = (bf16[2,128,128]{2,1,0:T(8,128)(2,1)S(1)}, bf16[2,128,128]{2,1,0:T(8,128)(2,1)S(1)}, u32[]{:S(2)}, u32[]{:S(2)}) collective-permute-start(bf16[2,128,128]{2,1,0:T(8,128)(2,1)S(1)} %get-tuple-element.40), channel_id=1, source_target_pairs={{0,4},{2,6},{4,0},{6,2},{1,5},{3,7},{5,1},{7,3},{8,12},{10,14},{12... | collective-permute-start | bytes 196616 | tf_op jit(solution)/shard_map/ppermute | solution.py:155
  16.6 1.3 %collective-permute-start.2 = (bf16[2,128,128]{2,1,0:T(8,128)(2,1)S(1)}, bf16[2,128,128]{2,1,0:T(8,128)(2,1)S(1)}, u32[]{:S(2)}, u32[]{:S(2)}) collective-permute-start(bf16[2,128,128]{2,1,0:T(8,128)(2,1)S(1)} %get-tuple-element.39), channel_id=1, source_target_pairs={{0,6},{2,0},{4,2},{6,4},{1,7},{3,1},{5,3},{7,5},{8,14},{10,8},{12,... | collective-permute-start | bytes 196616 | tf_op jit(solution)/shard_map/ppermute | solution.py:155
  18.6 2.5 %collective-permute-done.1 = bf16[2,128,128]{2,1,0:T(8,128)(2,1)S(1)} collective-permute-done((bf16[2,128,128]{2,1,0:T(8,128)(2,1)S(1)}, bf16[2,128,128]{2,1,0:T(8,128)(2,1)S(1)}, u32[]{:S(2)}, u32[]{:S(2)}) %collective-permute-start.1) | collective-permute-done | bytes 65568 | tf_op jit(solution)/shard_map/ppermute | solution.py:155
  21.4 1.6 %collective-permute-start.4 = (bf16[4,2,128,128]{3,2,1,0:T(8,128)(2,1)S(1)}, bf16[4,2,128,128]{3,2,1,0:T(8,128)(2,1)S(1)}, u32[]{:S(2)}, u32[]{:S(2)}) collective-permute-start(bf16[4,2,128,128]{3,2,1,0:T(8,128)(2,1)S(1)} %pad_maximum_fusion.refs_0_.refs_5_), channel_id=1, source_target_pairs={{0,16},{8,24},{16,0},{24,8},{1,17},{9,25},{17,1},{25,9},{2,18},{10... | collective-permute-start | bytes 786440 | tf_op jit(solution)/shard_map/ppermute | solution.py:180
  23.0 1.5 %collective-permute-start.3 = (bf16[4,2,128,128]{3,2,1,0:T(8,128)(2,1)S(1)}, bf16[4,2,128,128]{3,2,1,0:T(8,128)(2,1)S(1)}, u32[]{:S(2)}, u32[]{:S(2)}) collective-permute-start(bf16[4,2,128,128]{3,2,1,0:T(8,128)(2,1)S(1)} %pad_maximum_fusion.refs_0_.refs_5_), channel_id=1, source_target_pairs={{0,8},{8,0},{16,24},{24,16},{1,9},{9,1},{17,25},{25,17},{2,10},{10... | collective-permute-start | bytes 786440 | tf_op jit(solution)/shard_map/ppermute | solution.py:179
  24.5 1.6 %collective-permute-start.7 = (bf16[2,128,128]{2,1,0:T(8,128)(2,1)S(1)}, bf16[2,128,128]{2,1,0:T(8,128)(2,1)S(1)}, u32[]{:S(2)}, u32[]{:S(2)}) collective-permute-start(bf16[2,128,128]{2,1,0:T(8,128)(2,1)S(1)} %get-tuple-element.37), channel_id=1, source_target_pairs={{0,2},{2,4},{4,6},{6,0},{1,3},{3,5},{5,7},{7,1},{8,10},{10,12},{12... | collective-permute-start | bytes 196616 | tf_op jit(solution)/shard_map/ppermute | solution.py:155
  26.1 2.0 %collective-permute-start.8 = (bf16[2,128,128]{2,1,0:T(8,128)(2,1)S(1)}, bf16[2,128,128]{2,1,0:T(8,128)(2,1)S(1)}, u32[]{:S(2)}, u32[]{:S(2)}) collective-permute-start(bf16[2,128,128]{2,1,0:T(8,128)(2,1)S(1)} %get-tuple-element.36), channel_id=1, source_target_pairs={{0,4},{2,6},{4,0},{6,2},{1,5},{3,7},{5,1},{7,3},{8,12},{10,14},{12... | collective-permute-start | bytes 196616 | tf_op jit(solution)/shard_map/ppermute | solution.py:155
  30.1 1.6 %collective-permute-start.6 = (bf16[4,2,64,128]{3,2,1,0:T(8,128)(2,1)S(1)}, bf16[4,2,64,128]{3,2,1,0:T(8,128)(2,1)S(1)}, u32[]{:S(2)}, u32[]{:S(2)}) collective-permute-start(bf16[4,2,64,128]{3,2,1,0:T(8,128)(2,1)S(1)} %slice.74), channel_id=1, source_target_pairs={{0,16},{8,24},{16,0},{24,8},{1,17},{9,25},{17,1},{25,9},{2,18},{10... | collective-permute-start | bytes 393224 | tf_op jit(solution)/shard_map/ppermute | solution.py:183
  37.3 7.4 %shard_map.111 = (bf16[128,2048]{1,0:T(8,128)(2,1)}, bf16[128,1024]{1,0:T(8,128)(2,1)}, bf16[128,1024]{1,0:T(8,128)(2,1)}, bf16[4,2,128,128]{3,2,1,0:T(8,128)(2,...) custom-call(s32[4]{0:T(128)} %bitcast.79, s32[1]{0:T(128)} %bitcast.62.length_ref, ...), custom_call_target="tpu_custom_call" | custom-call | flops 1006632960 | bytes 3670016 | tf_op jit(solution)/shard_map/pallas_call | solution.py:136
  44.6 1.5 %collective-permute-start.18 = (bf16[4,2,192,128]{3,2,1,0:T(8,128)(2,1)}, bf16[4,2,192,128]{3,2,1,0:T(8,128)(2,1)S(1)}, u32[]{:S(2)}, u32[]{:S(2)}) collective-permute-start(bf16[4,2,192,128]{3,2,1,0:T(8,128)(2,1)} %get-tuple-element.26), channel_id=1, source_target_pairs={{0,8},{8,0},{16,24},{24,16},{1,9},{9,1},{17,25},{25,17},{2,10},{10... | collective-permute-start | bytes 1179656 | tf_op jit(solution)/shard_map/ppermute | solution.py:206
  46.7 1.3 %compare_convert_fusion = (f32[2]{0:T(128)S(1)}, f32[2]{0:T(128)S(1)}) fusion(s32[]{:T(128)} %bitcast.37, s32[]{:T(128)} %bitcast.34), kind=kLoop, calls=%fused_computation.59 | loop fusion | flops 8 | bytes 24 | tf_op jit(solution)/shard_map/convert_element_type | solution.py:224
  51.4 3.4 %collective-permute-done.12.refs_3_.refs_8_ = bf16[4,2,64,128]{3,2,1,0:T(8,128)(2,1)S(1)} collective-permute-done((bf16[4,2,64,128]{3,2,1,0:T(8,128)(2,1)S(1)}, bf16[4,2,64,128]{3,2,1,0:T(8,128)(2,1)S(1)}, u32[]{:S(2)}, u32[]{:S(2)}) %collective-permute-start.12) | collective-permute-done | bytes 131104 | tf_op jit(solution)/shard_map/ppermute | solution.py:182
  56.5 7.4 %shard_map.112 = (bf16[128,2048]{1,0:T(8,128)(2,1)}, bf16[128,1024]{1,0:T(8,128)(2,1)}, bf16[128,1024]{1,0:T(8,128)(2,1)}, bf16[4,2,128,128]{3,2,1,0:T(8,128)(2,...) custom-call(s32[4]{0:T(128)} %bitcast.80, s32[1]{0:T(128)} %bitcast.63.length_ref, ...), custom_call_target="tpu_custom_call" | custom-call | flops 1006632960 | bytes 3670016 | tf_op jit(solution)/shard_map/pallas_call | solution.py:136
  65.6 1.3 %collective-permute-start.20 = (bf16[4,2,64,128]{3,2,1,0:T(8,128)(2,1)S(1)}, bf16[4,2,64,128]{3,2,1,0:T(8,128)(2,1)S(1)}, u32[]{:S(2)}, u32[]{:S(2)}) collective-permute-start(bf16[4,2,64,128]{3,2,1,0:T(8,128)(2,1)S(1)} %slice.84), channel_id=1, source_target_pairs={{0,16},{8,24},{16,0},{24,8},{1,17},{9,25},{17,1},{25,9},{2,18},{10... | collective-permute-start | bytes 393224 | tf_op jit(solution)/shard_map/ppermute | solution.py:208
  66.8 1.3 %collective-permute-start.21 = (bf16[4,2,64,128]{3,2,1,0:T(8,128)(2,1)S(1)}, bf16[4,2,64,128]{3,2,1,0:T(8,128)(2,1)S(1)}, u32[]{:S(2)}, u32[]{:S(2)}) collective-permute-start(bf16[4,2,64,128]{3,2,1,0:T(8,128)(2,1)S(1)} %slice.85), channel_id=1, source_target_pairs={{0,8},{8,0},{16,24},{24,16},{1,9},{9,1},{17,25},{25,17},{2,10},{10... | collective-permute-start | bytes 393224 | tf_op jit(solution)/shard_map/ppermute | solution.py:209
  68.1 1.9 %select_bitcast_fusion = bf16[1,1,128,2048]{3,2,1,0:T(8,128)(2,1)} fusion(bf16[128,2048]{1,0:T(8,128)(2,1)S(1)} %copy-done, bf16[128,2048]{1,0:T(8,128)(2,1)} %get-tuple-element.17, pred[2048]{0:T(1024)(128)(4,1)S(1)} %fusion.8), kind=kLoop, calls=%fused_computation.9 | loop fusion | flops 262144 | bytes 1574912 | tf_op jit(solution)/shard_map/broadcast_in_dim | solution.py:265
  70.0 3.3 %collective-permute-done.14 = bf16[4,2,192,128]{3,2,1,0:T(8,128)(2,1)S(1)} collective-permute-done((bf16[4,2,192,128]{3,2,1,0:T(8,128)(2,1)}, bf16[4,2,192,128]{3,2,1,0:T(8,128)(2,1)S(1)}, u32[]{:S(2)}, u32[]{:S(2)}) %collective-permute-start.14) | collective-permute-done | bytes 393248 | tf_op jit(solution)/shard_map/ppermute | solution.py:206
  75.3 3.0 %collective-permute-done.16 = bf16[4,2,64,128]{3,2,1,0:T(8,128)(2,1)S(1)} collective-permute-done((bf16[4,2,64,128]{3,2,1,0:T(8,128)(2,1)S(1)}, bf16[4,2,64,128]{3,2,1,0:T(8,128)(2,1)S(1)}, u32[]{:S(2)}, u32[]{:S(2)}) %collective-permute-start.16) | collective-permute-done | bytes 131104 | tf_op jit(solution)/shard_map/ppermute | solution.py:208
  79.2 2.9 %collective-permute-start.22 = (bf16[2,128,256]{2,1,0:T(8,128)(2,1)S(1)}, bf16[2,128,256]{2,1,0:T(8,128)(2,1)S(1)}, u32[]{:S(2)}, u32[]{:S(2)}) collective-permute-start(bf16[2,128,256]{2,1,0:T(8,128)(2,1)S(1)} %get-tuple-element.29), channel_id=1, source_target_pairs={{0,2},{2,4},{4,6},{6,0},{1,3},{3,5},{5,7},{7,1},{8,10},{10,12},{12... | collective-permute-start | bytes 393224 | tf_op jit(solution)/shard_map/ppermute | solution.py:155
  83.0 1.3 %collective-permute-start.23 = (bf16[2,128,256]{2,1,0:T(8,128)(2,1)S(1)}, bf16[2,128,256]{2,1,0:T(8,128)(2,1)S(1)}, u32[]{:S(2)}, u32[]{:S(2)}) collective-permute-start(bf16[2,128,256]{2,1,0:T(8,128)(2,1)S(1)} %get-tuple-element.31), channel_id=1, source_target_pairs={{0,4},{2,6},{4,0},{6,2},{1,5},{3,7},{5,1},{7,3},{8,12},{10,14},{12... | collective-permute-start | bytes 393224 | tf_op jit(solution)/shard_map/ppermute | solution.py:155
  84.3 2.1 %collective-permute-start.24 = (bf16[2,128,256]{2,1,0:T(8,128)(2,1)S(1)}, bf16[2,128,256]{2,1,0:T(8,128)(2,1)S(1)}, u32[]{:S(2)}, u32[]{:S(2)}) collective-permute-start(bf16[2,128,256]{2,1,0:T(8,128)(2,1)S(1)} %get-tuple-element.30), channel_id=1, source_target_pairs={{0,6},{2,0},{4,2},{6,4},{1,7},{3,1},{5,3},{7,5},{8,14},{10,8},{12,... | collective-permute-start | bytes 393224 | tf_op jit(solution)/shard_map/ppermute | solution.py:155
  86.8 3.4 %collective-permute-done.23 = bf16[2,128,256]{2,1,0:T(8,128)(2,1)S(1)} collective-permute-done((bf16[2,128,256]{2,1,0:T(8,128)(2,1)S(1)}, bf16[2,128,256]{2,1,0:T(8,128)(2,1)S(1)}, u32[]{:S(2)}, u32[]{:S(2)}) %collective-permute-start.23) | collective-permute-done | bytes 131104 | tf_op jit(solution)/shard_map/ppermute | solution.py:155
  90.7 1.3 %multiply_add_fusion = f32[2,128,2,256]{3,2,1,0:T(2,128)} fusion(f32[128,2,256]{2,1,0:T(2,128)S(1)} %copy.16, f32[128,2,256]{2,1,0:T(2,128)S(1)} %copy.15, f32[128,2,256]{2,1,0:T(2,128)S(1)} %copy.14, f32[128,2,256]{2,1,0:T(2,128)S(1)} %copy.13, f32[2]{0:T(128)S(1)} %get-tuple-element.52, f32[2]{0:T(128)S(1)} %get-tuple-element.53, ...), kind=kLoop, calls=%fused_computation.6 | loop fusion | flops 917504 | bytes 1572896 | tf_op jit(solution)/shard_map/add | solution.py:226
  (97 shorter events, 21.9 us)
Async XLA Ops:
  10.9 7.6 %collective-permute-start = (bf16[2,128,128]{2,1,0:T(8,128)(2,1)S(1)}, bf16[2,128,128]{2,1,0:T(8,128)(2,1)S(1)}, u32[]{:S(2)}, u32[]{:S(2)}) collective-permute-start(bf16[2,128,128]{2,1,0:T(8,128)(2,1)S(1)} %get-tuple-element.41), channel_id=1, source_target_pairs={{0,2},{2,4},{4,6},{6,0},{1,3},{3,5},{5,7},{7,1},{8,10},{10,12},{12... | collective-permute-start | bytes 196616 | tf_op jit(solution)/shard_map/ppermute | solution.py:155
  14.0 7.1 %collective-permute-start.1 = (bf16[2,128,128]{2,1,0:T(8,128)(2,1)S(1)}, bf16[2,128,128]{2,1,0:T(8,128)(2,1)S(1)}, u32[]{:S(2)}, u32[]{:S(2)}) collective-permute-start(bf16[2,128,128]{2,1,0:T(8,128)(2,1)S(1)} %get-tuple-element.40), channel_id=1, source_target_pairs={{0,4},{2,6},{4,0},{6,2},{1,5},{3,7},{5,1},{7,3},{8,12},{10,14},{12... | collective-permute-start | bytes 196616 | tf_op jit(solution)/shard_map/ppermute | solution.py:155
  21.4 7.9 %collective-permute-start.4 = (bf16[4,2,128,128]{3,2,1,0:T(8,128)(2,1)S(1)}, bf16[4,2,128,128]{3,2,1,0:T(8,128)(2,1)S(1)}, u32[]{:S(2)}, u32[]{:S(2)}) collective-permute-start(bf16[4,2,128,128]{3,2,1,0:T(8,128)(2,1)S(1)} %pad_maximum_fusion.refs_0_.refs_5_), channel_id=1, source_target_pairs={{0,16},{8,24},{16,0},{24,8},{1,17},{9,25},{17,1},{25,9},{2,18},{10... | collective-permute-start | bytes 786440 | tf_op jit(solution)/shard_map/ppermute | solution.py:180
  23.0 7.1 %collective-permute-start.3 = (bf16[4,2,128,128]{3,2,1,0:T(8,128)(2,1)S(1)}, bf16[4,2,128,128]{3,2,1,0:T(8,128)(2,1)S(1)}, u32[]{:S(2)}, u32[]{:S(2)}) collective-permute-start(bf16[4,2,128,128]{3,2,1,0:T(8,128)(2,1)S(1)} %pad_maximum_fusion.refs_0_.refs_5_), channel_id=1, source_target_pairs={{0,8},{8,0},{16,24},{24,16},{1,9},{9,1},{17,25},{25,17},{2,10},{10... | collective-permute-start | bytes 786440 | tf_op jit(solution)/shard_map/ppermute | solution.py:179
  24.5 7.2 %collective-permute-start.7 = (bf16[2,128,128]{2,1,0:T(8,128)(2,1)S(1)}, bf16[2,128,128]{2,1,0:T(8,128)(2,1)S(1)}, u32[]{:S(2)}, u32[]{:S(2)}) collective-permute-start(bf16[2,128,128]{2,1,0:T(8,128)(2,1)S(1)} %get-tuple-element.37), channel_id=1, source_target_pairs={{0,2},{2,4},{4,6},{6,0},{1,3},{3,5},{5,7},{7,1},{8,10},{10,12},{12... | collective-permute-start | bytes 196616 | tf_op jit(solution)/shard_map/ppermute | solution.py:155
  26.1 6.5 %collective-permute-start.8 = (bf16[2,128,128]{2,1,0:T(8,128)(2,1)S(1)}, bf16[2,128,128]{2,1,0:T(8,128)(2,1)S(1)}, u32[]{:S(2)}, u32[]{:S(2)}) collective-permute-start(bf16[2,128,128]{2,1,0:T(8,128)(2,1)S(1)} %get-tuple-element.36), channel_id=1, source_target_pairs={{0,4},{2,6},{4,0},{6,2},{1,5},{3,7},{5,1},{7,3},{8,12},{10,14},{12... | collective-permute-start | bytes 196616 | tf_op jit(solution)/shard_map/ppermute | solution.py:155
  28.1 4.9 %collective-permute-start.9 = (bf16[2,128,128]{2,1,0:T(8,128)(2,1)S(1)}, bf16[2,128,128]{2,1,0:T(8,128)(2,1)S(1)}, u32[]{:S(2)}, u32[]{:S(2)}) collective-permute-start(bf16[2,128,128]{2,1,0:T(8,128)(2,1)S(1)} %get-tuple-element.35), channel_id=1, source_target_pairs={{0,6},{2,0},{4,2},{6,4},{1,7},{3,1},{5,3},{7,5},{8,14},{10,8},{12,... | collective-permute-start | bytes 196616 | tf_op jit(solution)/shard_map/ppermute | solution.py:155
  29.2 6.4 %collective-permute-start.5 = (bf16[4,2,64,128]{3,2,1,0:T(8,128)(2,1)S(1)}, bf16[4,2,64,128]{3,2,1,0:T(8,128)(2,1)S(1)}, u32[]{:S(2)}, u32[]{:S(2)}) collective-permute-start(bf16[4,2,64,128]{3,2,1,0:T(8,128)(2,1)S(1)} %slice.73), channel_id=1, source_target_pairs={{0,8},{8,0},{16,24},{24,16},{1,9},{9,1},{17,25},{25,17},{2,10},{10... | collective-permute-start | bytes 393224 | tf_op jit(solution)/shard_map/ppermute | solution.py:182
  30.1 6.5 %collective-permute-start.6 = (bf16[4,2,64,128]{3,2,1,0:T(8,128)(2,1)S(1)}, bf16[4,2,64,128]{3,2,1,0:T(8,128)(2,1)S(1)}, u32[]{:S(2)}, u32[]{:S(2)}) collective-permute-start(bf16[4,2,64,128]{3,2,1,0:T(8,128)(2,1)S(1)} %slice.74), channel_id=1, source_target_pairs={{0,16},{8,24},{16,0},{24,8},{1,17},{9,25},{17,1},{25,9},{2,18},{10... | collective-permute-start | bytes 393224 | tf_op jit(solution)/shard_map/ppermute | solution.py:183
  33.1 14.9 %collective-permute-start.11 = (bf16[4,2,128,128]{3,2,1,0:T(8,128)(2,1)S(1)}, bf16[4,2,128,128]{3,2,1,0:T(8,128)(2,1)S(1)}, u32[]{:S(2)}, u32[]{:S(2)}) collective-permute-start(bf16[4,2,128,128]{3,2,1,0:T(8,128)(2,1)S(1)} %pad_maximum_fusion.1.refs_0_.refs_5_), channel_id=1, source_target_pairs={{0,16},{8,24},{16,0},{24,8},{1,17},{9,25},{17,1},{25,9},{2,18},{10... | collective-permute-start | bytes 786440 | tf_op jit(solution)/shard_map/ppermute | solution.py:180
  33.6 15.5 %collective-permute-start.10 = (bf16[4,2,128,128]{3,2,1,0:T(8,128)(2,1)S(1)}, bf16[4,2,128,128]{3,2,1,0:T(8,128)(2,1)S(1)}, u32[]{:S(2)}, u32[]{:S(2)}) collective-permute-start(bf16[4,2,128,128]{3,2,1,0:T(8,128)(2,1)S(1)} %pad_maximum_fusion.1.refs_0_.refs_5_), channel_id=1, source_target_pairs={{0,8},{8,0},{16,24},{24,16},{1,9},{9,1},{17,25},{25,17},{2,10},{10... | collective-permute-start | bytes 786440 | tf_op jit(solution)/shard_map/ppermute | solution.py:179
  44.6 20.9 %collective-permute-start.18 = (bf16[4,2,192,128]{3,2,1,0:T(8,128)(2,1)}, bf16[4,2,192,128]{3,2,1,0:T(8,128)(2,1)S(1)}, u32[]{:S(2)}, u32[]{:S(2)}) collective-permute-start(bf16[4,2,192,128]{3,2,1,0:T(8,128)(2,1)} %get-tuple-element.26), channel_id=1, source_target_pairs={{0,8},{8,0},{16,24},{24,16},{1,9},{9,1},{17,25},{25,17},{2,10},{10... | collective-permute-start | bytes 1179656 | tf_op jit(solution)/shard_map/ppermute | solution.py:206
  46.1 20.7 %collective-permute-start.19 = (bf16[4,2,192,128]{3,2,1,0:T(8,128)(2,1)}, bf16[4,2,192,128]{3,2,1,0:T(8,128)(2,1)S(1)}, u32[]{:S(2)}, u32[]{:S(2)}) collective-permute-start(bf16[4,2,192,128]{3,2,1,0:T(8,128)(2,1)} %get-tuple-element.27), channel_id=1, source_target_pairs={{0,16},{8,24},{16,0},{24,8},{1,17},{9,25},{17,1},{25,9},{2,18},{10... | collective-permute-start | bytes 1179656 | tf_op jit(solution)/shard_map/ppermute | solution.py:207
  48.0 6.9 %collective-permute-start.12 = (bf16[4,2,64,128]{3,2,1,0:T(8,128)(2,1)S(1)}, bf16[4,2,64,128]{3,2,1,0:T(8,128)(2,1)S(1)}, u32[]{:S(2)}, u32[]{:S(2)}) collective-permute-start(bf16[4,2,64,128]{3,2,1,0:T(8,128)(2,1)S(1)} %slice.76), channel_id=1, source_target_pairs={{0,8},{8,0},{16,24},{24,16},{1,9},{9,1},{17,25},{25,17},{2,10},{10... | collective-permute-start | bytes 393224 | tf_op jit(solution)/shard_map/ppermute | solution.py:182
  49.2 6.6 %collective-permute-start.13 = (bf16[4,2,64,128]{3,2,1,0:T(8,128)(2,1)S(1)}, bf16[4,2,64,128]{3,2,1,0:T(8,128)(2,1)S(1)}, u32[]{:S(2)}, u32[]{:S(2)}) collective-permute-start(bf16[4,2,64,128]{3,2,1,0:T(8,128)(2,1)S(1)} %slice.77), channel_id=1, source_target_pairs={{0,16},{8,24},{16,0},{24,8},{1,17},{9,25},{17,1},{25,9},{2,18},{10... | collective-permute-start | bytes 393224 | tf_op jit(solution)/shard_map/ppermute | solution.py:183
  63.8 9.5 %collective-permute-start.14 = (bf16[4,2,192,128]{3,2,1,0:T(8,128)(2,1)}, bf16[4,2,192,128]{3,2,1,0:T(8,128)(2,1)S(1)}, u32[]{:S(2)}, u32[]{:S(2)}) collective-permute-start(bf16[4,2,192,128]{3,2,1,0:T(8,128)(2,1)} %get-tuple-element.23), channel_id=1, source_target_pairs={{0,8},{8,0},{16,24},{24,16},{1,9},{9,1},{17,25},{25,17},{2,10},{10... | collective-permute-start | bytes 1179656 | tf_op jit(solution)/shard_map/ppermute | solution.py:206
  64.7 9.2 %collective-permute-start.15 = (bf16[4,2,192,128]{3,2,1,0:T(8,128)(2,1)}, bf16[4,2,192,128]{3,2,1,0:T(8,128)(2,1)S(1)}, u32[]{:S(2)}, u32[]{:S(2)}) collective-permute-start(bf16[4,2,192,128]{3,2,1,0:T(8,128)(2,1)} %get-tuple-element.24), channel_id=1, source_target_pairs={{0,16},{8,24},{16,0},{24,8},{1,17},{9,25},{17,1},{25,9},{2,18},{10... | collective-permute-start | bytes 1179656 | tf_op jit(solution)/shard_map/ppermute | solution.py:207
  65.6 9.6 %collective-permute-start.20 = (bf16[4,2,64,128]{3,2,1,0:T(8,128)(2,1)S(1)}, bf16[4,2,64,128]{3,2,1,0:T(8,128)(2,1)S(1)}, u32[]{:S(2)}, u32[]{:S(2)}) collective-permute-start(bf16[4,2,64,128]{3,2,1,0:T(8,128)(2,1)S(1)} %slice.84), channel_id=1, source_target_pairs={{0,16},{8,24},{16,0},{24,8},{1,17},{9,25},{17,1},{25,9},{2,18},{10... | collective-permute-start | bytes 393224 | tf_op jit(solution)/shard_map/ppermute | solution.py:208
  66.8 8.3 %collective-permute-start.21 = (bf16[4,2,64,128]{3,2,1,0:T(8,128)(2,1)S(1)}, bf16[4,2,64,128]{3,2,1,0:T(8,128)(2,1)S(1)}, u32[]{:S(2)}, u32[]{:S(2)}) collective-permute-start(bf16[4,2,64,128]{3,2,1,0:T(8,128)(2,1)S(1)} %slice.85), channel_id=1, source_target_pairs={{0,8},{8,0},{16,24},{24,16},{1,9},{9,1},{17,25},{25,17},{2,10},{10... | collective-permute-start | bytes 393224 | tf_op jit(solution)/shard_map/ppermute | solution.py:209
  73.3 5.0 %collective-permute-start.16 = (bf16[4,2,64,128]{3,2,1,0:T(8,128)(2,1)S(1)}, bf16[4,2,64,128]{3,2,1,0:T(8,128)(2,1)S(1)}, u32[]{:S(2)}, u32[]{:S(2)}) collective-permute-start(bf16[4,2,64,128]{3,2,1,0:T(8,128)(2,1)S(1)} %slice.80), channel_id=1, source_target_pairs={{0,16},{8,24},{16,0},{24,8},{1,17},{9,25},{17,1},{25,9},{2,18},{10... | collective-permute-start | bytes 393224 | tf_op jit(solution)/shard_map/ppermute | solution.py:208
  73.9 5.0 %collective-permute-start.17 = (bf16[4,2,64,128]{3,2,1,0:T(8,128)(2,1)S(1)}, bf16[4,2,64,128]{3,2,1,0:T(8,128)(2,1)S(1)}, u32[]{:S(2)}, u32[]{:S(2)}) collective-permute-start(bf16[4,2,64,128]{3,2,1,0:T(8,128)(2,1)S(1)} %slice.81), channel_id=1, source_target_pairs={{0,8},{8,0},{16,24},{24,16},{1,9},{9,1},{17,25},{25,17},{2,10},{10... | collective-permute-start | bytes 393224 | tf_op jit(solution)/shard_map/ppermute | solution.py:209
  79.2 7.4 %collective-permute-start.22 = (bf16[2,128,256]{2,1,0:T(8,128)(2,1)S(1)}, bf16[2,128,256]{2,1,0:T(8,128)(2,1)S(1)}, u32[]{:S(2)}, u32[]{:S(2)}) collective-permute-start(bf16[2,128,256]{2,1,0:T(8,128)(2,1)S(1)} %get-tuple-element.29), channel_id=1, source_target_pairs={{0,2},{2,4},{4,6},{6,0},{1,3},{3,5},{5,7},{7,1},{8,10},{10,12},{12... | collective-permute-start | bytes 393224 | tf_op jit(solution)/shard_map/ppermute | solution.py:155
  83.0 7.3 %collective-permute-start.23 = (bf16[2,128,256]{2,1,0:T(8,128)(2,1)S(1)}, bf16[2,128,256]{2,1,0:T(8,128)(2,1)S(1)}, u32[]{:S(2)}, u32[]{:S(2)}) collective-permute-start(bf16[2,128,256]{2,1,0:T(8,128)(2,1)S(1)} %get-tuple-element.31), channel_id=1, source_target_pairs={{0,4},{2,6},{4,0},{6,2},{1,5},{3,7},{5,1},{7,3},{8,12},{10,14},{12... | collective-permute-start | bytes 393224 | tf_op jit(solution)/shard_map/ppermute | solution.py:155
  84.3 6.2 %collective-permute-start.24 = (bf16[2,128,256]{2,1,0:T(8,128)(2,1)S(1)}, bf16[2,128,256]{2,1,0:T(8,128)(2,1)S(1)}, u32[]{:S(2)}, u32[]{:S(2)}) collective-permute-start(bf16[2,128,256]{2,1,0:T(8,128)(2,1)S(1)} %get-tuple-element.30), channel_id=1, source_target_pairs={{0,6},{2,0},{4,2},{6,4},{1,7},{3,1},{5,3},{7,5},{8,14},{10,8},{12,... | collective-permute-start | bytes 393224 | tf_op jit(solution)/shard_map/ppermute | solution.py:155
  (19 other events, 60.3 us)

commit v9 on v7

--- a/solution.py
+++ b/solution.py
@@ -174,42 +174,22 @@
     if not tree_ctx():
         got = lax.all_gather(x, "ctx", axis=0, tiled=False)
         return [got[j] for j in range(n)]
-    along_x = [(i, i ^ 1) for i in range(n)]
-    along_y = [(i, i ^ 2) for i in range(n)]
-    from_x = lax.ppermute(x, "ctx", along_x)
-    from_y = lax.ppermute(x, "ctx", along_y)
-    half = x.shape[2] // 2
-    far_a = lax.ppermute(from_y[:, :, :half], "ctx", along_x)
-    far_b = lax.ppermute(from_x[:, :, half:], "ctx", along_y)
-    return [x, from_x, from_y, far_a, far_b]
+    return [x] + [lax.ppermute(x, "ctx", [(i, i ^ j) for i in range(n)]) for j in range(1, n)]
 
 
 def ctx_out_ranges(slot_rows):
     n = lax.axis_size("ctx")
-    if not tree_ctx():
-        return [[(j * slot_rows, slot_rows)] for j in range(n)]
-    half = slot_rows // 2
-    return [[(0, slot_rows)],
-            [(slot_rows, slot_rows), (3 * slot_rows, half)],
-            [(2 * slot_rows, slot_rows), (3 * slot_rows + half, half)]]
+    return [[(j * slot_rows, slot_rows)] for j in range(n)]
 
 
 def ctx_reduce(pieces):
+    n = lax.axis_size("ctx")
     if not tree_ctx():
         got = lax.all_to_all(jnp.stack(pieces), "ctx", split_axis=0, concat_axis=0, tiled=True)
         return jnp.sum(got.astype(jnp.float32), axis=0).astype(jnp.bfloat16)
-    n = lax.axis_size("ctx")
-    along_x = [(i, i ^ 1) for i in range(n)]
-    along_y = [(i, i ^ 2) for i in range(n)]
-    mine, send_x, send_y = pieces
-    rows = mine.shape[2]
-    got_x = lax.ppermute(send_x, "ctx", along_x)
-    got_y = lax.ppermute(send_y, "ctx", along_y)
-    far_a = lax.ppermute(got_x[:, :, rows:], "ctx", along_y)
-    far_b = lax.ppermute(got_y[:, :, rows:], "ctx", along_x)
-    far = jnp.concatenate([far_a, far_b], 2)
-    total = (mine.astype(jnp.float32) + got_x[:, :, :rows].astype(jnp.float32)) + (
-        got_y[:, :, :rows].astype(jnp.float32) + far.astype(jnp.float32))
+    got = [pieces[0]] + [lax.ppermute(pieces[j], "ctx", [(i, i ^ j) for i in range(n)]) for j in range(1, n)]
+    total = (got[0].astype(jnp.float32) + got[1].astype(jnp.float32)) + (
+        got[2].astype(jnp.float32) + got[3].astype(jnp.float32))
     return total.astype(jnp.bfloat16)
 
 

time: 88.3 us -> 90.5 us (1.025)
  waiting for transfers between devices: 10.6 us -> 16 us
  starting transfers between devices: 40.3 us -> 37 us
    ppermute x16 -> x12, waiting for transfers between devices: 5.4 us -> 13.3 us  [the longest x6 13.2 us: ctx_gather(): lax.ppermute(x, 'ctx', [(i, i ^ j) for i in range(n)])]
    ppermute x16 -> x12, starting transfers between devices: 18.9 us -> 14.3 us  [the longest x6 7.17 us: ctx_gather(): lax.ppermute(x, 'ctx', [(i, i ^ j) for i in range(n)])]
    ppermute x12, waiting for transfers between devices: 5.15 us -> 2.71 us  [ring_shift(): return lax.ppermute(x, axis, [(i, (i + d) % n) for i in range(n)])]
    ppermute x12, starting transfers between devices: 21.4 us -> 22.7 us  [ring_shift(): return lax.ppermute(x, axis, [(i, (i + d) % n) for i in range(n)])]
    unnamed x37 -> x35, local copies, waits for them, and re-layouts: 3.03 us -> 3.29 us
  transfers between devices with their start and end apart: 28 -> 24, of which waited for: 6 -> 3; matrix products, arithmetic and copies ran while one was open for 8% -> 8% of each run, Pallas kernels for 17% -> 16%
where the time goes in v9:
time: 90.5 us; the launch traced here: 90 us
  starting transfers between devices  37 us (41%)
  waiting for transfers between devices  16 us (18%)
  Pallas kernels  14.7 us (16%)
  between operations  9.35 us (10%)
  other arithmetic  8.09 us (9%)
  local copies, waits for them, and re-layouts  4.88 us (5%)
    ppermute x12, starting transfers between devices, ring_shift(): return lax.ppermute(x, axis, [(i, (i + d) % n) for i in range(n)])  22.7 us
    pallas_call x2, Pallas kernels, attention_grads(): pl.pallas_call(functools.partial(attention_grad_kernel, layout), out_shap...  14.7 us
    ppermute x6, waiting for transfers between devices, ctx_gather(): lax.ppermute(x, 'ctx', [(i, i ^ j) for i in range(n)])  13.2 us
    ppermute x6, starting transfers between devices, ctx_gather(): lax.ppermute(x, 'ctx', [(i, i ^ j) for i in range(n)])  7.17 us
    ppermute x6, starting transfers between devices, ctx_reduce(): lax.ppermute(pieces[j], 'ctx', [(i, i ^ j) for i in range(n)])  7.11 us
    unnamed x35, local copies, waits for them, and re-layouts  3.29 us
    broadcast_in_dim x2, other arithmetic, shards(): return (dq[None, None], dkr[None, None], dvr[None, None], d_prefix)  2.82 us
    ppermute x12, waiting for transfers between devices, ring_shift(): return lax.ppermute(x, axis, [(i, (i + d) % n) for i in range(n)])  2.71 us
  transfers between devices with their start and end apart: 24, of which 3 were waited for; matrix products, arithmetic and copies ran while one was open for 8% of the time, Pallas kernels for 16%

profile of v9, /device:TPU:0, one launch (start us, length us, event | category | flops | bytes accessed | tf_op | source)
XLA Modules:
  0.0 90.0 jit_solution(11366381146429092792)
XLA Ops:
  10.7 3.1 %collective-permute-start = (bf16[2,128,128]{2,1,0:T(8,128)(2,1)S(1)}, bf16[2,128,128]{2,1,0:T(8,128)(2,1)S(1)}, u32[]{:S(2)}, u32[]{:S(2)}) collective-permute-start(bf16[2,128,128]{2,1,0:T(8,128)(2,1)S(1)} %get-tuple-element.49), channel_id=1, source_target_pairs={{0,2},{2,4},{4,6},{6,0},{1,3},{3,5},{5,7},{7,1},{8,10},{10,12},{12... | collective-permute-start | bytes 196616 | tf_op jit(solution)/shard_map/ppermute | solution.py:155
  13.8 2.6 %collective-permute-start.1 = (bf16[2,128,128]{2,1,0:T(8,128)(2,1)S(1)}, bf16[2,128,128]{2,1,0:T(8,128)(2,1)S(1)}, u32[]{:S(2)}, u32[]{:S(2)}) collective-permute-start(bf16[2,128,128]{2,1,0:T(8,128)(2,1)S(1)} %get-tuple-element.48), channel_id=1, source_target_pairs={{0,4},{2,6},{4,0},{6,2},{1,5},{3,7},{5,1},{7,3},{8,12},{10,14},{12... | collective-permute-start | bytes 196616 | tf_op jit(solution)/shard_map/ppermute | solution.py:155
  16.4 1.3 %collective-permute-start.2 = (bf16[2,128,128]{2,1,0:T(8,128)(2,1)S(1)}, bf16[2,128,128]{2,1,0:T(8,128)(2,1)S(1)}, u32[]{:S(2)}, u32[]{:S(2)}) collective-permute-start(bf16[2,128,128]{2,1,0:T(8,128)(2,1)S(1)} %get-tuple-element.47), channel_id=1, source_target_pairs={{0,6},{2,0},{4,2},{6,4},{1,7},{3,1},{5,3},{7,5},{8,14},{10,8},{12,... | collective-permute-start | bytes 196616 | tf_op jit(solution)/shard_map/ppermute | solution.py:155
  18.8 2.9 %collective-permute-start.8 = (bf16[2,128,128]{2,1,0:T(8,128)(2,1)S(1)}, bf16[2,128,128]{2,1,0:T(8,128)(2,1)S(1)}, u32[]{:S(2)}, u32[]{:S(2)}) collective-permute-start(bf16[2,128,128]{2,1,0:T(8,128)(2,1)S(1)} %get-tuple-element.43), channel_id=1, source_target_pairs={{0,6},{2,0},{4,2},{6,4},{1,7},{3,1},{5,3},{7,5},{8,14},{10,8},{12,... | collective-permute-start | bytes 196616 | tf_op jit(solution)/shard_map/ppermute | solution.py:155
  21.8 1.6 %collective-permute-start.3 = (bf16[4,2,128,128]{3,2,1,0:T(8,128)(2,1)S(1)}, bf16[4,2,128,128]{3,2,1,0:T(8,128)(2,1)S(1)}, u32[]{:S(2)}, u32[]{:S(2)}) collective-permute-start(bf16[4,2,128,128]{3,2,1,0:T(8,128)(2,1)S(1)} %pad_maximum_fusion.1.refs_0_.refs_4_), channel_id=1, source_target_pairs={{0,8},{8,0},{16,24},{24,16},{1,9},{9,1},{17,25},{25,17},{2,10},{10... | collective-permute-start | bytes 786440 | tf_op jit(solution)/shard_map/ppermute | solution.py:177
  23.3 1.3 %compare_convert_fusion = (f32[2]{0:T(128)S(1)}, f32[2]{0:T(128)S(1)}) fusion(s32[]{:T(128)} %bitcast.37, s32[]{:T(128)} %bitcast.34), kind=kLoop, calls=%fused_computation.59 | loop fusion | flops 8 | bytes 24 | tf_op jit(solution)/shard_map/convert_element_type | solution.py:204
  24.6 1.3 %compare_convert_fusion.2 = (f32[2]{0:T(128)S(1)}, f32[2]{0:T(128)S(1)}) fusion(s32[]{:T(128)} %bitcast.31, s32[]{:T(128)} %bitcast.28), kind=kLoop, calls=%fused_computation.61 | loop fusion | flops 8 | bytes 24 | tf_op jit(solution)/shard_map/convert_element_type | solution.py:204
  25.9 1.6 %collective-permute-start.4 = (bf16[4,2,128,128]{3,2,1,0:T(8,128)(2,1)S(1)}, bf16[4,2,128,128]{3,2,1,0:T(8,128)(2,1)S(1)}, u32[]{:S(2)}, u32[]{:S(2)}) collective-permute-start(bf16[4,2,128,128]{3,2,1,0:T(8,128)(2,1)S(1)} %pad_maximum_fusion.1.refs_0_.refs_4_), channel_id=1, source_target_pairs={{0,16},{8,24},{16,0},{24,8},{1,17},{9,25},{17,1},{25,9},{2,18},{10... | collective-permute-start | bytes 786440 | tf_op jit(solution)/shard_map/ppermute | solution.py:177
  28.0 1.6 %collective-permute-start.10 = (bf16[4,2,128,128]{3,2,1,0:T(8,128)(2,1)S(1)}, bf16[4,2,128,128]{3,2,1,0:T(8,128)(2,1)S(1)}, u32[]{:S(2)}, u32[]{:S(2)}) collective-permute-start(bf16[4,2,128,128]{3,2,1,0:T(8,128)(2,1)S(1)} %pad_maximum_fusion.2.refs_0_.refs_4_), channel_id=1, source_target_pairs={{0,16},{8,24},{16,0},{24,8},{1,17},{9,25},{17,1},{25,9},{2,18},{10... | collective-permute-start | bytes 786440 | tf_op jit(solution)/shard_map/ppermute | solution.py:177
  29.6 1.4 %collective-permute-start.11 = (bf16[4,2,128,128]{3,2,1,0:T(8,128)(2,1)S(1)}, bf16[4,2,128,128]{3,2,1,0:T(8,128)(2,1)S(1)}, u32[]{:S(2)}, u32[]{:S(2)}) collective-permute-start(bf16[4,2,128,128]{3,2,1,0:T(8,128)(2,1)S(1)} %pad_maximum_fusion.2.refs_0_.refs_4_), channel_id=1, source_target_pairs={{0,24},{8,16},{16,8},{24,0},{1,25},{9,17},{17,9},{25,1},{2,26},{10... | collective-permute-start | bytes 786440 | tf_op jit(solution)/shard_map/ppermute | solution.py:177
  32.9 13.2 %collective-permute-done.4.refs_2_.refs_6_ = bf16[4,2,128,128]{3,2,1,0:T(8,128)(2,1)S(1)} collective-permute-done((bf16[4,2,128,128]{3,2,1,0:T(8,128)(2,1)S(1)}, bf16[4,2,128,128]{3,2,1,0:T(8,128)(2,1)S(1)}, u32[]{:S(2)}, u32[]{:S(2)}) %collective-permute-start.4) | collective-permute-done | bytes 262176 | tf_op jit(solution)/shard_map/ppermute | solution.py:177
  46.9 7.3 %shard_map.111 = (bf16[128,2048]{1,0:T(8,128)(2,1)}, bf16[128,1024]{1,0:T(8,128)(2,1)}, bf16[128,1024]{1,0:T(8,128)(2,1)}, bf16[4,2,128,128]{3,2,1,0:T(8,128)(2,...) custom-call(s32[4]{0:T(128)} %bitcast.98, ...), custom_call_target="tpu_custom_call" | custom-call | flops 1006632960 | bytes 3670016 | tf_op jit(solution)/shard_map/pallas_call | solution.py:136
  54.9 1.3 %collective-permute-start.19 = (bf16[4,2,128,128]{3,2,1,0:T(8,128)(2,1)}, bf16[4,2,128,128]{3,2,1,0:T(8,128)(2,1)S(1)}, u32[]{:S(2)}, u32[]{:S(2)}) collective-permute-start(bf16[4,2,128,128]{3,2,1,0:T(8,128)(2,1)} %get-tuple-element.30), channel_id=1, source_target_pairs={{0,16},{8,24},{16,0},{24,8},{1,17},{9,25},{17,1},{25,9},{2,18},{10... | collective-permute-start | bytes 786440 | tf_op jit(solution)/shard_map/ppermute | solution.py:190
  56.1 1.7 %collective-permute-start.20 = (bf16[4,2,128,128]{3,2,1,0:T(8,128)(2,1)}, bf16[4,2,128,128]{3,2,1,0:T(8,128)(2,1)S(1)}, u32[]{:S(2)}, u32[]{:S(2)}) collective-permute-start(bf16[4,2,128,128]{3,2,1,0:T(8,128)(2,1)} %get-tuple-element.31), channel_id=1, source_target_pairs={{0,24},{8,16},{16,8},{24,0},{1,25},{9,17},{17,9},{25,1},{2,26},{10... | collective-permute-start | bytes 786440 | tf_op jit(solution)/shard_map/ppermute | solution.py:190
  58.6 7.4 %shard_map.112 = (bf16[128,2048]{1,0:T(8,128)(2,1)}, bf16[128,1024]{1,0:T(8,128)(2,1)}, bf16[128,1024]{1,0:T(8,128)(2,1)}, bf16[4,2,128,128]{3,2,1,0:T(8,128)(2,...) custom-call(s32[4]{0:T(128)} %bitcast.99, ...), custom_call_target="tpu_custom_call" | custom-call | flops 1006632960 | bytes 3670016 | tf_op jit(solution)/shard_map/pallas_call | solution.py:136
  66.6 1.3 %collective-permute-start.13 = (bf16[4,2,128,128]{3,2,1,0:T(8,128)(2,1)}, bf16[4,2,128,128]{3,2,1,0:T(8,128)(2,1)S(1)}, u32[]{:S(2)}, u32[]{:S(2)}) collective-permute-start(bf16[4,2,128,128]{3,2,1,0:T(8,128)(2,1)} %get-tuple-element.26), channel_id=1, source_target_pairs={{0,16},{8,24},{16,0},{24,8},{1,17},{9,25},{17,1},{25,9},{2,18},{10... | collective-permute-start | bytes 786440 | tf_op jit(solution)/shard_map/ppermute | solution.py:190
  67.9 2.0 %select_bitcast_fusion = bf16[1,1,128,2048]{3,2,1,0:T(8,128)(2,1)} fusion(bf16[128,2048]{1,0:T(8,128)(2,1)S(1)} %copy-done, bf16[128,2048]{1,0:T(8,128)(2,1)} %get-tuple-element.19, pred[2048]{0:T(1024)(128)(4,1)S(1)} %fusion.1), kind=kLoop, calls=%fused_computation.3 | loop fusion | flops 262144 | bytes 1574912 | tf_op jit(solution)/shard_map/broadcast_in_dim | solution.py:245
  70.9 1.7 %collective-permute-start.14 = (bf16[4,2,128,128]{3,2,1,0:T(8,128)(2,1)S(1)}, bf16[4,2,128,128]{3,2,1,0:T(8,128)(2,1)S(1)}, u32[]{:S(2)}, u32[]{:S(2)}) collective-permute-start(bf16[4,2,128,128]{3,2,1,0:T(8,128)(2,1)S(1)} %copy-done.11), channel_id=1, source_target_pairs={{0,24},{8,16},{16,8},{24,0},{1,25},{9,17},{17,9},{25,1},{2,26},{10... | collective-permute-start | bytes 786440 | tf_op jit(solution)/shard_map/ppermute | solution.py:190
  72.8 3.9 %collective-permute-start.21 = (bf16[2,128,128]{2,1,0:T(8,128)(2,1)S(1)}, bf16[2,128,128]{2,1,0:T(8,128)(2,1)S(1)}, u32[]{:S(2)}, u32[]{:S(2)}) collective-permute-start(bf16[2,128,128]{2,1,0:T(8,128)(2,1)S(1)} %get-tuple-element.39), channel_id=1, source_target_pairs={{0,2},{2,4},{4,6},{6,0},{1,3},{3,5},{5,7},{7,1},{8,10},{10,12},{12... | collective-permute-start | bytes 196616 | tf_op jit(solution)/shard_map/ppermute | solution.py:155
  76.7 2.4 %collective-permute-start.23 = (bf16[2,128,128]{2,1,0:T(8,128)(2,1)S(1)}, bf16[2,128,128]{2,1,0:T(8,128)(2,1)S(1)}, u32[]{:S(2)}, u32[]{:S(2)}) collective-permute-start(bf16[2,128,128]{2,1,0:T(8,128)(2,1)S(1)} %get-tuple-element.37), channel_id=1, source_target_pairs={{0,6},{2,0},{4,2},{6,4},{1,7},{3,1},{5,3},{7,5},{8,14},{10,8},{12,... | collective-permute-start | bytes 196616 | tf_op jit(solution)/shard_map/ppermute | solution.py:155
  79.4 2.9 %collective-permute-start.15 = (bf16[2,128,128]{2,1,0:T(8,128)(2,1)S(1)}, bf16[2,128,128]{2,1,0:T(8,128)(2,1)S(1)}, u32[]{:S(2)}, u32[]{:S(2)}) collective-permute-start(bf16[2,128,128]{2,1,0:T(8,128)(2,1)S(1)} %get-tuple-element.35), channel_id=1, source_target_pairs={{0,2},{2,4},{4,6},{6,0},{1,3},{3,5},{5,7},{7,1},{8,10},{10,12},{12... | collective-permute-start | bytes 196616 | tf_op jit(solution)/shard_map/ppermute | solution.py:155
  82.5 2.5 %collective-permute-start.17 = (bf16[2,128,128]{2,1,0:T(8,128)(2,1)S(1)}, bf16[2,128,128]{2,1,0:T(8,128)(2,1)S(1)}, u32[]{:S(2)}, u32[]{:S(2)}) collective-permute-start(bf16[2,128,128]{2,1,0:T(8,128)(2,1)S(1)} %get-tuple-element.33), channel_id=1, source_target_pairs={{0,6},{2,0},{4,2},{6,4},{1,7},{3,1},{5,3},{7,5},{8,14},{10,8},{12,... | collective-permute-start | bytes 196616 | tf_op jit(solution)/shard_map/ppermute | solution.py:155
  85.6 2.2 %collective-permute-done.16 = bf16[2,128,128]{2,1,0:T(8,128)(2,1)S(1)} collective-permute-done((bf16[2,128,128]{2,1,0:T(8,128)(2,1)S(1)}, bf16[2,128,128]{2,1,0:T(8,128)(2,1)S(1)}, u32[]{:S(2)}, u32[]{:S(2)}) %collective-permute-start.16) | collective-permute-done | bytes 65568 | tf_op jit(solution)/shard_map/ppermute | solution.py:155
  89.0 1.0 %pad_maximum_fusion = f32[2,128,2,256]{3,2,1,0:T(2,128)} fusion(f32[2,128,2,128]{3,2,1,0:T(2,128)S(1)} %get-tuple-element.51, f32[2,128,2,128]{3,2,1,0:T(2,128)S(1)} %get-tuple-element.50), kind=kLoop, calls=%fused_computation | loop fusion | flops 131072 | bytes 1048576 | tf_op jit(solution)/shard_map/concatenate | solution.py:244
  (94 shorter events, 11.3 us)
Async XLA Ops:
  10.7 8.1 %collective-permute-start = (bf16[2,128,128]{2,1,0:T(8,128)(2,1)S(1)}, bf16[2,128,128]{2,1,0:T(8,128)(2,1)S(1)}, u32[]{:S(2)}, u32[]{:S(2)}) collective-permute-start(bf16[2,128,128]{2,1,0:T(8,128)(2,1)S(1)} %get-tuple-element.49), channel_id=1, source_target_pairs={{0,2},{2,4},{4,6},{6,0},{1,3},{3,5},{5,7},{7,1},{8,10},{10,12},{12... | collective-permute-start | bytes 196616 | tf_op jit(solution)/shard_map/ppermute | solution.py:155
  13.8 7.9 %collective-permute-start.1 = (bf16[2,128,128]{2,1,0:T(8,128)(2,1)S(1)}, bf16[2,128,128]{2,1,0:T(8,128)(2,1)S(1)}, u32[]{:S(2)}, u32[]{:S(2)}) collective-permute-start(bf16[2,128,128]{2,1,0:T(8,128)(2,1)S(1)} %get-tuple-element.48), channel_id=1, source_target_pairs={{0,4},{2,6},{4,0},{6,2},{1,5},{3,7},{5,1},{7,3},{8,12},{10,14},{12... | collective-permute-start | bytes 196616 | tf_op jit(solution)/shard_map/ppermute | solution.py:155
  16.4 5.3 %collective-permute-start.2 = (bf16[2,128,128]{2,1,0:T(8,128)(2,1)S(1)}, bf16[2,128,128]{2,1,0:T(8,128)(2,1)S(1)}, u32[]{:S(2)}, u32[]{:S(2)}) collective-permute-start(bf16[2,128,128]{2,1,0:T(8,128)(2,1)S(1)} %get-tuple-element.47), channel_id=1, source_target_pairs={{0,6},{2,0},{4,2},{6,4},{1,7},{3,1},{5,3},{7,5},{8,14},{10,8},{12,... | collective-permute-start | bytes 196616 | tf_op jit(solution)/shard_map/ppermute | solution.py:155
  17.8 9.7 %collective-permute-start.6 = (bf16[2,128,128]{2,1,0:T(8,128)(2,1)S(1)}, bf16[2,128,128]{2,1,0:T(8,128)(2,1)S(1)}, u32[]{:S(2)}, u32[]{:S(2)}) collective-permute-start(bf16[2,128,128]{2,1,0:T(8,128)(2,1)S(1)} %get-tuple-element.45), channel_id=1, source_target_pairs={{0,2},{2,4},{4,6},{6,0},{1,3},{3,5},{5,7},{7,1},{8,10},{10,12},{12... | collective-permute-start | bytes 196616 | tf_op jit(solution)/shard_map/ppermute | solution.py:155
  18.5 9.5 %collective-permute-start.7 = (bf16[2,128,128]{2,1,0:T(8,128)(2,1)S(1)}, bf16[2,128,128]{2,1,0:T(8,128)(2,1)S(1)}, u32[]{:S(2)}, u32[]{:S(2)}) collective-permute-start(bf16[2,128,128]{2,1,0:T(8,128)(2,1)S(1)} %get-tuple-element.44), channel_id=1, source_target_pairs={{0,4},{2,6},{4,0},{6,2},{1,5},{3,7},{5,1},{7,3},{8,12},{10,14},{12... | collective-permute-start | bytes 196616 | tf_op jit(solution)/shard_map/ppermute | solution.py:155
  18.8 9.1 %collective-permute-start.8 = (bf16[2,128,128]{2,1,0:T(8,128)(2,1)S(1)}, bf16[2,128,128]{2,1,0:T(8,128)(2,1)S(1)}, u32[]{:S(2)}, u32[]{:S(2)}) collective-permute-start(bf16[2,128,128]{2,1,0:T(8,128)(2,1)S(1)} %get-tuple-element.43), channel_id=1, source_target_pairs={{0,6},{2,0},{4,2},{6,4},{1,7},{3,1},{5,3},{7,5},{8,14},{10,8},{12,... | collective-permute-start | bytes 196616 | tf_op jit(solution)/shard_map/ppermute | solution.py:155
  21.8 9.3 %collective-permute-start.3 = (bf16[4,2,128,128]{3,2,1,0:T(8,128)(2,1)S(1)}, bf16[4,2,128,128]{3,2,1,0:T(8,128)(2,1)S(1)}, u32[]{:S(2)}, u32[]{:S(2)}) collective-permute-start(bf16[4,2,128,128]{3,2,1,0:T(8,128)(2,1)S(1)} %pad_maximum_fusion.1.refs_0_.refs_4_), channel_id=1, source_target_pairs={{0,8},{8,0},{16,24},{24,16},{1,9},{9,1},{17,25},{25,17},{2,10},{10... | collective-permute-start | bytes 786440 | tf_op jit(solution)/shard_map/ppermute | solution.py:177
  25.9 20.2 %collective-permute-start.4 = (bf16[4,2,128,128]{3,2,1,0:T(8,128)(2,1)S(1)}, bf16[4,2,128,128]{3,2,1,0:T(8,128)(2,1)S(1)}, u32[]{:S(2)}, u32[]{:S(2)}) collective-permute-start(bf16[4,2,128,128]{3,2,1,0:T(8,128)(2,1)S(1)} %pad_maximum_fusion.1.refs_0_.refs_4_), channel_id=1, source_target_pairs={{0,16},{8,24},{16,0},{24,8},{1,17},{9,25},{17,1},{25,9},{2,18},{10... | collective-permute-start | bytes 786440 | tf_op jit(solution)/shard_map/ppermute | solution.py:177
  27.5 18.7 %collective-permute-start.5 = (bf16[4,2,128,128]{3,2,1,0:T(8,128)(2,1)S(1)}, bf16[4,2,128,128]{3,2,1,0:T(8,128)(2,1)S(1)}, u32[]{:S(2)}, u32[]{:S(2)}) collective-permute-start(bf16[4,2,128,128]{3,2,1,0:T(8,128)(2,1)S(1)} %pad_maximum_fusion.1.refs_0_.refs_4_), channel_id=1, source_target_pairs={{0,24},{8,16},{16,8},{24,0},{1,25},{9,17},{17,9},{25,1},{2,26},{10... | collective-permute-start | bytes 786440 | tf_op jit(solution)/shard_map/ppermute | solution.py:177
  28.0 28.1 %collective-permute-start.10 = (bf16[4,2,128,128]{3,2,1,0:T(8,128)(2,1)S(1)}, bf16[4,2,128,128]{3,2,1,0:T(8,128)(2,1)S(1)}, u32[]{:S(2)}, u32[]{:S(2)}) collective-permute-start(bf16[4,2,128,128]{3,2,1,0:T(8,128)(2,1)S(1)} %pad_maximum_fusion.2.refs_0_.refs_4_), channel_id=1, source_target_pairs={{0,16},{8,24},{16,0},{24,8},{1,17},{9,25},{17,1},{25,9},{2,18},{10... | collective-permute-start | bytes 786440 | tf_op jit(solution)/shard_map/ppermute | solution.py:177
  29.6 28.2 %collective-permute-start.11 = (bf16[4,2,128,128]{3,2,1,0:T(8,128)(2,1)S(1)}, bf16[4,2,128,128]{3,2,1,0:T(8,128)(2,1)S(1)}, u32[]{:S(2)}, u32[]{:S(2)}) collective-permute-start(bf16[4,2,128,128]{3,2,1,0:T(8,128)(2,1)S(1)} %pad_maximum_fusion.2.refs_0_.refs_4_), channel_id=1, source_target_pairs={{0,24},{8,16},{16,8},{24,0},{1,25},{9,17},{17,9},{25,1},{2,26},{10... | collective-permute-start | bytes 786440 | tf_op jit(solution)/shard_map/ppermute | solution.py:177
  31.1 26.8 %collective-permute-start.9 = (bf16[4,2,128,128]{3,2,1,0:T(8,128)(2,1)S(1)}, bf16[4,2,128,128]{3,2,1,0:T(8,128)(2,1)S(1)}, u32[]{:S(2)}, u32[]{:S(2)}) collective-permute-start(bf16[4,2,128,128]{3,2,1,0:T(8,128)(2,1)S(1)} %pad_maximum_fusion.2.refs_0_.refs_4_), channel_id=1, source_target_pairs={{0,8},{8,0},{16,24},{24,16},{1,9},{9,1},{17,25},{25,17},{2,10},{10... | collective-permute-start | bytes 786440 | tf_op jit(solution)/shard_map/ppermute | solution.py:177
  54.2 16.6 %collective-permute-start.18 = (bf16[4,2,128,128]{3,2,1,0:T(8,128)(2,1)}, bf16[4,2,128,128]{3,2,1,0:T(8,128)(2,1)S(1)}, u32[]{:S(2)}, u32[]{:S(2)}) collective-permute-start(bf16[4,2,128,128]{3,2,1,0:T(8,128)(2,1)} %get-tuple-element.29), channel_id=1, source_target_pairs={{0,8},{8,0},{16,24},{24,16},{1,9},{9,1},{17,25},{25,17},{2,10},{10... | collective-permute-start | bytes 786440 | tf_op jit(solution)/shard_map/ppermute | solution.py:190
  54.9 17.7 %collective-permute-start.19 = (bf16[4,2,128,128]{3,2,1,0:T(8,128)(2,1)}, bf16[4,2,128,128]{3,2,1,0:T(8,128)(2,1)S(1)}, u32[]{:S(2)}, u32[]{:S(2)}) collective-permute-start(bf16[4,2,128,128]{3,2,1,0:T(8,128)(2,1)} %get-tuple-element.30), channel_id=1, source_target_pairs={{0,16},{8,24},{16,0},{24,8},{1,17},{9,25},{17,1},{25,9},{2,18},{10... | collective-permute-start | bytes 786440 | tf_op jit(solution)/shard_map/ppermute | solution.py:190
  56.1 16.4 %collective-permute-start.20 = (bf16[4,2,128,128]{3,2,1,0:T(8,128)(2,1)}, bf16[4,2,128,128]{3,2,1,0:T(8,128)(2,1)S(1)}, u32[]{:S(2)}, u32[]{:S(2)}) collective-permute-start(bf16[4,2,128,128]{3,2,1,0:T(8,128)(2,1)} %get-tuple-element.31), channel_id=1, source_target_pairs={{0,24},{8,16},{16,8},{24,0},{1,25},{9,17},{17,9},{25,1},{2,26},{10... | collective-permute-start | bytes 786440 | tf_op jit(solution)/shard_map/ppermute | solution.py:190
  66.0 10.7 %collective-permute-start.12 = (bf16[4,2,128,128]{3,2,1,0:T(8,128)(2,1)}, bf16[4,2,128,128]{3,2,1,0:T(8,128)(2,1)S(1)}, u32[]{:S(2)}, u32[]{:S(2)}) collective-permute-start(bf16[4,2,128,128]{3,2,1,0:T(8,128)(2,1)} %get-tuple-element.25), channel_id=1, source_target_pairs={{0,8},{8,0},{16,24},{24,16},{1,9},{9,1},{17,25},{25,17},{2,10},{10... | collective-permute-start | bytes 786440 | tf_op jit(solution)/shard_map/ppermute | solution.py:190
  66.6 12.5 %collective-permute-start.13 = (bf16[4,2,128,128]{3,2,1,0:T(8,128)(2,1)}, bf16[4,2,128,128]{3,2,1,0:T(8,128)(2,1)S(1)}, u32[]{:S(2)}, u32[]{:S(2)}) collective-permute-start(bf16[4,2,128,128]{3,2,1,0:T(8,128)(2,1)} %get-tuple-element.26), channel_id=1, source_target_pairs={{0,16},{8,24},{16,0},{24,8},{1,17},{9,25},{17,1},{25,9},{2,18},{10... | collective-permute-start | bytes 786440 | tf_op jit(solution)/shard_map/ppermute | solution.py:190
  70.9 8.2 %collective-permute-start.14 = (bf16[4,2,128,128]{3,2,1,0:T(8,128)(2,1)S(1)}, bf16[4,2,128,128]{3,2,1,0:T(8,128)(2,1)S(1)}, u32[]{:S(2)}, u32[]{:S(2)}) collective-permute-start(bf16[4,2,128,128]{3,2,1,0:T(8,128)(2,1)S(1)} %copy-done.11), channel_id=1, source_target_pairs={{0,24},{8,16},{16,8},{24,0},{1,25},{9,17},{17,9},{25,1},{2,26},{10... | collective-permute-start | bytes 786440 | tf_op jit(solution)/shard_map/ppermute | solution.py:190
  72.8 9.7 %collective-permute-start.21 = (bf16[2,128,128]{2,1,0:T(8,128)(2,1)S(1)}, bf16[2,128,128]{2,1,0:T(8,128)(2,1)S(1)}, u32[]{:S(2)}, u32[]{:S(2)}) collective-permute-start(bf16[2,128,128]{2,1,0:T(8,128)(2,1)S(1)} %get-tuple-element.39), channel_id=1, source_target_pairs={{0,2},{2,4},{4,6},{6,0},{1,3},{3,5},{5,7},{7,1},{8,10},{10,12},{12... | collective-permute-start | bytes 196616 | tf_op jit(solution)/shard_map/ppermute | solution.py:155
  76.7 8.3 %collective-permute-start.22 = (bf16[2,128,128]{2,1,0:T(8,128)(2,1)S(1)}, bf16[2,128,128]{2,1,0:T(8,128)(2,1)S(1)}, u32[]{:S(2)}, u32[]{:S(2)}) collective-permute-start(bf16[2,128,128]{2,1,0:T(8,128)(2,1)S(1)} %get-tuple-element.38), channel_id=1, source_target_pairs={{0,4},{2,6},{4,0},{6,2},{1,5},{3,7},{5,1},{7,3},{8,12},{10,14},{12... | collective-permute-start | bytes 196616 | tf_op jit(solution)/shard_map/ppermute | solution.py:155
  76.7 8.3 %collective-permute-start.23 = (bf16[2,128,128]{2,1,0:T(8,128)(2,1)S(1)}, bf16[2,128,128]{2,1,0:T(8,128)(2,1)S(1)}, u32[]{:S(2)}, u32[]{:S(2)}) collective-permute-start(bf16[2,128,128]{2,1,0:T(8,128)(2,1)S(1)} %get-tuple-element.37), channel_id=1, source_target_pairs={{0,6},{2,0},{4,2},{6,4},{1,7},{3,1},{5,3},{7,5},{8,14},{10,8},{12,... | collective-permute-start | bytes 196616 | tf_op jit(solution)/shard_map/ppermute | solution.py:155
  79.4 6.1 %collective-permute-start.15 = (bf16[2,128,128]{2,1,0:T(8,128)(2,1)S(1)}, bf16[2,128,128]{2,1,0:T(8,128)(2,1)S(1)}, u32[]{:S(2)}, u32[]{:S(2)}) collective-permute-start(bf16[2,128,128]{2,1,0:T(8,128)(2,1)S(1)} %get-tuple-element.35), channel_id=1, source_target_pairs={{0,2},{2,4},{4,6},{6,0},{1,3},{3,5},{5,7},{7,1},{8,10},{10,12},{12... | collective-permute-start | bytes 196616 | tf_op jit(solution)/shard_map/ppermute | solution.py:155
  82.4 5.4 %collective-permute-start.16 = (bf16[2,128,128]{2,1,0:T(8,128)(2,1)S(1)}, bf16[2,128,128]{2,1,0:T(8,128)(2,1)S(1)}, u32[]{:S(2)}, u32[]{:S(2)}) collective-permute-start(bf16[2,128,128]{2,1,0:T(8,128)(2,1)S(1)} %get-tuple-element.34), channel_id=1, source_target_pairs={{0,4},{2,6},{4,0},{6,2},{1,5},{3,7},{5,1},{7,3},{8,12},{10,14},{12... | collective-permute-start | bytes 196616 | tf_op jit(solution)/shard_map/ppermute | solution.py:155
  82.5 5.8 %collective-permute-start.17 = (bf16[2,128,128]{2,1,0:T(8,128)(2,1)S(1)}, bf16[2,128,128]{2,1,0:T(8,128)(2,1)S(1)}, u32[]{:S(2)}, u32[]{:S(2)}) collective-permute-start(bf16[2,128,128]{2,1,0:T(8,128)(2,1)S(1)} %get-tuple-element.33), channel_id=1, source_target_pairs={{0,6},{2,0},{4,2},{6,4},{1,7},{3,1},{5,3},{7,5},{8,14},{10,8},{12,... | collective-permute-start | bytes 196616 | tf_op jit(solution)/shard_map/ppermute | solution.py:155
  (17 other events, 80.2 us)

commit v10 on v7

--- a/solution.py
+++ b/solution.py
@@ -247,9 +247,10 @@
     group_heads = group_feats // HEAD_DIM
     earlier = None
     parts = []
+    gathered = pair_gather(planes, pair_prompt)
     for k in range(n_groups):
         cols = slice(k * group_feats, (k + 1) * group_feats)
-        pieces = ctx_gather(pair_gather(planes[..., cols], pair_prompt))
+        pieces = ctx_gather(gathered[..., cols])
         outs = attention_grads(
             prefix_blocks[0, 0], resp_lengths[0, 0].reshape(1), place, queries[0, 0], d_out[0, 0], pieces,
             tree_ctx(), ctx_out_ranges(slot_rows), resp_keys[0, 0], resp_values[0, 0],

time: 88.3 us -> 93.3 us (1.057)
  waiting for transfers between devices: 10.6 us -> 21 us
  starting transfers between devices: 40.3 us -> 34.7 us
    ppermute x12 -> x9, waiting for transfers between devices: 5.15 us -> 10.6 us  [ring_shift(): return lax.ppermute(x, axis, [(i, (i + d) % n) for i in range(n)])]
    ppermute x12 -> x9, starting transfers between devices: 21.4 us -> 17 us  [ring_shift(): return lax.ppermute(x, axis, [(i, (i + d) % n) for i in range(n)])]
    ppermute x2, waiting for transfers between devices: 0.4 us -> 2.76 us  [ctx_gather(): from_x = lax.ppermute(x, 'ctx', along_x)]
    ppermute x2, waiting for transfers between devices: 2.33 us -> 3.82 us  [ctx_gather(): from_y = lax.ppermute(x, 'ctx', along_y)]
    unnamed x37 -> x40, local copies, waits for them, and re-layouts: 3.03 us -> 1.55 us
    ppermute x2, starting transfers between devices: 3.44 us -> 2.09 us  [ctx_gather(): from_y = lax.ppermute(x, 'ctx', along_y)]
    ppermute x2, starting transfers between devices: 2.02 us -> 3.05 us  [ctx_gather(): far_a = lax.ppermute(from_y[:, :, :half], 'ctx', along_x)]
    ppermute x2, waiting for transfers between devices: 2.65 us -> 3.64 us  [ctx_reduce(): got_x = lax.ppermute(send_x, 'ctx', along_x)]
  transfers between devices with their start and end apart: 28 -> 25, of which waited for: 6 -> 8; matrix products, arithmetic and copies ran while one was open for 8% -> 8% of each run, Pallas kernels for 17% -> 16%
where the time goes in v10:
time: 93.3 us; the launch traced here: 92.9 us
  starting transfers between devices  34.7 us (37%)
  waiting for transfers between devices  21 us (23%)
  Pallas kernels  14.9 us (16%)
  between operations  9.65 us (10%)
  other arithmetic  7.99 us (9%)
  local copies, waits for them, and re-layouts  4.59 us (5%)
    ppermute x9, starting transfers between devices, ring_shift(): return lax.ppermute(x, axis, [(i, (i + d) % n) for i in range(n)])  17 us
    pallas_call x2, Pallas kernels, attention_grads(): pl.pallas_call(functools.partial(attention_grad_kernel, layout), out_shap...  14.9 us
    ppermute x9, waiting for transfers between devices, ring_shift(): return lax.ppermute(x, axis, [(i, (i + d) % n) for i in range(n)])  10.6 us
    ppermute x2, waiting for transfers between devices, ctx_gather(): from_y = lax.ppermute(x, 'ctx', along_y)  3.82 us
    ppermute x2, waiting for transfers between devices, ctx_reduce(): got_x = lax.ppermute(send_x, 'ctx', along_x)  3.64 us
    ppermute x2, starting transfers between devices, ctx_gather(): far_a = lax.ppermute(from_y[:, :, :half], 'ctx', along_x)  3.05 us
    broadcast_in_dim x2, other arithmetic, shards(): return (dq[None, None], dkr[None, None], dvr[None, None], d_prefix)  2.79 us
    ppermute x2, waiting for transfers between devices, ctx_gather(): from_x = lax.ppermute(x, 'ctx', along_x)  2.76 us
  transfers between devices with their start and end apart: 25, of which 8 were waited for; matrix products, arithmetic and copies ran while one was open for 8% of the time, Pallas kernels for 16%

profile of v10, /device:TPU:0, one launch (start us, length us, event | category | flops | bytes accessed | tf_op | source)
XLA Modules:
  0.0 92.9 jit_solution(9672988932925313690)
XLA Ops:
  0.8 1.6 %fusion.11 = (s32[1]{0:T(128)}, s32[1]{0:T(128)}, s32[1]{0:T(128)}, s32[1]{0:T(128)}, s32[1]{0:T(128)}, /*index=5*/s32[1]{0:T(128)}, s32[1]{0:T(128)}, s32[1]{0:T(128)}) fusion(s32[4]{0:T(128)} %param.15, s32[]{:T(128)S(6)} %select_n.160, s32[]{:T(128)S(6)} %select_n.162, s32[]{:T(128)S(6)} %select_n.152, s32[]{:T(128)S(6)} %select_n.149, s32[]{:T(128)S(6)} %select_n.146, ...), kind=kLoop, calls=%fused_computation.63 | loop fusion | bytes 96 | tf_op jit(solution)/shard_map/dynamic_slice | solution.py:224
  10.6 3.1 %collective-permute-start = (bf16[2,128,256]{2,1,0:T(8,128)(2,1)S(1)}, bf16[2,128,256]{2,1,0:T(8,128)(2,1)S(1)}, u32[]{:S(2)}, u32[]{:S(2)}) collective-permute-start(bf16[2,128,256]{2,1,0:T(8,128)(2,1)S(1)} %bitcast.84), channel_id=1, source_target_pairs={{0,2},{2,4},{4,6},{6,0},{1,3},{3,5},{5,7},{7,1},{8,10},{10,12},{12... | collective-permute-start | bytes 393224 | tf_op jit(solution)/shard_map/ppermute | solution.py:155
  13.7 2.7 %collective-permute-start.1 = (bf16[2,128,256]{2,1,0:T(8,128)(2,1)S(1)}, bf16[2,128,256]{2,1,0:T(8,128)(2,1)S(1)}, u32[]{:S(2)}, u32[]{:S(2)}) collective-permute-start(bf16[2,128,256]{2,1,0:T(8,128)(2,1)S(1)} %bitcast.85), channel_id=1, source_target_pairs={{0,4},{2,6},{4,0},{6,2},{1,5},{3,7},{5,1},{7,3},{8,12},{10,14},{12... | collective-permute-start | bytes 393224 | tf_op jit(solution)/shard_map/ppermute | solution.py:155
  16.4 1.4 %collective-permute-start.2 = (bf16[2,128,256]{2,1,0:T(8,128)(2,1)S(1)}, bf16[2,128,256]{2,1,0:T(8,128)(2,1)S(1)}, u32[]{:S(2)}, u32[]{:S(2)}) collective-permute-start(bf16[2,128,256]{2,1,0:T(8,128)(2,1)S(1)} %bitcast.86), channel_id=1, source_target_pairs={{0,6},{2,0},{4,2},{6,4},{1,7},{3,1},{5,3},{7,5},{8,14},{10,8},{12,... | collective-permute-start | bytes 393224 | tf_op jit(solution)/shard_map/ppermute | solution.py:155
  17.8 2.3 %collective-permute-done = bf16[2,128,256]{2,1,0:T(8,128)(2,1)S(1)} collective-permute-done((bf16[2,128,256]{2,1,0:T(8,128)(2,1)S(1)}, bf16[2,128,256]{2,1,0:T(8,128)(2,1)S(1)}, u32[]{:S(2)}, u32[]{:S(2)}) %collective-permute-start) | collective-permute-done | bytes 131104 | tf_op jit(solution)/shard_map/ppermute | solution.py:155
  20.2 4.8 %collective-permute-done.1 = bf16[2,128,256]{2,1,0:T(8,128)(2,1)S(1)} collective-permute-done((bf16[2,128,256]{2,1,0:T(8,128)(2,1)S(1)}, bf16[2,128,256]{2,1,0:T(8,128)(2,1)S(1)}, u32[]{:S(2)}, u32[]{:S(2)}) %collective-permute-start.1) | collective-permute-done | bytes 131104 | tf_op jit(solution)/shard_map/ppermute | solution.py:155
  25.2 1.6 %collective-permute-start.4 = (bf16[4,2,128,128]{3,2,1,0:T(8,128)(2,1)S(1)}, bf16[4,2,128,128]{3,2,1,0:T(8,128)(2,1)S(1)}, u32[]{:S(2)}, u32[]{:S(2)}) collective-permute-start(bf16[4,2,128,128]{3,2,1,0:T(8,128)(2,1)S(1)} %get-tuple-element.29.refs_0_.refs_5_), channel_id=1, source_target_pairs={{0,16},{8,24},{16,0},{24,8},{1,17},{9,25},{17,1},{25,9},{2,18},{10... | collective-permute-start | bytes 786440 | tf_op jit(solution)/shard_map/ppermute | solution.py:180
  26.8 1.5 %collective-permute-start.3 = (bf16[4,2,128,128]{3,2,1,0:T(8,128)(2,1)S(1)}, bf16[4,2,128,128]{3,2,1,0:T(8,128)(2,1)S(1)}, u32[]{:S(2)}, u32[]{:S(2)}) collective-permute-start(bf16[4,2,128,128]{3,2,1,0:T(8,128)(2,1)S(1)} %get-tuple-element.29.refs_0_.refs_5_), channel_id=1, source_target_pairs={{0,8},{8,0},{16,24},{24,16},{1,9},{9,1},{17,25},{25,17},{2,10},{10... | collective-permute-start | bytes 786440 | tf_op jit(solution)/shard_map/ppermute | solution.py:179
  30.6 3.8 %collective-permute-done.4.refs_2_.refs_7_ = bf16[4,2,128,128]{3,2,1,0:T(8,128)(2,1)S(1)} collective-permute-done((bf16[4,2,128,128]{3,2,1,0:T(8,128)(2,1)S(1)}, bf16[4,2,128,128]{3,2,1,0:T(8,128)(2,1)S(1)}, u32[]{:S(2)}, u32[]{:S(2)}) %collective-permute-start.4) | collective-permute-done | bytes 262176 | tf_op jit(solution)/shard_map/ppermute | solution.py:180
  34.5 1.6 %collective-permute-start.5 = (bf16[4,2,64,128]{3,2,1,0:T(8,128)(2,1)S(1)}, bf16[4,2,64,128]{3,2,1,0:T(8,128)(2,1)S(1)}, u32[]{:S(2)}, u32[]{:S(2)}) collective-permute-start(bf16[4,2,64,128]{3,2,1,0:T(8,128)(2,1)S(1)} %slice.89), channel_id=1, source_target_pairs={{0,8},{8,0},{16,24},{24,16},{1,9},{9,1},{17,25},{25,17},{2,10},{10... | collective-permute-start | bytes 393224 | tf_op jit(solution)/shard_map/ppermute | solution.py:182
  36.0 1.6 %collective-permute-start.6 = (bf16[4,2,64,128]{3,2,1,0:T(8,128)(2,1)S(1)}, bf16[4,2,64,128]{3,2,1,0:T(8,128)(2,1)S(1)}, u32[]{:S(2)}, u32[]{:S(2)}) collective-permute-start(bf16[4,2,64,128]{3,2,1,0:T(8,128)(2,1)S(1)} %slice.90), channel_id=1, source_target_pairs={{0,16},{8,24},{16,0},{24,8},{1,17},{9,25},{17,1},{25,9},{2,18},{10... | collective-permute-start | bytes 393224 | tf_op jit(solution)/shard_map/ppermute | solution.py:183
  38.8 2.8 %collective-permute-done.7.refs_1_.refs_6_ = bf16[4,2,128,128]{3,2,1,0:T(8,128)(2,1)S(1)} collective-permute-done((bf16[4,2,128,128]{3,2,1,0:T(8,128)(2,1)S(1)}, bf16[4,2,128,128]{3,2,1,0:T(8,128)(2,1)S(1)}, u32[]{:S(2)}, u32[]{:S(2)}) %collective-permute-start.7) | collective-permute-done | bytes 262176 | tf_op jit(solution)/shard_map/ppermute | solution.py:179
  42.3 1.5 %collective-permute-start.9 = (bf16[4,2,64,128]{3,2,1,0:T(8,128)(2,1)S(1)}, bf16[4,2,64,128]{3,2,1,0:T(8,128)(2,1)S(1)}, u32[]{:S(2)}, u32[]{:S(2)}) collective-permute-start(bf16[4,2,64,128]{3,2,1,0:T(8,128)(2,1)S(1)} %slice.92), channel_id=1, source_target_pairs={{0,8},{8,0},{16,24},{24,16},{1,9},{9,1},{17,25},{25,17},{2,10},{10... | collective-permute-start | bytes 393224 | tf_op jit(solution)/shard_map/ppermute | solution.py:182
  45.8 7.4 %shard_map.111 = (bf16[128,2048]{1,0:T(8,128)(2,1)}, bf16[128,1024]{1,0:T(8,128)(2,1)}, bf16[128,1024]{1,0:T(8,128)(2,1)}, bf16[4,2,128,128]{3,2,1,0:T(8,128)(2,...) custom-call(s32[4]{0:T(128)} %bitcast.98, s32[1]{0:T(128)} %bitcast.81.length_ref, ...), custom_call_target="tpu_custom_call" | custom-call | flops 1006632960 | bytes 3670016 | tf_op jit(solution)/shard_map/pallas_call | solution.py:136
  53.8 1.5 %collective-permute-start.19 = (bf16[4,2,192,128]{3,2,1,0:T(8,128)(2,1)}, bf16[4,2,192,128]{3,2,1,0:T(8,128)(2,1)S(1)}, u32[]{:S(2)}, u32[]{:S(2)}) collective-permute-start(bf16[4,2,192,128]{3,2,1,0:T(8,128)(2,1)} %get-tuple-element.27), channel_id=1, source_target_pairs={{0,16},{8,24},{16,0},{24,8},{1,17},{9,25},{17,1},{25,9},{2,18},{10... | collective-permute-start | bytes 1179656 | tf_op jit(solution)/shard_map/ppermute | solution.py:207
  56.0 7.5 %shard_map.112 = (bf16[128,2048]{1,0:T(8,128)(2,1)}, bf16[128,1024]{1,0:T(8,128)(2,1)}, bf16[128,1024]{1,0:T(8,128)(2,1)}, bf16[4,2,128,128]{3,2,1,0:T(8,128)(2,...) custom-call(s32[4]{0:T(128)} %bitcast.99, s32[1]{0:T(128)} %bitcast.82.length_ref, ...), custom_call_target="tpu_custom_call" | custom-call | flops 1006632960 | bytes 3670016 | tf_op jit(solution)/shard_map/pallas_call | solution.py:136
  63.5 1.6 %collective-permute-start.11 = (bf16[4,2,192,128]{3,2,1,0:T(8,128)(2,1)}, bf16[4,2,192,128]{3,2,1,0:T(8,128)(2,1)S(1)}, u32[]{:S(2)}, u32[]{:S(2)}) collective-permute-start(bf16[4,2,192,128]{3,2,1,0:T(8,128)(2,1)} %get-tuple-element.23), channel_id=1, source_target_pairs={{0,8},{8,0},{16,24},{24,16},{1,9},{9,1},{17,25},{25,17},{2,10},{10... | collective-permute-start | bytes 1179656 | tf_op jit(solution)/shard_map/ppermute | solution.py:206
  65.6 1.9 %select_bitcast_fusion = bf16[1,1,128,2048]{3,2,1,0:T(8,128)(2,1)} fusion(bf16[128,2048]{1,0:T(8,128)(2,1)S(1)} %copy-done.1, bf16[128,2048]{1,0:T(8,128)(2,1)} %get-tuple-element.17, pred[2048]{0:T(1024)(128)(4,1)S(1)} %fusion.1), kind=kLoop, calls=%fused_computation.4 | loop fusion | flops 262144 | bytes 1574912 | tf_op jit(solution)/shard_map/broadcast_in_dim | solution.py:266
  67.6 1.6 %collective-permute-start.20 = (bf16[4,2,64,128]{3,2,1,0:T(8,128)(2,1)S(1)}, bf16[4,2,64,128]{3,2,1,0:T(8,128)(2,1)S(1)}, u32[]{:S(2)}, u32[]{:S(2)}) collective-permute-start(bf16[4,2,64,128]{3,2,1,0:T(8,128)(2,1)S(1)} %slice.104), channel_id=1, source_target_pairs={{0,16},{8,24},{16,0},{24,8},{1,17},{9,25},{17,1},{25,9},{2,18},{10... | collective-permute-start | bytes 393224 | tf_op jit(solution)/shard_map/ppermute | solution.py:208
  70.6 3.6 %collective-permute-done.11 = bf16[4,2,192,128]{3,2,1,0:T(8,128)(2,1)S(1)} collective-permute-done((bf16[4,2,192,128]{3,2,1,0:T(8,128)(2,1)}, bf16[4,2,192,128]{3,2,1,0:T(8,128)(2,1)S(1)}, u32[]{:S(2)}, u32[]{:S(2)}) %collective-permute-start.11) | collective-permute-done | bytes 393248 | tf_op jit(solution)/shard_map/ppermute | solution.py:206
  76.7 3.5 %collective-permute-start.22 = (bf16[2,128,128]{2,1,0:T(8,128)(2,1)S(1)}, bf16[2,128,128]{2,1,0:T(8,128)(2,1)S(1)}, u32[]{:S(2)}, u32[]{:S(2)}) collective-permute-start(bf16[2,128,128]{2,1,0:T(8,128)(2,1)S(1)} %get-tuple-element.37), channel_id=1, source_target_pairs={{0,2},{2,4},{4,6},{6,0},{1,3},{3,5},{5,7},{7,1},{8,10},{10,12},{12... | collective-permute-start | bytes 196616 | tf_op jit(solution)/shard_map/ppermute | solution.py:155
  80.2 2.4 %collective-permute-start.24 = (bf16[2,128,128]{2,1,0:T(8,128)(2,1)S(1)}, bf16[2,128,128]{2,1,0:T(8,128)(2,1)S(1)}, u32[]{:S(2)}, u32[]{:S(2)}) collective-permute-start(bf16[2,128,128]{2,1,0:T(8,128)(2,1)S(1)} %get-tuple-element.35), channel_id=1, source_target_pairs={{0,6},{2,0},{4,2},{6,4},{1,7},{3,1},{5,3},{7,5},{8,14},{10,8},{12,... | collective-permute-start | bytes 196616 | tf_op jit(solution)/shard_map/ppermute | solution.py:155
  87.1 2.0 %collective-permute-done.15 = bf16[2,128,128]{2,1,0:T(8,128)(2,1)S(1)} collective-permute-done((bf16[2,128,128]{2,1,0:T(8,128)(2,1)S(1)}, bf16[2,128,128]{2,1,0:T(8,128)(2,1)S(1)}, u32[]{:S(2)}, u32[]{:S(2)}) %collective-permute-start.15) | collective-permute-done | bytes 65568 | tf_op jit(solution)/shard_map/ppermute | solution.py:155
  89.1 1.5 %collective-permute-done.16 = bf16[2,128,128]{2,1,0:T(8,128)(2,1)S(1)} collective-permute-done((bf16[2,128,128]{2,1,0:T(8,128)(2,1)S(1)}, bf16[2,128,128]{2,1,0:T(8,128)(2,1)S(1)}, u32[]{:S(2)}, u32[]{:S(2)}) %collective-permute-start.16) | collective-permute-done | bytes 65568 | tf_op jit(solution)/shard_map/ppermute | solution.py:155
  (107 shorter events, 18.5 us)
Async XLA Ops:
  10.6 9.5 %collective-permute-start = (bf16[2,128,256]{2,1,0:T(8,128)(2,1)S(1)}, bf16[2,128,256]{2,1,0:T(8,128)(2,1)S(1)}, u32[]{:S(2)}, u32[]{:S(2)}) collective-permute-start(bf16[2,128,256]{2,1,0:T(8,128)(2,1)S(1)} %bitcast.84), channel_id=1, source_target_pairs={{0,2},{2,4},{4,6},{6,0},{1,3},{3,5},{5,7},{7,1},{8,10},{10,12},{12... | collective-permute-start | bytes 393224 | tf_op jit(solution)/shard_map/ppermute | solution.py:155
  13.7 11.2 %collective-permute-start.1 = (bf16[2,128,256]{2,1,0:T(8,128)(2,1)S(1)}, bf16[2,128,256]{2,1,0:T(8,128)(2,1)S(1)}, u32[]{:S(2)}, u32[]{:S(2)}) collective-permute-start(bf16[2,128,256]{2,1,0:T(8,128)(2,1)S(1)} %bitcast.85), channel_id=1, source_target_pairs={{0,4},{2,6},{4,0},{6,2},{1,5},{3,7},{5,1},{7,3},{8,12},{10,14},{12... | collective-permute-start | bytes 393224 | tf_op jit(solution)/shard_map/ppermute | solution.py:155
  16.4 8.5 %collective-permute-start.2 = (bf16[2,128,256]{2,1,0:T(8,128)(2,1)S(1)}, bf16[2,128,256]{2,1,0:T(8,128)(2,1)S(1)}, u32[]{:S(2)}, u32[]{:S(2)}) collective-permute-start(bf16[2,128,256]{2,1,0:T(8,128)(2,1)S(1)} %bitcast.86), channel_id=1, source_target_pairs={{0,6},{2,0},{4,2},{6,4},{1,7},{3,1},{5,3},{7,5},{8,14},{10,8},{12,... | collective-permute-start | bytes 393224 | tf_op jit(solution)/shard_map/ppermute | solution.py:155
  25.2 9.2 %collective-permute-start.4 = (bf16[4,2,128,128]{3,2,1,0:T(8,128)(2,1)S(1)}, bf16[4,2,128,128]{3,2,1,0:T(8,128)(2,1)S(1)}, u32[]{:S(2)}, u32[]{:S(2)}) collective-permute-start(bf16[4,2,128,128]{3,2,1,0:T(8,128)(2,1)S(1)} %get-tuple-element.29.refs_0_.refs_5_), channel_id=1, source_target_pairs={{0,16},{8,24},{16,0},{24,8},{1,17},{9,25},{17,1},{25,9},{2,18},{10... | collective-permute-start | bytes 786440 | tf_op jit(solution)/shard_map/ppermute | solution.py:180
  26.8 9.2 %collective-permute-start.3 = (bf16[4,2,128,128]{3,2,1,0:T(8,128)(2,1)S(1)}, bf16[4,2,128,128]{3,2,1,0:T(8,128)(2,1)S(1)}, u32[]{:S(2)}, u32[]{:S(2)}) collective-permute-start(bf16[4,2,128,128]{3,2,1,0:T(8,128)(2,1)S(1)} %get-tuple-element.29.refs_0_.refs_5_), channel_id=1, source_target_pairs={{0,8},{8,0},{16,24},{24,16},{1,9},{9,1},{17,25},{25,17},{2,10},{10... | collective-permute-start | bytes 786440 | tf_op jit(solution)/shard_map/ppermute | solution.py:179
  28.3 13.3 %collective-permute-start.7 = (bf16[4,2,128,128]{3,2,1,0:T(8,128)(2,1)S(1)}, bf16[4,2,128,128]{3,2,1,0:T(8,128)(2,1)S(1)}, u32[]{:S(2)}, u32[]{:S(2)}) collective-permute-start(bf16[4,2,128,128]{3,2,1,0:T(8,128)(2,1)S(1)} %get-tuple-element.28.refs_0_.refs_5_), channel_id=1, source_target_pairs={{0,8},{8,0},{16,24},{24,16},{1,9},{9,1},{17,25},{25,17},{2,10},{10... | collective-permute-start | bytes 786440 | tf_op jit(solution)/shard_map/ppermute | solution.py:179
  28.8 13.4 %collective-permute-start.8 = (bf16[4,2,128,128]{3,2,1,0:T(8,128)(2,1)S(1)}, bf16[4,2,128,128]{3,2,1,0:T(8,128)(2,1)S(1)}, u32[]{:S(2)}, u32[]{:S(2)}) collective-permute-start(bf16[4,2,128,128]{3,2,1,0:T(8,128)(2,1)S(1)} %get-tuple-element.28.refs_0_.refs_5_), channel_id=1, source_target_pairs={{0,16},{8,24},{16,0},{24,8},{1,17},{9,25},{17,1},{25,9},{2,18},{10... | collective-permute-start | bytes 786440 | tf_op jit(solution)/shard_map/ppermute | solution.py:180
  34.5 10.7 %collective-permute-start.5 = (bf16[4,2,64,128]{3,2,1,0:T(8,128)(2,1)S(1)}, bf16[4,2,64,128]{3,2,1,0:T(8,128)(2,1)S(1)}, u32[]{:S(2)}, u32[]{:S(2)}) collective-permute-start(bf16[4,2,64,128]{3,2,1,0:T(8,128)(2,1)S(1)} %slice.89), channel_id=1, source_target_pairs={{0,8},{8,0},{16,24},{24,16},{1,9},{9,1},{17,25},{25,17},{2,10},{10... | collective-permute-start | bytes 393224 | tf_op jit(solution)/shard_map/ppermute | solution.py:182
  36.0 9.1 %collective-permute-start.6 = (bf16[4,2,64,128]{3,2,1,0:T(8,128)(2,1)S(1)}, bf16[4,2,64,128]{3,2,1,0:T(8,128)(2,1)S(1)}, u32[]{:S(2)}, u32[]{:S(2)}) collective-permute-start(bf16[4,2,64,128]{3,2,1,0:T(8,128)(2,1)S(1)} %slice.90), channel_id=1, source_target_pairs={{0,16},{8,24},{16,0},{24,8},{1,17},{9,25},{17,1},{25,9},{2,18},{10... | collective-permute-start | bytes 393224 | tf_op jit(solution)/shard_map/ppermute | solution.py:183
  41.6 13.7 %collective-permute-start.10 = (bf16[4,2,64,128]{3,2,1,0:T(8,128)(2,1)S(1)}, bf16[4,2,64,128]{3,2,1,0:T(8,128)(2,1)S(1)}, u32[]{:S(2)}, u32[]{:S(2)}) collective-permute-start(bf16[4,2,64,128]{3,2,1,0:T(8,128)(2,1)S(1)} %slice.93), channel_id=1, source_target_pairs={{0,16},{8,24},{16,0},{24,8},{1,17},{9,25},{17,1},{25,9},{2,18},{10... | collective-permute-start | bytes 393224 | tf_op jit(solution)/shard_map/ppermute | solution.py:183
  42.3 13.0 %collective-permute-start.9 = (bf16[4,2,64,128]{3,2,1,0:T(8,128)(2,1)S(1)}, bf16[4,2,64,128]{3,2,1,0:T(8,128)(2,1)S(1)}, u32[]{:S(2)}, u32[]{:S(2)}) collective-permute-start(bf16[4,2,64,128]{3,2,1,0:T(8,128)(2,1)S(1)} %slice.92), channel_id=1, source_target_pairs={{0,8},{8,0},{16,24},{24,16},{1,9},{9,1},{17,25},{25,17},{2,10},{10... | collective-permute-start | bytes 393224 | tf_op jit(solution)/shard_map/ppermute | solution.py:182
  53.2 14.4 %collective-permute-start.18 = (bf16[4,2,192,128]{3,2,1,0:T(8,128)(2,1)}, bf16[4,2,192,128]{3,2,1,0:T(8,128)(2,1)S(1)}, u32[]{:S(2)}, u32[]{:S(2)}) collective-permute-start(bf16[4,2,192,128]{3,2,1,0:T(8,128)(2,1)} %get-tuple-element.26), channel_id=1, source_target_pairs={{0,8},{8,0},{16,24},{24,16},{1,9},{9,1},{17,25},{25,17},{2,10},{10... | collective-permute-start | bytes 1179656 | tf_op jit(solution)/shard_map/ppermute | solution.py:206
  53.8 15.3 %collective-permute-start.19 = (bf16[4,2,192,128]{3,2,1,0:T(8,128)(2,1)}, bf16[4,2,192,128]{3,2,1,0:T(8,128)(2,1)S(1)}, u32[]{:S(2)}, u32[]{:S(2)}) collective-permute-start(bf16[4,2,192,128]{3,2,1,0:T(8,128)(2,1)} %get-tuple-element.27), channel_id=1, source_target_pairs={{0,16},{8,24},{16,0},{24,8},{1,17},{9,25},{17,1},{25,9},{2,18},{10... | collective-permute-start | bytes 1179656 | tf_op jit(solution)/shard_map/ppermute | solution.py:207
  63.5 10.7 %collective-permute-start.11 = (bf16[4,2,192,128]{3,2,1,0:T(8,128)(2,1)}, bf16[4,2,192,128]{3,2,1,0:T(8,128)(2,1)S(1)}, u32[]{:S(2)}, u32[]{:S(2)}) collective-permute-start(bf16[4,2,192,128]{3,2,1,0:T(8,128)(2,1)} %get-tuple-element.23), channel_id=1, source_target_pairs={{0,8},{8,0},{16,24},{24,16},{1,9},{9,1},{17,25},{25,17},{2,10},{10... | collective-permute-start | bytes 1179656 | tf_op jit(solution)/shard_map/ppermute | solution.py:206
  65.1 10.2 %collective-permute-start.12 = (bf16[4,2,192,128]{3,2,1,0:T(8,128)(2,1)}, bf16[4,2,192,128]{3,2,1,0:T(8,128)(2,1)S(1)}, u32[]{:S(2)}, u32[]{:S(2)}) collective-permute-start(bf16[4,2,192,128]{3,2,1,0:T(8,128)(2,1)} %get-tuple-element.24), channel_id=1, source_target_pairs={{0,16},{8,24},{16,0},{24,8},{1,17},{9,25},{17,1},{25,9},{2,18},{10... | collective-permute-start | bytes 1179656 | tf_op jit(solution)/shard_map/ppermute | solution.py:207
  67.6 8.9 %collective-permute-start.20 = (bf16[4,2,64,128]{3,2,1,0:T(8,128)(2,1)S(1)}, bf16[4,2,64,128]{3,2,1,0:T(8,128)(2,1)S(1)}, u32[]{:S(2)}, u32[]{:S(2)}) collective-permute-start(bf16[4,2,64,128]{3,2,1,0:T(8,128)(2,1)S(1)} %slice.104), channel_id=1, source_target_pairs={{0,16},{8,24},{16,0},{24,8},{1,17},{9,25},{17,1},{25,9},{2,18},{10... | collective-permute-start | bytes 393224 | tf_op jit(solution)/shard_map/ppermute | solution.py:208
  69.2 7.3 %collective-permute-start.21 = (bf16[4,2,64,128]{3,2,1,0:T(8,128)(2,1)S(1)}, bf16[4,2,64,128]{3,2,1,0:T(8,128)(2,1)S(1)}, u32[]{:S(2)}, u32[]{:S(2)}) collective-permute-start(bf16[4,2,64,128]{3,2,1,0:T(8,128)(2,1)S(1)} %slice.105), channel_id=1, source_target_pairs={{0,8},{8,0},{16,24},{24,16},{1,9},{9,1},{17,25},{25,17},{2,10},{10... | collective-permute-start | bytes 393224 | tf_op jit(solution)/shard_map/ppermute | solution.py:209
  74.3 8.4 %collective-permute-start.13 = (bf16[4,2,64,128]{3,2,1,0:T(8,128)(2,1)S(1)}, bf16[4,2,64,128]{3,2,1,0:T(8,128)(2,1)S(1)}, u32[]{:S(2)}, u32[]{:S(2)}) collective-permute-start(bf16[4,2,64,128]{3,2,1,0:T(8,128)(2,1)S(1)} %slice.96), channel_id=1, source_target_pairs={{0,16},{8,24},{16,0},{24,8},{1,17},{9,25},{17,1},{25,9},{2,18},{10... | collective-permute-start | bytes 393224 | tf_op jit(solution)/shard_map/ppermute | solution.py:208
  75.3 7.3 %collective-permute-start.14 = (bf16[4,2,64,128]{3,2,1,0:T(8,128)(2,1)S(1)}, bf16[4,2,64,128]{3,2,1,0:T(8,128)(2,1)S(1)}, u32[]{:S(2)}, u32[]{:S(2)}) collective-permute-start(bf16[4,2,64,128]{3,2,1,0:T(8,128)(2,1)S(1)} %slice.97), channel_id=1, source_target_pairs={{0,8},{8,0},{16,24},{24,16},{1,9},{9,1},{17,25},{25,17},{2,10},{10... | collective-permute-start | bytes 393224 | tf_op jit(solution)/shard_map/ppermute | solution.py:209
  76.7 8.9 %collective-permute-start.22 = (bf16[2,128,128]{2,1,0:T(8,128)(2,1)S(1)}, bf16[2,128,128]{2,1,0:T(8,128)(2,1)S(1)}, u32[]{:S(2)}, u32[]{:S(2)}) collective-permute-start(bf16[2,128,128]{2,1,0:T(8,128)(2,1)S(1)} %get-tuple-element.37), channel_id=1, source_target_pairs={{0,2},{2,4},{4,6},{6,0},{1,3},{3,5},{5,7},{7,1},{8,10},{10,12},{12... | collective-permute-start | bytes 196616 | tf_op jit(solution)/shard_map/ppermute | solution.py:155
  80.2 6.8 %collective-permute-start.23 = (bf16[2,128,128]{2,1,0:T(8,128)(2,1)S(1)}, bf16[2,128,128]{2,1,0:T(8,128)(2,1)S(1)}, u32[]{:S(2)}, u32[]{:S(2)}) collective-permute-start(bf16[2,128,128]{2,1,0:T(8,128)(2,1)S(1)} %get-tuple-element.36), channel_id=1, source_target_pairs={{0,4},{2,6},{4,0},{6,2},{1,5},{3,7},{5,1},{7,3},{8,12},{10,14},{12... | collective-permute-start | bytes 196616 | tf_op jit(solution)/shard_map/ppermute | solution.py:155
  80.2 6.8 %collective-permute-start.24 = (bf16[2,128,128]{2,1,0:T(8,128)(2,1)S(1)}, bf16[2,128,128]{2,1,0:T(8,128)(2,1)S(1)}, u32[]{:S(2)}, u32[]{:S(2)}) collective-permute-start(bf16[2,128,128]{2,1,0:T(8,128)(2,1)S(1)} %get-tuple-element.35), channel_id=1, source_target_pairs={{0,6},{2,0},{4,2},{6,4},{1,7},{3,1},{5,3},{7,5},{8,14},{10,8},{12,... | collective-permute-start | bytes 196616 | tf_op jit(solution)/shard_map/ppermute | solution.py:155
  82.9 6.2 %collective-permute-start.15 = (bf16[2,128,128]{2,1,0:T(8,128)(2,1)S(1)}, bf16[2,128,128]{2,1,0:T(8,128)(2,1)S(1)}, u32[]{:S(2)}, u32[]{:S(2)}) collective-permute-start(bf16[2,128,128]{2,1,0:T(8,128)(2,1)S(1)} %get-tuple-element.33), channel_id=1, source_target_pairs={{0,2},{2,4},{4,6},{6,0},{1,3},{3,5},{5,7},{7,1},{8,10},{10,12},{12... | collective-permute-start | bytes 196616 | tf_op jit(solution)/shard_map/ppermute | solution.py:155
  84.2 6.4 %collective-permute-start.16 = (bf16[2,128,128]{2,1,0:T(8,128)(2,1)S(1)}, bf16[2,128,128]{2,1,0:T(8,128)(2,1)S(1)}, u32[]{:S(2)}, u32[]{:S(2)}) collective-permute-start(bf16[2,128,128]{2,1,0:T(8,128)(2,1)S(1)} %get-tuple-element.32), channel_id=1, source_target_pairs={{0,4},{2,6},{4,0},{6,2},{1,5},{3,7},{5,1},{7,3},{8,12},{10,14},{12... | collective-permute-start | bytes 196616 | tf_op jit(solution)/shard_map/ppermute | solution.py:155
  (19 other events, 105.3 us)

commit v11 on v8

--- a/solution.py
+++ b/solution.py
@@ -213,18 +213,16 @@
     return total.astype(jnp.bfloat16)
 
 
-def pair_reduce(totals, pair_prompt, n_prompts):
+def pair_exchange(totals):
+    n = lax.axis_size("pair")
+    return [totals[0]] + [ring_shift(totals[(n - d) % n], "pair", n, d) for d in range(1, n)]
+
+
+def prompt_weights(pair_prompt, n_prompts):
     n = lax.axis_size("pair")
     r = lax.axis_index("pair")
-    out = None
-    for d in range(n):
-        chunk = totals[(n - d) % n]
-        got = chunk if d == 0 else ring_shift(chunk, "pair", n, d)
-        source = (r - d) % n
-        hits = (pair_prompt[source] == jnp.arange(n_prompts, dtype=jnp.int32)).astype(jnp.float32)
-        term = hits[:, None, None, None] * jnp.transpose(got.astype(jnp.float32), (1, 0, 2))[None]
-        out = term if out is None else out + term
-    return out
+    source = jnp.take(pair_prompt, (r - jnp.arange(n)) % n, mode="clip")
+    return (source[:, None] == jnp.arange(n_prompts, dtype=jnp.int32)[None, :]).astype(jnp.float32)
 
 
 def in_group(width, kv_heads, chunk_heads, group_heads, k):
@@ -259,9 +257,13 @@
         else:
             earlier = tuple(jnp.where(in_group(o.shape[1], kv_heads, chunk_heads, group_heads, k), o, e)
                             for o, e in zip(outs[:3], earlier))
-        parts.append(ctx_reduce(list(outs[3:])))
+        parts.append(pair_exchange(ctx_reduce(list(outs[3:]))))
     dq, dkr, dvr = earlier
-    d_prefix = pair_reduce(parts[0] if n_groups == 1 else jnp.concatenate(parts, -1), pair_prompt, n_prompts)
+    weights = prompt_weights(pair_prompt, n_prompts)
+    d_prefix = jnp.concatenate([
+        sum(weights[d][:, None, None, None] * jnp.transpose(got.astype(jnp.float32), (1, 0, 2))[None]
+            for d, got in enumerate(part))
+        for part in parts], -1)
     return (dq[None, None], dkr[None, None], dvr[None, None], d_prefix)
 
 

time: 92.6 us -> 88.4 us (0.955)
  waiting for transfers between devices: 21.3 us -> 10.9 us
  starting transfers between devices: 34.2 us -> 41.8 us
  other arithmetic: 7.64 us -> 5.6 us
    ppermute x2, waiting for transfers between devices: 3.7 us -> 0.01 us  [ctx_gather(): far_a = lax.ppermute(from_y[:, :, :half], 'ctx', along_x)]
    ppermute x9 -> x12, waiting for transfers between devices: 8.13 us -> 4.54 us  [ring_shift(): return lax.ppermute(x, axis, [(i, (i + d) % n) for i in range(n)])]
    ppermute x9 -> x12, starting transfers between devices: 17.4 us -> 20.5 us  [ring_shift(): return lax.ppermute(x, axis, [(i, (i + d) % n) for i in range(n)])]
    ppermute x2, waiting for transfers between devices: 3.08 us -> 0.01 us  [ctx_reduce(): far_a = lax.ppermute(got_x[:, :, rows:], 'ctx', along_y)]
    ppermute x2, waiting for transfers between devices: 0.67 us -> 3.19 us  [ctx_gather(): from_y = lax.ppermute(x, 'ctx', along_y)]
    convert_element_type x2 -> x1, other arithmetic: 2.43 us -> 0.07 us  [prompt_weights(): (source[:, None] == jnp.arange(n_prompts, dtype=jnp.int32)[None, :]).asty...]
    ppermute x2, waiting for transfers between devices: 1.87 us -> 0.01 us  [ctx_gather(): far_b = lax.ppermute(from_x[:, :, half:], 'ctx', along_y)]
    ppermute x2, starting transfers between devices: 2.2 us -> 3.39 us  [ctx_gather(): from_y = lax.ppermute(x, 'ctx', along_y)]
  transfers between devices with their start and end apart: 25 -> 28, of which waited for: 14 -> 5; matrix products, arithmetic and copies ran while one was open for 7% -> 6% of each run, Pallas kernels for 16% -> 17%
where the time goes in v11:
time: 88.4 us; the launch traced here: 88 us
  starting transfers between devices  41.8 us (47%)
  Pallas kernels  14.9 us (17%)
  waiting for transfers between devices  10.9 us (12%)
  between operations  9.52 us (11%)
  other arithmetic  5.6 us (6%)
  local copies, waits for them, and re-layouts  5.27 us (6%)
    ppermute x12, starting transfers between devices, ring_shift(): return lax.ppermute(x, axis, [(i, (i + d) % n) for i in range(n)])  20.5 us
    pallas_call x2, Pallas kernels, attention_grads(): pl.pallas_call(functools.partial(attention_grad_kernel, layout), out_shap...  14.9 us
    ppermute x12, waiting for transfers between devices, ring_shift(): return lax.ppermute(x, axis, [(i, (i + d) % n) for i in range(n)])  4.54 us
    ppermute x2, starting transfers between devices, ctx_gather(): from_y = lax.ppermute(x, 'ctx', along_y)  3.39 us
    ppermute x2, waiting for transfers between devices, ctx_gather(): from_y = lax.ppermute(x, 'ctx', along_y)  3.19 us
    ppermute x2, starting transfers between devices, ctx_gather(): far_b = lax.ppermute(from_x[:, :, half:], 'ctx', along_y)  3.17 us
    ppermute x2, waiting for transfers between devices, ctx_reduce(): got_x = lax.ppermute(send_x, 'ctx', along_x)  3.15 us
    unnamed x37, local copies, waits for them, and re-layouts  3.04 us
  transfers between devices with their start and end apart: 28, of which 5 were waited for; matrix products, arithmetic and copies ran while one was open for 6% of the time, Pallas kernels for 17%

profile of v11, /device:TPU:0, one launch (start us, length us, event | category | flops | bytes accessed | tf_op | source)
XLA Modules:
  0.0 88.0 jit_solution(1726416846094064091)
XLA Ops:
  10.8 3.1 %collective-permute-start = (bf16[2,128,128]{2,1,0:T(8,128)(2,1)S(1)}, bf16[2,128,128]{2,1,0:T(8,128)(2,1)S(1)}, u32[]{:S(2)}, u32[]{:S(2)}) collective-permute-start(bf16[2,128,128]{2,1,0:T(8,128)(2,1)S(1)} %get-tuple-element.45), channel_id=1, source_target_pairs={{0,2},{2,4},{4,6},{6,0},{1,3},{3,5},{5,7},{7,1},{8,10},{10,12},{12... | collective-permute-start | bytes 196616 | tf_op jit(solution)/shard_map/ppermute | solution.py:155
  13.9 2.6 %collective-permute-start.1 = (bf16[2,128,128]{2,1,0:T(8,128)(2,1)S(1)}, bf16[2,128,128]{2,1,0:T(8,128)(2,1)S(1)}, u32[]{:S(2)}, u32[]{:S(2)}) collective-permute-start(bf16[2,128,128]{2,1,0:T(8,128)(2,1)S(1)} %get-tuple-element.44), channel_id=1, source_target_pairs={{0,4},{2,6},{4,0},{6,2},{1,5},{3,7},{5,1},{7,3},{8,12},{10,14},{12... | collective-permute-start | bytes 196616 | tf_op jit(solution)/shard_map/ppermute | solution.py:155
  19.6 2.8 %collective-permute-start.9 = (bf16[2,128,128]{2,1,0:T(8,128)(2,1)S(1)}, bf16[2,128,128]{2,1,0:T(8,128)(2,1)S(1)}, u32[]{:S(2)}, u32[]{:S(2)}) collective-permute-start(bf16[2,128,128]{2,1,0:T(8,128)(2,1)S(1)} %get-tuple-element.39), channel_id=1, source_target_pairs={{0,6},{2,0},{4,2},{6,4},{1,7},{3,1},{5,3},{7,5},{8,14},{10,8},{12,... | collective-permute-start | bytes 196616 | tf_op jit(solution)/shard_map/ppermute | solution.py:155
  22.5 1.6 %collective-permute-start.4 = (bf16[4,2,128,128]{3,2,1,0:T(8,128)(2,1)S(1)}, bf16[4,2,128,128]{3,2,1,0:T(8,128)(2,1)S(1)}, u32[]{:S(2)}, u32[]{:S(2)}) collective-permute-start(bf16[4,2,128,128]{3,2,1,0:T(8,128)(2,1)S(1)} %pad_maximum_fusion.1.refs_0_.refs_5_), channel_id=1, source_target_pairs={{0,16},{8,24},{16,0},{24,8},{1,17},{9,25},{17,1},{25,9},{2,18},{10... | collective-permute-start | bytes 786440 | tf_op jit(solution)/shard_map/ppermute | solution.py:180
  24.1 1.5 %collective-permute-start.3 = (bf16[4,2,128,128]{3,2,1,0:T(8,128)(2,1)S(1)}, bf16[4,2,128,128]{3,2,1,0:T(8,128)(2,1)S(1)}, u32[]{:S(2)}, u32[]{:S(2)}) collective-permute-start(bf16[4,2,128,128]{3,2,1,0:T(8,128)(2,1)S(1)} %pad_maximum_fusion.1.refs_0_.refs_5_), channel_id=1, source_target_pairs={{0,8},{8,0},{16,24},{24,16},{1,9},{9,1},{17,25},{25,17},{2,10},{10... | collective-permute-start | bytes 786440 | tf_op jit(solution)/shard_map/ppermute | solution.py:179
  26.7 1.8 %collective-permute-start.11 = (bf16[4,2,128,128]{3,2,1,0:T(8,128)(2,1)S(1)}, bf16[4,2,128,128]{3,2,1,0:T(8,128)(2,1)S(1)}, u32[]{:S(2)}, u32[]{:S(2)}) collective-permute-start(bf16[4,2,128,128]{3,2,1,0:T(8,128)(2,1)S(1)} %pad_maximum_fusion.2.refs_0_.refs_5_), channel_id=1, source_target_pairs={{0,16},{8,24},{16,0},{24,8},{1,17},{9,25},{17,1},{25,9},{2,18},{10... | collective-permute-start | bytes 786440 | tf_op jit(solution)/shard_map/ppermute | solution.py:180
  28.5 1.5 %collective-permute-start.10 = (bf16[4,2,128,128]{3,2,1,0:T(8,128)(2,1)S(1)}, bf16[4,2,128,128]{3,2,1,0:T(8,128)(2,1)S(1)}, u32[]{:S(2)}, u32[]{:S(2)}) collective-permute-start(bf16[4,2,128,128]{3,2,1,0:T(8,128)(2,1)S(1)} %pad_maximum_fusion.2.refs_0_.refs_5_), channel_id=1, source_target_pairs={{0,8},{8,0},{16,24},{24,16},{1,9},{9,1},{17,25},{25,17},{2,10},{10... | collective-permute-start | bytes 786440 | tf_op jit(solution)/shard_map/ppermute | solution.py:179
  31.2 1.6 %collective-permute-start.6 = (bf16[4,2,64,128]{3,2,1,0:T(8,128)(2,1)S(1)}, bf16[4,2,64,128]{3,2,1,0:T(8,128)(2,1)S(1)}, u32[]{:S(2)}, u32[]{:S(2)}) collective-permute-start(bf16[4,2,64,128]{3,2,1,0:T(8,128)(2,1)S(1)} %slice.112), channel_id=1, source_target_pairs={{0,16},{8,24},{16,0},{24,8},{1,17},{9,25},{17,1},{25,9},{2,18},{10... | collective-permute-start | bytes 393224 | tf_op jit(solution)/shard_map/ppermute | solution.py:183
  32.8 3.2 %collective-permute-done.11.refs_2_.refs_7_ = bf16[4,2,128,128]{3,2,1,0:T(8,128)(2,1)S(1)} collective-permute-done((bf16[4,2,128,128]{3,2,1,0:T(8,128)(2,1)S(1)}, bf16[4,2,128,128]{3,2,1,0:T(8,128)(2,1)S(1)}, u32[]{:S(2)}, u32[]{:S(2)}) %collective-permute-start.11) | collective-permute-done | bytes 262176 | tf_op jit(solution)/shard_map/ppermute | solution.py:180
  36.0 1.8 %collective-permute-start.12 = (bf16[4,2,64,128]{3,2,1,0:T(8,128)(2,1)S(1)}, bf16[4,2,64,128]{3,2,1,0:T(8,128)(2,1)S(1)}, u32[]{:S(2)}, u32[]{:S(2)}) collective-permute-start(bf16[4,2,64,128]{3,2,1,0:T(8,128)(2,1)S(1)} %slice.114), channel_id=1, source_target_pairs={{0,8},{8,0},{16,24},{24,16},{1,9},{9,1},{17,25},{25,17},{2,10},{10... | collective-permute-start | bytes 393224 | tf_op jit(solution)/shard_map/ppermute | solution.py:182
  37.8 1.6 %collective-permute-start.13 = (bf16[4,2,64,128]{3,2,1,0:T(8,128)(2,1)S(1)}, bf16[4,2,64,128]{3,2,1,0:T(8,128)(2,1)S(1)}, u32[]{:S(2)}, u32[]{:S(2)}) collective-permute-start(bf16[4,2,64,128]{3,2,1,0:T(8,128)(2,1)S(1)} %slice.115), channel_id=1, source_target_pairs={{0,16},{8,24},{16,0},{24,8},{1,17},{9,25},{17,1},{25,9},{2,18},{10... | collective-permute-start | bytes 393224 | tf_op jit(solution)/shard_map/ppermute | solution.py:183
  41.4 7.4 %shard_map.111 = (bf16[128,2048]{1,0:T(8,128)(2,1)}, bf16[128,1024]{1,0:T(8,128)(2,1)}, bf16[128,1024]{1,0:T(8,128)(2,1)}, bf16[4,2,128,128]{3,2,1,0:T(8,128)(2,...) custom-call(s32[4]{0:T(128)} %bitcast.104, s32[1]{0:T(128)} %bitcast.87.length_ref, ...), custom_call_target="tpu_custom_call" | custom-call | flops 1006632960 | bytes 3670016 | tf_op jit(solution)/shard_map/pallas_call | solution.py:136
  51.5 7.5 %shard_map.112 = (bf16[128,2048]{1,0:T(8,128)(2,1)}, bf16[128,1024]{1,0:T(8,128)(2,1)}, bf16[128,1024]{1,0:T(8,128)(2,1)}, bf16[4,2,128,128]{3,2,1,0:T(8,128)(2,...) custom-call(s32[4]{0:T(128)} %bitcast.105, s32[1]{0:T(128)} %bitcast.88.length_ref, ...), custom_call_target="tpu_custom_call" | custom-call | flops 1006632960 | bytes 3670016 | tf_op jit(solution)/shard_map/pallas_call | solution.py:136
  59.7 1.5 %collective-permute-start.15 = (bf16[4,2,192,128]{3,2,1,0:T(8,128)(2,1)}, bf16[4,2,192,128]{3,2,1,0:T(8,128)(2,1)S(1)}, u32[]{:S(2)}, u32[]{:S(2)}) collective-permute-start(bf16[4,2,192,128]{3,2,1,0:T(8,128)(2,1)} %get-tuple-element.24), channel_id=1, source_target_pairs={{0,16},{8,24},{16,0},{24,8},{1,17},{9,25},{17,1},{25,9},{2,18},{10... | collective-permute-start | bytes 1179656 | tf_op jit(solution)/shard_map/ppermute | solution.py:207
  61.2 1.9 %select_bitcast_fusion = bf16[1,1,128,2048]{3,2,1,0:T(8,128)(2,1)} fusion(bf16[128,2048]{1,0:T(8,128)(2,1)S(1)} %copy-done.1, bf16[128,2048]{1,0:T(8,128)(2,1)} %get-tuple-element.17, pred[2048]{0:T(1024)(128)(4,1)S(1)} %fusion.1), kind=kLoop, calls=%fused_computation.4 | loop fusion | flops 262144 | bytes 1574912 | tf_op jit(solution)/shard_map/broadcast_in_dim | solution.py:267
  63.8 1.5 %collective-permute-start.24 = (bf16[4,2,64,128]{3,2,1,0:T(8,128)(2,1)S(1)}, bf16[4,2,64,128]{3,2,1,0:T(8,128)(2,1)S(1)}, u32[]{:S(2)}, u32[]{:S(2)}) collective-permute-start(bf16[4,2,64,128]{3,2,1,0:T(8,128)(2,1)S(1)} %slice.127), channel_id=1, source_target_pairs={{0,8},{8,0},{16,24},{24,16},{1,9},{9,1},{17,25},{25,17},{2,10},{10... | collective-permute-start | bytes 393224 | tf_op jit(solution)/shard_map/ppermute | solution.py:209
  66.1 3.2 %collective-permute-done.14 = bf16[4,2,192,128]{3,2,1,0:T(8,128)(2,1)S(1)} collective-permute-done((bf16[4,2,192,128]{3,2,1,0:T(8,128)(2,1)}, bf16[4,2,192,128]{3,2,1,0:T(8,128)(2,1)S(1)}, u32[]{:S(2)}, u32[]{:S(2)}) %collective-permute-start.14) | collective-permute-done | bytes 393248 | tf_op jit(solution)/shard_map/ppermute | solution.py:206
  69.3 1.6 %collective-permute-start.16 = (bf16[4,2,64,128]{3,2,1,0:T(8,128)(2,1)S(1)}, bf16[4,2,64,128]{3,2,1,0:T(8,128)(2,1)S(1)}, u32[]{:S(2)}, u32[]{:S(2)}) collective-permute-start(bf16[4,2,64,128]{3,2,1,0:T(8,128)(2,1)S(1)} %slice.118), channel_id=1, source_target_pairs={{0,16},{8,24},{16,0},{24,8},{1,17},{9,25},{17,1},{25,9},{2,18},{10... | collective-permute-start | bytes 393224 | tf_op jit(solution)/shard_map/ppermute | solution.py:208
  72.1 3.2 %collective-permute-start.25 = (bf16[2,128,128]{2,1,0:T(8,128)(2,1)S(1)}, bf16[2,128,128]{2,1,0:T(8,128)(2,1)S(1)}, u32[]{:S(2)}, u32[]{:S(2)}) collective-permute-start(bf16[2,128,128]{2,1,0:T(8,128)(2,1)S(1)} %get-tuple-element.35), channel_id=1, source_target_pairs={{0,2},{2,4},{4,6},{6,0},{1,3},{3,5},{5,7},{7,1},{8,10},{10,12},{12... | collective-permute-start | bytes 196616 | tf_op jit(solution)/shard_map/ppermute | solution.py:155
  76.0 1.8 %collective-permute-start.27 = (bf16[2,128,128]{2,1,0:T(8,128)(2,1)S(1)}, bf16[2,128,128]{2,1,0:T(8,128)(2,1)S(1)}, u32[]{:S(2)}, u32[]{:S(2)}) collective-permute-start(bf16[2,128,128]{2,1,0:T(8,128)(2,1)S(1)} %get-tuple-element.33), channel_id=1, source_target_pairs={{0,6},{2,0},{4,2},{6,4},{1,7},{3,1},{5,3},{7,5},{8,14},{10,8},{12,... | collective-permute-start | bytes 196616 | tf_op jit(solution)/shard_map/ppermute | solution.py:155
  78.1 1.4 %collective-permute-start.18 = (bf16[2,128,128]{2,1,0:T(8,128)(2,1)S(1)}, bf16[2,128,128]{2,1,0:T(8,128)(2,1)S(1)}, u32[]{:S(2)}, u32[]{:S(2)}) collective-permute-start(bf16[2,128,128]{2,1,0:T(8,128)(2,1)S(1)} %get-tuple-element.31), channel_id=1, source_target_pairs={{0,2},{2,4},{4,6},{6,0},{1,3},{3,5},{5,7},{7,1},{8,10},{10,12},{12... | collective-permute-start | bytes 196616 | tf_op jit(solution)/shard_map/ppermute | solution.py:155
  80.7 1.4 %collective-permute-start.20 = (bf16[2,128,128]{2,1,0:T(8,128)(2,1)S(1)}, bf16[2,128,128]{2,1,0:T(8,128)(2,1)S(1)}, u32[]{:S(2)}, u32[]{:S(2)}) collective-permute-start(bf16[2,128,128]{2,1,0:T(8,128)(2,1)S(1)} %get-tuple-element.29), channel_id=1, source_target_pairs={{0,6},{2,0},{4,2},{6,4},{1,7},{3,1},{5,3},{7,5},{8,14},{10,8},{12,... | collective-permute-start | bytes 196616 | tf_op jit(solution)/shard_map/ppermute | solution.py:155
  82.2 2.0 %collective-permute-done.18 = bf16[2,128,128]{2,1,0:T(8,128)(2,1)S(1)} collective-permute-done((bf16[2,128,128]{2,1,0:T(8,128)(2,1)S(1)}, bf16[2,128,128]{2,1,0:T(8,128)(2,1)S(1)}, u32[]{:S(2)}, u32[]{:S(2)}) %collective-permute-start.18) | collective-permute-done | bytes 65568 | tf_op jit(solution)/shard_map/ppermute | solution.py:155
  84.2 1.5 %collective-permute-done.19 = bf16[2,128,128]{2,1,0:T(8,128)(2,1)S(1)} collective-permute-done((bf16[2,128,128]{2,1,0:T(8,128)(2,1)S(1)}, bf16[2,128,128]{2,1,0:T(8,128)(2,1)S(1)}, u32[]{:S(2)}, u32[]{:S(2)}) %collective-permute-start.19) | collective-permute-done | bytes 65568 | tf_op jit(solution)/shard_map/ppermute | solution.py:155
  (115 shorter events, 19.6 us)
Async XLA Ops:
  10.8 8.8 %collective-permute-start = (bf16[2,128,128]{2,1,0:T(8,128)(2,1)S(1)}, bf16[2,128,128]{2,1,0:T(8,128)(2,1)S(1)}, u32[]{:S(2)}, u32[]{:S(2)}) collective-permute-start(bf16[2,128,128]{2,1,0:T(8,128)(2,1)S(1)} %get-tuple-element.45), channel_id=1, source_target_pairs={{0,2},{2,4},{4,6},{6,0},{1,3},{3,5},{5,7},{7,1},{8,10},{10,12},{12... | collective-permute-start | bytes 196616 | tf_op jit(solution)/shard_map/ppermute | solution.py:155
  13.9 8.6 %collective-permute-start.1 = (bf16[2,128,128]{2,1,0:T(8,128)(2,1)S(1)}, bf16[2,128,128]{2,1,0:T(8,128)(2,1)S(1)}, u32[]{:S(2)}, u32[]{:S(2)}) collective-permute-start(bf16[2,128,128]{2,1,0:T(8,128)(2,1)S(1)} %get-tuple-element.44), channel_id=1, source_target_pairs={{0,4},{2,6},{4,0},{6,2},{1,5},{3,7},{5,1},{7,3},{8,12},{10,14},{12... | collective-permute-start | bytes 196616 | tf_op jit(solution)/shard_map/ppermute | solution.py:155
  17.8 7.8 %collective-permute-start.7 = (bf16[2,128,128]{2,1,0:T(8,128)(2,1)S(1)}, bf16[2,128,128]{2,1,0:T(8,128)(2,1)S(1)}, u32[]{:S(2)}, u32[]{:S(2)}) collective-permute-start(bf16[2,128,128]{2,1,0:T(8,128)(2,1)S(1)} %get-tuple-element.41), channel_id=1, source_target_pairs={{0,2},{2,4},{4,6},{6,0},{1,3},{3,5},{5,7},{7,1},{8,10},{10,12},{12... | collective-permute-start | bytes 196616 | tf_op jit(solution)/shard_map/ppermute | solution.py:155
  18.5 8.0 %collective-permute-start.8 = (bf16[2,128,128]{2,1,0:T(8,128)(2,1)S(1)}, bf16[2,128,128]{2,1,0:T(8,128)(2,1)S(1)}, u32[]{:S(2)}, u32[]{:S(2)}) collective-permute-start(bf16[2,128,128]{2,1,0:T(8,128)(2,1)S(1)} %get-tuple-element.40), channel_id=1, source_target_pairs={{0,4},{2,6},{4,0},{6,2},{1,5},{3,7},{5,1},{7,3},{8,12},{10,14},{12... | collective-permute-start | bytes 196616 | tf_op jit(solution)/shard_map/ppermute | solution.py:155
  19.6 7.0 %collective-permute-start.9 = (bf16[2,128,128]{2,1,0:T(8,128)(2,1)S(1)}, bf16[2,128,128]{2,1,0:T(8,128)(2,1)S(1)}, u32[]{:S(2)}, u32[]{:S(2)}) collective-permute-start(bf16[2,128,128]{2,1,0:T(8,128)(2,1)S(1)} %get-tuple-element.39), channel_id=1, source_target_pairs={{0,6},{2,0},{4,2},{6,4},{1,7},{3,1},{5,3},{7,5},{8,14},{10,8},{12,... | collective-permute-start | bytes 196616 | tf_op jit(solution)/shard_map/ppermute | solution.py:155
  22.5 7.5 %collective-permute-start.4 = (bf16[4,2,128,128]{3,2,1,0:T(8,128)(2,1)S(1)}, bf16[4,2,128,128]{3,2,1,0:T(8,128)(2,1)S(1)}, u32[]{:S(2)}, u32[]{:S(2)}) collective-permute-start(bf16[4,2,128,128]{3,2,1,0:T(8,128)(2,1)S(1)} %pad_maximum_fusion.1.refs_0_.refs_5_), channel_id=1, source_target_pairs={{0,16},{8,24},{16,0},{24,8},{1,17},{9,25},{17,1},{25,9},{2,18},{10... | collective-permute-start | bytes 786440 | tf_op jit(solution)/shard_map/ppermute | solution.py:180
  24.1 7.0 %collective-permute-start.3 = (bf16[4,2,128,128]{3,2,1,0:T(8,128)(2,1)S(1)}, bf16[4,2,128,128]{3,2,1,0:T(8,128)(2,1)S(1)}, u32[]{:S(2)}, u32[]{:S(2)}) collective-permute-start(bf16[4,2,128,128]{3,2,1,0:T(8,128)(2,1)S(1)} %pad_maximum_fusion.1.refs_0_.refs_5_), channel_id=1, source_target_pairs={{0,8},{8,0},{16,24},{24,16},{1,9},{9,1},{17,25},{25,17},{2,10},{10... | collective-permute-start | bytes 786440 | tf_op jit(solution)/shard_map/ppermute | solution.py:179
  26.7 9.3 %collective-permute-start.11 = (bf16[4,2,128,128]{3,2,1,0:T(8,128)(2,1)S(1)}, bf16[4,2,128,128]{3,2,1,0:T(8,128)(2,1)S(1)}, u32[]{:S(2)}, u32[]{:S(2)}) collective-permute-start(bf16[4,2,128,128]{3,2,1,0:T(8,128)(2,1)S(1)} %pad_maximum_fusion.2.refs_0_.refs_5_), channel_id=1, source_target_pairs={{0,16},{8,24},{16,0},{24,8},{1,17},{9,25},{17,1},{25,9},{2,18},{10... | collective-permute-start | bytes 786440 | tf_op jit(solution)/shard_map/ppermute | solution.py:180
  28.5 9.3 %collective-permute-start.10 = (bf16[4,2,128,128]{3,2,1,0:T(8,128)(2,1)S(1)}, bf16[4,2,128,128]{3,2,1,0:T(8,128)(2,1)S(1)}, u32[]{:S(2)}, u32[]{:S(2)}) collective-permute-start(bf16[4,2,128,128]{3,2,1,0:T(8,128)(2,1)S(1)} %pad_maximum_fusion.2.refs_0_.refs_5_), channel_id=1, source_target_pairs={{0,8},{8,0},{16,24},{24,16},{1,9},{9,1},{17,25},{25,17},{2,10},{10... | collective-permute-start | bytes 786440 | tf_op jit(solution)/shard_map/ppermute | solution.py:179
  30.0 10.7 %collective-permute-start.5 = (bf16[4,2,64,128]{3,2,1,0:T(8,128)(2,1)S(1)}, bf16[4,2,64,128]{3,2,1,0:T(8,128)(2,1)S(1)}, u32[]{:S(2)}, u32[]{:S(2)}) collective-permute-start(bf16[4,2,64,128]{3,2,1,0:T(8,128)(2,1)S(1)} %slice.111), channel_id=1, source_target_pairs={{0,8},{8,0},{16,24},{24,16},{1,9},{9,1},{17,25},{25,17},{2,10},{10... | collective-permute-start | bytes 393224 | tf_op jit(solution)/shard_map/ppermute | solution.py:182
  31.2 9.6 %collective-permute-start.6 = (bf16[4,2,64,128]{3,2,1,0:T(8,128)(2,1)S(1)}, bf16[4,2,64,128]{3,2,1,0:T(8,128)(2,1)S(1)}, u32[]{:S(2)}, u32[]{:S(2)}) collective-permute-start(bf16[4,2,64,128]{3,2,1,0:T(8,128)(2,1)S(1)} %slice.112), channel_id=1, source_target_pairs={{0,16},{8,24},{16,0},{24,8},{1,17},{9,25},{17,1},{25,9},{2,18},{10... | collective-permute-start | bytes 393224 | tf_op jit(solution)/shard_map/ppermute | solution.py:183
  36.0 14.8 %collective-permute-start.12 = (bf16[4,2,64,128]{3,2,1,0:T(8,128)(2,1)S(1)}, bf16[4,2,64,128]{3,2,1,0:T(8,128)(2,1)S(1)}, u32[]{:S(2)}, u32[]{:S(2)}) collective-permute-start(bf16[4,2,64,128]{3,2,1,0:T(8,128)(2,1)S(1)} %slice.114), channel_id=1, source_target_pairs={{0,8},{8,0},{16,24},{24,16},{1,9},{9,1},{17,25},{25,17},{2,10},{10... | collective-permute-start | bytes 393224 | tf_op jit(solution)/shard_map/ppermute | solution.py:182
  37.8 13.0 %collective-permute-start.13 = (bf16[4,2,64,128]{3,2,1,0:T(8,128)(2,1)S(1)}, bf16[4,2,64,128]{3,2,1,0:T(8,128)(2,1)S(1)}, u32[]{:S(2)}, u32[]{:S(2)}) collective-permute-start(bf16[4,2,64,128]{3,2,1,0:T(8,128)(2,1)S(1)} %slice.115), channel_id=1, source_target_pairs={{0,16},{8,24},{16,0},{24,8},{1,17},{9,25},{17,1},{25,9},{2,18},{10... | collective-permute-start | bytes 393224 | tf_op jit(solution)/shard_map/ppermute | solution.py:183
  48.8 14.4 %collective-permute-start.21 = (bf16[4,2,192,128]{3,2,1,0:T(8,128)(2,1)}, bf16[4,2,192,128]{3,2,1,0:T(8,128)(2,1)S(1)}, u32[]{:S(2)}, u32[]{:S(2)}) collective-permute-start(bf16[4,2,192,128]{3,2,1,0:T(8,128)(2,1)} %get-tuple-element.26), channel_id=1, source_target_pairs={{0,8},{8,0},{16,24},{24,16},{1,9},{9,1},{17,25},{25,17},{2,10},{10... | collective-permute-start | bytes 1179656 | tf_op jit(solution)/shard_map/ppermute | solution.py:206
  49.9 13.8 %collective-permute-start.22 = (bf16[4,2,192,128]{3,2,1,0:T(8,128)(2,1)}, bf16[4,2,192,128]{3,2,1,0:T(8,128)(2,1)S(1)}, u32[]{:S(2)}, u32[]{:S(2)}) collective-permute-start(bf16[4,2,192,128]{3,2,1,0:T(8,128)(2,1)} %get-tuple-element.27), channel_id=1, source_target_pairs={{0,16},{8,24},{16,0},{24,8},{1,17},{9,25},{17,1},{25,9},{2,18},{10... | collective-permute-start | bytes 1179656 | tf_op jit(solution)/shard_map/ppermute | solution.py:207
  59.0 10.3 %collective-permute-start.14 = (bf16[4,2,192,128]{3,2,1,0:T(8,128)(2,1)}, bf16[4,2,192,128]{3,2,1,0:T(8,128)(2,1)S(1)}, u32[]{:S(2)}, u32[]{:S(2)}) collective-permute-start(bf16[4,2,192,128]{3,2,1,0:T(8,128)(2,1)} %get-tuple-element.23), channel_id=1, source_target_pairs={{0,8},{8,0},{16,24},{24,16},{1,9},{9,1},{17,25},{25,17},{2,10},{10... | collective-permute-start | bytes 1179656 | tf_op jit(solution)/shard_map/ppermute | solution.py:206
  59.7 11.2 %collective-permute-start.15 = (bf16[4,2,192,128]{3,2,1,0:T(8,128)(2,1)}, bf16[4,2,192,128]{3,2,1,0:T(8,128)(2,1)S(1)}, u32[]{:S(2)}, u32[]{:S(2)}) collective-permute-start(bf16[4,2,192,128]{3,2,1,0:T(8,128)(2,1)} %get-tuple-element.24), channel_id=1, source_target_pairs={{0,16},{8,24},{16,0},{24,8},{1,17},{9,25},{17,1},{25,9},{2,18},{10... | collective-permute-start | bytes 1179656 | tf_op jit(solution)/shard_map/ppermute | solution.py:207
  63.2 8.7 %collective-permute-start.23 = (bf16[4,2,64,128]{3,2,1,0:T(8,128)(2,1)S(1)}, bf16[4,2,64,128]{3,2,1,0:T(8,128)(2,1)S(1)}, u32[]{:S(2)}, u32[]{:S(2)}) collective-permute-start(bf16[4,2,64,128]{3,2,1,0:T(8,128)(2,1)S(1)} %slice.126), channel_id=1, source_target_pairs={{0,16},{8,24},{16,0},{24,8},{1,17},{9,25},{17,1},{25,9},{2,18},{10... | collective-permute-start | bytes 393224 | tf_op jit(solution)/shard_map/ppermute | solution.py:208
  63.8 8.1 %collective-permute-start.24 = (bf16[4,2,64,128]{3,2,1,0:T(8,128)(2,1)S(1)}, bf16[4,2,64,128]{3,2,1,0:T(8,128)(2,1)S(1)}, u32[]{:S(2)}, u32[]{:S(2)}) collective-permute-start(bf16[4,2,64,128]{3,2,1,0:T(8,128)(2,1)S(1)} %slice.127), channel_id=1, source_target_pairs={{0,8},{8,0},{16,24},{24,16},{1,9},{9,1},{17,25},{25,17},{2,10},{10... | collective-permute-start | bytes 393224 | tf_op jit(solution)/shard_map/ppermute | solution.py:209
  69.3 8.5 %collective-permute-start.16 = (bf16[4,2,64,128]{3,2,1,0:T(8,128)(2,1)S(1)}, bf16[4,2,64,128]{3,2,1,0:T(8,128)(2,1)S(1)}, u32[]{:S(2)}, u32[]{:S(2)}) collective-permute-start(bf16[4,2,64,128]{3,2,1,0:T(8,128)(2,1)S(1)} %slice.118), channel_id=1, source_target_pairs={{0,16},{8,24},{16,0},{24,8},{1,17},{9,25},{17,1},{25,9},{2,18},{10... | collective-permute-start | bytes 393224 | tf_op jit(solution)/shard_map/ppermute | solution.py:208
  70.9 6.9 %collective-permute-start.17 = (bf16[4,2,64,128]{3,2,1,0:T(8,128)(2,1)S(1)}, bf16[4,2,64,128]{3,2,1,0:T(8,128)(2,1)S(1)}, u32[]{:S(2)}, u32[]{:S(2)}) collective-permute-start(bf16[4,2,64,128]{3,2,1,0:T(8,128)(2,1)S(1)} %slice.119), channel_id=1, source_target_pairs={{0,8},{8,0},{16,24},{24,16},{1,9},{9,1},{17,25},{25,17},{2,10},{10... | collective-permute-start | bytes 393224 | tf_op jit(solution)/shard_map/ppermute | solution.py:209
  72.1 8.7 %collective-permute-start.25 = (bf16[2,128,128]{2,1,0:T(8,128)(2,1)S(1)}, bf16[2,128,128]{2,1,0:T(8,128)(2,1)S(1)}, u32[]{:S(2)}, u32[]{:S(2)}) collective-permute-start(bf16[2,128,128]{2,1,0:T(8,128)(2,1)S(1)} %get-tuple-element.35), channel_id=1, source_target_pairs={{0,2},{2,4},{4,6},{6,0},{1,3},{3,5},{5,7},{7,1},{8,10},{10,12},{12... | collective-permute-start | bytes 196616 | tf_op jit(solution)/shard_map/ppermute | solution.py:155
  75.3 6.8 %collective-permute-start.26 = (bf16[2,128,128]{2,1,0:T(8,128)(2,1)S(1)}, bf16[2,128,128]{2,1,0:T(8,128)(2,1)S(1)}, u32[]{:S(2)}, u32[]{:S(2)}) collective-permute-start(bf16[2,128,128]{2,1,0:T(8,128)(2,1)S(1)} %get-tuple-element.34), channel_id=1, source_target_pairs={{0,4},{2,6},{4,0},{6,2},{1,5},{3,7},{5,1},{7,3},{8,12},{10,14},{12... | collective-permute-start | bytes 196616 | tf_op jit(solution)/shard_map/ppermute | solution.py:155
  79.4 6.2 %collective-permute-start.19 = (bf16[2,128,128]{2,1,0:T(8,128)(2,1)S(1)}, bf16[2,128,128]{2,1,0:T(8,128)(2,1)S(1)}, u32[]{:S(2)}, u32[]{:S(2)}) collective-permute-start(bf16[2,128,128]{2,1,0:T(8,128)(2,1)S(1)} %get-tuple-element.30), channel_id=1, source_target_pairs={{0,4},{2,6},{4,0},{6,2},{1,5},{3,7},{5,1},{7,3},{8,12},{10,14},{12... | collective-permute-start | bytes 196616 | tf_op jit(solution)/shard_map/ppermute | solution.py:155
  (22 other events, 88.2 us)

commit v12 on v11

--- a/solution.py
+++ b/solution.py
@@ -186,30 +186,17 @@
 
 def ctx_out_ranges(slot_rows):
     n = lax.axis_size("ctx")
-    if not tree_ctx():
-        return [[(j * slot_rows, slot_rows)] for j in range(n)]
-    half = slot_rows // 2
-    return [[(0, slot_rows)],
-            [(slot_rows, slot_rows), (3 * slot_rows, half)],
-            [(2 * slot_rows, slot_rows), (3 * slot_rows + half, half)]]
+    return [[(j * slot_rows, slot_rows)] for j in range(n)]
 
 
 def ctx_reduce(pieces):
+    n = lax.axis_size("ctx")
     if not tree_ctx():
         got = lax.all_to_all(jnp.stack(pieces), "ctx", split_axis=0, concat_axis=0, tiled=True)
         return jnp.sum(got.astype(jnp.float32), axis=0).astype(jnp.bfloat16)
-    n = lax.axis_size("ctx")
-    along_x = [(i, i ^ 1) for i in range(n)]
-    along_y = [(i, i ^ 2) for i in range(n)]
-    mine, send_x, send_y = pieces
-    rows = mine.shape[2]
-    got_x = lax.ppermute(send_x, "ctx", along_x)
-    got_y = lax.ppermute(send_y, "ctx", along_y)
-    far_a = lax.ppermute(got_x[:, :, rows:], "ctx", along_y)
-    far_b = lax.ppermute(got_y[:, :, rows:], "ctx", along_x)
-    far = jnp.concatenate([far_a, far_b], 2)
-    total = (mine.astype(jnp.float32) + got_x[:, :, :rows].astype(jnp.float32)) + (
-        got_y[:, :, :rows].astype(jnp.float32) + far.astype(jnp.float32))
+    got = [pieces[0]] + [lax.ppermute(pieces[j], "ctx", [(i, i ^ j) for i in range(n)]) for j in range(1, n)]
+    total = (got[0].astype(jnp.float32) + got[1].astype(jnp.float32)) + (
+        got[2].astype(jnp.float32) + got[3].astype(jnp.float32))
     return total.astype(jnp.bfloat16)
 
 

time: 88.4 us -> 85.1 us (0.963)
  waiting for transfers between devices: 10.9 us -> 7.36 us
    ppermute x8 -> x6, waiting for transfers between devices: 3.17 us -> 0.32 us  [ctx_reduce(): lax.ppermute(pieces[j], 'ctx', [(i, i ^ j) for i in range(n)])]
    ppermute x12, starting transfers between devices: 20.5 us -> 22.5 us  [ring_shift(): return lax.ppermute(x, axis, [(i, (i + d) % n) for i in range(n)])]
    ppermute x8 -> x6, starting transfers between devices: 8.81 us -> 7.11 us  [ctx_reduce(): lax.ppermute(pieces[j], 'ctx', [(i, i ^ j) for i in range(n)])]
    unnamed x37 -> x39, local copies, waits for them, and re-layouts: 3.04 us -> 3.13 us
  transfers between devices with their start and end apart: 28 -> 26, of which waited for: 5 -> 5; matrix products, arithmetic and copies ran while one was open for 6% -> 6% of each run, Pallas kernels for 17% -> 17%
where the time goes in v12:
time: 85.1 us; the launch traced here: 84.7 us
  starting transfers between devices  42.1 us (49%)
  Pallas kernels  14.8 us (17%)
  between operations  9.53 us (11%)
  waiting for transfers between devices  7.36 us (9%)
  other arithmetic  5.56 us (7%)
  local copies, waits for them, and re-layouts  5.34 us (6%)
    ppermute x12, starting transfers between devices, ring_shift(): return lax.ppermute(x, axis, [(i, (i + d) % n) for i in range(n)])  22.5 us
    pallas_call x2, Pallas kernels, attention_grads(): pl.pallas_call(functools.partial(attention_grad_kernel, layout), out_shap...  14.8 us
    ppermute x6, starting transfers between devices, ctx_reduce(): lax.ppermute(pieces[j], 'ctx', [(i, i ^ j) for i in range(n)])  7.11 us
    ppermute x12, waiting for transfers between devices, ring_shift(): return lax.ppermute(x, axis, [(i, (i + d) % n) for i in range(n)])  3.84 us
    ppermute x2, starting transfers between devices, ctx_gather(): from_y = lax.ppermute(x, 'ctx', along_y)  3.39 us
    ppermute x2, waiting for transfers between devices, ctx_gather(): from_y = lax.ppermute(x, 'ctx', along_y)  3.19 us
    ppermute x2, starting transfers between devices, ctx_gather(): far_b = lax.ppermute(from_x[:, :, half:], 'ctx', along_y)  3.17 us
    unnamed x39, local copies, waits for them, and re-layouts  3.13 us
  transfers between devices with their start and end apart: 26, of which 5 were waited for; matrix products, arithmetic and copies ran while one was open for 6% of the time, Pallas kernels for 17%

profile of v12, /device:TPU:0, one launch (start us, length us, event | category | flops | bytes accessed | tf_op | source)
XLA Modules:
  0.0 84.7 jit_solution(17740140184988824840)
XLA Ops:
  10.8 3.1 %collective-permute-start = (bf16[2,128,128]{2,1,0:T(8,128)(2,1)S(1)}, bf16[2,128,128]{2,1,0:T(8,128)(2,1)S(1)}, u32[]{:S(2)}, u32[]{:S(2)}) collective-permute-start(bf16[2,128,128]{2,1,0:T(8,128)(2,1)S(1)} %get-tuple-element.49), channel_id=1, source_target_pairs={{0,2},{2,4},{4,6},{6,0},{1,3},{3,5},{5,7},{7,1},{8,10},{10,12},{12... | collective-permute-start | bytes 196616 | tf_op jit(solution)/shard_map/ppermute | solution.py:155
  13.9 2.6 %collective-permute-start.1 = (bf16[2,128,128]{2,1,0:T(8,128)(2,1)S(1)}, bf16[2,128,128]{2,1,0:T(8,128)(2,1)S(1)}, u32[]{:S(2)}, u32[]{:S(2)}) collective-permute-start(bf16[2,128,128]{2,1,0:T(8,128)(2,1)S(1)} %get-tuple-element.48), channel_id=1, source_target_pairs={{0,4},{2,6},{4,0},{6,2},{1,5},{3,7},{5,1},{7,3},{8,12},{10,14},{12... | collective-permute-start | bytes 196616 | tf_op jit(solution)/shard_map/ppermute | solution.py:155
  16.4 1.3 %collective-permute-start.2 = (bf16[2,128,128]{2,1,0:T(8,128)(2,1)S(1)}, bf16[2,128,128]{2,1,0:T(8,128)(2,1)S(1)}, u32[]{:S(2)}, u32[]{:S(2)}) collective-permute-start(bf16[2,128,128]{2,1,0:T(8,128)(2,1)S(1)} %get-tuple-element.47), channel_id=1, source_target_pairs={{0,6},{2,0},{4,2},{6,4},{1,7},{3,1},{5,3},{7,5},{8,14},{10,8},{12,... | collective-permute-start | bytes 196616 | tf_op jit(solution)/shard_map/ppermute | solution.py:155
  19.6 2.8 %collective-permute-start.9 = (bf16[2,128,128]{2,1,0:T(8,128)(2,1)S(1)}, bf16[2,128,128]{2,1,0:T(8,128)(2,1)S(1)}, u32[]{:S(2)}, u32[]{:S(2)}) collective-permute-start(bf16[2,128,128]{2,1,0:T(8,128)(2,1)S(1)} %get-tuple-element.43), channel_id=1, source_target_pairs={{0,6},{2,0},{4,2},{6,4},{1,7},{3,1},{5,3},{7,5},{8,14},{10,8},{12,... | collective-permute-start | bytes 196616 | tf_op jit(solution)/shard_map/ppermute | solution.py:155
  22.5 1.6 %collective-permute-start.4 = (bf16[4,2,128,128]{3,2,1,0:T(8,128)(2,1)S(1)}, bf16[4,2,128,128]{3,2,1,0:T(8,128)(2,1)S(1)}, u32[]{:S(2)}, u32[]{:S(2)}) collective-permute-start(bf16[4,2,128,128]{3,2,1,0:T(8,128)(2,1)S(1)} %pad_maximum_fusion.1.refs_0_.refs_5_), channel_id=1, source_target_pairs={{0,16},{8,24},{16,0},{24,8},{1,17},{9,25},{17,1},{25,9},{2,18},{10... | collective-permute-start | bytes 786440 | tf_op jit(solution)/shard_map/ppermute | solution.py:180
  24.1 1.5 %collective-permute-start.3 = (bf16[4,2,128,128]{3,2,1,0:T(8,128)(2,1)S(1)}, bf16[4,2,128,128]{3,2,1,0:T(8,128)(2,1)S(1)}, u32[]{:S(2)}, u32[]{:S(2)}) collective-permute-start(bf16[4,2,128,128]{3,2,1,0:T(8,128)(2,1)S(1)} %pad_maximum_fusion.1.refs_0_.refs_5_), channel_id=1, source_target_pairs={{0,8},{8,0},{16,24},{24,16},{1,9},{9,1},{17,25},{25,17},{2,10},{10... | collective-permute-start | bytes 786440 | tf_op jit(solution)/shard_map/ppermute | solution.py:179
  26.7 1.8 %collective-permute-start.11 = (bf16[4,2,128,128]{3,2,1,0:T(8,128)(2,1)S(1)}, bf16[4,2,128,128]{3,2,1,0:T(8,128)(2,1)S(1)}, u32[]{:S(2)}, u32[]{:S(2)}) collective-permute-start(bf16[4,2,128,128]{3,2,1,0:T(8,128)(2,1)S(1)} %pad_maximum_fusion.2.refs_0_.refs_5_), channel_id=1, source_target_pairs={{0,16},{8,24},{16,0},{24,8},{1,17},{9,25},{17,1},{25,9},{2,18},{10... | collective-permute-start | bytes 786440 | tf_op jit(solution)/shard_map/ppermute | solution.py:180
  28.5 1.5 %collective-permute-start.10 = (bf16[4,2,128,128]{3,2,1,0:T(8,128)(2,1)S(1)}, bf16[4,2,128,128]{3,2,1,0:T(8,128)(2,1)S(1)}, u32[]{:S(2)}, u32[]{:S(2)}) collective-permute-start(bf16[4,2,128,128]{3,2,1,0:T(8,128)(2,1)S(1)} %pad_maximum_fusion.2.refs_0_.refs_5_), channel_id=1, source_target_pairs={{0,8},{8,0},{16,24},{24,16},{1,9},{9,1},{17,25},{25,17},{2,10},{10... | collective-permute-start | bytes 786440 | tf_op jit(solution)/shard_map/ppermute | solution.py:179
  31.2 1.6 %collective-permute-start.6 = (bf16[4,2,64,128]{3,2,1,0:T(8,128)(2,1)S(1)}, bf16[4,2,64,128]{3,2,1,0:T(8,128)(2,1)S(1)}, u32[]{:S(2)}, u32[]{:S(2)}) collective-permute-start(bf16[4,2,64,128]{3,2,1,0:T(8,128)(2,1)S(1)} %slice.80), channel_id=1, source_target_pairs={{0,16},{8,24},{16,0},{24,8},{1,17},{9,25},{17,1},{25,9},{2,18},{10... | collective-permute-start | bytes 393224 | tf_op jit(solution)/shard_map/ppermute | solution.py:183
  32.8 3.2 %collective-permute-done.11.refs_2_.refs_7_ = bf16[4,2,128,128]{3,2,1,0:T(8,128)(2,1)S(1)} collective-permute-done((bf16[4,2,128,128]{3,2,1,0:T(8,128)(2,1)S(1)}, bf16[4,2,128,128]{3,2,1,0:T(8,128)(2,1)S(1)}, u32[]{:S(2)}, u32[]{:S(2)}) %collective-permute-start.11) | collective-permute-done | bytes 262176 | tf_op jit(solution)/shard_map/ppermute | solution.py:180
  36.0 1.8 %collective-permute-start.12 = (bf16[4,2,64,128]{3,2,1,0:T(8,128)(2,1)S(1)}, bf16[4,2,64,128]{3,2,1,0:T(8,128)(2,1)S(1)}, u32[]{:S(2)}, u32[]{:S(2)}) collective-permute-start(bf16[4,2,64,128]{3,2,1,0:T(8,128)(2,1)S(1)} %slice.82), channel_id=1, source_target_pairs={{0,8},{8,0},{16,24},{24,16},{1,9},{9,1},{17,25},{25,17},{2,10},{10... | collective-permute-start | bytes 393224 | tf_op jit(solution)/shard_map/ppermute | solution.py:182
  37.8 1.6 %collective-permute-start.13 = (bf16[4,2,64,128]{3,2,1,0:T(8,128)(2,1)S(1)}, bf16[4,2,64,128]{3,2,1,0:T(8,128)(2,1)S(1)}, u32[]{:S(2)}, u32[]{:S(2)}) collective-permute-start(bf16[4,2,64,128]{3,2,1,0:T(8,128)(2,1)S(1)} %slice.83), channel_id=1, source_target_pairs={{0,16},{8,24},{16,0},{24,8},{1,17},{9,25},{17,1},{25,9},{2,18},{10... | collective-permute-start | bytes 393224 | tf_op jit(solution)/shard_map/ppermute | solution.py:183
  41.3 7.3 %shard_map.111 = (bf16[128,2048]{1,0:T(8,128)(2,1)}, bf16[128,1024]{1,0:T(8,128)(2,1)}, bf16[128,1024]{1,0:T(8,128)(2,1)}, bf16[4,2,128,128]{3,2,1,0:T(8,128)(2,...) custom-call(s32[4]{0:T(128)} %bitcast.104, ...), custom_call_target="tpu_custom_call" | custom-call | flops 1006632960 | bytes 3670016 | tf_op jit(solution)/shard_map/pallas_call | solution.py:136
  48.7 1.2 %collective-permute-start.20 = (bf16[4,2,128,128]{3,2,1,0:T(8,128)(2,1)}, bf16[4,2,128,128]{3,2,1,0:T(8,128)(2,1)S(1)}, u32[]{:S(2)}, u32[]{:S(2)}) collective-permute-start(bf16[4,2,128,128]{3,2,1,0:T(8,128)(2,1)} %get-tuple-element.29), channel_id=1, source_target_pairs={{0,8},{8,0},{16,24},{24,16},{1,9},{9,1},{17,25},{25,17},{2,10},{10... | collective-permute-start | bytes 786440 | tf_op jit(solution)/shard_map/ppermute | solution.py:197
  50.7 1.6 %collective-permute-start.22 = (bf16[4,2,128,128]{3,2,1,0:T(8,128)(2,1)}, bf16[4,2,128,128]{3,2,1,0:T(8,128)(2,1)S(1)}, u32[]{:S(2)}, u32[]{:S(2)}) collective-permute-start(bf16[4,2,128,128]{3,2,1,0:T(8,128)(2,1)} %get-tuple-element.31), channel_id=1, source_target_pairs={{0,24},{8,16},{16,8},{24,0},{1,25},{9,17},{17,9},{25,1},{2,26},{10... | collective-permute-start | bytes 786440 | tf_op jit(solution)/shard_map/ppermute | solution.py:197
  53.0 7.5 %shard_map.112 = (bf16[128,2048]{1,0:T(8,128)(2,1)}, bf16[128,1024]{1,0:T(8,128)(2,1)}, bf16[128,1024]{1,0:T(8,128)(2,1)}, bf16[4,2,128,128]{3,2,1,0:T(8,128)(2,...) custom-call(s32[4]{0:T(128)} %bitcast.105, ...), custom_call_target="tpu_custom_call" | custom-call | flops 1006632960 | bytes 3670016 | tf_op jit(solution)/shard_map/pallas_call | solution.py:136
  60.4 1.2 %collective-permute-start.14 = (bf16[4,2,128,128]{3,2,1,0:T(8,128)(2,1)}, bf16[4,2,128,128]{3,2,1,0:T(8,128)(2,1)S(1)}, u32[]{:S(2)}, u32[]{:S(2)}) collective-permute-start(bf16[4,2,128,128]{3,2,1,0:T(8,128)(2,1)} %get-tuple-element.25), channel_id=1, source_target_pairs={{0,8},{8,0},{16,24},{24,16},{1,9},{9,1},{17,25},{25,17},{2,10},{10... | collective-permute-start | bytes 786440 | tf_op jit(solution)/shard_map/ppermute | solution.py:197
  62.5 2.0 %select_bitcast_fusion = bf16[1,1,128,2048]{3,2,1,0:T(8,128)(2,1)} fusion(bf16[128,2048]{1,0:T(8,128)(2,1)S(1)} %copy-done.1, bf16[128,2048]{1,0:T(8,128)(2,1)} %get-tuple-element.19, pred[2048]{0:T(1024)(128)(4,1)S(1)} %fusion.1), kind=kLoop, calls=%fused_computation.4 | loop fusion | flops 262144 | bytes 1574912 | tf_op jit(solution)/shard_map/broadcast_in_dim | solution.py:254
  65.4 1.6 %collective-permute-start.16 = (bf16[4,2,128,128]{3,2,1,0:T(8,128)(2,1)S(1)}, bf16[4,2,128,128]{3,2,1,0:T(8,128)(2,1)S(1)}, u32[]{:S(2)}, u32[]{:S(2)}) collective-permute-start(bf16[4,2,128,128]{3,2,1,0:T(8,128)(2,1)S(1)} %copy-done.14), channel_id=1, source_target_pairs={{0,24},{8,16},{16,8},{24,0},{1,25},{9,17},{17,9},{25,1},{2,26},{10... | collective-permute-start | bytes 786440 | tf_op jit(solution)/shard_map/ppermute | solution.py:197
  67.2 3.4 %collective-permute-start.23 = (bf16[2,128,128]{2,1,0:T(8,128)(2,1)S(1)}, bf16[2,128,128]{2,1,0:T(8,128)(2,1)S(1)}, u32[]{:S(2)}, u32[]{:S(2)}) collective-permute-start(bf16[2,128,128]{2,1,0:T(8,128)(2,1)S(1)} %get-tuple-element.39), channel_id=1, source_target_pairs={{0,2},{2,4},{4,6},{6,0},{1,3},{3,5},{5,7},{7,1},{8,10},{10,12},{12... | collective-permute-start | bytes 196616 | tf_op jit(solution)/shard_map/ppermute | solution.py:155
  70.8 2.2 %collective-permute-start.25 = (bf16[2,128,128]{2,1,0:T(8,128)(2,1)S(1)}, bf16[2,128,128]{2,1,0:T(8,128)(2,1)S(1)}, u32[]{:S(2)}, u32[]{:S(2)}) collective-permute-start(bf16[2,128,128]{2,1,0:T(8,128)(2,1)S(1)} %get-tuple-element.37), channel_id=1, source_target_pairs={{0,6},{2,0},{4,2},{6,4},{1,7},{3,1},{5,3},{7,5},{8,14},{10,8},{12,... | collective-permute-start | bytes 196616 | tf_op jit(solution)/shard_map/ppermute | solution.py:155
  73.6 3.4 %collective-permute-start.17 = (bf16[2,128,128]{2,1,0:T(8,128)(2,1)S(1)}, bf16[2,128,128]{2,1,0:T(8,128)(2,1)S(1)}, u32[]{:S(2)}, u32[]{:S(2)}) collective-permute-start(bf16[2,128,128]{2,1,0:T(8,128)(2,1)S(1)} %get-tuple-element.35), channel_id=1, source_target_pairs={{0,2},{2,4},{4,6},{6,0},{1,3},{3,5},{5,7},{7,1},{8,10},{10,12},{12... | collective-permute-start | bytes 196616 | tf_op jit(solution)/shard_map/ppermute | solution.py:155
  77.6 1.9 %collective-permute-start.19 = (bf16[2,128,128]{2,1,0:T(8,128)(2,1)S(1)}, bf16[2,128,128]{2,1,0:T(8,128)(2,1)S(1)}, u32[]{:S(2)}, u32[]{:S(2)}) collective-permute-start(bf16[2,128,128]{2,1,0:T(8,128)(2,1)S(1)} %get-tuple-element.33), channel_id=1, source_target_pairs={{0,6},{2,0},{4,2},{6,4},{1,7},{3,1},{5,3},{7,5},{8,14},{10,8},{12,... | collective-permute-start | bytes 196616 | tf_op jit(solution)/shard_map/ppermute | solution.py:155
  79.8 2.6 %collective-permute-done.18 = bf16[2,128,128]{2,1,0:T(8,128)(2,1)S(1)} collective-permute-done((bf16[2,128,128]{2,1,0:T(8,128)(2,1)S(1)}, bf16[2,128,128]{2,1,0:T(8,128)(2,1)S(1)}, u32[]{:S(2)}, u32[]{:S(2)}) %collective-permute-start.18) | collective-permute-done | bytes 65568 | tf_op jit(solution)/shard_map/ppermute | solution.py:155
  (109 shorter events, 15.1 us)
Async XLA Ops:
  10.8 8.8 %collective-permute-start = (bf16[2,128,128]{2,1,0:T(8,128)(2,1)S(1)}, bf16[2,128,128]{2,1,0:T(8,128)(2,1)S(1)}, u32[]{:S(2)}, u32[]{:S(2)}) collective-permute-start(bf16[2,128,128]{2,1,0:T(8,128)(2,1)S(1)} %get-tuple-element.49), channel_id=1, source_target_pairs={{0,2},{2,4},{4,6},{6,0},{1,3},{3,5},{5,7},{7,1},{8,10},{10,12},{12... | collective-permute-start | bytes 196616 | tf_op jit(solution)/shard_map/ppermute | solution.py:155
  13.9 8.6 %collective-permute-start.1 = (bf16[2,128,128]{2,1,0:T(8,128)(2,1)S(1)}, bf16[2,128,128]{2,1,0:T(8,128)(2,1)S(1)}, u32[]{:S(2)}, u32[]{:S(2)}) collective-permute-start(bf16[2,128,128]{2,1,0:T(8,128)(2,1)S(1)} %get-tuple-element.48), channel_id=1, source_target_pairs={{0,4},{2,6},{4,0},{6,2},{1,5},{3,7},{5,1},{7,3},{8,12},{10,14},{12... | collective-permute-start | bytes 196616 | tf_op jit(solution)/shard_map/ppermute | solution.py:155
  16.4 6.0 %collective-permute-start.2 = (bf16[2,128,128]{2,1,0:T(8,128)(2,1)S(1)}, bf16[2,128,128]{2,1,0:T(8,128)(2,1)S(1)}, u32[]{:S(2)}, u32[]{:S(2)}) collective-permute-start(bf16[2,128,128]{2,1,0:T(8,128)(2,1)S(1)} %get-tuple-element.47), channel_id=1, source_target_pairs={{0,6},{2,0},{4,2},{6,4},{1,7},{3,1},{5,3},{7,5},{8,14},{10,8},{12,... | collective-permute-start | bytes 196616 | tf_op jit(solution)/shard_map/ppermute | solution.py:155
  17.8 7.8 %collective-permute-start.7 = (bf16[2,128,128]{2,1,0:T(8,128)(2,1)S(1)}, bf16[2,128,128]{2,1,0:T(8,128)(2,1)S(1)}, u32[]{:S(2)}, u32[]{:S(2)}) collective-permute-start(bf16[2,128,128]{2,1,0:T(8,128)(2,1)S(1)} %get-tuple-element.45), channel_id=1, source_target_pairs={{0,2},{2,4},{4,6},{6,0},{1,3},{3,5},{5,7},{7,1},{8,10},{10,12},{12... | collective-permute-start | bytes 196616 | tf_op jit(solution)/shard_map/ppermute | solution.py:155
  18.5 8.0 %collective-permute-start.8 = (bf16[2,128,128]{2,1,0:T(8,128)(2,1)S(1)}, bf16[2,128,128]{2,1,0:T(8,128)(2,1)S(1)}, u32[]{:S(2)}, u32[]{:S(2)}) collective-permute-start(bf16[2,128,128]{2,1,0:T(8,128)(2,1)S(1)} %get-tuple-element.44), channel_id=1, source_target_pairs={{0,4},{2,6},{4,0},{6,2},{1,5},{3,7},{5,1},{7,3},{8,12},{10,14},{12... | collective-permute-start | bytes 196616 | tf_op jit(solution)/shard_map/ppermute | solution.py:155
  19.6 7.0 %collective-permute-start.9 = (bf16[2,128,128]{2,1,0:T(8,128)(2,1)S(1)}, bf16[2,128,128]{2,1,0:T(8,128)(2,1)S(1)}, u32[]{:S(2)}, u32[]{:S(2)}) collective-permute-start(bf16[2,128,128]{2,1,0:T(8,128)(2,1)S(1)} %get-tuple-element.43), channel_id=1, source_target_pairs={{0,6},{2,0},{4,2},{6,4},{1,7},{3,1},{5,3},{7,5},{8,14},{10,8},{12,... | collective-permute-start | bytes 196616 | tf_op jit(solution)/shard_map/ppermute | solution.py:155
  22.5 7.5 %collective-permute-start.4 = (bf16[4,2,128,128]{3,2,1,0:T(8,128)(2,1)S(1)}, bf16[4,2,128,128]{3,2,1,0:T(8,128)(2,1)S(1)}, u32[]{:S(2)}, u32[]{:S(2)}) collective-permute-start(bf16[4,2,128,128]{3,2,1,0:T(8,128)(2,1)S(1)} %pad_maximum_fusion.1.refs_0_.refs_5_), channel_id=1, source_target_pairs={{0,16},{8,24},{16,0},{24,8},{1,17},{9,25},{17,1},{25,9},{2,18},{10... | collective-permute-start | bytes 786440 | tf_op jit(solution)/shard_map/ppermute | solution.py:180
  24.1 7.0 %collective-permute-start.3 = (bf16[4,2,128,128]{3,2,1,0:T(8,128)(2,1)S(1)}, bf16[4,2,128,128]{3,2,1,0:T(8,128)(2,1)S(1)}, u32[]{:S(2)}, u32[]{:S(2)}) collective-permute-start(bf16[4,2,128,128]{3,2,1,0:T(8,128)(2,1)S(1)} %pad_maximum_fusion.1.refs_0_.refs_5_), channel_id=1, source_target_pairs={{0,8},{8,0},{16,24},{24,16},{1,9},{9,1},{17,25},{25,17},{2,10},{10... | collective-permute-start | bytes 786440 | tf_op jit(solution)/shard_map/ppermute | solution.py:179
  26.7 9.3 %collective-permute-start.11 = (bf16[4,2,128,128]{3,2,1,0:T(8,128)(2,1)S(1)}, bf16[4,2,128,128]{3,2,1,0:T(8,128)(2,1)S(1)}, u32[]{:S(2)}, u32[]{:S(2)}) collective-permute-start(bf16[4,2,128,128]{3,2,1,0:T(8,128)(2,1)S(1)} %pad_maximum_fusion.2.refs_0_.refs_5_), channel_id=1, source_target_pairs={{0,16},{8,24},{16,0},{24,8},{1,17},{9,25},{17,1},{25,9},{2,18},{10... | collective-permute-start | bytes 786440 | tf_op jit(solution)/shard_map/ppermute | solution.py:180
  28.5 9.3 %collective-permute-start.10 = (bf16[4,2,128,128]{3,2,1,0:T(8,128)(2,1)S(1)}, bf16[4,2,128,128]{3,2,1,0:T(8,128)(2,1)S(1)}, u32[]{:S(2)}, u32[]{:S(2)}) collective-permute-start(bf16[4,2,128,128]{3,2,1,0:T(8,128)(2,1)S(1)} %pad_maximum_fusion.2.refs_0_.refs_5_), channel_id=1, source_target_pairs={{0,8},{8,0},{16,24},{24,16},{1,9},{9,1},{17,25},{25,17},{2,10},{10... | collective-permute-start | bytes 786440 | tf_op jit(solution)/shard_map/ppermute | solution.py:179
  30.0 10.6 %collective-permute-start.5 = (bf16[4,2,64,128]{3,2,1,0:T(8,128)(2,1)S(1)}, bf16[4,2,64,128]{3,2,1,0:T(8,128)(2,1)S(1)}, u32[]{:S(2)}, u32[]{:S(2)}) collective-permute-start(bf16[4,2,64,128]{3,2,1,0:T(8,128)(2,1)S(1)} %slice.79), channel_id=1, source_target_pairs={{0,8},{8,0},{16,24},{24,16},{1,9},{9,1},{17,25},{25,17},{2,10},{10... | collective-permute-start | bytes 393224 | tf_op jit(solution)/shard_map/ppermute | solution.py:182
  31.2 9.5 %collective-permute-start.6 = (bf16[4,2,64,128]{3,2,1,0:T(8,128)(2,1)S(1)}, bf16[4,2,64,128]{3,2,1,0:T(8,128)(2,1)S(1)}, u32[]{:S(2)}, u32[]{:S(2)}) collective-permute-start(bf16[4,2,64,128]{3,2,1,0:T(8,128)(2,1)S(1)} %slice.80), channel_id=1, source_target_pairs={{0,16},{8,24},{16,0},{24,8},{1,17},{9,25},{17,1},{25,9},{2,18},{10... | collective-permute-start | bytes 393224 | tf_op jit(solution)/shard_map/ppermute | solution.py:183
  36.0 16.3 %collective-permute-start.12 = (bf16[4,2,64,128]{3,2,1,0:T(8,128)(2,1)S(1)}, bf16[4,2,64,128]{3,2,1,0:T(8,128)(2,1)S(1)}, u32[]{:S(2)}, u32[]{:S(2)}) collective-permute-start(bf16[4,2,64,128]{3,2,1,0:T(8,128)(2,1)S(1)} %slice.82), channel_id=1, source_target_pairs={{0,8},{8,0},{16,24},{24,16},{1,9},{9,1},{17,25},{25,17},{2,10},{10... | collective-permute-start | bytes 393224 | tf_op jit(solution)/shard_map/ppermute | solution.py:182
  37.8 14.5 %collective-permute-start.13 = (bf16[4,2,64,128]{3,2,1,0:T(8,128)(2,1)S(1)}, bf16[4,2,64,128]{3,2,1,0:T(8,128)(2,1)S(1)}, u32[]{:S(2)}, u32[]{:S(2)}) collective-permute-start(bf16[4,2,64,128]{3,2,1,0:T(8,128)(2,1)S(1)} %slice.83), channel_id=1, source_target_pairs={{0,16},{8,24},{16,0},{24,8},{1,17},{9,25},{17,1},{25,9},{2,18},{10... | collective-permute-start | bytes 393224 | tf_op jit(solution)/shard_map/ppermute | solution.py:183
  48.7 16.6 %collective-permute-start.20 = (bf16[4,2,128,128]{3,2,1,0:T(8,128)(2,1)}, bf16[4,2,128,128]{3,2,1,0:T(8,128)(2,1)S(1)}, u32[]{:S(2)}, u32[]{:S(2)}) collective-permute-start(bf16[4,2,128,128]{3,2,1,0:T(8,128)(2,1)} %get-tuple-element.29), channel_id=1, source_target_pairs={{0,8},{8,0},{16,24},{24,16},{1,9},{9,1},{17,25},{25,17},{2,10},{10... | collective-permute-start | bytes 786440 | tf_op jit(solution)/shard_map/ppermute | solution.py:197
  49.9 17.1 %collective-permute-start.21 = (bf16[4,2,128,128]{3,2,1,0:T(8,128)(2,1)}, bf16[4,2,128,128]{3,2,1,0:T(8,128)(2,1)S(1)}, u32[]{:S(2)}, u32[]{:S(2)}) collective-permute-start(bf16[4,2,128,128]{3,2,1,0:T(8,128)(2,1)} %get-tuple-element.30), channel_id=1, source_target_pairs={{0,16},{8,24},{16,0},{24,8},{1,17},{9,25},{17,1},{25,9},{2,18},{10... | collective-permute-start | bytes 786440 | tf_op jit(solution)/shard_map/ppermute | solution.py:197
  50.7 16.3 %collective-permute-start.22 = (bf16[4,2,128,128]{3,2,1,0:T(8,128)(2,1)}, bf16[4,2,128,128]{3,2,1,0:T(8,128)(2,1)S(1)}, u32[]{:S(2)}, u32[]{:S(2)}) collective-permute-start(bf16[4,2,128,128]{3,2,1,0:T(8,128)(2,1)} %get-tuple-element.31), channel_id=1, source_target_pairs={{0,24},{8,16},{16,8},{24,0},{1,25},{9,17},{17,9},{25,1},{2,26},{10... | collective-permute-start | bytes 786440 | tf_op jit(solution)/shard_map/ppermute | solution.py:197
  60.4 10.3 %collective-permute-start.14 = (bf16[4,2,128,128]{3,2,1,0:T(8,128)(2,1)}, bf16[4,2,128,128]{3,2,1,0:T(8,128)(2,1)S(1)}, u32[]{:S(2)}, u32[]{:S(2)}) collective-permute-start(bf16[4,2,128,128]{3,2,1,0:T(8,128)(2,1)} %get-tuple-element.25), channel_id=1, source_target_pairs={{0,8},{8,0},{16,24},{24,16},{1,9},{9,1},{17,25},{25,17},{2,10},{10... | collective-permute-start | bytes 786440 | tf_op jit(solution)/shard_map/ppermute | solution.py:197
  61.6 11.6 %collective-permute-start.15 = (bf16[4,2,128,128]{3,2,1,0:T(8,128)(2,1)}, bf16[4,2,128,128]{3,2,1,0:T(8,128)(2,1)S(1)}, u32[]{:S(2)}, u32[]{:S(2)}) collective-permute-start(bf16[4,2,128,128]{3,2,1,0:T(8,128)(2,1)} %get-tuple-element.26), channel_id=1, source_target_pairs={{0,16},{8,24},{16,0},{24,8},{1,17},{9,25},{17,1},{25,9},{2,18},{10... | collective-permute-start | bytes 786440 | tf_op jit(solution)/shard_map/ppermute | solution.py:197
  65.4 7.9 %collective-permute-start.16 = (bf16[4,2,128,128]{3,2,1,0:T(8,128)(2,1)S(1)}, bf16[4,2,128,128]{3,2,1,0:T(8,128)(2,1)S(1)}, u32[]{:S(2)}, u32[]{:S(2)}) collective-permute-start(bf16[4,2,128,128]{3,2,1,0:T(8,128)(2,1)S(1)} %copy-done.14), channel_id=1, source_target_pairs={{0,24},{8,16},{16,8},{24,0},{1,25},{9,17},{17,9},{25,1},{2,26},{10... | collective-permute-start | bytes 786440 | tf_op jit(solution)/shard_map/ppermute | solution.py:197
  67.2 10.4 %collective-permute-start.23 = (bf16[2,128,128]{2,1,0:T(8,128)(2,1)S(1)}, bf16[2,128,128]{2,1,0:T(8,128)(2,1)S(1)}, u32[]{:S(2)}, u32[]{:S(2)}) collective-permute-start(bf16[2,128,128]{2,1,0:T(8,128)(2,1)S(1)} %get-tuple-element.39), channel_id=1, source_target_pairs={{0,2},{2,4},{4,6},{6,0},{1,3},{3,5},{5,7},{7,1},{8,10},{10,12},{12... | collective-permute-start | bytes 196616 | tf_op jit(solution)/shard_map/ppermute | solution.py:155
  70.5 9.0 %collective-permute-start.24 = (bf16[2,128,128]{2,1,0:T(8,128)(2,1)S(1)}, bf16[2,128,128]{2,1,0:T(8,128)(2,1)S(1)}, u32[]{:S(2)}, u32[]{:S(2)}) collective-permute-start(bf16[2,128,128]{2,1,0:T(8,128)(2,1)S(1)} %get-tuple-element.38), channel_id=1, source_target_pairs={{0,4},{2,6},{4,0},{6,2},{1,5},{3,7},{5,1},{7,3},{8,12},{10,14},{12... | collective-permute-start | bytes 196616 | tf_op jit(solution)/shard_map/ppermute | solution.py:155
  70.8 8.8 %collective-permute-start.25 = (bf16[2,128,128]{2,1,0:T(8,128)(2,1)S(1)}, bf16[2,128,128]{2,1,0:T(8,128)(2,1)S(1)}, u32[]{:S(2)}, u32[]{:S(2)}) collective-permute-start(bf16[2,128,128]{2,1,0:T(8,128)(2,1)S(1)} %get-tuple-element.37), channel_id=1, source_target_pairs={{0,6},{2,0},{4,2},{6,4},{1,7},{3,1},{5,3},{7,5},{8,14},{10,8},{12,... | collective-permute-start | bytes 196616 | tf_op jit(solution)/shard_map/ppermute | solution.py:155
  73.6 6.2 %collective-permute-start.17 = (bf16[2,128,128]{2,1,0:T(8,128)(2,1)S(1)}, bf16[2,128,128]{2,1,0:T(8,128)(2,1)S(1)}, u32[]{:S(2)}, u32[]{:S(2)}) collective-permute-start(bf16[2,128,128]{2,1,0:T(8,128)(2,1)S(1)} %get-tuple-element.35), channel_id=1, source_target_pairs={{0,2},{2,4},{4,6},{6,0},{1,3},{3,5},{5,7},{7,1},{8,10},{10,12},{12... | collective-permute-start | bytes 196616 | tf_op jit(solution)/shard_map/ppermute | solution.py:155
  (21 other events, 68.7 us)

commit v13 on v12

--- a/solution.py
+++ b/solution.py
@@ -151,6 +151,27 @@
     )(*operands)
 
 
+def copy_blocks_kernel(*refs):
+    n = len(refs) // 3
+    for src, dst in zip(refs[n:2 * n], refs[2 * n:]):
+        dst[...] = src[...]
+
+
+def merge_heads(earlier, later, n_heads, heads):
+    resp_rows = earlier[0].shape[0]
+    kv_heads = later[1].shape[1] // HEAD_DIM
+    widths = [x.shape[1] // kv_heads for x in later]
+    specs = [pl.BlockSpec((resp_rows, w), lambda g: (0, heads(g))) for w in widths]
+    return pl.pallas_call(
+        copy_blocks_kernel,
+        out_shape=tuple(jax.ShapeDtypeStruct(x.shape, x.dtype) for x in earlier),
+        grid=(n_heads,),
+        in_specs=[pl.BlockSpec(memory_space=pl.ANY)] * len(earlier) + specs,
+        out_specs=specs,
+        input_output_aliases={i: i for i in range(len(earlier))},
+    )(*earlier, *later)
+
+
 def ring_shift(x, axis, n, d):
     return lax.ppermute(x, axis, [(i, (i + d) % n) for i in range(n)])
 
@@ -212,9 +233,8 @@
     return (source[:, None] == jnp.arange(n_prompts, dtype=jnp.int32)[None, :]).astype(jnp.float32)
 
 
-def in_group(width, kv_heads, chunk_heads, group_heads, k):
-    head = jnp.arange(width) // (width // kv_heads)
-    return ((head % chunk_heads) // group_heads == k)[None]
+def group_head(chunk_heads, group_heads, k, g):
+    return (g // group_heads) * chunk_heads + k * group_heads + g % group_heads
 
 
 def shards(
@@ -242,8 +262,9 @@
         if earlier is None:
             earlier = outs[:3]
         else:
-            earlier = tuple(jnp.where(in_group(o.shape[1], kv_heads, chunk_heads, group_heads, k), o, e)
-                            for o, e in zip(outs[:3], earlier))
+            earlier = merge_heads(
+                earlier, outs[:3], kv_heads // chunk_heads * group_heads,
+                functools.partial(group_head, chunk_heads, group_heads, k))
         parts.append(pair_exchange(ctx_reduce(list(outs[3:]))))
     dq, dkr, dvr = earlier
     weights = prompt_weights(pair_prompt, n_prompts)

time: 85.1 us -> 85.2 us (level)
  Pallas kernels: 14.8 us -> 17.8 us
  other arithmetic: 5.56 us -> 2.76 us
    pallas_call x0 -> x1, Pallas kernels: none -> 3.11 us  [merge_heads(): pl.pallas_call(copy_blocks_kernel, out_shape=tuple((jax.ShapeDtypeStruct(...]
    broadcast_in_dim x2 -> x0, other arithmetic: 2.82 us -> none  [shards(): return (dq[None, None], dkr[None, None], dvr[None, None], d_prefix)]
    ppermute x12, starting transfers between devices: 22.5 us -> 23.5 us  [ring_shift(): return lax.ppermute(x, axis, [(i, (i + d) % n) for i in range(n)])]
    ppermute x2, starting transfers between devices: 3.17 us -> 2.3 us  [ctx_gather(): far_b = lax.ppermute(from_x[:, :, half:], 'ctx', along_y)]
    unnamed x39 -> x29, local copies, waits for them, and re-layouts: 3.13 us -> 3.08 us
  transfers between devices with their start and end apart: 26 -> 26, of which waited for: 5 -> 5; matrix products, arithmetic and copies ran while one was open for 6% -> 3% of each run, Pallas kernels for 17% -> 21%
where the time goes in v13:
time: 85.2 us; the launch traced here: 84.7 us
  starting transfers between devices  41.5 us (49%)
  Pallas kernels  17.8 us (21%)
  between operations  9.45 us (11%)
  waiting for transfers between devices  7.89 us (9%)
  local copies, waits for them, and re-layouts  5.28 us (6%)
  other arithmetic  2.76 us (3%)
    ppermute x12, starting transfers between devices, ring_shift(): return lax.ppermute(x, axis, [(i, (i + d) % n) for i in range(n)])  23.5 us
    pallas_call x2, Pallas kernels, attention_grads(): pl.pallas_call(functools.partial(attention_grad_kernel, layout), out_shap...  14.7 us
    ppermute x6, starting transfers between devices, ctx_reduce(): lax.ppermute(pieces[j], 'ctx', [(i, i ^ j) for i in range(n)])  7.17 us
    ppermute x12, waiting for transfers between devices, ring_shift(): return lax.ppermute(x, axis, [(i, (i + d) % n) for i in range(n)])  3.85 us
    ppermute x2, starting transfers between devices, ctx_gather(): from_y = lax.ppermute(x, 'ctx', along_y)  3.44 us
    pallas_call x1, Pallas kernels, merge_heads(): pl.pallas_call(copy_blocks_kernel, out_shape=tuple((jax.ShapeDtypeStruct(...  3.11 us
    unnamed x29, local copies, waits for them, and re-layouts  3.08 us
    ppermute x2, starting transfers between devices, ctx_gather(): from_x = lax.ppermute(x, 'ctx', along_x)  2.98 us
  transfers between devices with their start and end apart: 26, of which 5 were waited for; matrix products, arithmetic and copies ran while one was open for 3% of the time, Pallas kernels for 21%

profile of v13, /device:TPU:0, one launch (start us, length us, event | category | flops | bytes accessed | tf_op | source)
XLA Modules:
  0.0 84.7 jit_solution(6157521784737687565)
XLA Ops:
  10.8 3.1 %collective-permute-start.7 = (bf16[2,128,128]{2,1,0:T(8,128)(2,1)S(1)}, bf16[2,128,128]{2,1,0:T(8,128)(2,1)S(1)}, u32[]{:S(2)}, u32[]{:S(2)}) collective-permute-start(bf16[2,128,128]{2,1,0:T(8,128)(2,1)S(1)} %get-tuple-element.51), channel_id=1, source_target_pairs={{0,2},{2,4},{4,6},{6,0},{1,3},{3,5},{5,7},{7,1},{8,10},{10,12},{12... | collective-permute-start | bytes 196616 | tf_op jit(solution)/shard_map/ppermute | solution.py:176
  13.9 2.6 %collective-permute-start.8 = (bf16[2,128,128]{2,1,0:T(8,128)(2,1)S(1)}, bf16[2,128,128]{2,1,0:T(8,128)(2,1)S(1)}, u32[]{:S(2)}, u32[]{:S(2)}) collective-permute-start(bf16[2,128,128]{2,1,0:T(8,128)(2,1)S(1)} %get-tuple-element.50), channel_id=1, source_target_pairs={{0,4},{2,6},{4,0},{6,2},{1,5},{3,7},{5,1},{7,3},{8,12},{10,14},{12... | collective-permute-start | bytes 196616 | tf_op jit(solution)/shard_map/ppermute | solution.py:176
  16.4 1.3 %collective-permute-start.9 = (bf16[2,128,128]{2,1,0:T(8,128)(2,1)S(1)}, bf16[2,128,128]{2,1,0:T(8,128)(2,1)S(1)}, u32[]{:S(2)}, u32[]{:S(2)}) collective-permute-start(bf16[2,128,128]{2,1,0:T(8,128)(2,1)S(1)} %get-tuple-element.49), channel_id=1, source_target_pairs={{0,6},{2,0},{4,2},{6,4},{1,7},{3,1},{5,3},{7,5},{8,14},{10,8},{12,... | collective-permute-start | bytes 196616 | tf_op jit(solution)/shard_map/ppermute | solution.py:176
  18.9 2.8 %collective-permute-start.2 = (bf16[2,128,128]{2,1,0:T(8,128)(2,1)S(1)}, bf16[2,128,128]{2,1,0:T(8,128)(2,1)S(1)}, u32[]{:S(2)}, u32[]{:S(2)}) collective-permute-start(bf16[2,128,128]{2,1,0:T(8,128)(2,1)S(1)} %get-tuple-element.53), channel_id=1, source_target_pairs={{0,6},{2,0},{4,2},{6,4},{1,7},{3,1},{5,3},{7,5},{8,14},{10,8},{12,... | collective-permute-start | bytes 196616 | tf_op jit(solution)/shard_map/ppermute | solution.py:176
  21.8 1.6 %collective-permute-start.11 = (bf16[4,2,128,128]{3,2,1,0:T(8,128)(2,1)S(1)}, bf16[4,2,128,128]{3,2,1,0:T(8,128)(2,1)S(1)}, u32[]{:S(2)}, u32[]{:S(2)}) collective-permute-start(bf16[4,2,128,128]{3,2,1,0:T(8,128)(2,1)S(1)} %pad_maximum_fusion.2.refs_0_.refs_5_), channel_id=1, source_target_pairs={{0,16},{8,24},{16,0},{24,8},{1,17},{9,25},{17,1},{25,9},{2,18},{10... | collective-permute-start | bytes 786440 | tf_op jit(solution)/shard_map/ppermute | solution.py:201
  23.3 1.5 %collective-permute-start.10 = (bf16[4,2,128,128]{3,2,1,0:T(8,128)(2,1)S(1)}, bf16[4,2,128,128]{3,2,1,0:T(8,128)(2,1)S(1)}, u32[]{:S(2)}, u32[]{:S(2)}) collective-permute-start(bf16[4,2,128,128]{3,2,1,0:T(8,128)(2,1)S(1)} %pad_maximum_fusion.2.refs_0_.refs_5_), channel_id=1, source_target_pairs={{0,8},{8,0},{16,24},{24,16},{1,9},{9,1},{17,25},{25,17},{2,10},{10... | collective-permute-start | bytes 786440 | tf_op jit(solution)/shard_map/ppermute | solution.py:200
  25.5 1.0 %collective-permute-done.1 = bf16[2,128,128]{2,1,0:T(8,128)(2,1)S(1)} collective-permute-done((bf16[2,128,128]{2,1,0:T(8,128)(2,1)S(1)}, bf16[2,128,128]{2,1,0:T(8,128)(2,1)S(1)}, u32[]{:S(2)}, u32[]{:S(2)}) %collective-permute-start.1) | collective-permute-done | bytes 65568 | tf_op jit(solution)/shard_map/ppermute | solution.py:176
  26.6 1.9 %collective-permute-start.4 = (bf16[4,2,128,128]{3,2,1,0:T(8,128)(2,1)S(1)}, bf16[4,2,128,128]{3,2,1,0:T(8,128)(2,1)S(1)}, u32[]{:S(2)}, u32[]{:S(2)}) collective-permute-start(bf16[4,2,128,128]{3,2,1,0:T(8,128)(2,1)S(1)} %pad_maximum_fusion.1.refs_0_.refs_5_), channel_id=1, source_target_pairs={{0,16},{8,24},{16,0},{24,8},{1,17},{9,25},{17,1},{25,9},{2,18},{10... | collective-permute-start | bytes 786440 | tf_op jit(solution)/shard_map/ppermute | solution.py:201
  28.5 1.5 %collective-permute-start.3 = (bf16[4,2,128,128]{3,2,1,0:T(8,128)(2,1)S(1)}, bf16[4,2,128,128]{3,2,1,0:T(8,128)(2,1)S(1)}, u32[]{:S(2)}, u32[]{:S(2)}) collective-permute-start(bf16[4,2,128,128]{3,2,1,0:T(8,128)(2,1)S(1)} %pad_maximum_fusion.1.refs_0_.refs_5_), channel_id=1, source_target_pairs={{0,8},{8,0},{16,24},{24,16},{1,9},{9,1},{17,25},{25,17},{2,10},{10... | collective-permute-start | bytes 786440 | tf_op jit(solution)/shard_map/ppermute | solution.py:200
  33.0 2.9 %collective-permute-done.4.refs_2_.refs_7_ = bf16[4,2,128,128]{3,2,1,0:T(8,128)(2,1)S(1)} collective-permute-done((bf16[4,2,128,128]{3,2,1,0:T(8,128)(2,1)S(1)}, bf16[4,2,128,128]{3,2,1,0:T(8,128)(2,1)S(1)}, u32[]{:S(2)}, u32[]{:S(2)}) %collective-permute-start.4) | collective-permute-done | bytes 262176 | tf_op jit(solution)/shard_map/ppermute | solution.py:201
  35.9 1.5 %collective-permute-start.5 = (bf16[4,2,64,128]{3,2,1,0:T(8,128)(2,1)S(1)}, bf16[4,2,64,128]{3,2,1,0:T(8,128)(2,1)S(1)}, u32[]{:S(2)}, u32[]{:S(2)}) collective-permute-start(bf16[4,2,64,128]{3,2,1,0:T(8,128)(2,1)S(1)} %slice.79), channel_id=1, source_target_pairs={{0,8},{8,0},{16,24},{24,16},{1,9},{9,1},{17,25},{25,17},{2,10},{10... | collective-permute-start | bytes 393224 | tf_op jit(solution)/shard_map/ppermute | solution.py:203
  37.7 1.3 %collective-permute-start.6 = (bf16[4,2,64,128]{3,2,1,0:T(8,128)(2,1)S(1)}, bf16[4,2,64,128]{3,2,1,0:T(8,128)(2,1)S(1)}, u32[]{:S(2)}, u32[]{:S(2)}) collective-permute-start(bf16[4,2,64,128]{3,2,1,0:T(8,128)(2,1)S(1)} %slice.80), channel_id=1, source_target_pairs={{0,16},{8,24},{16,0},{24,8},{1,17},{9,25},{17,1},{25,9},{2,18},{10... | collective-permute-start | bytes 393224 | tf_op jit(solution)/shard_map/ppermute | solution.py:204
  40.6 7.4 %shard_map.112 = (bf16[128,2048]{1,0:T(8,128)(2,1)}, bf16[128,1024]{1,0:T(8,128)(2,1)}, bf16[128,1024]{1,0:T(8,128)(2,1)}, bf16[4,2,128,128]{3,2,1,0:T(8,128)(2,...) custom-call(s32[4]{0:T(128)} %bitcast.104, ...), custom_call_target="tpu_custom_call" | custom-call | flops 1006632960 | bytes 3670016 | tf_op jit(solution)/shard_map/pallas_call | solution.py:136
  47.9 1.6 %collective-permute-start.20 = (bf16[4,2,128,128]{3,2,1,0:T(8,128)(2,1)}, bf16[4,2,128,128]{3,2,1,0:T(8,128)(2,1)S(1)}, u32[]{:S(2)}, u32[]{:S(2)}) collective-permute-start(bf16[4,2,128,128]{3,2,1,0:T(8,128)(2,1)} %get-tuple-element.35), channel_id=1, source_target_pairs={{0,8},{8,0},{16,24},{24,16},{1,9},{9,1},{17,25},{25,17},{2,10},{10... | collective-permute-start | bytes 786440 | tf_op jit(solution)/shard_map/ppermute | solution.py:218
  50.0 1.5 %collective-permute-start.22 = (bf16[4,2,128,128]{3,2,1,0:T(8,128)(2,1)}, bf16[4,2,128,128]{3,2,1,0:T(8,128)(2,1)S(1)}, u32[]{:S(2)}, u32[]{:S(2)}) collective-permute-start(bf16[4,2,128,128]{3,2,1,0:T(8,128)(2,1)} %get-tuple-element.37), channel_id=1, source_target_pairs={{0,24},{8,16},{16,8},{24,0},{1,25},{9,17},{17,9},{25,1},{2,26},{10... | collective-permute-start | bytes 786440 | tf_op jit(solution)/shard_map/ppermute | solution.py:218
  52.2 7.4 %shard_map.111 = (bf16[128,2048]{1,0:T(8,128)(2,1)}, bf16[128,1024]{1,0:T(8,128)(2,1)}, bf16[128,1024]{1,0:T(8,128)(2,1)}, bf16[4,2,128,128]{3,2,1,0:T(8,128)(2,...) custom-call(s32[4]{0:T(128)} %bitcast.105, ...), custom_call_target="tpu_custom_call" | custom-call | flops 1006632960 | bytes 3670016 | tf_op jit(solution)/shard_map/pallas_call | solution.py:136
  59.6 1.6 %collective-permute-start.14 = (bf16[4,2,128,128]{3,2,1,0:T(8,128)(2,1)}, bf16[4,2,128,128]{3,2,1,0:T(8,128)(2,1)S(1)}, u32[]{:S(2)}, u32[]{:S(2)}) collective-permute-start(bf16[4,2,128,128]{3,2,1,0:T(8,128)(2,1)} %get-tuple-element.31), channel_id=1, source_target_pairs={{0,8},{8,0},{16,24},{24,16},{1,9},{9,1},{17,25},{25,17},{2,10},{10... | collective-permute-start | bytes 786440 | tf_op jit(solution)/shard_map/ppermute | solution.py:218
  61.6 3.1 %shard_map.113 = (bf16[128,2048]{1,0:T(8,128)(2,1)}, bf16[128,1024]{1,0:T(8,128)(2,1)}, bf16[128,1024]{1,0:T(8,128)(2,1)}) custom-call(bf16[128,2048]{1,0:T(8,128)(2,1)} %get-tuple-element.21.refs_0_, bf16[128,1024]{1,0:T(8,128)(2,1)} %get-tuple-element.22.refs_1_, ...), custom_call_target="tpu_custom_call", output_to_operand_aliasing={{0}: (0, {}), {1}: (1, {}), {2}: (2, {})} | custom-call | tf_op jit(solution)/shard_map/pallas_call | solution.py:165
  64.8 1.6 %collective-permute-start.16 = (bf16[4,2,128,128]{3,2,1,0:T(8,128)(2,1)S(1)}, bf16[4,2,128,128]{3,2,1,0:T(8,128)(2,1)S(1)}, u32[]{:S(2)}, u32[]{:S(2)}) collective-permute-start(bf16[4,2,128,128]{3,2,1,0:T(8,128)(2,1)S(1)} %copy-done.9), channel_id=1, source_target_pairs={{0,24},{8,16},{16,8},{24,0},{1,25},{9,17},{17,9},{25,1},{2,26},{10... | collective-permute-start | bytes 786440 | tf_op jit(solution)/shard_map/ppermute | solution.py:218
  66.5 4.0 %collective-permute-start.23 = (bf16[2,128,128]{2,1,0:T(8,128)(2,1)S(1)}, bf16[2,128,128]{2,1,0:T(8,128)(2,1)S(1)}, u32[]{:S(2)}, u32[]{:S(2)}) collective-permute-start(bf16[2,128,128]{2,1,0:T(8,128)(2,1)S(1)} %get-tuple-element.45), channel_id=1, source_target_pairs={{0,2},{2,4},{4,6},{6,0},{1,3},{3,5},{5,7},{7,1},{8,10},{10,12},{12... | collective-permute-start | bytes 196616 | tf_op jit(solution)/shard_map/ppermute | solution.py:176
  70.7 2.2 %collective-permute-start.25 = (bf16[2,128,128]{2,1,0:T(8,128)(2,1)S(1)}, bf16[2,128,128]{2,1,0:T(8,128)(2,1)S(1)}, u32[]{:S(2)}, u32[]{:S(2)}) collective-permute-start(bf16[2,128,128]{2,1,0:T(8,128)(2,1)S(1)} %get-tuple-element.43), channel_id=1, source_target_pairs={{0,6},{2,0},{4,2},{6,4},{1,7},{3,1},{5,3},{7,5},{8,14},{10,8},{12,... | collective-permute-start | bytes 196616 | tf_op jit(solution)/shard_map/ppermute | solution.py:176
  73.3 3.7 %collective-permute-start.17 = (bf16[2,128,128]{2,1,0:T(8,128)(2,1)S(1)}, bf16[2,128,128]{2,1,0:T(8,128)(2,1)S(1)}, u32[]{:S(2)}, u32[]{:S(2)}) collective-permute-start(bf16[2,128,128]{2,1,0:T(8,128)(2,1)S(1)} %get-tuple-element.41), channel_id=1, source_target_pairs={{0,2},{2,4},{4,6},{6,0},{1,3},{3,5},{5,7},{7,1},{8,10},{10,12},{12... | collective-permute-start | bytes 196616 | tf_op jit(solution)/shard_map/ppermute | solution.py:176
  78.0 1.6 %collective-permute-start.19 = (bf16[2,128,128]{2,1,0:T(8,128)(2,1)S(1)}, bf16[2,128,128]{2,1,0:T(8,128)(2,1)S(1)}, u32[]{:S(2)}, u32[]{:S(2)}) collective-permute-start(bf16[2,128,128]{2,1,0:T(8,128)(2,1)S(1)} %get-tuple-element.39), channel_id=1, source_target_pairs={{0,6},{2,0},{4,2},{6,4},{1,7},{3,1},{5,3},{7,5},{8,14},{10,8},{12,... | collective-permute-start | bytes 196616 | tf_op jit(solution)/shard_map/ppermute | solution.py:176
  79.6 2.8 %collective-permute-done.18 = bf16[2,128,128]{2,1,0:T(8,128)(2,1)S(1)} collective-permute-done((bf16[2,128,128]{2,1,0:T(8,128)(2,1)S(1)}, bf16[2,128,128]{2,1,0:T(8,128)(2,1)S(1)}, u32[]{:S(2)}, u32[]{:S(2)}) %collective-permute-start.18) | collective-permute-done | bytes 65568 | tf_op jit(solution)/shard_map/ppermute | solution.py:176
  (96 shorter events, 14.1 us)
Async XLA Ops:
  10.8 8.1 %collective-permute-start.7 = (bf16[2,128,128]{2,1,0:T(8,128)(2,1)S(1)}, bf16[2,128,128]{2,1,0:T(8,128)(2,1)S(1)}, u32[]{:S(2)}, u32[]{:S(2)}) collective-permute-start(bf16[2,128,128]{2,1,0:T(8,128)(2,1)S(1)} %get-tuple-element.51), channel_id=1, source_target_pairs={{0,2},{2,4},{4,6},{6,0},{1,3},{3,5},{5,7},{7,1},{8,10},{10,12},{12... | collective-permute-start | bytes 196616 | tf_op jit(solution)/shard_map/ppermute | solution.py:176
  13.9 7.8 %collective-permute-start.8 = (bf16[2,128,128]{2,1,0:T(8,128)(2,1)S(1)}, bf16[2,128,128]{2,1,0:T(8,128)(2,1)S(1)}, u32[]{:S(2)}, u32[]{:S(2)}) collective-permute-start(bf16[2,128,128]{2,1,0:T(8,128)(2,1)S(1)} %get-tuple-element.50), channel_id=1, source_target_pairs={{0,4},{2,6},{4,0},{6,2},{1,5},{3,7},{5,1},{7,3},{8,12},{10,14},{12... | collective-permute-start | bytes 196616 | tf_op jit(solution)/shard_map/ppermute | solution.py:176
  17.8 7.7 %collective-permute-start = (bf16[2,128,128]{2,1,0:T(8,128)(2,1)S(1)}, bf16[2,128,128]{2,1,0:T(8,128)(2,1)S(1)}, u32[]{:S(2)}, u32[]{:S(2)}) collective-permute-start(bf16[2,128,128]{2,1,0:T(8,128)(2,1)S(1)} %get-tuple-element.55), channel_id=1, source_target_pairs={{0,2},{2,4},{4,6},{6,0},{1,3},{3,5},{5,7},{7,1},{8,10},{10,12},{12... | collective-permute-start | bytes 196616 | tf_op jit(solution)/shard_map/ppermute | solution.py:176
  18.5 8.0 %collective-permute-start.1 = (bf16[2,128,128]{2,1,0:T(8,128)(2,1)S(1)}, bf16[2,128,128]{2,1,0:T(8,128)(2,1)S(1)}, u32[]{:S(2)}, u32[]{:S(2)}) collective-permute-start(bf16[2,128,128]{2,1,0:T(8,128)(2,1)S(1)} %get-tuple-element.54), channel_id=1, source_target_pairs={{0,4},{2,6},{4,0},{6,2},{1,5},{3,7},{5,1},{7,3},{8,12},{10,14},{12... | collective-permute-start | bytes 196616 | tf_op jit(solution)/shard_map/ppermute | solution.py:176
  18.9 7.7 %collective-permute-start.2 = (bf16[2,128,128]{2,1,0:T(8,128)(2,1)S(1)}, bf16[2,128,128]{2,1,0:T(8,128)(2,1)S(1)}, u32[]{:S(2)}, u32[]{:S(2)}) collective-permute-start(bf16[2,128,128]{2,1,0:T(8,128)(2,1)S(1)} %get-tuple-element.53), channel_id=1, source_target_pairs={{0,6},{2,0},{4,2},{6,4},{1,7},{3,1},{5,3},{7,5},{8,14},{10,8},{12,... | collective-permute-start | bytes 196616 | tf_op jit(solution)/shard_map/ppermute | solution.py:176
  21.8 8.2 %collective-permute-start.11 = (bf16[4,2,128,128]{3,2,1,0:T(8,128)(2,1)S(1)}, bf16[4,2,128,128]{3,2,1,0:T(8,128)(2,1)S(1)}, u32[]{:S(2)}, u32[]{:S(2)}) collective-permute-start(bf16[4,2,128,128]{3,2,1,0:T(8,128)(2,1)S(1)} %pad_maximum_fusion.2.refs_0_.refs_5_), channel_id=1, source_target_pairs={{0,16},{8,24},{16,0},{24,8},{1,17},{9,25},{17,1},{25,9},{2,18},{10... | collective-permute-start | bytes 786440 | tf_op jit(solution)/shard_map/ppermute | solution.py:201
  23.3 7.2 %collective-permute-start.10 = (bf16[4,2,128,128]{3,2,1,0:T(8,128)(2,1)S(1)}, bf16[4,2,128,128]{3,2,1,0:T(8,128)(2,1)S(1)}, u32[]{:S(2)}, u32[]{:S(2)}) collective-permute-start(bf16[4,2,128,128]{3,2,1,0:T(8,128)(2,1)S(1)} %pad_maximum_fusion.2.refs_0_.refs_5_), channel_id=1, source_target_pairs={{0,8},{8,0},{16,24},{24,16},{1,9},{9,1},{17,25},{25,17},{2,10},{10... | collective-permute-start | bytes 786440 | tf_op jit(solution)/shard_map/ppermute | solution.py:200
  26.6 9.3 %collective-permute-start.4 = (bf16[4,2,128,128]{3,2,1,0:T(8,128)(2,1)S(1)}, bf16[4,2,128,128]{3,2,1,0:T(8,128)(2,1)S(1)}, u32[]{:S(2)}, u32[]{:S(2)}) collective-permute-start(bf16[4,2,128,128]{3,2,1,0:T(8,128)(2,1)S(1)} %pad_maximum_fusion.1.refs_0_.refs_5_), channel_id=1, source_target_pairs={{0,16},{8,24},{16,0},{24,8},{1,17},{9,25},{17,1},{25,9},{2,18},{10... | collective-permute-start | bytes 786440 | tf_op jit(solution)/shard_map/ppermute | solution.py:201
  28.5 9.2 %collective-permute-start.3 = (bf16[4,2,128,128]{3,2,1,0:T(8,128)(2,1)S(1)}, bf16[4,2,128,128]{3,2,1,0:T(8,128)(2,1)S(1)}, u32[]{:S(2)}, u32[]{:S(2)}) collective-permute-start(bf16[4,2,128,128]{3,2,1,0:T(8,128)(2,1)S(1)} %pad_maximum_fusion.1.refs_0_.refs_5_), channel_id=1, source_target_pairs={{0,8},{8,0},{16,24},{24,16},{1,9},{9,1},{17,25},{25,17},{2,10},{10... | collective-permute-start | bytes 786440 | tf_op jit(solution)/shard_map/ppermute | solution.py:200
  30.0 9.9 %collective-permute-start.12 = (bf16[4,2,64,128]{3,2,1,0:T(8,128)(2,1)S(1)}, bf16[4,2,64,128]{3,2,1,0:T(8,128)(2,1)S(1)}, u32[]{:S(2)}, u32[]{:S(2)}) collective-permute-start(bf16[4,2,64,128]{3,2,1,0:T(8,128)(2,1)S(1)} %slice.82), channel_id=1, source_target_pairs={{0,8},{8,0},{16,24},{24,16},{1,9},{9,1},{17,25},{25,17},{2,10},{10... | collective-permute-start | bytes 393224 | tf_op jit(solution)/shard_map/ppermute | solution.py:203
  30.7 9.2 %collective-permute-start.13 = (bf16[4,2,64,128]{3,2,1,0:T(8,128)(2,1)S(1)}, bf16[4,2,64,128]{3,2,1,0:T(8,128)(2,1)S(1)}, u32[]{:S(2)}, u32[]{:S(2)}) collective-permute-start(bf16[4,2,64,128]{3,2,1,0:T(8,128)(2,1)S(1)} %slice.83), channel_id=1, source_target_pairs={{0,16},{8,24},{16,0},{24,8},{1,17},{9,25},{17,1},{25,9},{2,18},{10... | collective-permute-start | bytes 393224 | tf_op jit(solution)/shard_map/ppermute | solution.py:204
  35.9 15.6 %collective-permute-start.5 = (bf16[4,2,64,128]{3,2,1,0:T(8,128)(2,1)S(1)}, bf16[4,2,64,128]{3,2,1,0:T(8,128)(2,1)S(1)}, u32[]{:S(2)}, u32[]{:S(2)}) collective-permute-start(bf16[4,2,64,128]{3,2,1,0:T(8,128)(2,1)S(1)} %slice.79), channel_id=1, source_target_pairs={{0,8},{8,0},{16,24},{24,16},{1,9},{9,1},{17,25},{25,17},{2,10},{10... | collective-permute-start | bytes 393224 | tf_op jit(solution)/shard_map/ppermute | solution.py:203
  37.7 13.8 %collective-permute-start.6 = (bf16[4,2,64,128]{3,2,1,0:T(8,128)(2,1)S(1)}, bf16[4,2,64,128]{3,2,1,0:T(8,128)(2,1)S(1)}, u32[]{:S(2)}, u32[]{:S(2)}) collective-permute-start(bf16[4,2,64,128]{3,2,1,0:T(8,128)(2,1)S(1)} %slice.80), channel_id=1, source_target_pairs={{0,16},{8,24},{16,0},{24,8},{1,17},{9,25},{17,1},{25,9},{2,18},{10... | collective-permute-start | bytes 393224 | tf_op jit(solution)/shard_map/ppermute | solution.py:204
  47.9 16.8 %collective-permute-start.20 = (bf16[4,2,128,128]{3,2,1,0:T(8,128)(2,1)}, bf16[4,2,128,128]{3,2,1,0:T(8,128)(2,1)S(1)}, u32[]{:S(2)}, u32[]{:S(2)}) collective-permute-start(bf16[4,2,128,128]{3,2,1,0:T(8,128)(2,1)} %get-tuple-element.35), channel_id=1, source_target_pairs={{0,8},{8,0},{16,24},{24,16},{1,9},{9,1},{17,25},{25,17},{2,10},{10... | collective-permute-start | bytes 786440 | tf_op jit(solution)/shard_map/ppermute | solution.py:218
  49.5 16.8 %collective-permute-start.21 = (bf16[4,2,128,128]{3,2,1,0:T(8,128)(2,1)}, bf16[4,2,128,128]{3,2,1,0:T(8,128)(2,1)S(1)}, u32[]{:S(2)}, u32[]{:S(2)}) collective-permute-start(bf16[4,2,128,128]{3,2,1,0:T(8,128)(2,1)} %get-tuple-element.36), channel_id=1, source_target_pairs={{0,16},{8,24},{16,0},{24,8},{1,17},{9,25},{17,1},{25,9},{2,18},{10... | collective-permute-start | bytes 786440 | tf_op jit(solution)/shard_map/ppermute | solution.py:218
  50.0 16.3 %collective-permute-start.22 = (bf16[4,2,128,128]{3,2,1,0:T(8,128)(2,1)}, bf16[4,2,128,128]{3,2,1,0:T(8,128)(2,1)S(1)}, u32[]{:S(2)}, u32[]{:S(2)}) collective-permute-start(bf16[4,2,128,128]{3,2,1,0:T(8,128)(2,1)} %get-tuple-element.37), channel_id=1, source_target_pairs={{0,24},{8,16},{16,8},{24,0},{1,25},{9,17},{17,9},{25,1},{2,26},{10... | collective-permute-start | bytes 786440 | tf_op jit(solution)/shard_map/ppermute | solution.py:218
  59.6 11.2 %collective-permute-start.14 = (bf16[4,2,128,128]{3,2,1,0:T(8,128)(2,1)}, bf16[4,2,128,128]{3,2,1,0:T(8,128)(2,1)S(1)}, u32[]{:S(2)}, u32[]{:S(2)}) collective-permute-start(bf16[4,2,128,128]{3,2,1,0:T(8,128)(2,1)} %get-tuple-element.31), channel_id=1, source_target_pairs={{0,8},{8,0},{16,24},{24,16},{1,9},{9,1},{17,25},{25,17},{2,10},{10... | collective-permute-start | bytes 786440 | tf_op jit(solution)/shard_map/ppermute | solution.py:218
  61.1 11.9 %collective-permute-start.15 = (bf16[4,2,128,128]{3,2,1,0:T(8,128)(2,1)}, bf16[4,2,128,128]{3,2,1,0:T(8,128)(2,1)S(1)}, u32[]{:S(2)}, u32[]{:S(2)}) collective-permute-start(bf16[4,2,128,128]{3,2,1,0:T(8,128)(2,1)} %get-tuple-element.32), channel_id=1, source_target_pairs={{0,16},{8,24},{16,0},{24,8},{1,17},{9,25},{17,1},{25,9},{2,18},{10... | collective-permute-start | bytes 786440 | tf_op jit(solution)/shard_map/ppermute | solution.py:218
  64.8 8.2 %collective-permute-start.16 = (bf16[4,2,128,128]{3,2,1,0:T(8,128)(2,1)S(1)}, bf16[4,2,128,128]{3,2,1,0:T(8,128)(2,1)S(1)}, u32[]{:S(2)}, u32[]{:S(2)}) collective-permute-start(bf16[4,2,128,128]{3,2,1,0:T(8,128)(2,1)S(1)} %copy-done.9), channel_id=1, source_target_pairs={{0,24},{8,16},{16,8},{24,0},{1,25},{9,17},{17,9},{25,1},{2,26},{10... | collective-permute-start | bytes 786440 | tf_op jit(solution)/shard_map/ppermute | solution.py:218
  66.5 11.4 %collective-permute-start.23 = (bf16[2,128,128]{2,1,0:T(8,128)(2,1)S(1)}, bf16[2,128,128]{2,1,0:T(8,128)(2,1)S(1)}, u32[]{:S(2)}, u32[]{:S(2)}) collective-permute-start(bf16[2,128,128]{2,1,0:T(8,128)(2,1)S(1)} %get-tuple-element.45), channel_id=1, source_target_pairs={{0,2},{2,4},{4,6},{6,0},{1,3},{3,5},{5,7},{7,1},{8,10},{10,12},{12... | collective-permute-start | bytes 196616 | tf_op jit(solution)/shard_map/ppermute | solution.py:176
  70.5 9.0 %collective-permute-start.24 = (bf16[2,128,128]{2,1,0:T(8,128)(2,1)S(1)}, bf16[2,128,128]{2,1,0:T(8,128)(2,1)S(1)}, u32[]{:S(2)}, u32[]{:S(2)}) collective-permute-start(bf16[2,128,128]{2,1,0:T(8,128)(2,1)S(1)} %get-tuple-element.44), channel_id=1, source_target_pairs={{0,4},{2,6},{4,0},{6,2},{1,5},{3,7},{5,1},{7,3},{8,12},{10,14},{12... | collective-permute-start | bytes 196616 | tf_op jit(solution)/shard_map/ppermute | solution.py:176
  70.7 8.8 %collective-permute-start.25 = (bf16[2,128,128]{2,1,0:T(8,128)(2,1)S(1)}, bf16[2,128,128]{2,1,0:T(8,128)(2,1)S(1)}, u32[]{:S(2)}, u32[]{:S(2)}) collective-permute-start(bf16[2,128,128]{2,1,0:T(8,128)(2,1)S(1)} %get-tuple-element.43), channel_id=1, source_target_pairs={{0,6},{2,0},{4,2},{6,4},{1,7},{3,1},{5,3},{7,5},{8,14},{10,8},{12,... | collective-permute-start | bytes 196616 | tf_op jit(solution)/shard_map/ppermute | solution.py:176
  73.3 6.3 %collective-permute-start.17 = (bf16[2,128,128]{2,1,0:T(8,128)(2,1)S(1)}, bf16[2,128,128]{2,1,0:T(8,128)(2,1)S(1)}, u32[]{:S(2)}, u32[]{:S(2)}) collective-permute-start(bf16[2,128,128]{2,1,0:T(8,128)(2,1)S(1)} %get-tuple-element.41), channel_id=1, source_target_pairs={{0,2},{2,4},{4,6},{6,0},{1,3},{3,5},{5,7},{7,1},{8,10},{10,12},{12... | collective-permute-start | bytes 196616 | tf_op jit(solution)/shard_map/ppermute | solution.py:176
  76.9 5.5 %collective-permute-start.18 = (bf16[2,128,128]{2,1,0:T(8,128)(2,1)S(1)}, bf16[2,128,128]{2,1,0:T(8,128)(2,1)S(1)}, u32[]{:S(2)}, u32[]{:S(2)}) collective-permute-start(bf16[2,128,128]{2,1,0:T(8,128)(2,1)S(1)} %get-tuple-element.40), channel_id=1, source_target_pairs={{0,4},{2,6},{4,0},{6,2},{1,5},{3,7},{5,1},{7,3},{8,12},{10,14},{12... | collective-permute-start | bytes 196616 | tf_op jit(solution)/shard_map/ppermute | solution.py:176
  (16 other events, 53.8 us)

commit v14 on v12

--- a/solution.py
+++ b/solution.py
@@ -247,10 +247,10 @@
         parts.append(pair_exchange(ctx_reduce(list(outs[3:]))))
     dq, dkr, dvr = earlier
     weights = prompt_weights(pair_prompt, n_prompts)
-    d_prefix = jnp.concatenate([
-        sum(weights[d][:, None, None, None] * jnp.transpose(got.astype(jnp.float32), (1, 0, 2))[None]
-            for d, got in enumerate(part))
-        for part in parts], -1)
+    d_prefix = sum(
+        weights[d][:, None, None, None] * jnp.transpose(
+            jnp.concatenate([part[d] for part in parts], -1).astype(jnp.float32), (1, 0, 2))[None]
+        for d in range(len(parts[0])))
     return (dq[None, None], dkr[None, None], dvr[None, None], d_prefix)
 
 

time: 85.1 us -> 90.2 us (1.060)
  waiting for transfers between devices: 7.36 us -> 14 us
  starting transfers between devices: 42.1 us -> 40.7 us
    ppermute x6, waiting for transfers between devices: 0.32 us -> 6.02 us  [ctx_reduce(): lax.ppermute(pieces[j], 'ctx', [(i, i ^ j) for i in range(n)])]
    ppermute x12, starting transfers between devices: 22.5 us -> 21.2 us  [ring_shift(): return lax.ppermute(x, axis, [(i, (i + d) % n) for i in range(n)])]
    concatenate x1 -> x0, other arithmetic: 1.03 us -> none  [shards(): jnp.concatenate([sum((weights[d][:, None, None, None] * jnp.transpose(got...]
    ppermute x12, waiting for transfers between devices: 3.84 us -> 4.8 us  [ring_shift(): return lax.ppermute(x, axis, [(i, (i + d) % n) for i in range(n)])]
  transfers between devices with their start and end apart: 26 -> 26, of which waited for: 5 -> 7; matrix products, arithmetic and copies ran while one was open for 6% -> 6% of each run, Pallas kernels for 17% -> 17%
where the time goes in v14:
time: 90.2 us; the launch traced here: 89.8 us
  starting transfers between devices  40.7 us (45%)
  Pallas kernels  14.8 us (16%)
  waiting for transfers between devices  14 us (16%)
  between operations  9.46 us (10%)
  local copies, waits for them, and re-layouts  5.37 us (6%)
  other arithmetic  5.37 us (6%)
    ppermute x12, starting transfers between devices, ring_shift(): return lax.ppermute(x, axis, [(i, (i + d) % n) for i in range(n)])  21.2 us
    pallas_call x2, Pallas kernels, attention_grads(): pl.pallas_call(functools.partial(attention_grad_kernel, layout), out_shap...  14.8 us
    ppermute x6, starting transfers between devices, ctx_reduce(): lax.ppermute(pieces[j], 'ctx', [(i, i ^ j) for i in range(n)])  7.11 us
    ppermute x6, waiting for transfers between devices, ctx_reduce(): lax.ppermute(pieces[j], 'ctx', [(i, i ^ j) for i in range(n)])  6.02 us
    ppermute x12, waiting for transfers between devices, ring_shift(): return lax.ppermute(x, axis, [(i, (i + d) % n) for i in range(n)])  4.8 us
    ppermute x2, starting transfers between devices, ctx_gather(): from_y = lax.ppermute(x, 'ctx', along_y)  3.39 us
    ppermute x2, waiting for transfers between devices, ctx_gather(): from_y = lax.ppermute(x, 'ctx', along_y)  3.19 us
    ppermute x2, starting transfers between devices, ctx_gather(): far_b = lax.ppermute(from_x[:, :, half:], 'ctx', along_y)  3.17 us
  transfers between devices with their start and end apart: 26, of which 7 were waited for; matrix products, arithmetic and copies ran while one was open for 6% of the time, Pallas kernels for 17%

profile of v14, /device:TPU:0, one launch (start us, length us, event | category | flops | bytes accessed | tf_op | source)
XLA Modules:
  0.0 89.8 jit_solution(11579225723217615676)
XLA Ops:
  10.8 3.1 %collective-permute-start.7 = (bf16[2,128,128]{2,1,0:T(8,128)(2,1)S(1)}, bf16[2,128,128]{2,1,0:T(8,128)(2,1)S(1)}, u32[]{:S(2)}, u32[]{:S(2)}) collective-permute-start(bf16[2,128,128]{2,1,0:T(8,128)(2,1)S(1)} %get-tuple-element.45), channel_id=1, source_target_pairs={{0,2},{2,4},{4,6},{6,0},{1,3},{3,5},{5,7},{7,1},{8,10},{10,12},{12... | collective-permute-start | bytes 196616 | tf_op jit(solution)/shard_map/ppermute | solution.py:155
  13.9 2.6 %collective-permute-start.8 = (bf16[2,128,128]{2,1,0:T(8,128)(2,1)S(1)}, bf16[2,128,128]{2,1,0:T(8,128)(2,1)S(1)}, u32[]{:S(2)}, u32[]{:S(2)}) collective-permute-start(bf16[2,128,128]{2,1,0:T(8,128)(2,1)S(1)} %get-tuple-element.44), channel_id=1, source_target_pairs={{0,4},{2,6},{4,0},{6,2},{1,5},{3,7},{5,1},{7,3},{8,12},{10,14},{12... | collective-permute-start | bytes 196616 | tf_op jit(solution)/shard_map/ppermute | solution.py:155
  16.4 1.3 %collective-permute-start.9 = (bf16[2,128,128]{2,1,0:T(8,128)(2,1)S(1)}, bf16[2,128,128]{2,1,0:T(8,128)(2,1)S(1)}, u32[]{:S(2)}, u32[]{:S(2)}) collective-permute-start(bf16[2,128,128]{2,1,0:T(8,128)(2,1)S(1)} %get-tuple-element.43), channel_id=1, source_target_pairs={{0,6},{2,0},{4,2},{6,4},{1,7},{3,1},{5,3},{7,5},{8,14},{10,8},{12,... | collective-permute-start | bytes 196616 | tf_op jit(solution)/shard_map/ppermute | solution.py:155
  19.6 2.8 %collective-permute-start.2 = (bf16[2,128,128]{2,1,0:T(8,128)(2,1)S(1)}, bf16[2,128,128]{2,1,0:T(8,128)(2,1)S(1)}, u32[]{:S(2)}, u32[]{:S(2)}) collective-permute-start(bf16[2,128,128]{2,1,0:T(8,128)(2,1)S(1)} %get-tuple-element.47), channel_id=1, source_target_pairs={{0,6},{2,0},{4,2},{6,4},{1,7},{3,1},{5,3},{7,5},{8,14},{10,8},{12,... | collective-permute-start | bytes 196616 | tf_op jit(solution)/shard_map/ppermute | solution.py:155
  22.5 1.6 %collective-permute-start.11 = (bf16[4,2,128,128]{3,2,1,0:T(8,128)(2,1)S(1)}, bf16[4,2,128,128]{3,2,1,0:T(8,128)(2,1)S(1)}, u32[]{:S(2)}, u32[]{:S(2)}) collective-permute-start(bf16[4,2,128,128]{3,2,1,0:T(8,128)(2,1)S(1)} %pad_maximum_fusion.1.refs_0_.refs_5_), channel_id=1, source_target_pairs={{0,16},{8,24},{16,0},{24,8},{1,17},{9,25},{17,1},{25,9},{2,18},{10... | collective-permute-start | bytes 786440 | tf_op jit(solution)/shard_map/ppermute | solution.py:180
  24.1 1.5 %collective-permute-start.10 = (bf16[4,2,128,128]{3,2,1,0:T(8,128)(2,1)S(1)}, bf16[4,2,128,128]{3,2,1,0:T(8,128)(2,1)S(1)}, u32[]{:S(2)}, u32[]{:S(2)}) collective-permute-start(bf16[4,2,128,128]{3,2,1,0:T(8,128)(2,1)S(1)} %pad_maximum_fusion.1.refs_0_.refs_5_), channel_id=1, source_target_pairs={{0,8},{8,0},{16,24},{24,16},{1,9},{9,1},{17,25},{25,17},{2,10},{10... | collective-permute-start | bytes 786440 | tf_op jit(solution)/shard_map/ppermute | solution.py:179
  26.7 1.8 %collective-permute-start.4 = (bf16[4,2,128,128]{3,2,1,0:T(8,128)(2,1)S(1)}, bf16[4,2,128,128]{3,2,1,0:T(8,128)(2,1)S(1)}, u32[]{:S(2)}, u32[]{:S(2)}) collective-permute-start(bf16[4,2,128,128]{3,2,1,0:T(8,128)(2,1)S(1)} %pad_maximum_fusion.refs_0_.refs_5_), channel_id=1, source_target_pairs={{0,16},{8,24},{16,0},{24,8},{1,17},{9,25},{17,1},{25,9},{2,18},{10... | collective-permute-start | bytes 786440 | tf_op jit(solution)/shard_map/ppermute | solution.py:180
  28.5 1.5 %collective-permute-start.3 = (bf16[4,2,128,128]{3,2,1,0:T(8,128)(2,1)S(1)}, bf16[4,2,128,128]{3,2,1,0:T(8,128)(2,1)S(1)}, u32[]{:S(2)}, u32[]{:S(2)}) collective-permute-start(bf16[4,2,128,128]{3,2,1,0:T(8,128)(2,1)S(1)} %pad_maximum_fusion.refs_0_.refs_5_), channel_id=1, source_target_pairs={{0,8},{8,0},{16,24},{24,16},{1,9},{9,1},{17,25},{25,17},{2,10},{10... | collective-permute-start | bytes 786440 | tf_op jit(solution)/shard_map/ppermute | solution.py:179
  31.2 1.6 %collective-permute-start.13 = (bf16[4,2,64,128]{3,2,1,0:T(8,128)(2,1)S(1)}, bf16[4,2,64,128]{3,2,1,0:T(8,128)(2,1)S(1)}, u32[]{:S(2)}, u32[]{:S(2)}) collective-permute-start(bf16[4,2,64,128]{3,2,1,0:T(8,128)(2,1)S(1)} %slice.79), channel_id=1, source_target_pairs={{0,16},{8,24},{16,0},{24,8},{1,17},{9,25},{17,1},{25,9},{2,18},{10... | collective-permute-start | bytes 393224 | tf_op jit(solution)/shard_map/ppermute | solution.py:183
  32.7 3.2 %collective-permute-done.4.refs_2_.refs_7_ = bf16[4,2,128,128]{3,2,1,0:T(8,128)(2,1)S(1)} collective-permute-done((bf16[4,2,128,128]{3,2,1,0:T(8,128)(2,1)S(1)}, bf16[4,2,128,128]{3,2,1,0:T(8,128)(2,1)S(1)}, u32[]{:S(2)}, u32[]{:S(2)}) %collective-permute-start.4) | collective-permute-done | bytes 262176 | tf_op jit(solution)/shard_map/ppermute | solution.py:180
  36.0 1.8 %collective-permute-start.5 = (bf16[4,2,64,128]{3,2,1,0:T(8,128)(2,1)S(1)}, bf16[4,2,64,128]{3,2,1,0:T(8,128)(2,1)S(1)}, u32[]{:S(2)}, u32[]{:S(2)}) collective-permute-start(bf16[4,2,64,128]{3,2,1,0:T(8,128)(2,1)S(1)} %slice.75), channel_id=1, source_target_pairs={{0,8},{8,0},{16,24},{24,16},{1,9},{9,1},{17,25},{25,17},{2,10},{10... | collective-permute-start | bytes 393224 | tf_op jit(solution)/shard_map/ppermute | solution.py:182
  37.8 1.6 %collective-permute-start.6 = (bf16[4,2,64,128]{3,2,1,0:T(8,128)(2,1)S(1)}, bf16[4,2,64,128]{3,2,1,0:T(8,128)(2,1)S(1)}, u32[]{:S(2)}, u32[]{:S(2)}) collective-permute-start(bf16[4,2,64,128]{3,2,1,0:T(8,128)(2,1)S(1)} %slice.76), channel_id=1, source_target_pairs={{0,16},{8,24},{16,0},{24,8},{1,17},{9,25},{17,1},{25,9},{2,18},{10... | collective-permute-start | bytes 393224 | tf_op jit(solution)/shard_map/ppermute | solution.py:183
  41.4 7.3 %shard_map.112 = (bf16[128,2048]{1,0:T(8,128)(2,1)}, bf16[128,1024]{1,0:T(8,128)(2,1)}, bf16[128,1024]{1,0:T(8,128)(2,1)}, bf16[4,2,128,128]{3,2,1,0:T(8,128)(2,...) custom-call(s32[4]{0:T(128)} %bitcast.90, ...), custom_call_target="tpu_custom_call" | custom-call | flops 1006632960 | bytes 3670016 | tf_op jit(solution)/shard_map/pallas_call | solution.py:136
  50.8 1.6 %collective-permute-start.16 = (bf16[4,2,128,128]{3,2,1,0:T(8,128)(2,1)}, bf16[4,2,128,128]{3,2,1,0:T(8,128)(2,1)S(1)}, u32[]{:S(2)}, u32[]{:S(2)}) collective-permute-start(bf16[4,2,128,128]{3,2,1,0:T(8,128)(2,1)} %get-tuple-element.27), channel_id=1, source_target_pairs={{0,24},{8,16},{16,8},{24,0},{1,25},{9,17},{17,9},{25,1},{2,26},{10... | collective-permute-start | bytes 786440 | tf_op jit(solution)/shard_map/ppermute | solution.py:197
  53.1 7.5 %shard_map.111 = (bf16[128,2048]{1,0:T(8,128)(2,1)}, bf16[128,1024]{1,0:T(8,128)(2,1)}, bf16[128,1024]{1,0:T(8,128)(2,1)}, bf16[4,2,128,128]{3,2,1,0:T(8,128)(2,...) custom-call(s32[4]{0:T(128)} %bitcast.91, ...), custom_call_target="tpu_custom_call" | custom-call | flops 1006632960 | bytes 3670016 | tf_op jit(solution)/shard_map/pallas_call | solution.py:136
  62.6 2.0 %select_bitcast_fusion = bf16[1,1,128,2048]{3,2,1,0:T(8,128)(2,1)} fusion(bf16[128,2048]{1,0:T(8,128)(2,1)} %get-tuple-element.18, bf16[128,2048]{1,0:T(8,128)(2,1)S(1)} %copy-done.1, pred[2048]{0:T(1024)(128)(4,1)S(1)} %fusion.1), kind=kLoop, calls=%fused_computation.4 | loop fusion | flops 262144 | bytes 1574912 | tf_op jit(solution)/shard_map/broadcast_in_dim | solution.py:254
  65.5 1.6 %collective-permute-start.19 = (bf16[4,2,128,128]{3,2,1,0:T(8,128)(2,1)S(1)}, bf16[4,2,128,128]{3,2,1,0:T(8,128)(2,1)S(1)}, u32[]{:S(2)}, u32[]{:S(2)}) collective-permute-start(bf16[4,2,128,128]{3,2,1,0:T(8,128)(2,1)S(1)} %copy-done.14), channel_id=1, source_target_pairs={{0,24},{8,16},{16,8},{24,0},{1,25},{9,17},{17,9},{25,1},{2,26},{10... | collective-permute-start | bytes 786440 | tf_op jit(solution)/shard_map/ppermute | solution.py:197
  67.3 2.7 %collective-permute-done.17 = bf16[4,2,128,128]{3,2,1,0:T(8,128)(2,1)S(1)} collective-permute-done((bf16[4,2,128,128]{3,2,1,0:T(8,128)(2,1)}, bf16[4,2,128,128]{3,2,1,0:T(8,128)(2,1)S(1)}, u32[]{:S(2)}, u32[]{:S(2)}) %collective-permute-start.17) | collective-permute-done | bytes 262176 | tf_op jit(solution)/shard_map/ppermute | solution.py:197
  70.0 3.3 %collective-permute-done.18 = bf16[4,2,128,128]{3,2,1,0:T(8,128)(2,1)S(1)} collective-permute-done((bf16[4,2,128,128]{3,2,1,0:T(8,128)(2,1)}, bf16[4,2,128,128]{3,2,1,0:T(8,128)(2,1)S(1)}, u32[]{:S(2)}, u32[]{:S(2)}) %collective-permute-start.18) | collective-permute-done | bytes 262176 | tf_op jit(solution)/shard_map/ppermute | solution.py:197
  73.5 3.4 %collective-permute-start.20 = (bf16[2,128,128]{2,1,0:T(8,128)(2,1)S(1)}, bf16[2,128,128]{2,1,0:T(8,128)(2,1)S(1)}, u32[]{:S(2)}, u32[]{:S(2)}) collective-permute-start(bf16[2,128,128]{2,1,0:T(8,128)(2,1)S(1)} %get-tuple-element.35), channel_id=1, source_target_pairs={{0,2},{2,4},{4,6},{6,0},{1,3},{3,5},{5,7},{7,1},{8,10},{10,12},{12... | collective-permute-start | bytes 196616 | tf_op jit(solution)/shard_map/ppermute | solution.py:155
  78.2 2.0 %collective-permute-start.23 = (bf16[2,128,128]{2,1,0:T(8,128)(2,1)S(1)}, bf16[2,128,128]{2,1,0:T(8,128)(2,1)S(1)}, u32[]{:S(2)}, u32[]{:S(2)}) collective-permute-start(bf16[2,128,128]{2,1,0:T(8,128)(2,1)S(1)} %get-tuple-element.38), channel_id=1, source_target_pairs={{0,4},{2,6},{4,0},{6,2},{1,5},{3,7},{5,1},{7,3},{8,12},{10,14},{12... | collective-permute-start | bytes 196616 | tf_op jit(solution)/shard_map/ppermute | solution.py:155
  80.2 3.8 %collective-permute-start.24 = (bf16[2,128,128]{2,1,0:T(8,128)(2,1)S(1)}, bf16[2,128,128]{2,1,0:T(8,128)(2,1)S(1)}, u32[]{:S(2)}, u32[]{:S(2)}) collective-permute-start(bf16[2,128,128]{2,1,0:T(8,128)(2,1)S(1)} %get-tuple-element.33), channel_id=1, source_target_pairs={{0,6},{2,0},{4,2},{6,4},{1,7},{3,1},{5,3},{7,5},{8,14},{10,8},{12,... | collective-permute-start | bytes 196616 | tf_op jit(solution)/shard_map/ppermute | solution.py:155
  85.9 2.4 %collective-permute-done.25 = bf16[2,128,128]{2,1,0:T(8,128)(2,1)S(1)} collective-permute-done((bf16[2,128,128]{2,1,0:T(8,128)(2,1)S(1)}, bf16[2,128,128]{2,1,0:T(8,128)(2,1)S(1)}, u32[]{:S(2)}, u32[]{:S(2)}) %collective-permute-start.25) | collective-permute-done | bytes 65568 | tf_op jit(solution)/shard_map/ppermute | solution.py:155
  88.5 1.3 %multiply_add_fusion = f32[2,128,2,256]{3,2,1,0:T(2,128)} fusion(f32[128,2,256]{2,1,0:T(2,128)S(1)} %copy.21, f32[128,2,256]{2,1,0:T(2,128)S(1)} %copy.20, f32[128,2,256]{2,1,0:T(2,128)S(1)} %copy.19, f32[128,2,256]{2,1,0:T(2,128)S(1)} %copy.18, f32[2]{0:T(128)S(1)} %get-tuple-element.51, f32[2]{0:T(128)S(1)} %get-tuple-element.52, ...), kind=kLoop, calls=%fused_computation.1 | loop fusion | flops 917504 | bytes 1572896 | tf_op jit(solution)/shard_map/add | solution.py:250
  (102 shorter events, 17.1 us)
Async XLA Ops:
  10.8 8.8 %collective-permute-start.7 = (bf16[2,128,128]{2,1,0:T(8,128)(2,1)S(1)}, bf16[2,128,128]{2,1,0:T(8,128)(2,1)S(1)}, u32[]{:S(2)}, u32[]{:S(2)}) collective-permute-start(bf16[2,128,128]{2,1,0:T(8,128)(2,1)S(1)} %get-tuple-element.45), channel_id=1, source_target_pairs={{0,2},{2,4},{4,6},{6,0},{1,3},{3,5},{5,7},{7,1},{8,10},{10,12},{12... | collective-permute-start | bytes 196616 | tf_op jit(solution)/shard_map/ppermute | solution.py:155
  13.9 8.6 %collective-permute-start.8 = (bf16[2,128,128]{2,1,0:T(8,128)(2,1)S(1)}, bf16[2,128,128]{2,1,0:T(8,128)(2,1)S(1)}, u32[]{:S(2)}, u32[]{:S(2)}) collective-permute-start(bf16[2,128,128]{2,1,0:T(8,128)(2,1)S(1)} %get-tuple-element.44), channel_id=1, source_target_pairs={{0,4},{2,6},{4,0},{6,2},{1,5},{3,7},{5,1},{7,3},{8,12},{10,14},{12... | collective-permute-start | bytes 196616 | tf_op jit(solution)/shard_map/ppermute | solution.py:155
  16.4 6.0 %collective-permute-start.9 = (bf16[2,128,128]{2,1,0:T(8,128)(2,1)S(1)}, bf16[2,128,128]{2,1,0:T(8,128)(2,1)S(1)}, u32[]{:S(2)}, u32[]{:S(2)}) collective-permute-start(bf16[2,128,128]{2,1,0:T(8,128)(2,1)S(1)} %get-tuple-element.43), channel_id=1, source_target_pairs={{0,6},{2,0},{4,2},{6,4},{1,7},{3,1},{5,3},{7,5},{8,14},{10,8},{12,... | collective-permute-start | bytes 196616 | tf_op jit(solution)/shard_map/ppermute | solution.py:155
  17.8 7.8 %collective-permute-start = (bf16[2,128,128]{2,1,0:T(8,128)(2,1)S(1)}, bf16[2,128,128]{2,1,0:T(8,128)(2,1)S(1)}, u32[]{:S(2)}, u32[]{:S(2)}) collective-permute-start(bf16[2,128,128]{2,1,0:T(8,128)(2,1)S(1)} %get-tuple-element.49), channel_id=1, source_target_pairs={{0,2},{2,4},{4,6},{6,0},{1,3},{3,5},{5,7},{7,1},{8,10},{10,12},{12... | collective-permute-start | bytes 196616 | tf_op jit(solution)/shard_map/ppermute | solution.py:155
  18.5 8.0 %collective-permute-start.1 = (bf16[2,128,128]{2,1,0:T(8,128)(2,1)S(1)}, bf16[2,128,128]{2,1,0:T(8,128)(2,1)S(1)}, u32[]{:S(2)}, u32[]{:S(2)}) collective-permute-start(bf16[2,128,128]{2,1,0:T(8,128)(2,1)S(1)} %get-tuple-element.48), channel_id=1, source_target_pairs={{0,4},{2,6},{4,0},{6,2},{1,5},{3,7},{5,1},{7,3},{8,12},{10,14},{12... | collective-permute-start | bytes 196616 | tf_op jit(solution)/shard_map/ppermute | solution.py:155
  19.6 7.0 %collective-permute-start.2 = (bf16[2,128,128]{2,1,0:T(8,128)(2,1)S(1)}, bf16[2,128,128]{2,1,0:T(8,128)(2,1)S(1)}, u32[]{:S(2)}, u32[]{:S(2)}) collective-permute-start(bf16[2,128,128]{2,1,0:T(8,128)(2,1)S(1)} %get-tuple-element.47), channel_id=1, source_target_pairs={{0,6},{2,0},{4,2},{6,4},{1,7},{3,1},{5,3},{7,5},{8,14},{10,8},{12,... | collective-permute-start | bytes 196616 | tf_op jit(solution)/shard_map/ppermute | solution.py:155
  22.5 7.5 %collective-permute-start.11 = (bf16[4,2,128,128]{3,2,1,0:T(8,128)(2,1)S(1)}, bf16[4,2,128,128]{3,2,1,0:T(8,128)(2,1)S(1)}, u32[]{:S(2)}, u32[]{:S(2)}) collective-permute-start(bf16[4,2,128,128]{3,2,1,0:T(8,128)(2,1)S(1)} %pad_maximum_fusion.1.refs_0_.refs_5_), channel_id=1, source_target_pairs={{0,16},{8,24},{16,0},{24,8},{1,17},{9,25},{17,1},{25,9},{2,18},{10... | collective-permute-start | bytes 786440 | tf_op jit(solution)/shard_map/ppermute | solution.py:180
  24.1 7.0 %collective-permute-start.10 = (bf16[4,2,128,128]{3,2,1,0:T(8,128)(2,1)S(1)}, bf16[4,2,128,128]{3,2,1,0:T(8,128)(2,1)S(1)}, u32[]{:S(2)}, u32[]{:S(2)}) collective-permute-start(bf16[4,2,128,128]{3,2,1,0:T(8,128)(2,1)S(1)} %pad_maximum_fusion.1.refs_0_.refs_5_), channel_id=1, source_target_pairs={{0,8},{8,0},{16,24},{24,16},{1,9},{9,1},{17,25},{25,17},{2,10},{10... | collective-permute-start | bytes 786440 | tf_op jit(solution)/shard_map/ppermute | solution.py:179
  26.7 9.3 %collective-permute-start.4 = (bf16[4,2,128,128]{3,2,1,0:T(8,128)(2,1)S(1)}, bf16[4,2,128,128]{3,2,1,0:T(8,128)(2,1)S(1)}, u32[]{:S(2)}, u32[]{:S(2)}) collective-permute-start(bf16[4,2,128,128]{3,2,1,0:T(8,128)(2,1)S(1)} %pad_maximum_fusion.refs_0_.refs_5_), channel_id=1, source_target_pairs={{0,16},{8,24},{16,0},{24,8},{1,17},{9,25},{17,1},{25,9},{2,18},{10... | collective-permute-start | bytes 786440 | tf_op jit(solution)/shard_map/ppermute | solution.py:180
  28.5 9.3 %collective-permute-start.3 = (bf16[4,2,128,128]{3,2,1,0:T(8,128)(2,1)S(1)}, bf16[4,2,128,128]{3,2,1,0:T(8,128)(2,1)S(1)}, u32[]{:S(2)}, u32[]{:S(2)}) collective-permute-start(bf16[4,2,128,128]{3,2,1,0:T(8,128)(2,1)S(1)} %pad_maximum_fusion.refs_0_.refs_5_), channel_id=1, source_target_pairs={{0,8},{8,0},{16,24},{24,16},{1,9},{9,1},{17,25},{25,17},{2,10},{10... | collective-permute-start | bytes 786440 | tf_op jit(solution)/shard_map/ppermute | solution.py:179
  30.0 10.7 %collective-permute-start.12 = (bf16[4,2,64,128]{3,2,1,0:T(8,128)(2,1)S(1)}, bf16[4,2,64,128]{3,2,1,0:T(8,128)(2,1)S(1)}, u32[]{:S(2)}, u32[]{:S(2)}) collective-permute-start(bf16[4,2,64,128]{3,2,1,0:T(8,128)(2,1)S(1)} %slice.78), channel_id=1, source_target_pairs={{0,8},{8,0},{16,24},{24,16},{1,9},{9,1},{17,25},{25,17},{2,10},{10... | collective-permute-start | bytes 393224 | tf_op jit(solution)/shard_map/ppermute | solution.py:182
  31.2 9.6 %collective-permute-start.13 = (bf16[4,2,64,128]{3,2,1,0:T(8,128)(2,1)S(1)}, bf16[4,2,64,128]{3,2,1,0:T(8,128)(2,1)S(1)}, u32[]{:S(2)}, u32[]{:S(2)}) collective-permute-start(bf16[4,2,64,128]{3,2,1,0:T(8,128)(2,1)S(1)} %slice.79), channel_id=1, source_target_pairs={{0,16},{8,24},{16,0},{24,8},{1,17},{9,25},{17,1},{25,9},{2,18},{10... | collective-permute-start | bytes 393224 | tf_op jit(solution)/shard_map/ppermute | solution.py:183
  36.0 16.4 %collective-permute-start.5 = (bf16[4,2,64,128]{3,2,1,0:T(8,128)(2,1)S(1)}, bf16[4,2,64,128]{3,2,1,0:T(8,128)(2,1)S(1)}, u32[]{:S(2)}, u32[]{:S(2)}) collective-permute-start(bf16[4,2,64,128]{3,2,1,0:T(8,128)(2,1)S(1)} %slice.75), channel_id=1, source_target_pairs={{0,8},{8,0},{16,24},{24,16},{1,9},{9,1},{17,25},{25,17},{2,10},{10... | collective-permute-start | bytes 393224 | tf_op jit(solution)/shard_map/ppermute | solution.py:182
  37.8 14.5 %collective-permute-start.6 = (bf16[4,2,64,128]{3,2,1,0:T(8,128)(2,1)S(1)}, bf16[4,2,64,128]{3,2,1,0:T(8,128)(2,1)S(1)}, u32[]{:S(2)}, u32[]{:S(2)}) collective-permute-start(bf16[4,2,64,128]{3,2,1,0:T(8,128)(2,1)S(1)} %slice.76), channel_id=1, source_target_pairs={{0,16},{8,24},{16,0},{24,8},{1,17},{9,25},{17,1},{25,9},{2,18},{10... | collective-permute-start | bytes 393224 | tf_op jit(solution)/shard_map/ppermute | solution.py:183
  48.8 16.7 %collective-permute-start.14 = (bf16[4,2,128,128]{3,2,1,0:T(8,128)(2,1)}, bf16[4,2,128,128]{3,2,1,0:T(8,128)(2,1)S(1)}, u32[]{:S(2)}, u32[]{:S(2)}) collective-permute-start(bf16[4,2,128,128]{3,2,1,0:T(8,128)(2,1)} %get-tuple-element.25), channel_id=1, source_target_pairs={{0,8},{8,0},{16,24},{24,16},{1,9},{9,1},{17,25},{25,17},{2,10},{10... | collective-permute-start | bytes 786440 | tf_op jit(solution)/shard_map/ppermute | solution.py:197
  49.9 17.2 %collective-permute-start.15 = (bf16[4,2,128,128]{3,2,1,0:T(8,128)(2,1)}, bf16[4,2,128,128]{3,2,1,0:T(8,128)(2,1)S(1)}, u32[]{:S(2)}, u32[]{:S(2)}) collective-permute-start(bf16[4,2,128,128]{3,2,1,0:T(8,128)(2,1)} %get-tuple-element.26), channel_id=1, source_target_pairs={{0,16},{8,24},{16,0},{24,8},{1,17},{9,25},{17,1},{25,9},{2,18},{10... | collective-permute-start | bytes 786440 | tf_op jit(solution)/shard_map/ppermute | solution.py:197
  50.8 16.3 %collective-permute-start.16 = (bf16[4,2,128,128]{3,2,1,0:T(8,128)(2,1)}, bf16[4,2,128,128]{3,2,1,0:T(8,128)(2,1)S(1)}, u32[]{:S(2)}, u32[]{:S(2)}) collective-permute-start(bf16[4,2,128,128]{3,2,1,0:T(8,128)(2,1)} %get-tuple-element.27), channel_id=1, source_target_pairs={{0,24},{8,16},{16,8},{24,0},{1,25},{9,17},{17,9},{25,1},{2,26},{10... | collective-permute-start | bytes 786440 | tf_op jit(solution)/shard_map/ppermute | solution.py:197
  60.6 9.4 %collective-permute-start.17 = (bf16[4,2,128,128]{3,2,1,0:T(8,128)(2,1)}, bf16[4,2,128,128]{3,2,1,0:T(8,128)(2,1)S(1)}, u32[]{:S(2)}, u32[]{:S(2)}) collective-permute-start(bf16[4,2,128,128]{3,2,1,0:T(8,128)(2,1)} %get-tuple-element.29), channel_id=1, source_target_pairs={{0,8},{8,0},{16,24},{24,16},{1,9},{9,1},{17,25},{25,17},{2,10},{10... | collective-permute-start | bytes 786440 | tf_op jit(solution)/shard_map/ppermute | solution.py:197
  61.7 11.6 %collective-permute-start.18 = (bf16[4,2,128,128]{3,2,1,0:T(8,128)(2,1)}, bf16[4,2,128,128]{3,2,1,0:T(8,128)(2,1)S(1)}, u32[]{:S(2)}, u32[]{:S(2)}) collective-permute-start(bf16[4,2,128,128]{3,2,1,0:T(8,128)(2,1)} %get-tuple-element.30), channel_id=1, source_target_pairs={{0,16},{8,24},{16,0},{24,8},{1,17},{9,25},{17,1},{25,9},{2,18},{10... | collective-permute-start | bytes 786440 | tf_op jit(solution)/shard_map/ppermute | solution.py:197
  65.5 7.8 %collective-permute-start.19 = (bf16[4,2,128,128]{3,2,1,0:T(8,128)(2,1)S(1)}, bf16[4,2,128,128]{3,2,1,0:T(8,128)(2,1)S(1)}, u32[]{:S(2)}, u32[]{:S(2)}) collective-permute-start(bf16[4,2,128,128]{3,2,1,0:T(8,128)(2,1)S(1)} %copy-done.14), channel_id=1, source_target_pairs={{0,24},{8,16},{16,8},{24,0},{1,25},{9,17},{17,9},{25,1},{2,26},{10... | collective-permute-start | bytes 786440 | tf_op jit(solution)/shard_map/ppermute | solution.py:197
  73.5 10.5 %collective-permute-start.20 = (bf16[2,128,128]{2,1,0:T(8,128)(2,1)S(1)}, bf16[2,128,128]{2,1,0:T(8,128)(2,1)S(1)}, u32[]{:S(2)}, u32[]{:S(2)}) collective-permute-start(bf16[2,128,128]{2,1,0:T(8,128)(2,1)S(1)} %get-tuple-element.35), channel_id=1, source_target_pairs={{0,2},{2,4},{4,6},{6,0},{1,3},{3,5},{5,7},{7,1},{8,10},{10,12},{12... | collective-permute-start | bytes 196616 | tf_op jit(solution)/shard_map/ppermute | solution.py:155
  76.9 7.1 %collective-permute-start.21 = (bf16[2,128,128]{2,1,0:T(8,128)(2,1)S(1)}, bf16[2,128,128]{2,1,0:T(8,128)(2,1)S(1)}, u32[]{:S(2)}, u32[]{:S(2)}) collective-permute-start(bf16[2,128,128]{2,1,0:T(8,128)(2,1)S(1)} %get-tuple-element.39), channel_id=1, source_target_pairs={{0,2},{2,4},{4,6},{6,0},{1,3},{3,5},{5,7},{7,1},{8,10},{10,12},{12... | collective-permute-start | bytes 196616 | tf_op jit(solution)/shard_map/ppermute | solution.py:155
  77.2 7.0 %collective-permute-start.22 = (bf16[2,128,128]{2,1,0:T(8,128)(2,1)S(1)}, bf16[2,128,128]{2,1,0:T(8,128)(2,1)S(1)}, u32[]{:S(2)}, u32[]{:S(2)}) collective-permute-start(bf16[2,128,128]{2,1,0:T(8,128)(2,1)S(1)} %get-tuple-element.34), channel_id=1, source_target_pairs={{0,4},{2,6},{4,0},{6,2},{1,5},{3,7},{5,1},{7,3},{8,12},{10,14},{12... | collective-permute-start | bytes 196616 | tf_op jit(solution)/shard_map/ppermute | solution.py:155
  78.2 6.4 %collective-permute-start.23 = (bf16[2,128,128]{2,1,0:T(8,128)(2,1)S(1)}, bf16[2,128,128]{2,1,0:T(8,128)(2,1)S(1)}, u32[]{:S(2)}, u32[]{:S(2)}) collective-permute-start(bf16[2,128,128]{2,1,0:T(8,128)(2,1)S(1)} %get-tuple-element.38), channel_id=1, source_target_pairs={{0,4},{2,6},{4,0},{6,2},{1,5},{3,7},{5,1},{7,3},{8,12},{10,14},{12... | collective-permute-start | bytes 196616 | tf_op jit(solution)/shard_map/ppermute | solution.py:155
  (21 other events, 67.8 us)

commit v15 on v12

--- a/solution.py
+++ b/solution.py
@@ -23,14 +23,14 @@
 
 def attention_grad_kernel(layout, blocks_ref, length_ref, place_ref, q_ref, do_ref, *refs):
     n_in, n_slots, slot_rows, xor_slots, out_ranges, aliased = layout
-    kp_refs, vp_refs = refs[:n_in], refs[n_in:2 * n_in]
-    kr_ref, vr_ref = refs[2 * n_in:2 * n_in + 2]
-    outs = refs[2 * n_in + 2 + (3 if aliased else 0):]
+    kv_refs = refs[:n_in]
+    kr_ref, vr_ref = refs[n_in:n_in + 2]
+    outs = refs[n_in + 2 + (3 if aliased else 0):]
     dq_ref, dkr_ref, dvr_ref = outs[:3]
     piece_refs = outs[3:]
     resp_rows = q_ref.shape[0]
-    kp = jnp.concatenate([r[...] for r in kp_refs], 0)
-    vp = jnp.concatenate([r[...] for r in vp_refs], 0)
+    kp = jnp.concatenate([r[0] for r in kv_refs], 0)
+    vp = jnp.concatenate([r[1] for r in kv_refs], 0)
     pre_rows = kp.shape[0]
     kr = kr_ref[...]
     vr = vr_ref[...]
@@ -108,15 +108,15 @@
     def head(g, r):
         return ((r[0] + n_pair - g // per_chunk) % n_pair) * chunk_heads + first_head + g % per_chunk
 
-    def piece_spec(rows, kv):
-        return pl.BlockSpec((None, None, rows, HEAD_DIM), lambda g, b, n, r: (g // per_chunk, kv, 0, g % per_chunk))
+    def piece_spec(rows):
+        return pl.BlockSpec((None, 2, rows, HEAD_DIM), lambda g, b, n, r: (g // per_chunk, 0, 0, g % per_chunk))
 
     qspec = pl.BlockSpec((resp_rows, GROUP * HEAD_DIM), lambda g, b, n, r: (0, head(g, r)))
     rspec = pl.BlockSpec((resp_rows, HEAD_DIM), lambda g, b, n, r: (0, head(g, r)))
     in_specs = [qspec, qspec]
-    in_specs += [piece_spec(p.shape[2], 0) for p in pieces] + [piece_spec(p.shape[2], 1) for p in pieces]
+    in_specs += [piece_spec(p.shape[2]) for p in pieces]
     in_specs += [rspec, rspec]
-    operands = [blocks, length, place, q, do] + list(pieces) + list(pieces) + [kr, vr]
+    operands = [blocks, length, place, q, do] + list(pieces) + [kr, vr]
     aliases = {}
     if earlier is not None:
         in_specs += [pl.BlockSpec(memory_space=pl.ANY)] * 3

time: 85.1 us -> 85.1 us (level)
  no operation moved by 1% of the time
where the time goes in v15:
time: 85.1 us; the launch traced here: 84.7 us
  starting transfers between devices  42.1 us (49%)
  Pallas kernels  14.8 us (17%)
  between operations  9.53 us (11%)
  waiting for transfers between devices  7.39 us (9%)
  other arithmetic  5.56 us (7%)
  local copies, waits for them, and re-layouts  5.34 us (6%)
    ppermute x12, starting transfers between devices, ring_shift(): return lax.ppermute(x, axis, [(i, (i + d) % n) for i in range(n)])  22.5 us
    pallas_call x2, Pallas kernels, attention_grads(): pl.pallas_call(functools.partial(attention_grad_kernel, layout), out_shap...  14.8 us
    ppermute x6, starting transfers between devices, ctx_reduce(): lax.ppermute(pieces[j], 'ctx', [(i, i ^ j) for i in range(n)])  7.11 us
    ppermute x12, waiting for transfers between devices, ring_shift(): return lax.ppermute(x, axis, [(i, (i + d) % n) for i in range(n)])  3.84 us
    ppermute x2, starting transfers between devices, ctx_gather(): from_y = lax.ppermute(x, 'ctx', along_y)  3.39 us
    ppermute x2, waiting for transfers between devices, ctx_gather(): from_y = lax.ppermute(x, 'ctx', along_y)  3.19 us
    ppermute x2, starting transfers between devices, ctx_gather(): far_b = lax.ppermute(from_x[:, :, half:], 'ctx', along_y)  3.17 us
    unnamed x39, local copies, waits for them, and re-layouts  3.13 us
  transfers between devices with their start and end apart: 26, of which 5 were waited for; matrix products, arithmetic and copies ran while one was open for 6% of the time, Pallas kernels for 17%

profile of v15, /device:TPU:0, one launch (start us, length us, event | category | flops | bytes accessed | tf_op | source)
XLA Modules:
  0.0 84.7 jit_solution(12218207617877642022)
XLA Ops:
  10.8 3.1 %collective-permute-start = (bf16[2,128,128]{2,1,0:T(8,128)(2,1)S(1)}, bf16[2,128,128]{2,1,0:T(8,128)(2,1)S(1)}, u32[]{:S(2)}, u32[]{:S(2)}) collective-permute-start(bf16[2,128,128]{2,1,0:T(8,128)(2,1)S(1)} %get-tuple-element.49), channel_id=1, source_target_pairs={{0,2},{2,4},{4,6},{6,0},{1,3},{3,5},{5,7},{7,1},{8,10},{10,12},{12... | collective-permute-start | bytes 196616 | tf_op jit(solution)/shard_map/ppermute | solution.py:155
  13.9 2.6 %collective-permute-start.1 = (bf16[2,128,128]{2,1,0:T(8,128)(2,1)S(1)}, bf16[2,128,128]{2,1,0:T(8,128)(2,1)S(1)}, u32[]{:S(2)}, u32[]{:S(2)}) collective-permute-start(bf16[2,128,128]{2,1,0:T(8,128)(2,1)S(1)} %get-tuple-element.48), channel_id=1, source_target_pairs={{0,4},{2,6},{4,0},{6,2},{1,5},{3,7},{5,1},{7,3},{8,12},{10,14},{12... | collective-permute-start | bytes 196616 | tf_op jit(solution)/shard_map/ppermute | solution.py:155
  16.4 1.3 %collective-permute-start.2 = (bf16[2,128,128]{2,1,0:T(8,128)(2,1)S(1)}, bf16[2,128,128]{2,1,0:T(8,128)(2,1)S(1)}, u32[]{:S(2)}, u32[]{:S(2)}) collective-permute-start(bf16[2,128,128]{2,1,0:T(8,128)(2,1)S(1)} %get-tuple-element.47), channel_id=1, source_target_pairs={{0,6},{2,0},{4,2},{6,4},{1,7},{3,1},{5,3},{7,5},{8,14},{10,8},{12,... | collective-permute-start | bytes 196616 | tf_op jit(solution)/shard_map/ppermute | solution.py:155
  19.6 2.8 %collective-permute-start.9 = (bf16[2,128,128]{2,1,0:T(8,128)(2,1)S(1)}, bf16[2,128,128]{2,1,0:T(8,128)(2,1)S(1)}, u32[]{:S(2)}, u32[]{:S(2)}) collective-permute-start(bf16[2,128,128]{2,1,0:T(8,128)(2,1)S(1)} %get-tuple-element.43), channel_id=1, source_target_pairs={{0,6},{2,0},{4,2},{6,4},{1,7},{3,1},{5,3},{7,5},{8,14},{10,8},{12,... | collective-permute-start | bytes 196616 | tf_op jit(solution)/shard_map/ppermute | solution.py:155
  22.5 1.6 %collective-permute-start.4 = (bf16[4,2,128,128]{3,2,1,0:T(8,128)(2,1)S(1)}, bf16[4,2,128,128]{3,2,1,0:T(8,128)(2,1)S(1)}, u32[]{:S(2)}, u32[]{:S(2)}) collective-permute-start(bf16[4,2,128,128]{3,2,1,0:T(8,128)(2,1)S(1)} %pad_maximum_fusion.1.refs_0_), channel_id=1, source_target_pairs={{0,16},{8,24},{16,0},{24,8},{1,17},{9,25},{17,1},{25,9},{2,18},{10... | collective-permute-start | bytes 786440 | tf_op jit(solution)/shard_map/ppermute | solution.py:180
  24.1 1.5 %collective-permute-start.3 = (bf16[4,2,128,128]{3,2,1,0:T(8,128)(2,1)S(1)}, bf16[4,2,128,128]{3,2,1,0:T(8,128)(2,1)S(1)}, u32[]{:S(2)}, u32[]{:S(2)}) collective-permute-start(bf16[4,2,128,128]{3,2,1,0:T(8,128)(2,1)S(1)} %pad_maximum_fusion.1.refs_0_), channel_id=1, source_target_pairs={{0,8},{8,0},{16,24},{24,16},{1,9},{9,1},{17,25},{25,17},{2,10},{10... | collective-permute-start | bytes 786440 | tf_op jit(solution)/shard_map/ppermute | solution.py:179
  26.7 1.8 %collective-permute-start.11 = (bf16[4,2,128,128]{3,2,1,0:T(8,128)(2,1)S(1)}, bf16[4,2,128,128]{3,2,1,0:T(8,128)(2,1)S(1)}, u32[]{:S(2)}, u32[]{:S(2)}) collective-permute-start(bf16[4,2,128,128]{3,2,1,0:T(8,128)(2,1)S(1)} %pad_maximum_fusion.2.refs_0_), channel_id=1, source_target_pairs={{0,16},{8,24},{16,0},{24,8},{1,17},{9,25},{17,1},{25,9},{2,18},{10... | collective-permute-start | bytes 786440 | tf_op jit(solution)/shard_map/ppermute | solution.py:180
  28.5 1.5 %collective-permute-start.10 = (bf16[4,2,128,128]{3,2,1,0:T(8,128)(2,1)S(1)}, bf16[4,2,128,128]{3,2,1,0:T(8,128)(2,1)S(1)}, u32[]{:S(2)}, u32[]{:S(2)}) collective-permute-start(bf16[4,2,128,128]{3,2,1,0:T(8,128)(2,1)S(1)} %pad_maximum_fusion.2.refs_0_), channel_id=1, source_target_pairs={{0,8},{8,0},{16,24},{24,16},{1,9},{9,1},{17,25},{25,17},{2,10},{10... | collective-permute-start | bytes 786440 | tf_op jit(solution)/shard_map/ppermute | solution.py:179
  31.2 1.6 %collective-permute-start.6 = (bf16[4,2,64,128]{3,2,1,0:T(8,128)(2,1)S(1)}, bf16[4,2,64,128]{3,2,1,0:T(8,128)(2,1)S(1)}, u32[]{:S(2)}, u32[]{:S(2)}) collective-permute-start(bf16[4,2,64,128]{3,2,1,0:T(8,128)(2,1)S(1)} %slice.80), channel_id=1, source_target_pairs={{0,16},{8,24},{16,0},{24,8},{1,17},{9,25},{17,1},{25,9},{2,18},{10... | collective-permute-start | bytes 393224 | tf_op jit(solution)/shard_map/ppermute | solution.py:183
  32.8 3.2 %collective-permute-done.11.refs_2_ = bf16[4,2,128,128]{3,2,1,0:T(8,128)(2,1)S(1)} collective-permute-done((bf16[4,2,128,128]{3,2,1,0:T(8,128)(2,1)S(1)}, bf16[4,2,128,128]{3,2,1,0:T(8,128)(2,1)S(1)}, u32[]{:S(2)}, u32[]{:S(2)}) %collective-permute-start.11) | collective-permute-done | bytes 262176 | tf_op jit(solution)/shard_map/ppermute | solution.py:180
  36.0 1.8 %collective-permute-start.12 = (bf16[4,2,64,128]{3,2,1,0:T(8,128)(2,1)S(1)}, bf16[4,2,64,128]{3,2,1,0:T(8,128)(2,1)S(1)}, u32[]{:S(2)}, u32[]{:S(2)}) collective-permute-start(bf16[4,2,64,128]{3,2,1,0:T(8,128)(2,1)S(1)} %slice.82), channel_id=1, source_target_pairs={{0,8},{8,0},{16,24},{24,16},{1,9},{9,1},{17,25},{25,17},{2,10},{10... | collective-permute-start | bytes 393224 | tf_op jit(solution)/shard_map/ppermute | solution.py:182
  37.8 1.6 %collective-permute-start.13 = (bf16[4,2,64,128]{3,2,1,0:T(8,128)(2,1)S(1)}, bf16[4,2,64,128]{3,2,1,0:T(8,128)(2,1)S(1)}, u32[]{:S(2)}, u32[]{:S(2)}) collective-permute-start(bf16[4,2,64,128]{3,2,1,0:T(8,128)(2,1)S(1)} %slice.83), channel_id=1, source_target_pairs={{0,16},{8,24},{16,0},{24,8},{1,17},{9,25},{17,1},{25,9},{2,18},{10... | collective-permute-start | bytes 393224 | tf_op jit(solution)/shard_map/ppermute | solution.py:183
  41.3 7.4 %shard_map.111 = (bf16[128,2048]{1,0:T(8,128)(2,1)}, bf16[128,1024]{1,0:T(8,128)(2,1)}, bf16[128,1024]{1,0:T(8,128)(2,1)}, bf16[4,2,128,128]{3,2,1,0:T(8,128)(2,...) custom-call(s32[4]{0:T(128)} %bitcast.104, ...), custom_call_target="tpu_custom_call" | custom-call | flops 1006632960 | bytes 3670016 | tf_op jit(solution)/shard_map/pallas_call | solution.py:136
  48.7 1.2 %collective-permute-start.20 = (bf16[4,2,128,128]{3,2,1,0:T(8,128)(2,1)}, bf16[4,2,128,128]{3,2,1,0:T(8,128)(2,1)S(1)}, u32[]{:S(2)}, u32[]{:S(2)}) collective-permute-start(bf16[4,2,128,128]{3,2,1,0:T(8,128)(2,1)} %get-tuple-element.29), channel_id=1, source_target_pairs={{0,8},{8,0},{16,24},{24,16},{1,9},{9,1},{17,25},{25,17},{2,10},{10... | collective-permute-start | bytes 786440 | tf_op jit(solution)/shard_map/ppermute | solution.py:197
  50.7 1.6 %collective-permute-start.22 = (bf16[4,2,128,128]{3,2,1,0:T(8,128)(2,1)}, bf16[4,2,128,128]{3,2,1,0:T(8,128)(2,1)S(1)}, u32[]{:S(2)}, u32[]{:S(2)}) collective-permute-start(bf16[4,2,128,128]{3,2,1,0:T(8,128)(2,1)} %get-tuple-element.31), channel_id=1, source_target_pairs={{0,24},{8,16},{16,8},{24,0},{1,25},{9,17},{17,9},{25,1},{2,26},{10... | collective-permute-start | bytes 786440 | tf_op jit(solution)/shard_map/ppermute | solution.py:197
  53.0 7.4 %shard_map.112 = (bf16[128,2048]{1,0:T(8,128)(2,1)}, bf16[128,1024]{1,0:T(8,128)(2,1)}, bf16[128,1024]{1,0:T(8,128)(2,1)}, bf16[4,2,128,128]{3,2,1,0:T(8,128)(2,...) custom-call(s32[4]{0:T(128)} %bitcast.105, ...), custom_call_target="tpu_custom_call" | custom-call | flops 1006632960 | bytes 3670016 | tf_op jit(solution)/shard_map/pallas_call | solution.py:136
  60.4 1.2 %collective-permute-start.14 = (bf16[4,2,128,128]{3,2,1,0:T(8,128)(2,1)}, bf16[4,2,128,128]{3,2,1,0:T(8,128)(2,1)S(1)}, u32[]{:S(2)}, u32[]{:S(2)}) collective-permute-start(bf16[4,2,128,128]{3,2,1,0:T(8,128)(2,1)} %get-tuple-element.25), channel_id=1, source_target_pairs={{0,8},{8,0},{16,24},{24,16},{1,9},{9,1},{17,25},{25,17},{2,10},{10... | collective-permute-start | bytes 786440 | tf_op jit(solution)/shard_map/ppermute | solution.py:197
  62.4 2.0 %select_bitcast_fusion = bf16[1,1,128,2048]{3,2,1,0:T(8,128)(2,1)} fusion(bf16[128,2048]{1,0:T(8,128)(2,1)S(1)} %copy-done.1, bf16[128,2048]{1,0:T(8,128)(2,1)} %get-tuple-element.19, pred[2048]{0:T(1024)(128)(4,1)S(1)} %fusion.1), kind=kLoop, calls=%fused_computation.4 | loop fusion | flops 262144 | bytes 1574912 | tf_op jit(solution)/shard_map/broadcast_in_dim | solution.py:254
  65.4 1.5 %collective-permute-start.16 = (bf16[4,2,128,128]{3,2,1,0:T(8,128)(2,1)S(1)}, bf16[4,2,128,128]{3,2,1,0:T(8,128)(2,1)S(1)}, u32[]{:S(2)}, u32[]{:S(2)}) collective-permute-start(bf16[4,2,128,128]{3,2,1,0:T(8,128)(2,1)S(1)} %copy-done.14), channel_id=1, source_target_pairs={{0,24},{8,16},{16,8},{24,0},{1,25},{9,17},{17,9},{25,1},{2,26},{10... | collective-permute-start | bytes 786440 | tf_op jit(solution)/shard_map/ppermute | solution.py:197
  67.2 3.3 %collective-permute-start.23 = (bf16[2,128,128]{2,1,0:T(8,128)(2,1)S(1)}, bf16[2,128,128]{2,1,0:T(8,128)(2,1)S(1)}, u32[]{:S(2)}, u32[]{:S(2)}) collective-permute-start(bf16[2,128,128]{2,1,0:T(8,128)(2,1)S(1)} %get-tuple-element.39), channel_id=1, source_target_pairs={{0,2},{2,4},{4,6},{6,0},{1,3},{3,5},{5,7},{7,1},{8,10},{10,12},{12... | collective-permute-start | bytes 196616 | tf_op jit(solution)/shard_map/ppermute | solution.py:155
  70.8 2.2 %collective-permute-start.25 = (bf16[2,128,128]{2,1,0:T(8,128)(2,1)S(1)}, bf16[2,128,128]{2,1,0:T(8,128)(2,1)S(1)}, u32[]{:S(2)}, u32[]{:S(2)}) collective-permute-start(bf16[2,128,128]{2,1,0:T(8,128)(2,1)S(1)} %get-tuple-element.37), channel_id=1, source_target_pairs={{0,6},{2,0},{4,2},{6,4},{1,7},{3,1},{5,3},{7,5},{8,14},{10,8},{12,... | collective-permute-start | bytes 196616 | tf_op jit(solution)/shard_map/ppermute | solution.py:155
  73.6 3.3 %collective-permute-start.17 = (bf16[2,128,128]{2,1,0:T(8,128)(2,1)S(1)}, bf16[2,128,128]{2,1,0:T(8,128)(2,1)S(1)}, u32[]{:S(2)}, u32[]{:S(2)}) collective-permute-start(bf16[2,128,128]{2,1,0:T(8,128)(2,1)S(1)} %get-tuple-element.35), channel_id=1, source_target_pairs={{0,2},{2,4},{4,6},{6,0},{1,3},{3,5},{5,7},{7,1},{8,10},{10,12},{12... | collective-permute-start | bytes 196616 | tf_op jit(solution)/shard_map/ppermute | solution.py:155
  77.6 1.9 %collective-permute-start.19 = (bf16[2,128,128]{2,1,0:T(8,128)(2,1)S(1)}, bf16[2,128,128]{2,1,0:T(8,128)(2,1)S(1)}, u32[]{:S(2)}, u32[]{:S(2)}) collective-permute-start(bf16[2,128,128]{2,1,0:T(8,128)(2,1)S(1)} %get-tuple-element.33), channel_id=1, source_target_pairs={{0,6},{2,0},{4,2},{6,4},{1,7},{3,1},{5,3},{7,5},{8,14},{10,8},{12,... | collective-permute-start | bytes 196616 | tf_op jit(solution)/shard_map/ppermute | solution.py:155
  79.8 2.6 %collective-permute-done.18 = bf16[2,128,128]{2,1,0:T(8,128)(2,1)S(1)} collective-permute-done((bf16[2,128,128]{2,1,0:T(8,128)(2,1)S(1)}, bf16[2,128,128]{2,1,0:T(8,128)(2,1)S(1)}, u32[]{:S(2)}, u32[]{:S(2)}) %collective-permute-start.18) | collective-permute-done | bytes 65568 | tf_op jit(solution)/shard_map/ppermute | solution.py:155
  (109 shorter events, 15.1 us)
Async XLA Ops:
  10.8 8.8 %collective-permute-start = (bf16[2,128,128]{2,1,0:T(8,128)(2,1)S(1)}, bf16[2,128,128]{2,1,0:T(8,128)(2,1)S(1)}, u32[]{:S(2)}, u32[]{:S(2)}) collective-permute-start(bf16[2,128,128]{2,1,0:T(8,128)(2,1)S(1)} %get-tuple-element.49), channel_id=1, source_target_pairs={{0,2},{2,4},{4,6},{6,0},{1,3},{3,5},{5,7},{7,1},{8,10},{10,12},{12... | collective-permute-start | bytes 196616 | tf_op jit(solution)/shard_map/ppermute | solution.py:155
  13.9 8.6 %collective-permute-start.1 = (bf16[2,128,128]{2,1,0:T(8,128)(2,1)S(1)}, bf16[2,128,128]{2,1,0:T(8,128)(2,1)S(1)}, u32[]{:S(2)}, u32[]{:S(2)}) collective-permute-start(bf16[2,128,128]{2,1,0:T(8,128)(2,1)S(1)} %get-tuple-element.48), channel_id=1, source_target_pairs={{0,4},{2,6},{4,0},{6,2},{1,5},{3,7},{5,1},{7,3},{8,12},{10,14},{12... | collective-permute-start | bytes 196616 | tf_op jit(solution)/shard_map/ppermute | solution.py:155
  16.4 6.0 %collective-permute-start.2 = (bf16[2,128,128]{2,1,0:T(8,128)(2,1)S(1)}, bf16[2,128,128]{2,1,0:T(8,128)(2,1)S(1)}, u32[]{:S(2)}, u32[]{:S(2)}) collective-permute-start(bf16[2,128,128]{2,1,0:T(8,128)(2,1)S(1)} %get-tuple-element.47), channel_id=1, source_target_pairs={{0,6},{2,0},{4,2},{6,4},{1,7},{3,1},{5,3},{7,5},{8,14},{10,8},{12,... | collective-permute-start | bytes 196616 | tf_op jit(solution)/shard_map/ppermute | solution.py:155
  17.8 7.8 %collective-permute-start.7 = (bf16[2,128,128]{2,1,0:T(8,128)(2,1)S(1)}, bf16[2,128,128]{2,1,0:T(8,128)(2,1)S(1)}, u32[]{:S(2)}, u32[]{:S(2)}) collective-permute-start(bf16[2,128,128]{2,1,0:T(8,128)(2,1)S(1)} %get-tuple-element.45), channel_id=1, source_target_pairs={{0,2},{2,4},{4,6},{6,0},{1,3},{3,5},{5,7},{7,1},{8,10},{10,12},{12... | collective-permute-start | bytes 196616 | tf_op jit(solution)/shard_map/ppermute | solution.py:155
  18.5 8.0 %collective-permute-start.8 = (bf16[2,128,128]{2,1,0:T(8,128)(2,1)S(1)}, bf16[2,128,128]{2,1,0:T(8,128)(2,1)S(1)}, u32[]{:S(2)}, u32[]{:S(2)}) collective-permute-start(bf16[2,128,128]{2,1,0:T(8,128)(2,1)S(1)} %get-tuple-element.44), channel_id=1, source_target_pairs={{0,4},{2,6},{4,0},{6,2},{1,5},{3,7},{5,1},{7,3},{8,12},{10,14},{12... | collective-permute-start | bytes 196616 | tf_op jit(solution)/shard_map/ppermute | solution.py:155
  19.6 7.0 %collective-permute-start.9 = (bf16[2,128,128]{2,1,0:T(8,128)(2,1)S(1)}, bf16[2,128,128]{2,1,0:T(8,128)(2,1)S(1)}, u32[]{:S(2)}, u32[]{:S(2)}) collective-permute-start(bf16[2,128,128]{2,1,0:T(8,128)(2,1)S(1)} %get-tuple-element.43), channel_id=1, source_target_pairs={{0,6},{2,0},{4,2},{6,4},{1,7},{3,1},{5,3},{7,5},{8,14},{10,8},{12,... | collective-permute-start | bytes 196616 | tf_op jit(solution)/shard_map/ppermute | solution.py:155
  22.5 7.5 %collective-permute-start.4 = (bf16[4,2,128,128]{3,2,1,0:T(8,128)(2,1)S(1)}, bf16[4,2,128,128]{3,2,1,0:T(8,128)(2,1)S(1)}, u32[]{:S(2)}, u32[]{:S(2)}) collective-permute-start(bf16[4,2,128,128]{3,2,1,0:T(8,128)(2,1)S(1)} %pad_maximum_fusion.1.refs_0_), channel_id=1, source_target_pairs={{0,16},{8,24},{16,0},{24,8},{1,17},{9,25},{17,1},{25,9},{2,18},{10... | collective-permute-start | bytes 786440 | tf_op jit(solution)/shard_map/ppermute | solution.py:180
  24.1 7.0 %collective-permute-start.3 = (bf16[4,2,128,128]{3,2,1,0:T(8,128)(2,1)S(1)}, bf16[4,2,128,128]{3,2,1,0:T(8,128)(2,1)S(1)}, u32[]{:S(2)}, u32[]{:S(2)}) collective-permute-start(bf16[4,2,128,128]{3,2,1,0:T(8,128)(2,1)S(1)} %pad_maximum_fusion.1.refs_0_), channel_id=1, source_target_pairs={{0,8},{8,0},{16,24},{24,16},{1,9},{9,1},{17,25},{25,17},{2,10},{10... | collective-permute-start | bytes 786440 | tf_op jit(solution)/shard_map/ppermute | solution.py:179
  26.7 9.3 %collective-permute-start.11 = (bf16[4,2,128,128]{3,2,1,0:T(8,128)(2,1)S(1)}, bf16[4,2,128,128]{3,2,1,0:T(8,128)(2,1)S(1)}, u32[]{:S(2)}, u32[]{:S(2)}) collective-permute-start(bf16[4,2,128,128]{3,2,1,0:T(8,128)(2,1)S(1)} %pad_maximum_fusion.2.refs_0_), channel_id=1, source_target_pairs={{0,16},{8,24},{16,0},{24,8},{1,17},{9,25},{17,1},{25,9},{2,18},{10... | collective-permute-start | bytes 786440 | tf_op jit(solution)/shard_map/ppermute | solution.py:180
  28.5 9.3 %collective-permute-start.10 = (bf16[4,2,128,128]{3,2,1,0:T(8,128)(2,1)S(1)}, bf16[4,2,128,128]{3,2,1,0:T(8,128)(2,1)S(1)}, u32[]{:S(2)}, u32[]{:S(2)}) collective-permute-start(bf16[4,2,128,128]{3,2,1,0:T(8,128)(2,1)S(1)} %pad_maximum_fusion.2.refs_0_), channel_id=1, source_target_pairs={{0,8},{8,0},{16,24},{24,16},{1,9},{9,1},{17,25},{25,17},{2,10},{10... | collective-permute-start | bytes 786440 | tf_op jit(solution)/shard_map/ppermute | solution.py:179
  30.0 10.6 %collective-permute-start.5 = (bf16[4,2,64,128]{3,2,1,0:T(8,128)(2,1)S(1)}, bf16[4,2,64,128]{3,2,1,0:T(8,128)(2,1)S(1)}, u32[]{:S(2)}, u32[]{:S(2)}) collective-permute-start(bf16[4,2,64,128]{3,2,1,0:T(8,128)(2,1)S(1)} %slice.79), channel_id=1, source_target_pairs={{0,8},{8,0},{16,24},{24,16},{1,9},{9,1},{17,25},{25,17},{2,10},{10... | collective-permute-start | bytes 393224 | tf_op jit(solution)/shard_map/ppermute | solution.py:182
  31.2 9.5 %collective-permute-start.6 = (bf16[4,2,64,128]{3,2,1,0:T(8,128)(2,1)S(1)}, bf16[4,2,64,128]{3,2,1,0:T(8,128)(2,1)S(1)}, u32[]{:S(2)}, u32[]{:S(2)}) collective-permute-start(bf16[4,2,64,128]{3,2,1,0:T(8,128)(2,1)S(1)} %slice.80), channel_id=1, source_target_pairs={{0,16},{8,24},{16,0},{24,8},{1,17},{9,25},{17,1},{25,9},{2,18},{10... | collective-permute-start | bytes 393224 | tf_op jit(solution)/shard_map/ppermute | solution.py:183
  36.0 16.3 %collective-permute-start.12 = (bf16[4,2,64,128]{3,2,1,0:T(8,128)(2,1)S(1)}, bf16[4,2,64,128]{3,2,1,0:T(8,128)(2,1)S(1)}, u32[]{:S(2)}, u32[]{:S(2)}) collective-permute-start(bf16[4,2,64,128]{3,2,1,0:T(8,128)(2,1)S(1)} %slice.82), channel_id=1, source_target_pairs={{0,8},{8,0},{16,24},{24,16},{1,9},{9,1},{17,25},{25,17},{2,10},{10... | collective-permute-start | bytes 393224 | tf_op jit(solution)/shard_map/ppermute | solution.py:182
  37.8 14.5 %collective-permute-start.13 = (bf16[4,2,64,128]{3,2,1,0:T(8,128)(2,1)S(1)}, bf16[4,2,64,128]{3,2,1,0:T(8,128)(2,1)S(1)}, u32[]{:S(2)}, u32[]{:S(2)}) collective-permute-start(bf16[4,2,64,128]{3,2,1,0:T(8,128)(2,1)S(1)} %slice.83), channel_id=1, source_target_pairs={{0,16},{8,24},{16,0},{24,8},{1,17},{9,25},{17,1},{25,9},{2,18},{10... | collective-permute-start | bytes 393224 | tf_op jit(solution)/shard_map/ppermute | solution.py:183
  48.7 16.6 %collective-permute-start.20 = (bf16[4,2,128,128]{3,2,1,0:T(8,128)(2,1)}, bf16[4,2,128,128]{3,2,1,0:T(8,128)(2,1)S(1)}, u32[]{:S(2)}, u32[]{:S(2)}) collective-permute-start(bf16[4,2,128,128]{3,2,1,0:T(8,128)(2,1)} %get-tuple-element.29), channel_id=1, source_target_pairs={{0,8},{8,0},{16,24},{24,16},{1,9},{9,1},{17,25},{25,17},{2,10},{10... | collective-permute-start | bytes 786440 | tf_op jit(solution)/shard_map/ppermute | solution.py:197
  49.9 17.0 %collective-permute-start.21 = (bf16[4,2,128,128]{3,2,1,0:T(8,128)(2,1)}, bf16[4,2,128,128]{3,2,1,0:T(8,128)(2,1)S(1)}, u32[]{:S(2)}, u32[]{:S(2)}) collective-permute-start(bf16[4,2,128,128]{3,2,1,0:T(8,128)(2,1)} %get-tuple-element.30), channel_id=1, source_target_pairs={{0,16},{8,24},{16,0},{24,8},{1,17},{9,25},{17,1},{25,9},{2,18},{10... | collective-permute-start | bytes 786440 | tf_op jit(solution)/shard_map/ppermute | solution.py:197
  50.7 16.3 %collective-permute-start.22 = (bf16[4,2,128,128]{3,2,1,0:T(8,128)(2,1)}, bf16[4,2,128,128]{3,2,1,0:T(8,128)(2,1)S(1)}, u32[]{:S(2)}, u32[]{:S(2)}) collective-permute-start(bf16[4,2,128,128]{3,2,1,0:T(8,128)(2,1)} %get-tuple-element.31), channel_id=1, source_target_pairs={{0,24},{8,16},{16,8},{24,0},{1,25},{9,17},{17,9},{25,1},{2,26},{10... | collective-permute-start | bytes 786440 | tf_op jit(solution)/shard_map/ppermute | solution.py:197
  60.4 10.3 %collective-permute-start.14 = (bf16[4,2,128,128]{3,2,1,0:T(8,128)(2,1)}, bf16[4,2,128,128]{3,2,1,0:T(8,128)(2,1)S(1)}, u32[]{:S(2)}, u32[]{:S(2)}) collective-permute-start(bf16[4,2,128,128]{3,2,1,0:T(8,128)(2,1)} %get-tuple-element.25), channel_id=1, source_target_pairs={{0,8},{8,0},{16,24},{24,16},{1,9},{9,1},{17,25},{25,17},{2,10},{10... | collective-permute-start | bytes 786440 | tf_op jit(solution)/shard_map/ppermute | solution.py:197
  61.6 11.6 %collective-permute-start.15 = (bf16[4,2,128,128]{3,2,1,0:T(8,128)(2,1)}, bf16[4,2,128,128]{3,2,1,0:T(8,128)(2,1)S(1)}, u32[]{:S(2)}, u32[]{:S(2)}) collective-permute-start(bf16[4,2,128,128]{3,2,1,0:T(8,128)(2,1)} %get-tuple-element.26), channel_id=1, source_target_pairs={{0,16},{8,24},{16,0},{24,8},{1,17},{9,25},{17,1},{25,9},{2,18},{10... | collective-permute-start | bytes 786440 | tf_op jit(solution)/shard_map/ppermute | solution.py:197
  65.4 7.9 %collective-permute-start.16 = (bf16[4,2,128,128]{3,2,1,0:T(8,128)(2,1)S(1)}, bf16[4,2,128,128]{3,2,1,0:T(8,128)(2,1)S(1)}, u32[]{:S(2)}, u32[]{:S(2)}) collective-permute-start(bf16[4,2,128,128]{3,2,1,0:T(8,128)(2,1)S(1)} %copy-done.14), channel_id=1, source_target_pairs={{0,24},{8,16},{16,8},{24,0},{1,25},{9,17},{17,9},{25,1},{2,26},{10... | collective-permute-start | bytes 786440 | tf_op jit(solution)/shard_map/ppermute | solution.py:197
  67.2 10.4 %collective-permute-start.23 = (bf16[2,128,128]{2,1,0:T(8,128)(2,1)S(1)}, bf16[2,128,128]{2,1,0:T(8,128)(2,1)S(1)}, u32[]{:S(2)}, u32[]{:S(2)}) collective-permute-start(bf16[2,128,128]{2,1,0:T(8,128)(2,1)S(1)} %get-tuple-element.39), channel_id=1, source_target_pairs={{0,2},{2,4},{4,6},{6,0},{1,3},{3,5},{5,7},{7,1},{8,10},{10,12},{12... | collective-permute-start | bytes 196616 | tf_op jit(solution)/shard_map/ppermute | solution.py:155
  70.5 9.0 %collective-permute-start.24 = (bf16[2,128,128]{2,1,0:T(8,128)(2,1)S(1)}, bf16[2,128,128]{2,1,0:T(8,128)(2,1)S(1)}, u32[]{:S(2)}, u32[]{:S(2)}) collective-permute-start(bf16[2,128,128]{2,1,0:T(8,128)(2,1)S(1)} %get-tuple-element.38), channel_id=1, source_target_pairs={{0,4},{2,6},{4,0},{6,2},{1,5},{3,7},{5,1},{7,3},{8,12},{10,14},{12... | collective-permute-start | bytes 196616 | tf_op jit(solution)/shard_map/ppermute | solution.py:155
  70.8 8.8 %collective-permute-start.25 = (bf16[2,128,128]{2,1,0:T(8,128)(2,1)S(1)}, bf16[2,128,128]{2,1,0:T(8,128)(2,1)S(1)}, u32[]{:S(2)}, u32[]{:S(2)}) collective-permute-start(bf16[2,128,128]{2,1,0:T(8,128)(2,1)S(1)} %get-tuple-element.37), channel_id=1, source_target_pairs={{0,6},{2,0},{4,2},{6,4},{1,7},{3,1},{5,3},{7,5},{8,14},{10,8},{12,... | collective-permute-start | bytes 196616 | tf_op jit(solution)/shard_map/ppermute | solution.py:155
  73.6 6.2 %collective-permute-start.17 = (bf16[2,128,128]{2,1,0:T(8,128)(2,1)S(1)}, bf16[2,128,128]{2,1,0:T(8,128)(2,1)S(1)}, u32[]{:S(2)}, u32[]{:S(2)}) collective-permute-start(bf16[2,128,128]{2,1,0:T(8,128)(2,1)S(1)} %get-tuple-element.35), channel_id=1, source_target_pairs={{0,2},{2,4},{4,6},{6,0},{1,3},{3,5},{5,7},{7,1},{8,10},{10,12},{12... | collective-permute-start | bytes 196616 | tf_op jit(solution)/shard_map/ppermute | solution.py:155
  (21 other events, 68.7 us)

commit v16 on v15

--- a/solution.py
+++ b/solution.py
@@ -11,7 +11,7 @@
 GROUP = 2
 HEAD_DIM = 128
 BLOCK = 128
-HEAD_GROUPS = 2
+HEAD_GROUPS = 1
 
 
 scale_factor = 144.0 ** (-0.5)

time: 85.1 us -> 100 us (1.18)
  waiting for transfers between devices: 7.39 us -> 47.5 us
  starting transfers between devices: 42.1 us -> 23 us
  other arithmetic: 5.56 us -> 2.54 us
  Pallas kernels: 14.8 us -> 12.5 us
    ppermute x6 -> x3, waiting for transfers between devices: 0.34 us -> 19.9 us  [ctx_reduce(): lax.ppermute(pieces[j], 'ctx', [(i, i ^ j) for i in range(n)])]
    ppermute x12 -> x6, starting transfers between devices: 22.5 us -> 13.2 us  [ring_shift(): return lax.ppermute(x, axis, [(i, (i + d) % n) for i in range(n)])]
    ppermute x12 -> x6, waiting for transfers between devices: 3.84 us -> 12.7 us  [ring_shift(): return lax.ppermute(x, axis, [(i, (i + d) % n) for i in range(n)])]
    ppermute x2 -> x1, waiting for transfers between devices: 3.19 us -> 10.7 us  [ctx_gather(): from_y = lax.ppermute(x, 'ctx', along_y)]
    ppermute x6 -> x3, starting transfers between devices: 7.11 us -> 3.55 us  [ctx_reduce(): lax.ppermute(pieces[j], 'ctx', [(i, i ^ j) for i in range(n)])]
    ppermute x2 -> x1, waiting for transfers between devices: 0.01 us -> 2.85 us  [ctx_gather(): far_a = lax.ppermute(from_y[:, :, :half], 'ctx', along_x)]
    broadcast_in_dim x2 -> x0, other arithmetic: 2.82 us -> none  [shards(): return (dq[None, None], dkr[None, None], dvr[None, None], d_prefix)]
    pallas_call x2 -> x1, Pallas kernels: 14.8 us -> 12.5 us  [attention_grads(): pl.pallas_call(functools.partial(attention_grad_kernel, layout), out_shap...]
  transfers between devices with their start and end apart: 26 -> 13, of which waited for: 5 -> 10; matrix products, arithmetic and copies ran while one was open for 6% -> 2% of each run, Pallas kernels for 17% -> 0%
where the time goes in v16:
time: 100 us; the launch traced here: 99.8 us
  waiting for transfers between devices  47.5 us (48%)
  starting transfers between devices  23 us (23%)
  Pallas kernels  12.5 us (12%)
  between operations  9.24 us (9%)
  local copies, waits for them, and re-layouts  4.98 us (5%)
  other arithmetic  2.54 us (3%)
    ppermute x3, waiting for transfers between devices, ctx_reduce(): lax.ppermute(pieces[j], 'ctx', [(i, i ^ j) for i in range(n)])  19.9 us
    ppermute x6, starting transfers between devices, ring_shift(): return lax.ppermute(x, axis, [(i, (i + d) % n) for i in range(n)])  13.2 us
    ppermute x6, waiting for transfers between devices, ring_shift(): return lax.ppermute(x, axis, [(i, (i + d) % n) for i in range(n)])  12.7 us
    pallas_call x1, Pallas kernels, attention_grads(): pl.pallas_call(functools.partial(attention_grad_kernel, layout), out_shap...  12.5 us
    ppermute x1, waiting for transfers between devices, ctx_gather(): from_y = lax.ppermute(x, 'ctx', along_y)  10.7 us
    ppermute x3, starting transfers between devices, ctx_reduce(): lax.ppermute(pieces[j], 'ctx', [(i, i ^ j) for i in range(n)])  3.55 us
    ppermute x1, waiting for transfers between devices, ctx_gather(): far_a = lax.ppermute(from_y[:, :, :half], 'ctx', along_x)  2.85 us
  transfers between devices with their start and end apart: 13, of which 10 were waited for; matrix products, arithmetic and copies ran while one was open for 2% of the time, Pallas kernels for 0%

profile of v16, /device:TPU:0, one launch (start us, length us, event | category | flops | bytes accessed | tf_op | source)
XLA Modules:
  0.0 99.8 jit_solution(2619611605387908910)
XLA Ops:
  9.7 1.5 %constant_dynamic-slice_fusion.3 = (bf16[1,128,2,256]{3,2,1,0:T(2,128)(2,1)S(1)}, bf16[1,128,2,256]{3,2,1,0:T(2,128)(2,1)S(1)}, bf16[1,128,2,256]{3,2,1,0:T(2,128)(2,1)S(1)}, bf16[1,128,2,256]{3,2,1,0:T(2,128)(2,1)S(1)}) fusion(bf16[2,128,2,256]{3,2,1,0:T(2,128)(2,1)} %param.12, s32[]{:T(128)S(6)} %select_n.54, s32[]{:T(128)S(6)} %select_n.60, ...), kind=kLoop, calls=%fused_computation.25 | loop fusion | bytes 1048592 | tf_op jit(solution)/shard_map/dynamic-slice
  11.2 3.1 %collective-permute-start = (bf16[2,128,256]{2,1,0:T(8,128)(2,1)S(1)}, bf16[2,128,256]{2,1,0:T(8,128)(2,1)S(1)}, u32[]{:S(2)}, u32[]{:S(2)}) collective-permute-start(bf16[2,128,256]{2,1,0:T(8,128)(2,1)S(1)} %bitcast.67), channel_id=1, source_target_pairs={{0,2},{2,4},{4,6},{6,0},{1,3},{3,5},{5,7},{7,1},{8,10},{10,12},{12... | collective-permute-start | bytes 393224 | tf_op jit(solution)/shard_map/ppermute | solution.py:155
  14.3 2.7 %collective-permute-start.1 = (bf16[2,128,256]{2,1,0:T(8,128)(2,1)S(1)}, bf16[2,128,256]{2,1,0:T(8,128)(2,1)S(1)}, u32[]{:S(2)}, u32[]{:S(2)}) collective-permute-start(bf16[2,128,256]{2,1,0:T(8,128)(2,1)S(1)} %bitcast.68), channel_id=1, source_target_pairs={{0,4},{2,6},{4,0},{6,2},{1,5},{3,7},{5,1},{7,3},{8,12},{10,14},{12... | collective-permute-start | bytes 393224 | tf_op jit(solution)/shard_map/ppermute | solution.py:155
  17.0 1.4 %collective-permute-start.2 = (bf16[2,128,256]{2,1,0:T(8,128)(2,1)S(1)}, bf16[2,128,256]{2,1,0:T(8,128)(2,1)S(1)}, u32[]{:S(2)}, u32[]{:S(2)}) collective-permute-start(bf16[2,128,256]{2,1,0:T(8,128)(2,1)S(1)} %bitcast.69), channel_id=1, source_target_pairs={{0,6},{2,0},{4,2},{6,4},{1,7},{3,1},{5,3},{7,5},{8,14},{10,8},{12,... | collective-permute-start | bytes 393224 | tf_op jit(solution)/shard_map/ppermute | solution.py:155
  18.4 2.3 %collective-permute-done = bf16[2,128,256]{2,1,0:T(8,128)(2,1)S(1)} collective-permute-done((bf16[2,128,256]{2,1,0:T(8,128)(2,1)S(1)}, bf16[2,128,256]{2,1,0:T(8,128)(2,1)S(1)}, u32[]{:S(2)}, u32[]{:S(2)}) %collective-permute-start) | collective-permute-done | bytes 131104 | tf_op jit(solution)/shard_map/ppermute | solution.py:155
  20.7 4.8 %collective-permute-done.1 = bf16[2,128,256]{2,1,0:T(8,128)(2,1)S(1)} collective-permute-done((bf16[2,128,256]{2,1,0:T(8,128)(2,1)S(1)}, bf16[2,128,256]{2,1,0:T(8,128)(2,1)S(1)}, u32[]{:S(2)}, u32[]{:S(2)}) %collective-permute-start.1) | collective-permute-done | bytes 131104 | tf_op jit(solution)/shard_map/ppermute | solution.py:155
  25.6 1.6 %collective-permute-start.4 = (bf16[4,2,128,256]{3,2,1,0:T(8,128)(2,1)S(1)}, bf16[4,2,128,256]{3,2,1,0:T(8,128)(2,1)S(1)}, u32[]{:S(2)}, u32[]{:S(2)}) collective-permute-start(bf16[4,2,128,256]{3,2,1,0:T(8,128)(2,1)S(1)} %pad_maximum_fusion.refs_0_), channel_id=1, source_target_pairs={{0,16},{8,24},{16,0},{24,8},{1,17},{9,25},{17,1},{25,9},{2,18},{10... | collective-permute-start | bytes 1572872 | tf_op jit(solution)/shard_map/ppermute | solution.py:180
  27.2 1.5 %collective-permute-start.3 = (bf16[4,2,128,256]{3,2,1,0:T(8,128)(2,1)S(1)}, bf16[4,2,128,256]{3,2,1,0:T(8,128)(2,1)S(1)}, u32[]{:S(2)}, u32[]{:S(2)}) collective-permute-start(bf16[4,2,128,256]{3,2,1,0:T(8,128)(2,1)S(1)} %pad_maximum_fusion.refs_0_), channel_id=1, source_target_pairs={{0,8},{8,0},{16,24},{24,16},{1,9},{9,1},{17,25},{25,17},{2,10},{10... | collective-permute-start | bytes 1572872 | tf_op jit(solution)/shard_map/ppermute | solution.py:179
  28.7 10.7 %collective-permute-done.4.refs_2_ = bf16[4,2,128,256]{3,2,1,0:T(8,128)(2,1)S(1)} collective-permute-done((bf16[4,2,128,256]{3,2,1,0:T(8,128)(2,1)S(1)}, bf16[4,2,128,256]{3,2,1,0:T(8,128)(2,1)S(1)}, u32[]{:S(2)}, u32[]{:S(2)}) %collective-permute-start.4) | collective-permute-done | bytes 524320 | tf_op jit(solution)/shard_map/ppermute | solution.py:180
  39.4 1.6 %collective-permute-start.5 = (bf16[4,2,64,256]{3,2,1,0:T(8,128)(2,1)S(1)}, bf16[4,2,64,256]{3,2,1,0:T(8,128)(2,1)S(1)}, u32[]{:S(2)}, u32[]{:S(2)}) collective-permute-start(bf16[4,2,64,256]{3,2,1,0:T(8,128)(2,1)S(1)} %slice.42), channel_id=1, source_target_pairs={{0,8},{8,0},{16,24},{24,16},{1,9},{9,1},{17,25},{25,17},{2,10},{10... | collective-permute-start | bytes 786440 | tf_op jit(solution)/shard_map/ppermute | solution.py:182
  41.0 1.6 %collective-permute-start.6 = (bf16[4,2,64,256]{3,2,1,0:T(8,128)(2,1)S(1)}, bf16[4,2,64,256]{3,2,1,0:T(8,128)(2,1)S(1)}, u32[]{:S(2)}, u32[]{:S(2)}) collective-permute-start(bf16[4,2,64,256]{3,2,1,0:T(8,128)(2,1)S(1)} %slice.43), channel_id=1, source_target_pairs={{0,16},{8,24},{16,0},{24,8},{1,17},{9,25},{17,1},{25,9},{2,18},{10... | collective-permute-start | bytes 786440 | tf_op jit(solution)/shard_map/ppermute | solution.py:183
  43.9 2.8 %collective-permute-done.5.refs_3_ = bf16[4,2,64,256]{3,2,1,0:T(8,128)(2,1)S(1)} collective-permute-done((bf16[4,2,64,256]{3,2,1,0:T(8,128)(2,1)S(1)}, bf16[4,2,64,256]{3,2,1,0:T(8,128)(2,1)S(1)}, u32[]{:S(2)}, u32[]{:S(2)}) %collective-permute-start.5) | collective-permute-done | bytes 262176 | tf_op jit(solution)/shard_map/ppermute | solution.py:182
  46.8 1.3 %collective-permute-done.6.refs_4_ = bf16[4,2,64,256]{3,2,1,0:T(8,128)(2,1)S(1)} collective-permute-done((bf16[4,2,64,256]{3,2,1,0:T(8,128)(2,1)S(1)}, bf16[4,2,64,256]{3,2,1,0:T(8,128)(2,1)S(1)}, u32[]{:S(2)}, u32[]{:S(2)}) %collective-permute-start.6) | collective-permute-done | bytes 262176 | tf_op jit(solution)/shard_map/ppermute | solution.py:183
  48.8 12.5 %shard_map.111 = (bf16[128,2048]{1,0:T(8,128)(2,1)}, bf16[128,1024]{1,0:T(8,128)(2,1)}, bf16[128,1024]{1,0:T(8,128)(2,1)}, bf16[4,2,128,256]{3,2,1,0:T(8,128)(2,...) custom-call(s32[4]{0:T(128)} %bitcast.77, ...), custom_call_target="tpu_custom_call" | custom-call | flops 2013265920 | bytes 7340032 | tf_op jit(solution)/shard_map/pallas_call | solution.py:136
  61.3 1.2 %collective-permute-start.7 = (bf16[4,2,128,256]{3,2,1,0:T(8,128)(2,1)}, bf16[4,2,128,256]{3,2,1,0:T(8,128)(2,1)S(1)}, u32[]{:S(2)}, u32[]{:S(2)}) collective-permute-start(bf16[4,2,128,256]{3,2,1,0:T(8,128)(2,1)} %get-tuple-element.15), channel_id=1, source_target_pairs={{0,8},{8,0},{16,24},{24,16},{1,9},{9,1},{17,25},{25,17},{2,10},{10... | collective-permute-start | bytes 1572872 | tf_op jit(solution)/shard_map/ppermute | solution.py:197
  62.5 1.3 %collective-permute-start.8 = (bf16[4,2,128,256]{3,2,1,0:T(8,128)(2,1)}, bf16[4,2,128,256]{3,2,1,0:T(8,128)(2,1)S(1)}, u32[]{:S(2)}, u32[]{:S(2)}) collective-permute-start(bf16[4,2,128,256]{3,2,1,0:T(8,128)(2,1)} %get-tuple-element.16), channel_id=1, source_target_pairs={{0,16},{8,24},{16,0},{24,8},{1,17},{9,25},{17,1},{25,9},{2,18},{10... | collective-permute-start | bytes 1572872 | tf_op jit(solution)/shard_map/ppermute | solution.py:197
  63.8 1.1 %collective-permute-start.9 = (bf16[4,2,128,256]{3,2,1,0:T(8,128)(2,1)}, bf16[4,2,128,256]{3,2,1,0:T(8,128)(2,1)S(1)}, u32[]{:S(2)}, u32[]{:S(2)}) collective-permute-start(bf16[4,2,128,256]{3,2,1,0:T(8,128)(2,1)} %get-tuple-element.17), channel_id=1, source_target_pairs={{0,24},{8,16},{16,8},{24,0},{1,25},{9,17},{17,9},{25,1},{2,26},{10... | collective-permute-start | bytes 1572872 | tf_op jit(solution)/shard_map/ppermute | solution.py:197
  65.6 10.9 %collective-permute-done.7 = bf16[4,2,128,256]{3,2,1,0:T(8,128)(2,1)S(1)} collective-permute-done((bf16[4,2,128,256]{3,2,1,0:T(8,128)(2,1)}, bf16[4,2,128,256]{3,2,1,0:T(8,128)(2,1)S(1)}, u32[]{:S(2)}, u32[]{:S(2)}) %collective-permute-start.7) | collective-permute-done | bytes 524320 | tf_op jit(solution)/shard_map/ppermute | solution.py:197
  76.5 8.1 %collective-permute-done.8 = bf16[4,2,128,256]{3,2,1,0:T(8,128)(2,1)S(1)} collective-permute-done((bf16[4,2,128,256]{3,2,1,0:T(8,128)(2,1)}, bf16[4,2,128,256]{3,2,1,0:T(8,128)(2,1)S(1)}, u32[]{:S(2)}, u32[]{:S(2)}) %collective-permute-start.8) | collective-permute-done | bytes 524320 | tf_op jit(solution)/shard_map/ppermute | solution.py:197
  85.8 3.6 %collective-permute-start.10 = (bf16[2,128,256]{2,1,0:T(8,128)(2,1)S(1)}, bf16[2,128,256]{2,1,0:T(8,128)(2,1)S(1)}, u32[]{:S(2)}, u32[]{:S(2)}) collective-permute-start(bf16[2,128,256]{2,1,0:T(8,128)(2,1)S(1)} %get-tuple-element.21), channel_id=1, source_target_pairs={{0,2},{2,4},{4,6},{6,0},{1,3},{3,5},{5,7},{7,1},{8,10},{10,12},{12... | collective-permute-start | bytes 393224 | tf_op jit(solution)/shard_map/ppermute | solution.py:155
  89.5 2.4 %collective-permute-start.12 = (bf16[2,128,256]{2,1,0:T(8,128)(2,1)S(1)}, bf16[2,128,256]{2,1,0:T(8,128)(2,1)S(1)}, u32[]{:S(2)}, u32[]{:S(2)}) collective-permute-start(bf16[2,128,256]{2,1,0:T(8,128)(2,1)S(1)} %get-tuple-element.19), channel_id=1, source_target_pairs={{0,6},{2,0},{4,2},{6,4},{1,7},{3,1},{5,3},{7,5},{8,14},{10,8},{12,... | collective-permute-start | bytes 393224 | tf_op jit(solution)/shard_map/ppermute | solution.py:155
  92.1 1.7 %collective-permute-done.10 = bf16[2,128,256]{2,1,0:T(8,128)(2,1)S(1)} collective-permute-done((bf16[2,128,256]{2,1,0:T(8,128)(2,1)S(1)}, bf16[2,128,256]{2,1,0:T(8,128)(2,1)S(1)}, u32[]{:S(2)}, u32[]{:S(2)}) %collective-permute-start.10) | collective-permute-done | bytes 131104 | tf_op jit(solution)/shard_map/ppermute | solution.py:155
  94.1 3.9 %collective-permute-done.11 = bf16[2,128,256]{2,1,0:T(8,128)(2,1)S(1)} collective-permute-done((bf16[2,128,256]{2,1,0:T(8,128)(2,1)S(1)}, bf16[2,128,256]{2,1,0:T(8,128)(2,1)S(1)}, u32[]{:S(2)}, u32[]{:S(2)}) %collective-permute-start.11) | collective-permute-done | bytes 131104 | tf_op jit(solution)/shard_map/ppermute | solution.py:155
  98.5 1.3 %multiply_add_fusion = f32[2,128,2,256]{3,2,1,0:T(2,128)} fusion(f32[128,2,256]{2,1,0:T(2,128)S(1)} %copy.27, f32[128,2,256]{2,1,0:T(2,128)S(1)} %copy.26, f32[128,2,256]{2,1,0:T(2,128)S(1)} %copy.25, f32[128,2,256]{2,1,0:T(2,128)S(1)} %copy.24, f32[2]{0:T(128)S(1)} %get-tuple-element.27, f32[2]{0:T(128)S(1)} %get-tuple-element.28, ...), kind=kLoop, calls=%fused_computation.3 | loop fusion | flops 917504 | bytes 1572896 | tf_op jit(solution)/shard_map/add | solution.py:251
  (42 shorter events, 5.7 us)
Async XLA Ops:
  0.7 0.7 copy-start
  11.2 9.5 %collective-permute-start = (bf16[2,128,256]{2,1,0:T(8,128)(2,1)S(1)}, bf16[2,128,256]{2,1,0:T(8,128)(2,1)S(1)}, u32[]{:S(2)}, u32[]{:S(2)}) collective-permute-start(bf16[2,128,256]{2,1,0:T(8,128)(2,1)S(1)} %bitcast.67), channel_id=1, source_target_pairs={{0,2},{2,4},{4,6},{6,0},{1,3},{3,5},{5,7},{7,1},{8,10},{10,12},{12... | collective-permute-start | bytes 393224 | tf_op jit(solution)/shard_map/ppermute | solution.py:155
  14.3 11.2 %collective-permute-start.1 = (bf16[2,128,256]{2,1,0:T(8,128)(2,1)S(1)}, bf16[2,128,256]{2,1,0:T(8,128)(2,1)S(1)}, u32[]{:S(2)}, u32[]{:S(2)}) collective-permute-start(bf16[2,128,256]{2,1,0:T(8,128)(2,1)S(1)} %bitcast.68), channel_id=1, source_target_pairs={{0,4},{2,6},{4,0},{6,2},{1,5},{3,7},{5,1},{7,3},{8,12},{10,14},{12... | collective-permute-start | bytes 393224 | tf_op jit(solution)/shard_map/ppermute | solution.py:155
  17.0 8.5 %collective-permute-start.2 = (bf16[2,128,256]{2,1,0:T(8,128)(2,1)S(1)}, bf16[2,128,256]{2,1,0:T(8,128)(2,1)S(1)}, u32[]{:S(2)}, u32[]{:S(2)}) collective-permute-start(bf16[2,128,256]{2,1,0:T(8,128)(2,1)S(1)} %bitcast.69), channel_id=1, source_target_pairs={{0,6},{2,0},{4,2},{6,4},{1,7},{3,1},{5,3},{7,5},{8,14},{10,8},{12,... | collective-permute-start | bytes 393224 | tf_op jit(solution)/shard_map/ppermute | solution.py:155
  25.6 15.4 %copy-start.2 = (bf16[4,2,128,256]{3,2,1,0:T(8,128)(2,1)}, bf16[4,2,128,256]{3,2,1,0:T(8,128)(2,1)S(1)}, u32[]{:S(2)}) copy-start(bf16[4,2,128,256]{3,2,1,0:T(8,128)(2,1)S(1)} %pad_maximum_fusion.refs_0_) | copy-start | bytes 1572868
  25.6 13.8 %collective-permute-start.4 = (bf16[4,2,128,256]{3,2,1,0:T(8,128)(2,1)S(1)}, bf16[4,2,128,256]{3,2,1,0:T(8,128)(2,1)S(1)}, u32[]{:S(2)}, u32[]{:S(2)}) collective-permute-start(bf16[4,2,128,256]{3,2,1,0:T(8,128)(2,1)S(1)} %pad_maximum_fusion.refs_0_), channel_id=1, source_target_pairs={{0,16},{8,24},{16,0},{24,8},{1,17},{9,25},{17,1},{25,9},{2,18},{10... | collective-permute-start | bytes 1572872 | tf_op jit(solution)/shard_map/ppermute | solution.py:180
  27.2 13.8 %collective-permute-start.3 = (bf16[4,2,128,256]{3,2,1,0:T(8,128)(2,1)S(1)}, bf16[4,2,128,256]{3,2,1,0:T(8,128)(2,1)S(1)}, u32[]{:S(2)}, u32[]{:S(2)}) collective-permute-start(bf16[4,2,128,256]{3,2,1,0:T(8,128)(2,1)S(1)} %pad_maximum_fusion.refs_0_), channel_id=1, source_target_pairs={{0,8},{8,0},{16,24},{24,16},{1,9},{9,1},{17,25},{25,17},{2,10},{10... | collective-permute-start | bytes 1572872 | tf_op jit(solution)/shard_map/ppermute | solution.py:179
  39.4 1.6 %copy-start.3 = (bf16[4,2,128,256]{3,2,1,0:T(8,128)(2,1)}, bf16[4,2,128,256]{3,2,1,0:T(8,128)(2,1)S(1)}, u32[]{:S(2)}) copy-start(bf16[4,2,128,256]{3,2,1,0:T(8,128)(2,1)S(1)} %collective-permute-done.4.refs_2_) | copy-start | bytes 1572868
  39.4 7.3 %collective-permute-start.5 = (bf16[4,2,64,256]{3,2,1,0:T(8,128)(2,1)S(1)}, bf16[4,2,64,256]{3,2,1,0:T(8,128)(2,1)S(1)}, u32[]{:S(2)}, u32[]{:S(2)}) collective-permute-start(bf16[4,2,64,256]{3,2,1,0:T(8,128)(2,1)S(1)} %slice.42), channel_id=1, source_target_pairs={{0,8},{8,0},{16,24},{24,16},{1,9},{9,1},{17,25},{25,17},{2,10},{10... | collective-permute-start | bytes 786440 | tf_op jit(solution)/shard_map/ppermute | solution.py:182
  41.0 7.1 %copy-start.4 = (bf16[4,2,128,256]{3,2,1,0:T(8,128)(2,1)}, bf16[4,2,128,256]{3,2,1,0:T(8,128)(2,1)S(1)}, u32[]{:S(2)}) copy-start(bf16[4,2,128,256]{3,2,1,0:T(8,128)(2,1)S(1)} %collective-permute-done.3.refs_1_) | copy-start | bytes 1572868
  41.0 7.1 %collective-permute-start.6 = (bf16[4,2,64,256]{3,2,1,0:T(8,128)(2,1)S(1)}, bf16[4,2,64,256]{3,2,1,0:T(8,128)(2,1)S(1)}, u32[]{:S(2)}, u32[]{:S(2)}) collective-permute-start(bf16[4,2,64,256]{3,2,1,0:T(8,128)(2,1)S(1)} %slice.43), channel_id=1, source_target_pairs={{0,16},{8,24},{16,0},{24,8},{1,17},{9,25},{17,1},{25,9},{2,18},{10... | collective-permute-start | bytes 786440 | tf_op jit(solution)/shard_map/ppermute | solution.py:183
  46.8 1.3 %copy-start.5 = (bf16[4,2,64,256]{3,2,1,0:T(8,128)(2,1)}, bf16[4,2,64,256]{3,2,1,0:T(8,128)(2,1)S(1)}, u32[]{:S(2)}) copy-start(bf16[4,2,64,256]{3,2,1,0:T(8,128)(2,1)S(1)} %collective-permute-done.5.refs_3_) | copy-start | bytes 786436
  48.1 0.7 copy-start.6
  61.3 24.2 %copy-start.1 = (bf16[4,2,128,256]{3,2,1,0:T(8,128)(2,1)S(1)}, bf16[4,2,128,256]{3,2,1,0:T(8,128)(2,1)}, u32[]{:S(2)}) copy-start(bf16[4,2,128,256]{3,2,1,0:T(8,128)(2,1)} %get-tuple-element.14) | copy-start | bytes 1572868
  61.3 15.1 %collective-permute-start.7 = (bf16[4,2,128,256]{3,2,1,0:T(8,128)(2,1)}, bf16[4,2,128,256]{3,2,1,0:T(8,128)(2,1)S(1)}, u32[]{:S(2)}, u32[]{:S(2)}) collective-permute-start(bf16[4,2,128,256]{3,2,1,0:T(8,128)(2,1)} %get-tuple-element.15), channel_id=1, source_target_pairs={{0,8},{8,0},{16,24},{24,16},{1,9},{9,1},{17,25},{25,17},{2,10},{10... | collective-permute-start | bytes 1572872 | tf_op jit(solution)/shard_map/ppermute | solution.py:197
  62.5 22.0 %collective-permute-start.8 = (bf16[4,2,128,256]{3,2,1,0:T(8,128)(2,1)}, bf16[4,2,128,256]{3,2,1,0:T(8,128)(2,1)S(1)}, u32[]{:S(2)}, u32[]{:S(2)}) collective-permute-start(bf16[4,2,128,256]{3,2,1,0:T(8,128)(2,1)} %get-tuple-element.16), channel_id=1, source_target_pairs={{0,16},{8,24},{16,0},{24,8},{1,17},{9,25},{17,1},{25,9},{2,18},{10... | collective-permute-start | bytes 1572872 | tf_op jit(solution)/shard_map/ppermute | solution.py:197
  63.8 21.7 %collective-permute-start.9 = (bf16[4,2,128,256]{3,2,1,0:T(8,128)(2,1)}, bf16[4,2,128,256]{3,2,1,0:T(8,128)(2,1)S(1)}, u32[]{:S(2)}, u32[]{:S(2)}) collective-permute-start(bf16[4,2,128,256]{3,2,1,0:T(8,128)(2,1)} %get-tuple-element.17), channel_id=1, source_target_pairs={{0,24},{8,16},{16,8},{24,0},{1,25},{9,17},{17,9},{25,1},{2,26},{10... | collective-permute-start | bytes 1572872 | tf_op jit(solution)/shard_map/ppermute | solution.py:197
  85.8 8.0 %collective-permute-start.10 = (bf16[2,128,256]{2,1,0:T(8,128)(2,1)S(1)}, bf16[2,128,256]{2,1,0:T(8,128)(2,1)S(1)}, u32[]{:S(2)}, u32[]{:S(2)}) collective-permute-start(bf16[2,128,256]{2,1,0:T(8,128)(2,1)S(1)} %get-tuple-element.21), channel_id=1, source_target_pairs={{0,2},{2,4},{4,6},{6,0},{1,3},{3,5},{5,7},{7,1},{8,10},{10,12},{12... | collective-permute-start | bytes 393224 | tf_op jit(solution)/shard_map/ppermute | solution.py:155
  89.5 8.5 %collective-permute-start.11 = (bf16[2,128,256]{2,1,0:T(8,128)(2,1)S(1)}, bf16[2,128,256]{2,1,0:T(8,128)(2,1)S(1)}, u32[]{:S(2)}, u32[]{:S(2)}) collective-permute-start(bf16[2,128,256]{2,1,0:T(8,128)(2,1)S(1)} %get-tuple-element.20), channel_id=1, source_target_pairs={{0,4},{2,6},{4,0},{6,2},{1,5},{3,7},{5,1},{7,3},{8,12},{10,14},{12... | collective-permute-start | bytes 393224 | tf_op jit(solution)/shard_map/ppermute | solution.py:155
  89.5 8.7 %collective-permute-start.12 = (bf16[2,128,256]{2,1,0:T(8,128)(2,1)S(1)}, bf16[2,128,256]{2,1,0:T(8,128)(2,1)S(1)}, u32[]{:S(2)}, u32[]{:S(2)}) collective-permute-start(bf16[2,128,256]{2,1,0:T(8,128)(2,1)S(1)} %get-tuple-element.19), channel_id=1, source_target_pairs={{0,6},{2,0},{4,2},{6,4},{1,7},{3,1},{5,3},{7,5},{8,14},{10,8},{12,... | collective-permute-start | bytes 393224 | tf_op jit(solution)/shard_map/ppermute | solution.py:155

commit v17 on v15

--- a/solution.py
+++ b/solution.py
@@ -227,6 +227,8 @@
     n_groups = HEAD_GROUPS if chunk_feats % (HEAD_GROUPS * HEAD_DIM) == 0 else 1
     group_feats = chunk_feats // n_groups
     place = jnp.stack([lax.axis_index("pair"), lax.axis_index("ctx")]).astype(jnp.int32)
+    planes, place, blocks, length = lax.optimization_barrier(
+        (planes, place, prefix_blocks[0, 0], resp_lengths[0, 0].reshape(1)))
     kv_heads = resp_keys.shape[-1] // HEAD_DIM
     chunk_heads = chunk_feats // HEAD_DIM
     group_heads = group_feats // HEAD_DIM
@@ -236,7 +238,7 @@
         cols = slice(k * group_feats, (k + 1) * group_feats)
         pieces = ctx_gather(pair_gather(planes[..., cols], pair_prompt))
         outs = attention_grads(
-            prefix_blocks[0, 0], resp_lengths[0, 0].reshape(1), place, queries[0, 0], d_out[0, 0], pieces,
+            blocks, length, place, queries[0, 0], d_out[0, 0], pieces,
             tree_ctx(), ctx_out_ranges(slot_rows), resp_keys[0, 0], resp_values[0, 0],
             k * (group_feats // HEAD_DIM), None)
         if earlier is None:

time: 85.1 us -> 85.8 us (level)
  transfers between devices with their start and end apart: 26 -> 26, of which waited for: 5 -> 6; matrix products, arithmetic and copies ran while one was open for 6% -> 6% of each run, Pallas kernels for 17% -> 17%
where the time goes in v17:
time: 85.8 us; the launch traced here: 85.3 us
  starting transfers between devices  42.4 us (49%)
  Pallas kernels  14.8 us (17%)
  between operations  9.44 us (11%)
  waiting for transfers between devices  7.68 us (9%)
  other arithmetic  5.57 us (6%)
  local copies, waits for them, and re-layouts  5.41 us (6%)
    ppermute x12, starting transfers between devices, ring_shift(): return lax.ppermute(x, axis, [(i, (i + d) % n) for i in range(n)])  22.9 us
    pallas_call x2, Pallas kernels, attention_grads(): pl.pallas_call(functools.partial(attention_grad_kernel, layout), out_shap...  14.8 us
    ppermute x6, starting transfers between devices, ctx_reduce(): lax.ppermute(pieces[j], 'ctx', [(i, i ^ j) for i in range(n)])  7.11 us
    ppermute x12, waiting for transfers between devices, ring_shift(): return lax.ppermute(x, axis, [(i, (i + d) % n) for i in range(n)])  3.84 us
    ppermute x2, starting transfers between devices, ctx_gather(): from_y = lax.ppermute(x, 'ctx', along_y)  3.39 us
    ppermute x2, waiting for transfers between devices, ctx_gather(): from_y = lax.ppermute(x, 'ctx', along_y)  3.19 us
    ppermute x2, starting transfers between devices, ctx_gather(): far_b = lax.ppermute(from_x[:, :, half:], 'ctx', along_y)  3.17 us
    unnamed x39, local copies, waits for them, and re-layouts  3.15 us
  transfers between devices with their start and end apart: 26, of which 6 were waited for; matrix products, arithmetic and copies ran while one was open for 6% of the time, Pallas kernels for 17%

profile of v17, /device:TPU:0, one launch (start us, length us, event | category | flops | bytes accessed | tf_op | source)
XLA Modules:
  0.0 85.3 jit_solution(7198493848651599533)
XLA Ops:
  11.4 3.1 %collective-permute-start = (bf16[2,128,128]{2,1,0:T(8,128)(2,1)S(1)}, bf16[2,128,128]{2,1,0:T(8,128)(2,1)S(1)}, u32[]{:S(2)}, u32[]{:S(2)}) collective-permute-start(bf16[2,128,128]{2,1,0:T(8,128)(2,1)S(1)} %get-tuple-element.57), channel_id=1, source_target_pairs={{0,2},{2,4},{4,6},{6,0},{1,3},{3,5},{5,7},{7,1},{8,10},{10,12},{12... | collective-permute-start | bytes 196616 | tf_op jit(solution)/shard_map/ppermute | solution.py:155
  14.4 2.6 %collective-permute-start.1 = (bf16[2,128,128]{2,1,0:T(8,128)(2,1)S(1)}, bf16[2,128,128]{2,1,0:T(8,128)(2,1)S(1)}, u32[]{:S(2)}, u32[]{:S(2)}) collective-permute-start(bf16[2,128,128]{2,1,0:T(8,128)(2,1)S(1)} %get-tuple-element.56), channel_id=1, source_target_pairs={{0,4},{2,6},{4,0},{6,2},{1,5},{3,7},{5,1},{7,3},{8,12},{10,14},{12... | collective-permute-start | bytes 196616 | tf_op jit(solution)/shard_map/ppermute | solution.py:155
  17.0 1.3 %collective-permute-start.2 = (bf16[2,128,128]{2,1,0:T(8,128)(2,1)S(1)}, bf16[2,128,128]{2,1,0:T(8,128)(2,1)S(1)}, u32[]{:S(2)}, u32[]{:S(2)}) collective-permute-start(bf16[2,128,128]{2,1,0:T(8,128)(2,1)S(1)} %get-tuple-element.55), channel_id=1, source_target_pairs={{0,6},{2,0},{4,2},{6,4},{1,7},{3,1},{5,3},{7,5},{8,14},{10,8},{12,... | collective-permute-start | bytes 196616 | tf_op jit(solution)/shard_map/ppermute | solution.py:155
  20.2 2.8 %collective-permute-start.9 = (bf16[2,128,128]{2,1,0:T(8,128)(2,1)S(1)}, bf16[2,128,128]{2,1,0:T(8,128)(2,1)S(1)}, u32[]{:S(2)}, u32[]{:S(2)}) collective-permute-start(bf16[2,128,128]{2,1,0:T(8,128)(2,1)S(1)} %get-tuple-element.51), channel_id=1, source_target_pairs={{0,6},{2,0},{4,2},{6,4},{1,7},{3,1},{5,3},{7,5},{8,14},{10,8},{12,... | collective-permute-start | bytes 196616 | tf_op jit(solution)/shard_map/ppermute | solution.py:155
  23.1 1.6 %collective-permute-start.4 = (bf16[4,2,128,128]{3,2,1,0:T(8,128)(2,1)S(1)}, bf16[4,2,128,128]{3,2,1,0:T(8,128)(2,1)S(1)}, u32[]{:S(2)}, u32[]{:S(2)}) collective-permute-start(bf16[4,2,128,128]{3,2,1,0:T(8,128)(2,1)S(1)} %pad_maximum_fusion.1.refs_0_), channel_id=1, source_target_pairs={{0,16},{8,24},{16,0},{24,8},{1,17},{9,25},{17,1},{25,9},{2,18},{10... | collective-permute-start | bytes 786440 | tf_op jit(solution)/shard_map/ppermute | solution.py:180
  24.7 1.5 %collective-permute-start.3 = (bf16[4,2,128,128]{3,2,1,0:T(8,128)(2,1)S(1)}, bf16[4,2,128,128]{3,2,1,0:T(8,128)(2,1)S(1)}, u32[]{:S(2)}, u32[]{:S(2)}) collective-permute-start(bf16[4,2,128,128]{3,2,1,0:T(8,128)(2,1)S(1)} %pad_maximum_fusion.1.refs_0_), channel_id=1, source_target_pairs={{0,8},{8,0},{16,24},{24,16},{1,9},{9,1},{17,25},{25,17},{2,10},{10... | collective-permute-start | bytes 786440 | tf_op jit(solution)/shard_map/ppermute | solution.py:179
  27.3 1.8 %collective-permute-start.11 = (bf16[4,2,128,128]{3,2,1,0:T(8,128)(2,1)S(1)}, bf16[4,2,128,128]{3,2,1,0:T(8,128)(2,1)S(1)}, u32[]{:S(2)}, u32[]{:S(2)}) collective-permute-start(bf16[4,2,128,128]{3,2,1,0:T(8,128)(2,1)S(1)} %pad_maximum_fusion.2.refs_0_), channel_id=1, source_target_pairs={{0,16},{8,24},{16,0},{24,8},{1,17},{9,25},{17,1},{25,9},{2,18},{10... | collective-permute-start | bytes 786440 | tf_op jit(solution)/shard_map/ppermute | solution.py:180
  29.1 1.5 %collective-permute-start.10 = (bf16[4,2,128,128]{3,2,1,0:T(8,128)(2,1)S(1)}, bf16[4,2,128,128]{3,2,1,0:T(8,128)(2,1)S(1)}, u32[]{:S(2)}, u32[]{:S(2)}) collective-permute-start(bf16[4,2,128,128]{3,2,1,0:T(8,128)(2,1)S(1)} %pad_maximum_fusion.2.refs_0_), channel_id=1, source_target_pairs={{0,8},{8,0},{16,24},{24,16},{1,9},{9,1},{17,25},{25,17},{2,10},{10... | collective-permute-start | bytes 786440 | tf_op jit(solution)/shard_map/ppermute | solution.py:179
  31.7 1.6 %collective-permute-start.6 = (bf16[4,2,64,128]{3,2,1,0:T(8,128)(2,1)S(1)}, bf16[4,2,64,128]{3,2,1,0:T(8,128)(2,1)S(1)}, u32[]{:S(2)}, u32[]{:S(2)}) collective-permute-start(bf16[4,2,64,128]{3,2,1,0:T(8,128)(2,1)S(1)} %slice.79), channel_id=1, source_target_pairs={{0,16},{8,24},{16,0},{24,8},{1,17},{9,25},{17,1},{25,9},{2,18},{10... | collective-permute-start | bytes 393224 | tf_op jit(solution)/shard_map/ppermute | solution.py:183
  33.3 3.2 %collective-permute-done.11.refs_2_ = bf16[4,2,128,128]{3,2,1,0:T(8,128)(2,1)S(1)} collective-permute-done((bf16[4,2,128,128]{3,2,1,0:T(8,128)(2,1)S(1)}, bf16[4,2,128,128]{3,2,1,0:T(8,128)(2,1)S(1)}, u32[]{:S(2)}, u32[]{:S(2)}) %collective-permute-start.11) | collective-permute-done | bytes 262176 | tf_op jit(solution)/shard_map/ppermute | solution.py:180
  36.6 1.8 %collective-permute-start.12 = (bf16[4,2,64,128]{3,2,1,0:T(8,128)(2,1)S(1)}, bf16[4,2,64,128]{3,2,1,0:T(8,128)(2,1)S(1)}, u32[]{:S(2)}, u32[]{:S(2)}) collective-permute-start(bf16[4,2,64,128]{3,2,1,0:T(8,128)(2,1)S(1)} %slice.80), channel_id=1, source_target_pairs={{0,8},{8,0},{16,24},{24,16},{1,9},{9,1},{17,25},{25,17},{2,10},{10... | collective-permute-start | bytes 393224 | tf_op jit(solution)/shard_map/ppermute | solution.py:182
  38.4 1.6 %collective-permute-start.13 = (bf16[4,2,64,128]{3,2,1,0:T(8,128)(2,1)S(1)}, bf16[4,2,64,128]{3,2,1,0:T(8,128)(2,1)S(1)}, u32[]{:S(2)}, u32[]{:S(2)}) collective-permute-start(bf16[4,2,64,128]{3,2,1,0:T(8,128)(2,1)S(1)} %slice.81), channel_id=1, source_target_pairs={{0,16},{8,24},{16,0},{24,8},{1,17},{9,25},{17,1},{25,9},{2,18},{10... | collective-permute-start | bytes 393224 | tf_op jit(solution)/shard_map/ppermute | solution.py:183
  41.6 7.4 %shard_map.111 = (bf16[128,2048]{1,0:T(8,128)(2,1)}, bf16[128,1024]{1,0:T(8,128)(2,1)}, bf16[128,1024]{1,0:T(8,128)(2,1)}, bf16[4,2,128,128]{3,2,1,0:T(8,128)(2,...) custom-call(s32[4]{0:T(128)} %bitcast.104, ...), custom_call_target="tpu_custom_call" | custom-call | flops 1006632960 | bytes 3670016 | tf_op jit(solution)/shard_map/pallas_call | solution.py:136
  48.9 1.6 %collective-permute-start.20 = (bf16[4,2,128,128]{3,2,1,0:T(8,128)(2,1)}, bf16[4,2,128,128]{3,2,1,0:T(8,128)(2,1)S(1)}, u32[]{:S(2)}, u32[]{:S(2)}) collective-permute-start(bf16[4,2,128,128]{3,2,1,0:T(8,128)(2,1)} %get-tuple-element.37), channel_id=1, source_target_pairs={{0,8},{8,0},{16,24},{24,16},{1,9},{9,1},{17,25},{25,17},{2,10},{10... | collective-permute-start | bytes 786440 | tf_op jit(solution)/shard_map/ppermute | solution.py:197
  51.0 1.5 %collective-permute-start.22 = (bf16[4,2,128,128]{3,2,1,0:T(8,128)(2,1)}, bf16[4,2,128,128]{3,2,1,0:T(8,128)(2,1)S(1)}, u32[]{:S(2)}, u32[]{:S(2)}) collective-permute-start(bf16[4,2,128,128]{3,2,1,0:T(8,128)(2,1)} %get-tuple-element.39), channel_id=1, source_target_pairs={{0,24},{8,16},{16,8},{24,0},{1,25},{9,17},{17,9},{25,1},{2,26},{10... | collective-permute-start | bytes 786440 | tf_op jit(solution)/shard_map/ppermute | solution.py:197
  53.2 7.5 %shard_map.112 = (bf16[128,2048]{1,0:T(8,128)(2,1)}, bf16[128,1024]{1,0:T(8,128)(2,1)}, bf16[128,1024]{1,0:T(8,128)(2,1)}, bf16[4,2,128,128]{3,2,1,0:T(8,128)(2,...) custom-call(s32[4]{0:T(128)} %bitcast.105, ...), custom_call_target="tpu_custom_call" | custom-call | flops 1006632960 | bytes 3670016 | tf_op jit(solution)/shard_map/pallas_call | solution.py:136
  60.7 1.6 %collective-permute-start.14 = (bf16[4,2,128,128]{3,2,1,0:T(8,128)(2,1)}, bf16[4,2,128,128]{3,2,1,0:T(8,128)(2,1)S(1)}, u32[]{:S(2)}, u32[]{:S(2)}) collective-permute-start(bf16[4,2,128,128]{3,2,1,0:T(8,128)(2,1)} %get-tuple-element.33), channel_id=1, source_target_pairs={{0,8},{8,0},{16,24},{24,16},{1,9},{9,1},{17,25},{25,17},{2,10},{10... | collective-permute-start | bytes 786440 | tf_op jit(solution)/shard_map/ppermute | solution.py:197
  62.8 2.0 %select_bitcast_fusion = bf16[1,1,128,2048]{3,2,1,0:T(8,128)(2,1)} fusion(bf16[128,2048]{1,0:T(8,128)(2,1)S(1)} %copy-done.1, bf16[128,2048]{1,0:T(8,128)(2,1)} %get-tuple-element.27, pred[2048]{0:T(1024)(128)(4,1)S(1)} %fusion.1), kind=kLoop, calls=%fused_computation.4 | loop fusion | flops 262144 | bytes 1574912 | tf_op jit(solution)/shard_map/broadcast_in_dim | solution.py:256
  65.7 1.5 %collective-permute-start.16 = (bf16[4,2,128,128]{3,2,1,0:T(8,128)(2,1)S(1)}, bf16[4,2,128,128]{3,2,1,0:T(8,128)(2,1)S(1)}, u32[]{:S(2)}, u32[]{:S(2)}) collective-permute-start(bf16[4,2,128,128]{3,2,1,0:T(8,128)(2,1)S(1)} %copy-done.14), channel_id=1, source_target_pairs={{0,24},{8,16},{16,8},{24,0},{1,25},{9,17},{17,9},{25,1},{2,26},{10... | collective-permute-start | bytes 786440 | tf_op jit(solution)/shard_map/ppermute | solution.py:197
  67.4 3.6 %collective-permute-start.23 = (bf16[2,128,128]{2,1,0:T(8,128)(2,1)S(1)}, bf16[2,128,128]{2,1,0:T(8,128)(2,1)S(1)}, u32[]{:S(2)}, u32[]{:S(2)}) collective-permute-start(bf16[2,128,128]{2,1,0:T(8,128)(2,1)S(1)} %get-tuple-element.47), channel_id=1, source_target_pairs={{0,2},{2,4},{4,6},{6,0},{1,3},{3,5},{5,7},{7,1},{8,10},{10,12},{12... | collective-permute-start | bytes 196616 | tf_op jit(solution)/shard_map/ppermute | solution.py:155
  71.2 2.2 %collective-permute-start.25 = (bf16[2,128,128]{2,1,0:T(8,128)(2,1)S(1)}, bf16[2,128,128]{2,1,0:T(8,128)(2,1)S(1)}, u32[]{:S(2)}, u32[]{:S(2)}) collective-permute-start(bf16[2,128,128]{2,1,0:T(8,128)(2,1)S(1)} %get-tuple-element.45), channel_id=1, source_target_pairs={{0,6},{2,0},{4,2},{6,4},{1,7},{3,1},{5,3},{7,5},{8,14},{10,8},{12,... | collective-permute-start | bytes 196616 | tf_op jit(solution)/shard_map/ppermute | solution.py:155
  74.1 3.4 %collective-permute-start.17 = (bf16[2,128,128]{2,1,0:T(8,128)(2,1)S(1)}, bf16[2,128,128]{2,1,0:T(8,128)(2,1)S(1)}, u32[]{:S(2)}, u32[]{:S(2)}) collective-permute-start(bf16[2,128,128]{2,1,0:T(8,128)(2,1)S(1)} %get-tuple-element.43), channel_id=1, source_target_pairs={{0,2},{2,4},{4,6},{6,0},{1,3},{3,5},{5,7},{7,1},{8,10},{10,12},{12... | collective-permute-start | bytes 196616 | tf_op jit(solution)/shard_map/ppermute | solution.py:155
  78.2 2.0 %collective-permute-start.19 = (bf16[2,128,128]{2,1,0:T(8,128)(2,1)S(1)}, bf16[2,128,128]{2,1,0:T(8,128)(2,1)S(1)}, u32[]{:S(2)}, u32[]{:S(2)}) collective-permute-start(bf16[2,128,128]{2,1,0:T(8,128)(2,1)S(1)} %get-tuple-element.41), channel_id=1, source_target_pairs={{0,6},{2,0},{4,2},{6,4},{1,7},{3,1},{5,3},{7,5},{8,14},{10,8},{12,... | collective-permute-start | bytes 196616 | tf_op jit(solution)/shard_map/ppermute | solution.py:155
  80.4 2.7 %collective-permute-done.18 = bf16[2,128,128]{2,1,0:T(8,128)(2,1)S(1)} collective-permute-done((bf16[2,128,128]{2,1,0:T(8,128)(2,1)S(1)}, bf16[2,128,128]{2,1,0:T(8,128)(2,1)S(1)}, u32[]{:S(2)}, u32[]{:S(2)}) %collective-permute-start.18) | collective-permute-done | bytes 65568 | tf_op jit(solution)/shard_map/ppermute | solution.py:155
  (109 shorter events, 14.8 us)
Async XLA Ops:
  11.4 8.8 %collective-permute-start = (bf16[2,128,128]{2,1,0:T(8,128)(2,1)S(1)}, bf16[2,128,128]{2,1,0:T(8,128)(2,1)S(1)}, u32[]{:S(2)}, u32[]{:S(2)}) collective-permute-start(bf16[2,128,128]{2,1,0:T(8,128)(2,1)S(1)} %get-tuple-element.57), channel_id=1, source_target_pairs={{0,2},{2,4},{4,6},{6,0},{1,3},{3,5},{5,7},{7,1},{8,10},{10,12},{12... | collective-permute-start | bytes 196616 | tf_op jit(solution)/shard_map/ppermute | solution.py:155
  14.4 8.6 %collective-permute-start.1 = (bf16[2,128,128]{2,1,0:T(8,128)(2,1)S(1)}, bf16[2,128,128]{2,1,0:T(8,128)(2,1)S(1)}, u32[]{:S(2)}, u32[]{:S(2)}) collective-permute-start(bf16[2,128,128]{2,1,0:T(8,128)(2,1)S(1)} %get-tuple-element.56), channel_id=1, source_target_pairs={{0,4},{2,6},{4,0},{6,2},{1,5},{3,7},{5,1},{7,3},{8,12},{10,14},{12... | collective-permute-start | bytes 196616 | tf_op jit(solution)/shard_map/ppermute | solution.py:155
  17.0 6.0 %collective-permute-start.2 = (bf16[2,128,128]{2,1,0:T(8,128)(2,1)S(1)}, bf16[2,128,128]{2,1,0:T(8,128)(2,1)S(1)}, u32[]{:S(2)}, u32[]{:S(2)}) collective-permute-start(bf16[2,128,128]{2,1,0:T(8,128)(2,1)S(1)} %get-tuple-element.55), channel_id=1, source_target_pairs={{0,6},{2,0},{4,2},{6,4},{1,7},{3,1},{5,3},{7,5},{8,14},{10,8},{12,... | collective-permute-start | bytes 196616 | tf_op jit(solution)/shard_map/ppermute | solution.py:155
  18.4 7.8 %collective-permute-start.7 = (bf16[2,128,128]{2,1,0:T(8,128)(2,1)S(1)}, bf16[2,128,128]{2,1,0:T(8,128)(2,1)S(1)}, u32[]{:S(2)}, u32[]{:S(2)}) collective-permute-start(bf16[2,128,128]{2,1,0:T(8,128)(2,1)S(1)} %get-tuple-element.53), channel_id=1, source_target_pairs={{0,2},{2,4},{4,6},{6,0},{1,3},{3,5},{5,7},{7,1},{8,10},{10,12},{12... | collective-permute-start | bytes 196616 | tf_op jit(solution)/shard_map/ppermute | solution.py:155
  19.1 8.0 %collective-permute-start.8 = (bf16[2,128,128]{2,1,0:T(8,128)(2,1)S(1)}, bf16[2,128,128]{2,1,0:T(8,128)(2,1)S(1)}, u32[]{:S(2)}, u32[]{:S(2)}) collective-permute-start(bf16[2,128,128]{2,1,0:T(8,128)(2,1)S(1)} %get-tuple-element.52), channel_id=1, source_target_pairs={{0,4},{2,6},{4,0},{6,2},{1,5},{3,7},{5,1},{7,3},{8,12},{10,14},{12... | collective-permute-start | bytes 196616 | tf_op jit(solution)/shard_map/ppermute | solution.py:155
  20.2 7.0 %collective-permute-start.9 = (bf16[2,128,128]{2,1,0:T(8,128)(2,1)S(1)}, bf16[2,128,128]{2,1,0:T(8,128)(2,1)S(1)}, u32[]{:S(2)}, u32[]{:S(2)}) collective-permute-start(bf16[2,128,128]{2,1,0:T(8,128)(2,1)S(1)} %get-tuple-element.51), channel_id=1, source_target_pairs={{0,6},{2,0},{4,2},{6,4},{1,7},{3,1},{5,3},{7,5},{8,14},{10,8},{12,... | collective-permute-start | bytes 196616 | tf_op jit(solution)/shard_map/ppermute | solution.py:155
  23.1 7.5 %collective-permute-start.4 = (bf16[4,2,128,128]{3,2,1,0:T(8,128)(2,1)S(1)}, bf16[4,2,128,128]{3,2,1,0:T(8,128)(2,1)S(1)}, u32[]{:S(2)}, u32[]{:S(2)}) collective-permute-start(bf16[4,2,128,128]{3,2,1,0:T(8,128)(2,1)S(1)} %pad_maximum_fusion.1.refs_0_), channel_id=1, source_target_pairs={{0,16},{8,24},{16,0},{24,8},{1,17},{9,25},{17,1},{25,9},{2,18},{10... | collective-permute-start | bytes 786440 | tf_op jit(solution)/shard_map/ppermute | solution.py:180
  24.7 7.0 %collective-permute-start.3 = (bf16[4,2,128,128]{3,2,1,0:T(8,128)(2,1)S(1)}, bf16[4,2,128,128]{3,2,1,0:T(8,128)(2,1)S(1)}, u32[]{:S(2)}, u32[]{:S(2)}) collective-permute-start(bf16[4,2,128,128]{3,2,1,0:T(8,128)(2,1)S(1)} %pad_maximum_fusion.1.refs_0_), channel_id=1, source_target_pairs={{0,8},{8,0},{16,24},{24,16},{1,9},{9,1},{17,25},{25,17},{2,10},{10... | collective-permute-start | bytes 786440 | tf_op jit(solution)/shard_map/ppermute | solution.py:179
  27.3 9.3 %collective-permute-start.11 = (bf16[4,2,128,128]{3,2,1,0:T(8,128)(2,1)S(1)}, bf16[4,2,128,128]{3,2,1,0:T(8,128)(2,1)S(1)}, u32[]{:S(2)}, u32[]{:S(2)}) collective-permute-start(bf16[4,2,128,128]{3,2,1,0:T(8,128)(2,1)S(1)} %pad_maximum_fusion.2.refs_0_), channel_id=1, source_target_pairs={{0,16},{8,24},{16,0},{24,8},{1,17},{9,25},{17,1},{25,9},{2,18},{10... | collective-permute-start | bytes 786440 | tf_op jit(solution)/shard_map/ppermute | solution.py:180
  29.1 9.3 %collective-permute-start.10 = (bf16[4,2,128,128]{3,2,1,0:T(8,128)(2,1)S(1)}, bf16[4,2,128,128]{3,2,1,0:T(8,128)(2,1)S(1)}, u32[]{:S(2)}, u32[]{:S(2)}) collective-permute-start(bf16[4,2,128,128]{3,2,1,0:T(8,128)(2,1)S(1)} %pad_maximum_fusion.2.refs_0_), channel_id=1, source_target_pairs={{0,8},{8,0},{16,24},{24,16},{1,9},{9,1},{17,25},{25,17},{2,10},{10... | collective-permute-start | bytes 786440 | tf_op jit(solution)/shard_map/ppermute | solution.py:179
  30.6 10.3 %collective-permute-start.5 = (bf16[4,2,64,128]{3,2,1,0:T(8,128)(2,1)S(1)}, bf16[4,2,64,128]{3,2,1,0:T(8,128)(2,1)S(1)}, u32[]{:S(2)}, u32[]{:S(2)}) collective-permute-start(bf16[4,2,64,128]{3,2,1,0:T(8,128)(2,1)S(1)} %slice.78), channel_id=1, source_target_pairs={{0,8},{8,0},{16,24},{24,16},{1,9},{9,1},{17,25},{25,17},{2,10},{10... | collective-permute-start | bytes 393224 | tf_op jit(solution)/shard_map/ppermute | solution.py:182
  31.7 9.1 %collective-permute-start.6 = (bf16[4,2,64,128]{3,2,1,0:T(8,128)(2,1)S(1)}, bf16[4,2,64,128]{3,2,1,0:T(8,128)(2,1)S(1)}, u32[]{:S(2)}, u32[]{:S(2)}) collective-permute-start(bf16[4,2,64,128]{3,2,1,0:T(8,128)(2,1)S(1)} %slice.79), channel_id=1, source_target_pairs={{0,16},{8,24},{16,0},{24,8},{1,17},{9,25},{17,1},{25,9},{2,18},{10... | collective-permute-start | bytes 393224 | tf_op jit(solution)/shard_map/ppermute | solution.py:183
  36.6 16.0 %collective-permute-start.12 = (bf16[4,2,64,128]{3,2,1,0:T(8,128)(2,1)S(1)}, bf16[4,2,64,128]{3,2,1,0:T(8,128)(2,1)S(1)}, u32[]{:S(2)}, u32[]{:S(2)}) collective-permute-start(bf16[4,2,64,128]{3,2,1,0:T(8,128)(2,1)S(1)} %slice.80), channel_id=1, source_target_pairs={{0,8},{8,0},{16,24},{24,16},{1,9},{9,1},{17,25},{25,17},{2,10},{10... | collective-permute-start | bytes 393224 | tf_op jit(solution)/shard_map/ppermute | solution.py:182
  38.4 14.1 %collective-permute-start.13 = (bf16[4,2,64,128]{3,2,1,0:T(8,128)(2,1)S(1)}, bf16[4,2,64,128]{3,2,1,0:T(8,128)(2,1)S(1)}, u32[]{:S(2)}, u32[]{:S(2)}) collective-permute-start(bf16[4,2,64,128]{3,2,1,0:T(8,128)(2,1)S(1)} %slice.81), channel_id=1, source_target_pairs={{0,16},{8,24},{16,0},{24,8},{1,17},{9,25},{17,1},{25,9},{2,18},{10... | collective-permute-start | bytes 393224 | tf_op jit(solution)/shard_map/ppermute | solution.py:183
  48.9 16.7 %collective-permute-start.20 = (bf16[4,2,128,128]{3,2,1,0:T(8,128)(2,1)}, bf16[4,2,128,128]{3,2,1,0:T(8,128)(2,1)S(1)}, u32[]{:S(2)}, u32[]{:S(2)}) collective-permute-start(bf16[4,2,128,128]{3,2,1,0:T(8,128)(2,1)} %get-tuple-element.37), channel_id=1, source_target_pairs={{0,8},{8,0},{16,24},{24,16},{1,9},{9,1},{17,25},{25,17},{2,10},{10... | collective-permute-start | bytes 786440 | tf_op jit(solution)/shard_map/ppermute | solution.py:197
  50.5 16.7 %collective-permute-start.21 = (bf16[4,2,128,128]{3,2,1,0:T(8,128)(2,1)}, bf16[4,2,128,128]{3,2,1,0:T(8,128)(2,1)S(1)}, u32[]{:S(2)}, u32[]{:S(2)}) collective-permute-start(bf16[4,2,128,128]{3,2,1,0:T(8,128)(2,1)} %get-tuple-element.38), channel_id=1, source_target_pairs={{0,16},{8,24},{16,0},{24,8},{1,17},{9,25},{17,1},{25,9},{2,18},{10... | collective-permute-start | bytes 786440 | tf_op jit(solution)/shard_map/ppermute | solution.py:197
  51.0 16.2 %collective-permute-start.22 = (bf16[4,2,128,128]{3,2,1,0:T(8,128)(2,1)}, bf16[4,2,128,128]{3,2,1,0:T(8,128)(2,1)S(1)}, u32[]{:S(2)}, u32[]{:S(2)}) collective-permute-start(bf16[4,2,128,128]{3,2,1,0:T(8,128)(2,1)} %get-tuple-element.39), channel_id=1, source_target_pairs={{0,24},{8,16},{16,8},{24,0},{1,25},{9,17},{17,9},{25,1},{2,26},{10... | collective-permute-start | bytes 786440 | tf_op jit(solution)/shard_map/ppermute | solution.py:197
  60.7 10.6 %collective-permute-start.14 = (bf16[4,2,128,128]{3,2,1,0:T(8,128)(2,1)}, bf16[4,2,128,128]{3,2,1,0:T(8,128)(2,1)S(1)}, u32[]{:S(2)}, u32[]{:S(2)}) collective-permute-start(bf16[4,2,128,128]{3,2,1,0:T(8,128)(2,1)} %get-tuple-element.33), channel_id=1, source_target_pairs={{0,8},{8,0},{16,24},{24,16},{1,9},{9,1},{17,25},{25,17},{2,10},{10... | collective-permute-start | bytes 786440 | tf_op jit(solution)/shard_map/ppermute | solution.py:197
  62.2 11.6 %collective-permute-start.15 = (bf16[4,2,128,128]{3,2,1,0:T(8,128)(2,1)}, bf16[4,2,128,128]{3,2,1,0:T(8,128)(2,1)S(1)}, u32[]{:S(2)}, u32[]{:S(2)}) collective-permute-start(bf16[4,2,128,128]{3,2,1,0:T(8,128)(2,1)} %get-tuple-element.34), channel_id=1, source_target_pairs={{0,16},{8,24},{16,0},{24,8},{1,17},{9,25},{17,1},{25,9},{2,18},{10... | collective-permute-start | bytes 786440 | tf_op jit(solution)/shard_map/ppermute | solution.py:197
  65.7 8.1 %collective-permute-start.16 = (bf16[4,2,128,128]{3,2,1,0:T(8,128)(2,1)S(1)}, bf16[4,2,128,128]{3,2,1,0:T(8,128)(2,1)S(1)}, u32[]{:S(2)}, u32[]{:S(2)}) collective-permute-start(bf16[4,2,128,128]{3,2,1,0:T(8,128)(2,1)S(1)} %copy-done.14), channel_id=1, source_target_pairs={{0,24},{8,16},{16,8},{24,0},{1,25},{9,17},{17,9},{25,1},{2,26},{10... | collective-permute-start | bytes 786440 | tf_op jit(solution)/shard_map/ppermute | solution.py:197
  67.4 10.8 %collective-permute-start.23 = (bf16[2,128,128]{2,1,0:T(8,128)(2,1)S(1)}, bf16[2,128,128]{2,1,0:T(8,128)(2,1)S(1)}, u32[]{:S(2)}, u32[]{:S(2)}) collective-permute-start(bf16[2,128,128]{2,1,0:T(8,128)(2,1)S(1)} %get-tuple-element.47), channel_id=1, source_target_pairs={{0,2},{2,4},{4,6},{6,0},{1,3},{3,5},{5,7},{7,1},{8,10},{10,12},{12... | collective-permute-start | bytes 196616 | tf_op jit(solution)/shard_map/ppermute | solution.py:155
  71.0 9.2 %collective-permute-start.24 = (bf16[2,128,128]{2,1,0:T(8,128)(2,1)S(1)}, bf16[2,128,128]{2,1,0:T(8,128)(2,1)S(1)}, u32[]{:S(2)}, u32[]{:S(2)}) collective-permute-start(bf16[2,128,128]{2,1,0:T(8,128)(2,1)S(1)} %get-tuple-element.46), channel_id=1, source_target_pairs={{0,4},{2,6},{4,0},{6,2},{1,5},{3,7},{5,1},{7,3},{8,12},{10,14},{12... | collective-permute-start | bytes 196616 | tf_op jit(solution)/shard_map/ppermute | solution.py:155
  71.2 9.0 %collective-permute-start.25 = (bf16[2,128,128]{2,1,0:T(8,128)(2,1)S(1)}, bf16[2,128,128]{2,1,0:T(8,128)(2,1)S(1)}, u32[]{:S(2)}, u32[]{:S(2)}) collective-permute-start(bf16[2,128,128]{2,1,0:T(8,128)(2,1)S(1)} %get-tuple-element.45), channel_id=1, source_target_pairs={{0,6},{2,0},{4,2},{6,4},{1,7},{3,1},{5,3},{7,5},{8,14},{10,8},{12,... | collective-permute-start | bytes 196616 | tf_op jit(solution)/shard_map/ppermute | solution.py:155
  74.1 6.2 %collective-permute-start.17 = (bf16[2,128,128]{2,1,0:T(8,128)(2,1)S(1)}, bf16[2,128,128]{2,1,0:T(8,128)(2,1)S(1)}, u32[]{:S(2)}, u32[]{:S(2)}) collective-permute-start(bf16[2,128,128]{2,1,0:T(8,128)(2,1)S(1)} %get-tuple-element.43), channel_id=1, source_target_pairs={{0,2},{2,4},{4,6},{6,0},{1,3},{3,5},{5,7},{7,1},{8,10},{10,12},{12... | collective-permute-start | bytes 196616 | tf_op jit(solution)/shard_map/ppermute | solution.py:155
  (21 other events, 68.7 us)

commit v18 on v15

--- a/solution.py
+++ b/solution.py
@@ -22,15 +22,18 @@
 
 
 def attention_grad_kernel(layout, blocks_ref, length_ref, place_ref, q_ref, do_ref, *refs):
-    n_in, n_slots, slot_rows, xor_slots, out_ranges, aliased = layout
+    n_in, n_slots, slot_rows, xor_slots, out_ranges, aliased, per_chunk = layout
+    g = pl.program_id(0)
+    slot_in = g // per_chunk
+    feat = slice(None) if per_chunk == 1 else pl.ds(pl.multiple_of((g % per_chunk) * HEAD_DIM, HEAD_DIM), HEAD_DIM)
     kv_refs = refs[:n_in]
     kr_ref, vr_ref = refs[n_in:n_in + 2]
     outs = refs[n_in + 2 + (3 if aliased else 0):]
     dq_ref, dkr_ref, dvr_ref = outs[:3]
     piece_refs = outs[3:]
     resp_rows = q_ref.shape[0]
-    kp = jnp.concatenate([r[0] for r in kv_refs], 0)
-    vp = jnp.concatenate([r[1] for r in kv_refs], 0)
+    kp = jnp.concatenate([r[slot_in, 0, :, feat] for r in kv_refs], 0)
+    vp = jnp.concatenate([r[slot_in, 1, :, feat] for r in kv_refs], 0)
     pre_rows = kp.shape[0]
     kr = kr_ref[...]
     vr = vr_ref[...]
@@ -109,7 +112,7 @@
         return ((r[0] + n_pair - g // per_chunk) % n_pair) * chunk_heads + first_head + g % per_chunk
 
     def piece_spec(rows):
-        return pl.BlockSpec((None, 2, rows, HEAD_DIM), lambda g, b, n, r: (g // per_chunk, 0, 0, g % per_chunk))
+        return pl.BlockSpec(memory_space=pltpu.VMEM)
 
     qspec = pl.BlockSpec((resp_rows, GROUP * HEAD_DIM), lambda g, b, n, r: (0, head(g, r)))
     rspec = pl.BlockSpec((resp_rows, HEAD_DIM), lambda g, b, n, r: (0, head(g, r)))
@@ -131,7 +134,8 @@
         jax.ShapeDtypeStruct((resp_rows, kv_width), jnp.bfloat16),
         jax.ShapeDtypeStruct((resp_rows, kv_width), jnp.bfloat16),
     ] + [jax.ShapeDtypeStruct((n_pair, 2, rows, chunk_feats), jnp.bfloat16) for rows in out_rows]
-    layout = (len(pieces), n_slots, slot_rows, xor_slots, tuple(tuple(r) for r in out_ranges), earlier is not None)
+    layout = (len(pieces), n_slots, slot_rows, xor_slots, tuple(tuple(r) for r in out_ranges), earlier is not None,
+              per_chunk)
     flops = 2 * 6 * resp_rows * GROUP * heads * (pre_rows + resp_rows) * HEAD_DIM
     return pl.pallas_call(
         functools.partial(attention_grad_kernel, layout),

time: 85.1 us -> 85.7 us (level)
  transfers between devices with their start and end apart: 26 -> 26, of which waited for: 5 -> 5; matrix products, arithmetic and copies ran while one was open for 6% -> 6% of each run, Pallas kernels for 17% -> 18%
where the time goes in v18:
time: 85.7 us; the launch traced here: 85.3 us
  starting transfers between devices  42.1 us (49%)
  Pallas kernels  15.4 us (18%)
  between operations  9.53 us (11%)
  waiting for transfers between devices  7.37 us (9%)
  other arithmetic  5.56 us (6%)
  local copies, waits for them, and re-layouts  5.34 us (6%)
    ppermute x12, starting transfers between devices, ring_shift(): return lax.ppermute(x, axis, [(i, (i + d) % n) for i in range(n)])  22.5 us
    pallas_call x2, Pallas kernels, attention_grads(): pl.pallas_call(functools.partial(attention_grad_kernel, layout), out_shap...  15.4 us
    ppermute x6, starting transfers between devices, ctx_reduce(): lax.ppermute(pieces[j], 'ctx', [(i, i ^ j) for i in range(n)])  7.11 us
    ppermute x12, waiting for transfers between devices, ring_shift(): return lax.ppermute(x, axis, [(i, (i + d) % n) for i in range(n)])  3.84 us
    ppermute x2, starting transfers between devices, ctx_gather(): from_y = lax.ppermute(x, 'ctx', along_y)  3.39 us
    ppermute x2, waiting for transfers between devices, ctx_gather(): from_y = lax.ppermute(x, 'ctx', along_y)  3.19 us
    ppermute x2, starting transfers between devices, ctx_gather(): far_b = lax.ppermute(from_x[:, :, half:], 'ctx', along_y)  3.17 us
    unnamed x39, local copies, waits for them, and re-layouts  3.13 us
  transfers between devices with their start and end apart: 26, of which 5 were waited for; matrix products, arithmetic and copies ran while one was open for 6% of the time, Pallas kernels for 18%

profile of v18, /device:TPU:0, one launch (start us, length us, event | category | flops | bytes accessed | tf_op | source)
XLA Modules:
  0.0 85.3 jit_solution(8833670283438278168)
XLA Ops:
  10.8 3.1 %collective-permute-start = (bf16[2,128,128]{2,1,0:T(8,128)(2,1)S(1)}, bf16[2,128,128]{2,1,0:T(8,128)(2,1)S(1)}, u32[]{:S(2)}, u32[]{:S(2)}) collective-permute-start(bf16[2,128,128]{2,1,0:T(8,128)(2,1)S(1)} %get-tuple-element.49), channel_id=1, source_target_pairs={{0,2},{2,4},{4,6},{6,0},{1,3},{3,5},{5,7},{7,1},{8,10},{10,12},{12... | collective-permute-start | bytes 196616 | tf_op jit(solution)/shard_map/ppermute | solution.py:159
  13.9 2.6 %collective-permute-start.1 = (bf16[2,128,128]{2,1,0:T(8,128)(2,1)S(1)}, bf16[2,128,128]{2,1,0:T(8,128)(2,1)S(1)}, u32[]{:S(2)}, u32[]{:S(2)}) collective-permute-start(bf16[2,128,128]{2,1,0:T(8,128)(2,1)S(1)} %get-tuple-element.48), channel_id=1, source_target_pairs={{0,4},{2,6},{4,0},{6,2},{1,5},{3,7},{5,1},{7,3},{8,12},{10,14},{12... | collective-permute-start | bytes 196616 | tf_op jit(solution)/shard_map/ppermute | solution.py:159
  16.4 1.3 %collective-permute-start.2 = (bf16[2,128,128]{2,1,0:T(8,128)(2,1)S(1)}, bf16[2,128,128]{2,1,0:T(8,128)(2,1)S(1)}, u32[]{:S(2)}, u32[]{:S(2)}) collective-permute-start(bf16[2,128,128]{2,1,0:T(8,128)(2,1)S(1)} %get-tuple-element.47), channel_id=1, source_target_pairs={{0,6},{2,0},{4,2},{6,4},{1,7},{3,1},{5,3},{7,5},{8,14},{10,8},{12,... | collective-permute-start | bytes 196616 | tf_op jit(solution)/shard_map/ppermute | solution.py:159
  19.6 2.8 %collective-permute-start.9 = (bf16[2,128,128]{2,1,0:T(8,128)(2,1)S(1)}, bf16[2,128,128]{2,1,0:T(8,128)(2,1)S(1)}, u32[]{:S(2)}, u32[]{:S(2)}) collective-permute-start(bf16[2,128,128]{2,1,0:T(8,128)(2,1)S(1)} %get-tuple-element.43), channel_id=1, source_target_pairs={{0,6},{2,0},{4,2},{6,4},{1,7},{3,1},{5,3},{7,5},{8,14},{10,8},{12,... | collective-permute-start | bytes 196616 | tf_op jit(solution)/shard_map/ppermute | solution.py:159
  22.5 1.6 %collective-permute-start.4 = (bf16[4,2,128,128]{3,2,1,0:T(8,128)(2,1)S(1)}, bf16[4,2,128,128]{3,2,1,0:T(8,128)(2,1)S(1)}, u32[]{:S(2)}, u32[]{:S(2)}) collective-permute-start(bf16[4,2,128,128]{3,2,1,0:T(8,128)(2,1)S(1)} %pad_maximum_fusion.1.refs_0_), channel_id=1, source_target_pairs={{0,16},{8,24},{16,0},{24,8},{1,17},{9,25},{17,1},{25,9},{2,18},{10... | collective-permute-start | bytes 786440 | tf_op jit(solution)/shard_map/ppermute | solution.py:184
  24.1 1.5 %collective-permute-start.3 = (bf16[4,2,128,128]{3,2,1,0:T(8,128)(2,1)S(1)}, bf16[4,2,128,128]{3,2,1,0:T(8,128)(2,1)S(1)}, u32[]{:S(2)}, u32[]{:S(2)}) collective-permute-start(bf16[4,2,128,128]{3,2,1,0:T(8,128)(2,1)S(1)} %pad_maximum_fusion.1.refs_0_), channel_id=1, source_target_pairs={{0,8},{8,0},{16,24},{24,16},{1,9},{9,1},{17,25},{25,17},{2,10},{10... | collective-permute-start | bytes 786440 | tf_op jit(solution)/shard_map/ppermute | solution.py:183
  26.7 1.8 %collective-permute-start.11 = (bf16[4,2,128,128]{3,2,1,0:T(8,128)(2,1)S(1)}, bf16[4,2,128,128]{3,2,1,0:T(8,128)(2,1)S(1)}, u32[]{:S(2)}, u32[]{:S(2)}) collective-permute-start(bf16[4,2,128,128]{3,2,1,0:T(8,128)(2,1)S(1)} %pad_maximum_fusion.2.refs_0_), channel_id=1, source_target_pairs={{0,16},{8,24},{16,0},{24,8},{1,17},{9,25},{17,1},{25,9},{2,18},{10... | collective-permute-start | bytes 786440 | tf_op jit(solution)/shard_map/ppermute | solution.py:184
  28.5 1.5 %collective-permute-start.10 = (bf16[4,2,128,128]{3,2,1,0:T(8,128)(2,1)S(1)}, bf16[4,2,128,128]{3,2,1,0:T(8,128)(2,1)S(1)}, u32[]{:S(2)}, u32[]{:S(2)}) collective-permute-start(bf16[4,2,128,128]{3,2,1,0:T(8,128)(2,1)S(1)} %pad_maximum_fusion.2.refs_0_), channel_id=1, source_target_pairs={{0,8},{8,0},{16,24},{24,16},{1,9},{9,1},{17,25},{25,17},{2,10},{10... | collective-permute-start | bytes 786440 | tf_op jit(solution)/shard_map/ppermute | solution.py:183
  31.2 1.6 %collective-permute-start.6 = (bf16[4,2,64,128]{3,2,1,0:T(8,128)(2,1)S(1)}, bf16[4,2,64,128]{3,2,1,0:T(8,128)(2,1)S(1)}, u32[]{:S(2)}, u32[]{:S(2)}) collective-permute-start(bf16[4,2,64,128]{3,2,1,0:T(8,128)(2,1)S(1)} %slice.80), channel_id=1, source_target_pairs={{0,16},{8,24},{16,0},{24,8},{1,17},{9,25},{17,1},{25,9},{2,18},{10... | collective-permute-start | bytes 393224 | tf_op jit(solution)/shard_map/ppermute | solution.py:187
  32.8 3.2 %collective-permute-done.11.refs_2_ = bf16[4,2,128,128]{3,2,1,0:T(8,128)(2,1)S(1)} collective-permute-done((bf16[4,2,128,128]{3,2,1,0:T(8,128)(2,1)S(1)}, bf16[4,2,128,128]{3,2,1,0:T(8,128)(2,1)S(1)}, u32[]{:S(2)}, u32[]{:S(2)}) %collective-permute-start.11) | collective-permute-done | bytes 262176 | tf_op jit(solution)/shard_map/ppermute | solution.py:184
  36.0 1.8 %collective-permute-start.12 = (bf16[4,2,64,128]{3,2,1,0:T(8,128)(2,1)S(1)}, bf16[4,2,64,128]{3,2,1,0:T(8,128)(2,1)S(1)}, u32[]{:S(2)}, u32[]{:S(2)}) collective-permute-start(bf16[4,2,64,128]{3,2,1,0:T(8,128)(2,1)S(1)} %slice.82), channel_id=1, source_target_pairs={{0,8},{8,0},{16,24},{24,16},{1,9},{9,1},{17,25},{25,17},{2,10},{10... | collective-permute-start | bytes 393224 | tf_op jit(solution)/shard_map/ppermute | solution.py:186
  37.8 1.6 %collective-permute-start.13 = (bf16[4,2,64,128]{3,2,1,0:T(8,128)(2,1)S(1)}, bf16[4,2,64,128]{3,2,1,0:T(8,128)(2,1)S(1)}, u32[]{:S(2)}, u32[]{:S(2)}) collective-permute-start(bf16[4,2,64,128]{3,2,1,0:T(8,128)(2,1)S(1)} %slice.83), channel_id=1, source_target_pairs={{0,16},{8,24},{16,0},{24,8},{1,17},{9,25},{17,1},{25,9},{2,18},{10... | collective-permute-start | bytes 393224 | tf_op jit(solution)/shard_map/ppermute | solution.py:187
  41.3 7.7 %shard_map.111 = (bf16[128,2048]{1,0:T(8,128)(2,1)}, bf16[128,1024]{1,0:T(8,128)(2,1)}, bf16[128,1024]{1,0:T(8,128)(2,1)}, bf16[4,2,128,128]{3,2,1,0:T(8,128)(2,...) custom-call(s32[4]{0:T(128)} %bitcast.104, ...), custom_call_target="tpu_custom_call" | custom-call | flops 1006632960 | bytes 3670016 | tf_op jit(solution)/shard_map/pallas_call | solution.py:140
  49.0 1.2 %collective-permute-start.20 = (bf16[4,2,128,128]{3,2,1,0:T(8,128)(2,1)}, bf16[4,2,128,128]{3,2,1,0:T(8,128)(2,1)S(1)}, u32[]{:S(2)}, u32[]{:S(2)}) collective-permute-start(bf16[4,2,128,128]{3,2,1,0:T(8,128)(2,1)} %get-tuple-element.29), channel_id=1, source_target_pairs={{0,8},{8,0},{16,24},{24,16},{1,9},{9,1},{17,25},{25,17},{2,10},{10... | collective-permute-start | bytes 786440 | tf_op jit(solution)/shard_map/ppermute | solution.py:201
  51.0 1.6 %collective-permute-start.22 = (bf16[4,2,128,128]{3,2,1,0:T(8,128)(2,1)}, bf16[4,2,128,128]{3,2,1,0:T(8,128)(2,1)S(1)}, u32[]{:S(2)}, u32[]{:S(2)}) collective-permute-start(bf16[4,2,128,128]{3,2,1,0:T(8,128)(2,1)} %get-tuple-element.31), channel_id=1, source_target_pairs={{0,24},{8,16},{16,8},{24,0},{1,25},{9,17},{17,9},{25,1},{2,26},{10... | collective-permute-start | bytes 786440 | tf_op jit(solution)/shard_map/ppermute | solution.py:201
  53.3 7.8 %shard_map.112 = (bf16[128,2048]{1,0:T(8,128)(2,1)}, bf16[128,1024]{1,0:T(8,128)(2,1)}, bf16[128,1024]{1,0:T(8,128)(2,1)}, bf16[4,2,128,128]{3,2,1,0:T(8,128)(2,...) custom-call(s32[4]{0:T(128)} %bitcast.105, ...), custom_call_target="tpu_custom_call" | custom-call | flops 1006632960 | bytes 3670016 | tf_op jit(solution)/shard_map/pallas_call | solution.py:140
  61.1 1.2 %collective-permute-start.14 = (bf16[4,2,128,128]{3,2,1,0:T(8,128)(2,1)}, bf16[4,2,128,128]{3,2,1,0:T(8,128)(2,1)S(1)}, u32[]{:S(2)}, u32[]{:S(2)}) collective-permute-start(bf16[4,2,128,128]{3,2,1,0:T(8,128)(2,1)} %get-tuple-element.25), channel_id=1, source_target_pairs={{0,8},{8,0},{16,24},{24,16},{1,9},{9,1},{17,25},{25,17},{2,10},{10... | collective-permute-start | bytes 786440 | tf_op jit(solution)/shard_map/ppermute | solution.py:201
  63.1 2.0 %select_bitcast_fusion = bf16[1,1,128,2048]{3,2,1,0:T(8,128)(2,1)} fusion(bf16[128,2048]{1,0:T(8,128)(2,1)S(1)} %copy-done.1, bf16[128,2048]{1,0:T(8,128)(2,1)} %get-tuple-element.19, pred[2048]{0:T(1024)(128)(4,1)S(1)} %fusion.1), kind=kLoop, calls=%fused_computation.4 | loop fusion | flops 262144 | bytes 1574912 | tf_op jit(solution)/shard_map/broadcast_in_dim | solution.py:258
  66.0 1.6 %collective-permute-start.16 = (bf16[4,2,128,128]{3,2,1,0:T(8,128)(2,1)S(1)}, bf16[4,2,128,128]{3,2,1,0:T(8,128)(2,1)S(1)}, u32[]{:S(2)}, u32[]{:S(2)}) collective-permute-start(bf16[4,2,128,128]{3,2,1,0:T(8,128)(2,1)S(1)} %copy-done.14), channel_id=1, source_target_pairs={{0,24},{8,16},{16,8},{24,0},{1,25},{9,17},{17,9},{25,1},{2,26},{10... | collective-permute-start | bytes 786440 | tf_op jit(solution)/shard_map/ppermute | solution.py:201
  67.8 3.4 %collective-permute-start.23 = (bf16[2,128,128]{2,1,0:T(8,128)(2,1)S(1)}, bf16[2,128,128]{2,1,0:T(8,128)(2,1)S(1)}, u32[]{:S(2)}, u32[]{:S(2)}) collective-permute-start(bf16[2,128,128]{2,1,0:T(8,128)(2,1)S(1)} %get-tuple-element.39), channel_id=1, source_target_pairs={{0,2},{2,4},{4,6},{6,0},{1,3},{3,5},{5,7},{7,1},{8,10},{10,12},{12... | collective-permute-start | bytes 196616 | tf_op jit(solution)/shard_map/ppermute | solution.py:159
  71.4 2.2 %collective-permute-start.25 = (bf16[2,128,128]{2,1,0:T(8,128)(2,1)S(1)}, bf16[2,128,128]{2,1,0:T(8,128)(2,1)S(1)}, u32[]{:S(2)}, u32[]{:S(2)}) collective-permute-start(bf16[2,128,128]{2,1,0:T(8,128)(2,1)S(1)} %get-tuple-element.37), channel_id=1, source_target_pairs={{0,6},{2,0},{4,2},{6,4},{1,7},{3,1},{5,3},{7,5},{8,14},{10,8},{12,... | collective-permute-start | bytes 196616 | tf_op jit(solution)/shard_map/ppermute | solution.py:159
  74.2 3.3 %collective-permute-start.17 = (bf16[2,128,128]{2,1,0:T(8,128)(2,1)S(1)}, bf16[2,128,128]{2,1,0:T(8,128)(2,1)S(1)}, u32[]{:S(2)}, u32[]{:S(2)}) collective-permute-start(bf16[2,128,128]{2,1,0:T(8,128)(2,1)S(1)} %get-tuple-element.35), channel_id=1, source_target_pairs={{0,2},{2,4},{4,6},{6,0},{1,3},{3,5},{5,7},{7,1},{8,10},{10,12},{12... | collective-permute-start | bytes 196616 | tf_op jit(solution)/shard_map/ppermute | solution.py:159
  78.2 1.9 %collective-permute-start.19 = (bf16[2,128,128]{2,1,0:T(8,128)(2,1)S(1)}, bf16[2,128,128]{2,1,0:T(8,128)(2,1)S(1)}, u32[]{:S(2)}, u32[]{:S(2)}) collective-permute-start(bf16[2,128,128]{2,1,0:T(8,128)(2,1)S(1)} %get-tuple-element.33), channel_id=1, source_target_pairs={{0,6},{2,0},{4,2},{6,4},{1,7},{3,1},{5,3},{7,5},{8,14},{10,8},{12,... | collective-permute-start | bytes 196616 | tf_op jit(solution)/shard_map/ppermute | solution.py:159
  80.4 2.6 %collective-permute-done.18 = bf16[2,128,128]{2,1,0:T(8,128)(2,1)S(1)} collective-permute-done((bf16[2,128,128]{2,1,0:T(8,128)(2,1)S(1)}, bf16[2,128,128]{2,1,0:T(8,128)(2,1)S(1)}, u32[]{:S(2)}, u32[]{:S(2)}) %collective-permute-start.18) | collective-permute-done | bytes 65568 | tf_op jit(solution)/shard_map/ppermute | solution.py:159
  (109 shorter events, 15.1 us)
Async XLA Ops:
  10.8 8.8 %collective-permute-start = (bf16[2,128,128]{2,1,0:T(8,128)(2,1)S(1)}, bf16[2,128,128]{2,1,0:T(8,128)(2,1)S(1)}, u32[]{:S(2)}, u32[]{:S(2)}) collective-permute-start(bf16[2,128,128]{2,1,0:T(8,128)(2,1)S(1)} %get-tuple-element.49), channel_id=1, source_target_pairs={{0,2},{2,4},{4,6},{6,0},{1,3},{3,5},{5,7},{7,1},{8,10},{10,12},{12... | collective-permute-start | bytes 196616 | tf_op jit(solution)/shard_map/ppermute | solution.py:159
  13.9 8.6 %collective-permute-start.1 = (bf16[2,128,128]{2,1,0:T(8,128)(2,1)S(1)}, bf16[2,128,128]{2,1,0:T(8,128)(2,1)S(1)}, u32[]{:S(2)}, u32[]{:S(2)}) collective-permute-start(bf16[2,128,128]{2,1,0:T(8,128)(2,1)S(1)} %get-tuple-element.48), channel_id=1, source_target_pairs={{0,4},{2,6},{4,0},{6,2},{1,5},{3,7},{5,1},{7,3},{8,12},{10,14},{12... | collective-permute-start | bytes 196616 | tf_op jit(solution)/shard_map/ppermute | solution.py:159
  16.4 6.0 %collective-permute-start.2 = (bf16[2,128,128]{2,1,0:T(8,128)(2,1)S(1)}, bf16[2,128,128]{2,1,0:T(8,128)(2,1)S(1)}, u32[]{:S(2)}, u32[]{:S(2)}) collective-permute-start(bf16[2,128,128]{2,1,0:T(8,128)(2,1)S(1)} %get-tuple-element.47), channel_id=1, source_target_pairs={{0,6},{2,0},{4,2},{6,4},{1,7},{3,1},{5,3},{7,5},{8,14},{10,8},{12,... | collective-permute-start | bytes 196616 | tf_op jit(solution)/shard_map/ppermute | solution.py:159
  17.8 7.8 %collective-permute-start.7 = (bf16[2,128,128]{2,1,0:T(8,128)(2,1)S(1)}, bf16[2,128,128]{2,1,0:T(8,128)(2,1)S(1)}, u32[]{:S(2)}, u32[]{:S(2)}) collective-permute-start(bf16[2,128,128]{2,1,0:T(8,128)(2,1)S(1)} %get-tuple-element.45), channel_id=1, source_target_pairs={{0,2},{2,4},{4,6},{6,0},{1,3},{3,5},{5,7},{7,1},{8,10},{10,12},{12... | collective-permute-start | bytes 196616 | tf_op jit(solution)/shard_map/ppermute | solution.py:159
  18.5 8.0 %collective-permute-start.8 = (bf16[2,128,128]{2,1,0:T(8,128)(2,1)S(1)}, bf16[2,128,128]{2,1,0:T(8,128)(2,1)S(1)}, u32[]{:S(2)}, u32[]{:S(2)}) collective-permute-start(bf16[2,128,128]{2,1,0:T(8,128)(2,1)S(1)} %get-tuple-element.44), channel_id=1, source_target_pairs={{0,4},{2,6},{4,0},{6,2},{1,5},{3,7},{5,1},{7,3},{8,12},{10,14},{12... | collective-permute-start | bytes 196616 | tf_op jit(solution)/shard_map/ppermute | solution.py:159
  19.6 7.0 %collective-permute-start.9 = (bf16[2,128,128]{2,1,0:T(8,128)(2,1)S(1)}, bf16[2,128,128]{2,1,0:T(8,128)(2,1)S(1)}, u32[]{:S(2)}, u32[]{:S(2)}) collective-permute-start(bf16[2,128,128]{2,1,0:T(8,128)(2,1)S(1)} %get-tuple-element.43), channel_id=1, source_target_pairs={{0,6},{2,0},{4,2},{6,4},{1,7},{3,1},{5,3},{7,5},{8,14},{10,8},{12,... | collective-permute-start | bytes 196616 | tf_op jit(solution)/shard_map/ppermute | solution.py:159
  22.5 7.5 %collective-permute-start.4 = (bf16[4,2,128,128]{3,2,1,0:T(8,128)(2,1)S(1)}, bf16[4,2,128,128]{3,2,1,0:T(8,128)(2,1)S(1)}, u32[]{:S(2)}, u32[]{:S(2)}) collective-permute-start(bf16[4,2,128,128]{3,2,1,0:T(8,128)(2,1)S(1)} %pad_maximum_fusion.1.refs_0_), channel_id=1, source_target_pairs={{0,16},{8,24},{16,0},{24,8},{1,17},{9,25},{17,1},{25,9},{2,18},{10... | collective-permute-start | bytes 786440 | tf_op jit(solution)/shard_map/ppermute | solution.py:184
  24.1 7.0 %collective-permute-start.3 = (bf16[4,2,128,128]{3,2,1,0:T(8,128)(2,1)S(1)}, bf16[4,2,128,128]{3,2,1,0:T(8,128)(2,1)S(1)}, u32[]{:S(2)}, u32[]{:S(2)}) collective-permute-start(bf16[4,2,128,128]{3,2,1,0:T(8,128)(2,1)S(1)} %pad_maximum_fusion.1.refs_0_), channel_id=1, source_target_pairs={{0,8},{8,0},{16,24},{24,16},{1,9},{9,1},{17,25},{25,17},{2,10},{10... | collective-permute-start | bytes 786440 | tf_op jit(solution)/shard_map/ppermute | solution.py:183
  26.7 9.3 %collective-permute-start.11 = (bf16[4,2,128,128]{3,2,1,0:T(8,128)(2,1)S(1)}, bf16[4,2,128,128]{3,2,1,0:T(8,128)(2,1)S(1)}, u32[]{:S(2)}, u32[]{:S(2)}) collective-permute-start(bf16[4,2,128,128]{3,2,1,0:T(8,128)(2,1)S(1)} %pad_maximum_fusion.2.refs_0_), channel_id=1, source_target_pairs={{0,16},{8,24},{16,0},{24,8},{1,17},{9,25},{17,1},{25,9},{2,18},{10... | collective-permute-start | bytes 786440 | tf_op jit(solution)/shard_map/ppermute | solution.py:184
  28.5 9.3 %collective-permute-start.10 = (bf16[4,2,128,128]{3,2,1,0:T(8,128)(2,1)S(1)}, bf16[4,2,128,128]{3,2,1,0:T(8,128)(2,1)S(1)}, u32[]{:S(2)}, u32[]{:S(2)}) collective-permute-start(bf16[4,2,128,128]{3,2,1,0:T(8,128)(2,1)S(1)} %pad_maximum_fusion.2.refs_0_), channel_id=1, source_target_pairs={{0,8},{8,0},{16,24},{24,16},{1,9},{9,1},{17,25},{25,17},{2,10},{10... | collective-permute-start | bytes 786440 | tf_op jit(solution)/shard_map/ppermute | solution.py:183
  30.0 10.6 %collective-permute-start.5 = (bf16[4,2,64,128]{3,2,1,0:T(8,128)(2,1)S(1)}, bf16[4,2,64,128]{3,2,1,0:T(8,128)(2,1)S(1)}, u32[]{:S(2)}, u32[]{:S(2)}) collective-permute-start(bf16[4,2,64,128]{3,2,1,0:T(8,128)(2,1)S(1)} %slice.79), channel_id=1, source_target_pairs={{0,8},{8,0},{16,24},{24,16},{1,9},{9,1},{17,25},{25,17},{2,10},{10... | collective-permute-start | bytes 393224 | tf_op jit(solution)/shard_map/ppermute | solution.py:186
  31.2 9.5 %collective-permute-start.6 = (bf16[4,2,64,128]{3,2,1,0:T(8,128)(2,1)S(1)}, bf16[4,2,64,128]{3,2,1,0:T(8,128)(2,1)S(1)}, u32[]{:S(2)}, u32[]{:S(2)}) collective-permute-start(bf16[4,2,64,128]{3,2,1,0:T(8,128)(2,1)S(1)} %slice.80), channel_id=1, source_target_pairs={{0,16},{8,24},{16,0},{24,8},{1,17},{9,25},{17,1},{25,9},{2,18},{10... | collective-permute-start | bytes 393224 | tf_op jit(solution)/shard_map/ppermute | solution.py:187
  36.0 16.6 %collective-permute-start.12 = (bf16[4,2,64,128]{3,2,1,0:T(8,128)(2,1)S(1)}, bf16[4,2,64,128]{3,2,1,0:T(8,128)(2,1)S(1)}, u32[]{:S(2)}, u32[]{:S(2)}) collective-permute-start(bf16[4,2,64,128]{3,2,1,0:T(8,128)(2,1)S(1)} %slice.82), channel_id=1, source_target_pairs={{0,8},{8,0},{16,24},{24,16},{1,9},{9,1},{17,25},{25,17},{2,10},{10... | collective-permute-start | bytes 393224 | tf_op jit(solution)/shard_map/ppermute | solution.py:186
  37.8 14.8 %collective-permute-start.13 = (bf16[4,2,64,128]{3,2,1,0:T(8,128)(2,1)S(1)}, bf16[4,2,64,128]{3,2,1,0:T(8,128)(2,1)S(1)}, u32[]{:S(2)}, u32[]{:S(2)}) collective-permute-start(bf16[4,2,64,128]{3,2,1,0:T(8,128)(2,1)S(1)} %slice.83), channel_id=1, source_target_pairs={{0,16},{8,24},{16,0},{24,8},{1,17},{9,25},{17,1},{25,9},{2,18},{10... | collective-permute-start | bytes 393224 | tf_op jit(solution)/shard_map/ppermute | solution.py:187
  49.0 16.9 %collective-permute-start.20 = (bf16[4,2,128,128]{3,2,1,0:T(8,128)(2,1)}, bf16[4,2,128,128]{3,2,1,0:T(8,128)(2,1)S(1)}, u32[]{:S(2)}, u32[]{:S(2)}) collective-permute-start(bf16[4,2,128,128]{3,2,1,0:T(8,128)(2,1)} %get-tuple-element.29), channel_id=1, source_target_pairs={{0,8},{8,0},{16,24},{24,16},{1,9},{9,1},{17,25},{25,17},{2,10},{10... | collective-permute-start | bytes 786440 | tf_op jit(solution)/shard_map/ppermute | solution.py:201
  50.2 17.4 %collective-permute-start.21 = (bf16[4,2,128,128]{3,2,1,0:T(8,128)(2,1)}, bf16[4,2,128,128]{3,2,1,0:T(8,128)(2,1)S(1)}, u32[]{:S(2)}, u32[]{:S(2)}) collective-permute-start(bf16[4,2,128,128]{3,2,1,0:T(8,128)(2,1)} %get-tuple-element.30), channel_id=1, source_target_pairs={{0,16},{8,24},{16,0},{24,8},{1,17},{9,25},{17,1},{25,9},{2,18},{10... | collective-permute-start | bytes 786440 | tf_op jit(solution)/shard_map/ppermute | solution.py:201
  51.0 16.6 %collective-permute-start.22 = (bf16[4,2,128,128]{3,2,1,0:T(8,128)(2,1)}, bf16[4,2,128,128]{3,2,1,0:T(8,128)(2,1)S(1)}, u32[]{:S(2)}, u32[]{:S(2)}) collective-permute-start(bf16[4,2,128,128]{3,2,1,0:T(8,128)(2,1)} %get-tuple-element.31), channel_id=1, source_target_pairs={{0,24},{8,16},{16,8},{24,0},{1,25},{9,17},{17,9},{25,1},{2,26},{10... | collective-permute-start | bytes 786440 | tf_op jit(solution)/shard_map/ppermute | solution.py:201
  61.1 10.4 %collective-permute-start.14 = (bf16[4,2,128,128]{3,2,1,0:T(8,128)(2,1)}, bf16[4,2,128,128]{3,2,1,0:T(8,128)(2,1)S(1)}, u32[]{:S(2)}, u32[]{:S(2)}) collective-permute-start(bf16[4,2,128,128]{3,2,1,0:T(8,128)(2,1)} %get-tuple-element.25), channel_id=1, source_target_pairs={{0,8},{8,0},{16,24},{24,16},{1,9},{9,1},{17,25},{25,17},{2,10},{10... | collective-permute-start | bytes 786440 | tf_op jit(solution)/shard_map/ppermute | solution.py:201
  62.3 11.6 %collective-permute-start.15 = (bf16[4,2,128,128]{3,2,1,0:T(8,128)(2,1)}, bf16[4,2,128,128]{3,2,1,0:T(8,128)(2,1)S(1)}, u32[]{:S(2)}, u32[]{:S(2)}) collective-permute-start(bf16[4,2,128,128]{3,2,1,0:T(8,128)(2,1)} %get-tuple-element.26), channel_id=1, source_target_pairs={{0,16},{8,24},{16,0},{24,8},{1,17},{9,25},{17,1},{25,9},{2,18},{10... | collective-permute-start | bytes 786440 | tf_op jit(solution)/shard_map/ppermute | solution.py:201
  66.0 7.9 %collective-permute-start.16 = (bf16[4,2,128,128]{3,2,1,0:T(8,128)(2,1)S(1)}, bf16[4,2,128,128]{3,2,1,0:T(8,128)(2,1)S(1)}, u32[]{:S(2)}, u32[]{:S(2)}) collective-permute-start(bf16[4,2,128,128]{3,2,1,0:T(8,128)(2,1)S(1)} %copy-done.14), channel_id=1, source_target_pairs={{0,24},{8,16},{16,8},{24,0},{1,25},{9,17},{17,9},{25,1},{2,26},{10... | collective-permute-start | bytes 786440 | tf_op jit(solution)/shard_map/ppermute | solution.py:201
  67.8 10.4 %collective-permute-start.23 = (bf16[2,128,128]{2,1,0:T(8,128)(2,1)S(1)}, bf16[2,128,128]{2,1,0:T(8,128)(2,1)S(1)}, u32[]{:S(2)}, u32[]{:S(2)}) collective-permute-start(bf16[2,128,128]{2,1,0:T(8,128)(2,1)S(1)} %get-tuple-element.39), channel_id=1, source_target_pairs={{0,2},{2,4},{4,6},{6,0},{1,3},{3,5},{5,7},{7,1},{8,10},{10,12},{12... | collective-permute-start | bytes 196616 | tf_op jit(solution)/shard_map/ppermute | solution.py:159
  71.1 9.0 %collective-permute-start.24 = (bf16[2,128,128]{2,1,0:T(8,128)(2,1)S(1)}, bf16[2,128,128]{2,1,0:T(8,128)(2,1)S(1)}, u32[]{:S(2)}, u32[]{:S(2)}) collective-permute-start(bf16[2,128,128]{2,1,0:T(8,128)(2,1)S(1)} %get-tuple-element.38), channel_id=1, source_target_pairs={{0,4},{2,6},{4,0},{6,2},{1,5},{3,7},{5,1},{7,3},{8,12},{10,14},{12... | collective-permute-start | bytes 196616 | tf_op jit(solution)/shard_map/ppermute | solution.py:159
  71.4 8.8 %collective-permute-start.25 = (bf16[2,128,128]{2,1,0:T(8,128)(2,1)S(1)}, bf16[2,128,128]{2,1,0:T(8,128)(2,1)S(1)}, u32[]{:S(2)}, u32[]{:S(2)}) collective-permute-start(bf16[2,128,128]{2,1,0:T(8,128)(2,1)S(1)} %get-tuple-element.37), channel_id=1, source_target_pairs={{0,6},{2,0},{4,2},{6,4},{1,7},{3,1},{5,3},{7,5},{8,14},{10,8},{12,... | collective-permute-start | bytes 196616 | tf_op jit(solution)/shard_map/ppermute | solution.py:159
  74.2 6.2 %collective-permute-start.17 = (bf16[2,128,128]{2,1,0:T(8,128)(2,1)S(1)}, bf16[2,128,128]{2,1,0:T(8,128)(2,1)S(1)}, u32[]{:S(2)}, u32[]{:S(2)}) collective-permute-start(bf16[2,128,128]{2,1,0:T(8,128)(2,1)S(1)} %get-tuple-element.35), channel_id=1, source_target_pairs={{0,2},{2,4},{4,6},{6,0},{1,3},{3,5},{5,7},{7,1},{8,10},{10,12},{12... | collective-permute-start | bytes 196616 | tf_op jit(solution)/shard_map/ppermute | solution.py:159
  (21 other events, 69.3 us)

commit v19 on v15

--- a/solution.py
+++ b/solution.py
@@ -169,11 +169,13 @@
     return lax.axis_size("ctx") == 4
 
 
-def ctx_gather(x):
+def ctx_gather(x, direct=False):
     n = lax.axis_size("ctx")
     if not tree_ctx():
         got = lax.all_gather(x, "ctx", axis=0, tiled=False)
         return [got[j] for j in range(n)]
+    if direct:
+        return [x] + [lax.ppermute(x, "ctx", [(i, i ^ j) for i in range(n)]) for j in range(1, n)]
     along_x = [(i, i ^ 1) for i in range(n)]
     along_y = [(i, i ^ 2) for i in range(n)]
     from_x = lax.ppermute(x, "ctx", along_x)
@@ -234,7 +236,7 @@
     parts = []
     for k in range(n_groups):
         cols = slice(k * group_feats, (k + 1) * group_feats)
-        pieces = ctx_gather(pair_gather(planes[..., cols], pair_prompt))
+        pieces = ctx_gather(pair_gather(planes[..., cols], pair_prompt), direct=k > 0)
         outs = attention_grads(
             prefix_blocks[0, 0], resp_lengths[0, 0].reshape(1), place, queries[0, 0], d_out[0, 0], pieces,
             tree_ctx(), ctx_out_ranges(slot_rows), resp_keys[0, 0], resp_values[0, 0],

time: 85.1 us -> 93.2 us (1.095)
  waiting for transfers between devices: 7.39 us -> 22 us
  starting transfers between devices: 42.1 us -> 36 us
    ppermute x0 -> x3, waiting for transfers between devices: none -> 7.93 us  [ctx_gather(): lax.ppermute(x, 'ctx', [(i, i ^ j) for i in range(n)])]
    ppermute x12, waiting for transfers between devices: 3.84 us -> 11.5 us  [ring_shift(): return lax.ppermute(x, axis, [(i, (i + d) % n) for i in range(n)])]
    ppermute x0 -> x3, starting transfers between devices: none -> 3.55 us  [ctx_gather(): lax.ppermute(x, 'ctx', [(i, i ^ j) for i in range(n)])]
    ppermute x12, starting transfers between devices: 22.5 us -> 19 us  [ring_shift(): return lax.ppermute(x, axis, [(i, (i + d) % n) for i in range(n)])]
    ppermute x2 -> x1, starting transfers between devices: 3.39 us -> 1.65 us  [ctx_gather(): from_y = lax.ppermute(x, 'ctx', along_y)]
    ppermute x2 -> x1, starting transfers between devices: 3.17 us -> 1.58 us  [ctx_gather(): far_b = lax.ppermute(from_x[:, :, half:], 'ctx', along_y)]
    ppermute x2 -> x1, starting transfers between devices: 2.98 us -> 1.49 us  [ctx_gather(): from_x = lax.ppermute(x, 'ctx', along_x)]
    ppermute x2 -> x1, starting transfers between devices: 2.91 us -> 1.64 us  [ctx_gather(): far_a = lax.ppermute(from_y[:, :, :half], 'ctx', along_x)]
  transfers between devices with their start and end apart: 26 -> 25, of which waited for: 5 -> 13; matrix products, arithmetic and copies ran while one was open for 6% -> 6% of each run, Pallas kernels for 17% -> 16%
where the time goes in v19:
time: 93.2 us; the launch traced here: 92.8 us
  starting transfers between devices  36 us (39%)
  waiting for transfers between devices  22 us (24%)
  Pallas kernels  14.8 us (16%)
  between operations  9.18 us (10%)
  other arithmetic  5.62 us (6%)
  local copies, waits for them, and re-layouts  5.24 us (6%)
    ppermute x12, starting transfers between devices, ring_shift(): return lax.ppermute(x, axis, [(i, (i + d) % n) for i in range(n)])  19 us
    pallas_call x2, Pallas kernels, attention_grads(): pl.pallas_call(functools.partial(attention_grad_kernel, layout), out_shap...  14.8 us
    ppermute x12, waiting for transfers between devices, ring_shift(): return lax.ppermute(x, axis, [(i, (i + d) % n) for i in range(n)])  11.5 us
    ppermute x3, waiting for transfers between devices, ctx_gather(): lax.ppermute(x, 'ctx', [(i, i ^ j) for i in range(n)])  7.93 us
    ppermute x6, starting transfers between devices, ctx_reduce(): lax.ppermute(pieces[j], 'ctx', [(i, i ^ j) for i in range(n)])  7.11 us
    ppermute x3, starting transfers between devices, ctx_gather(): lax.ppermute(x, 'ctx', [(i, i ^ j) for i in range(n)])  3.55 us
    unnamed x37, local copies, waits for them, and re-layouts  3.06 us
    broadcast_in_dim x2, other arithmetic, shards(): return (dq[None, None], dkr[None, None], dvr[None, None], d_prefix)  2.79 us
  transfers between devices with their start and end apart: 25, of which 13 were waited for; matrix products, arithmetic and copies ran while one was open for 6% of the time, Pallas kernels for 16%

profile of v19, /device:TPU:0, one launch (start us, length us, event | category | flops | bytes accessed | tf_op | source)
XLA Modules:
  0.0 92.8 jit_solution(13472523077160522336)
XLA Ops:
  10.5 3.1 %collective-permute-start = (bf16[2,128,128]{2,1,0:T(8,128)(2,1)S(1)}, bf16[2,128,128]{2,1,0:T(8,128)(2,1)S(1)}, u32[]{:S(2)}, u32[]{:S(2)}) collective-permute-start(bf16[2,128,128]{2,1,0:T(8,128)(2,1)S(1)} %get-tuple-element.49), channel_id=1, source_target_pairs={{0,2},{2,4},{4,6},{6,0},{1,3},{3,5},{5,7},{7,1},{8,10},{10,12},{12... | collective-permute-start | bytes 196616 | tf_op jit(solution)/shard_map/ppermute | solution.py:155
  13.6 2.6 %collective-permute-start.1 = (bf16[2,128,128]{2,1,0:T(8,128)(2,1)S(1)}, bf16[2,128,128]{2,1,0:T(8,128)(2,1)S(1)}, u32[]{:S(2)}, u32[]{:S(2)}) collective-permute-start(bf16[2,128,128]{2,1,0:T(8,128)(2,1)S(1)} %get-tuple-element.48), channel_id=1, source_target_pairs={{0,4},{2,6},{4,0},{6,2},{1,5},{3,7},{5,1},{7,3},{8,12},{10,14},{12... | collective-permute-start | bytes 196616 | tf_op jit(solution)/shard_map/ppermute | solution.py:155
  16.3 1.8 %collective-permute-start.7 = (bf16[2,128,128]{2,1,0:T(8,128)(2,1)S(1)}, bf16[2,128,128]{2,1,0:T(8,128)(2,1)S(1)}, u32[]{:S(2)}, u32[]{:S(2)}) collective-permute-start(bf16[2,128,128]{2,1,0:T(8,128)(2,1)S(1)} %get-tuple-element.44), channel_id=1, source_target_pairs={{0,4},{2,6},{4,0},{6,2},{1,5},{3,7},{5,1},{7,3},{8,12},{10,14},{12... | collective-permute-start | bytes 196616 | tf_op jit(solution)/shard_map/ppermute | solution.py:155
  18.2 1.9 %collective-permute-start.8 = (bf16[2,128,128]{2,1,0:T(8,128)(2,1)S(1)}, bf16[2,128,128]{2,1,0:T(8,128)(2,1)S(1)}, u32[]{:S(2)}, u32[]{:S(2)}) collective-permute-start(bf16[2,128,128]{2,1,0:T(8,128)(2,1)S(1)} %get-tuple-element.43), channel_id=1, source_target_pairs={{0,6},{2,0},{4,2},{6,4},{1,7},{3,1},{5,3},{7,5},{8,14},{10,8},{12,... | collective-permute-start | bytes 196616 | tf_op jit(solution)/shard_map/ppermute | solution.py:155
  20.8 2.0 %collective-permute-done.6 = bf16[2,128,128]{2,1,0:T(8,128)(2,1)S(1)} collective-permute-done((bf16[2,128,128]{2,1,0:T(8,128)(2,1)S(1)}, bf16[2,128,128]{2,1,0:T(8,128)(2,1)S(1)}, u32[]{:S(2)}, u32[]{:S(2)}) %collective-permute-start.6) | collective-permute-done | bytes 65568 | tf_op jit(solution)/shard_map/ppermute | solution.py:155
  22.8 2.1 %collective-permute-done.7 = bf16[2,128,128]{2,1,0:T(8,128)(2,1)S(1)} collective-permute-done((bf16[2,128,128]{2,1,0:T(8,128)(2,1)S(1)}, bf16[2,128,128]{2,1,0:T(8,128)(2,1)S(1)}, u32[]{:S(2)}, u32[]{:S(2)}) %collective-permute-start.7) | collective-permute-done | bytes 65568 | tf_op jit(solution)/shard_map/ppermute | solution.py:155
  25.1 1.6 %collective-permute-start.10 = (bf16[4,2,128,128]{3,2,1,0:T(8,128)(2,1)S(1)}, bf16[4,2,128,128]{3,2,1,0:T(8,128)(2,1)S(1)}, u32[]{:S(2)}, u32[]{:S(2)}) collective-permute-start(bf16[4,2,128,128]{3,2,1,0:T(8,128)(2,1)S(1)} %pad_maximum_fusion.2.refs_0_), channel_id=1, source_target_pairs={{0,16},{8,24},{16,0},{24,8},{1,17},{9,25},{17,1},{25,9},{2,18},{10... | collective-permute-start | bytes 786440 | tf_op jit(solution)/shard_map/ppermute | solution.py:182
  29.2 1.5 %collective-permute-start.4 = (bf16[4,2,128,128]{3,2,1,0:T(8,128)(2,1)S(1)}, bf16[4,2,128,128]{3,2,1,0:T(8,128)(2,1)S(1)}, u32[]{:S(2)}, u32[]{:S(2)}) collective-permute-start(bf16[4,2,128,128]{3,2,1,0:T(8,128)(2,1)S(1)} %pad_maximum_fusion.1.refs_0_), channel_id=1, source_target_pairs={{0,16},{8,24},{16,0},{24,8},{1,17},{9,25},{17,1},{25,9},{2,18},{10... | collective-permute-start | bytes 786440 | tf_op jit(solution)/shard_map/ppermute | solution.py:178
  31.9 2.5 %collective-permute-done.10.refs_2_ = bf16[4,2,128,128]{3,2,1,0:T(8,128)(2,1)S(1)} collective-permute-done((bf16[4,2,128,128]{3,2,1,0:T(8,128)(2,1)S(1)}, bf16[4,2,128,128]{3,2,1,0:T(8,128)(2,1)S(1)}, u32[]{:S(2)}, u32[]{:S(2)}) %collective-permute-start.10) | collective-permute-done | bytes 262176 | tf_op jit(solution)/shard_map/ppermute | solution.py:182
  34.4 1.6 %collective-permute-start.11 = (bf16[4,2,64,128]{3,2,1,0:T(8,128)(2,1)S(1)}, bf16[4,2,64,128]{3,2,1,0:T(8,128)(2,1)S(1)}, u32[]{:S(2)}, u32[]{:S(2)}) collective-permute-start(bf16[4,2,64,128]{3,2,1,0:T(8,128)(2,1)S(1)} %slice.72), channel_id=1, source_target_pairs={{0,8},{8,0},{16,24},{24,16},{1,9},{9,1},{17,25},{25,17},{2,10},{10... | collective-permute-start | bytes 393224 | tf_op jit(solution)/shard_map/ppermute | solution.py:184
  36.1 1.6 %collective-permute-start.12 = (bf16[4,2,64,128]{3,2,1,0:T(8,128)(2,1)S(1)}, bf16[4,2,64,128]{3,2,1,0:T(8,128)(2,1)S(1)}, u32[]{:S(2)}, u32[]{:S(2)}) collective-permute-start(bf16[4,2,64,128]{3,2,1,0:T(8,128)(2,1)S(1)} %slice.73), channel_id=1, source_target_pairs={{0,16},{8,24},{16,0},{24,8},{1,17},{9,25},{17,1},{25,9},{2,18},{10... | collective-permute-start | bytes 393224 | tf_op jit(solution)/shard_map/ppermute | solution.py:185
  39.0 2.6 %collective-permute-done.3.refs_1_ = bf16[4,2,128,128]{3,2,1,0:T(8,128)(2,1)S(1)} collective-permute-done((bf16[4,2,128,128]{3,2,1,0:T(8,128)(2,1)S(1)}, bf16[4,2,128,128]{3,2,1,0:T(8,128)(2,1)S(1)}, u32[]{:S(2)}, u32[]{:S(2)}) %collective-permute-start.3) | collective-permute-done | bytes 262176 | tf_op jit(solution)/shard_map/ppermute | solution.py:178
  41.7 2.5 %collective-permute-done.4.refs_2_ = bf16[4,2,128,128]{3,2,1,0:T(8,128)(2,1)S(1)} collective-permute-done((bf16[4,2,128,128]{3,2,1,0:T(8,128)(2,1)S(1)}, bf16[4,2,128,128]{3,2,1,0:T(8,128)(2,1)S(1)}, u32[]{:S(2)}, u32[]{:S(2)}) %collective-permute-start.4) | collective-permute-done | bytes 262176 | tf_op jit(solution)/shard_map/ppermute | solution.py:178
  44.1 2.8 %collective-permute-done.5.refs_3_ = bf16[4,2,128,128]{3,2,1,0:T(8,128)(2,1)S(1)} collective-permute-done((bf16[4,2,128,128]{3,2,1,0:T(8,128)(2,1)S(1)}, bf16[4,2,128,128]{3,2,1,0:T(8,128)(2,1)S(1)}, u32[]{:S(2)}, u32[]{:S(2)}) %collective-permute-start.5) | collective-permute-done | bytes 262176 | tf_op jit(solution)/shard_map/ppermute | solution.py:178
  47.7 7.3 %shard_map.111 = (bf16[128,2048]{1,0:T(8,128)(2,1)}, bf16[128,1024]{1,0:T(8,128)(2,1)}, bf16[128,1024]{1,0:T(8,128)(2,1)}, bf16[4,2,128,128]{3,2,1,0:T(8,128)(2,...) custom-call(s32[4]{0:T(128)} %bitcast.104, ...), custom_call_target="tpu_custom_call" | custom-call | flops 1006632960 | bytes 3670016 | tf_op jit(solution)/shard_map/pallas_call | solution.py:136
  59.3 7.5 %shard_map.112 = (bf16[128,2048]{1,0:T(8,128)(2,1)}, bf16[128,1024]{1,0:T(8,128)(2,1)}, bf16[128,1024]{1,0:T(8,128)(2,1)}, bf16[4,2,128,128]{3,2,1,0:T(8,128)(2,...) custom-call(s32[4]{0:T(128)} %bitcast.105, ...), custom_call_target="tpu_custom_call" | custom-call | flops 1006632960 | bytes 3670016 | tf_op jit(solution)/shard_map/pallas_call | solution.py:136
  68.0 1.5 %collective-permute-start.14 = (bf16[4,2,128,128]{3,2,1,0:T(8,128)(2,1)}, bf16[4,2,128,128]{3,2,1,0:T(8,128)(2,1)S(1)}, u32[]{:S(2)}, u32[]{:S(2)}) collective-permute-start(bf16[4,2,128,128]{3,2,1,0:T(8,128)(2,1)} %get-tuple-element.26), channel_id=1, source_target_pairs={{0,16},{8,24},{16,0},{24,8},{1,17},{9,25},{17,1},{25,9},{2,18},{10... | collective-permute-start | bytes 786440 | tf_op jit(solution)/shard_map/ppermute | solution.py:199
  69.5 1.9 %select_bitcast_fusion = bf16[1,1,128,2048]{3,2,1,0:T(8,128)(2,1)} fusion(bf16[128,2048]{1,0:T(8,128)(2,1)S(1)} %copy-done.1, bf16[128,2048]{1,0:T(8,128)(2,1)} %get-tuple-element.19, pred[2048]{0:T(1024)(128)(4,1)S(1)} %fusion.1), kind=kLoop, calls=%fused_computation.4 | loop fusion | flops 262144 | bytes 1574912 | tf_op jit(solution)/shard_map/broadcast_in_dim | solution.py:256
  72.5 2.0 %collective-permute-start.22 = (bf16[2,128,128]{2,1,0:T(8,128)(2,1)S(1)}, bf16[2,128,128]{2,1,0:T(8,128)(2,1)S(1)}, u32[]{:S(2)}, u32[]{:S(2)}) collective-permute-start(bf16[2,128,128]{2,1,0:T(8,128)(2,1)S(1)} %get-tuple-element.39), channel_id=1, source_target_pairs={{0,2},{2,4},{4,6},{6,0},{1,3},{3,5},{5,7},{7,1},{8,10},{10,12},{12... | collective-permute-start | bytes 196616 | tf_op jit(solution)/shard_map/ppermute | solution.py:155
  75.3 1.8 %collective-permute-start.23 = (bf16[2,128,128]{2,1,0:T(8,128)(2,1)S(1)}, bf16[2,128,128]{2,1,0:T(8,128)(2,1)S(1)}, u32[]{:S(2)}, u32[]{:S(2)}) collective-permute-start(bf16[2,128,128]{2,1,0:T(8,128)(2,1)S(1)} %get-tuple-element.38), channel_id=1, source_target_pairs={{0,4},{2,6},{4,0},{6,2},{1,5},{3,7},{5,1},{7,3},{8,12},{10,14},{12... | collective-permute-start | bytes 196616 | tf_op jit(solution)/shard_map/ppermute | solution.py:155
  78.6 2.1 %collective-permute-start.24 = (bf16[2,128,128]{2,1,0:T(8,128)(2,1)S(1)}, bf16[2,128,128]{2,1,0:T(8,128)(2,1)S(1)}, u32[]{:S(2)}, u32[]{:S(2)}) collective-permute-start(bf16[2,128,128]{2,1,0:T(8,128)(2,1)S(1)} %get-tuple-element.37), channel_id=1, source_target_pairs={{0,6},{2,0},{4,2},{6,4},{1,7},{3,1},{5,3},{7,5},{8,14},{10,8},{12,... | collective-permute-start | bytes 196616 | tf_op jit(solution)/shard_map/ppermute | solution.py:155
  80.7 2.0 %collective-permute-done.23 = bf16[2,128,128]{2,1,0:T(8,128)(2,1)S(1)} collective-permute-done((bf16[2,128,128]{2,1,0:T(8,128)(2,1)S(1)}, bf16[2,128,128]{2,1,0:T(8,128)(2,1)S(1)}, u32[]{:S(2)}, u32[]{:S(2)}) %collective-permute-start.23) | collective-permute-done | bytes 65568 | tf_op jit(solution)/shard_map/ppermute | solution.py:155
  83.9 2.7 %collective-permute-start.17 = (bf16[2,128,128]{2,1,0:T(8,128)(2,1)S(1)}, bf16[2,128,128]{2,1,0:T(8,128)(2,1)S(1)}, u32[]{:S(2)}, u32[]{:S(2)}) collective-permute-start(bf16[2,128,128]{2,1,0:T(8,128)(2,1)S(1)} %get-tuple-element.34), channel_id=1, source_target_pairs={{0,4},{2,6},{4,0},{6,2},{1,5},{3,7},{5,1},{7,3},{8,12},{10,14},{12... | collective-permute-start | bytes 196616 | tf_op jit(solution)/shard_map/ppermute | solution.py:155
  87.4 1.6 %collective-permute-done.16 = bf16[2,128,128]{2,1,0:T(8,128)(2,1)S(1)} collective-permute-done((bf16[2,128,128]{2,1,0:T(8,128)(2,1)S(1)}, bf16[2,128,128]{2,1,0:T(8,128)(2,1)S(1)}, u32[]{:S(2)}, u32[]{:S(2)}) %collective-permute-start.16) | collective-permute-done | bytes 65568 | tf_op jit(solution)/shard_map/ppermute | solution.py:155
  (103 shorter events, 22.9 us)
Async XLA Ops:
  10.5 17.8 %collective-permute-start = (bf16[2,128,128]{2,1,0:T(8,128)(2,1)S(1)}, bf16[2,128,128]{2,1,0:T(8,128)(2,1)S(1)}, u32[]{:S(2)}, u32[]{:S(2)}) collective-permute-start(bf16[2,128,128]{2,1,0:T(8,128)(2,1)S(1)} %get-tuple-element.49), channel_id=1, source_target_pairs={{0,2},{2,4},{4,6},{6,0},{1,3},{3,5},{5,7},{7,1},{8,10},{10,12},{12... | collective-permute-start | bytes 196616 | tf_op jit(solution)/shard_map/ppermute | solution.py:155
  13.6 14.7 %collective-permute-start.1 = (bf16[2,128,128]{2,1,0:T(8,128)(2,1)S(1)}, bf16[2,128,128]{2,1,0:T(8,128)(2,1)S(1)}, u32[]{:S(2)}, u32[]{:S(2)}) collective-permute-start(bf16[2,128,128]{2,1,0:T(8,128)(2,1)S(1)} %get-tuple-element.48), channel_id=1, source_target_pairs={{0,4},{2,6},{4,0},{6,2},{1,5},{3,7},{5,1},{7,3},{8,12},{10,14},{12... | collective-permute-start | bytes 196616 | tf_op jit(solution)/shard_map/ppermute | solution.py:155
  16.2 6.6 %collective-permute-start.6 = (bf16[2,128,128]{2,1,0:T(8,128)(2,1)S(1)}, bf16[2,128,128]{2,1,0:T(8,128)(2,1)S(1)}, u32[]{:S(2)}, u32[]{:S(2)}) collective-permute-start(bf16[2,128,128]{2,1,0:T(8,128)(2,1)S(1)} %get-tuple-element.45), channel_id=1, source_target_pairs={{0,2},{2,4},{4,6},{6,0},{1,3},{3,5},{5,7},{7,1},{8,10},{10,12},{12... | collective-permute-start | bytes 196616 | tf_op jit(solution)/shard_map/ppermute | solution.py:155
  16.3 8.6 %collective-permute-start.7 = (bf16[2,128,128]{2,1,0:T(8,128)(2,1)S(1)}, bf16[2,128,128]{2,1,0:T(8,128)(2,1)S(1)}, u32[]{:S(2)}, u32[]{:S(2)}) collective-permute-start(bf16[2,128,128]{2,1,0:T(8,128)(2,1)S(1)} %get-tuple-element.44), channel_id=1, source_target_pairs={{0,4},{2,6},{4,0},{6,2},{1,5},{3,7},{5,1},{7,3},{8,12},{10,14},{12... | collective-permute-start | bytes 196616 | tf_op jit(solution)/shard_map/ppermute | solution.py:155
  18.2 6.9 %collective-permute-start.8 = (bf16[2,128,128]{2,1,0:T(8,128)(2,1)S(1)}, bf16[2,128,128]{2,1,0:T(8,128)(2,1)S(1)}, u32[]{:S(2)}, u32[]{:S(2)}) collective-permute-start(bf16[2,128,128]{2,1,0:T(8,128)(2,1)S(1)} %get-tuple-element.43), channel_id=1, source_target_pairs={{0,6},{2,0},{4,2},{6,4},{1,7},{3,1},{5,3},{7,5},{8,14},{10,8},{12,... | collective-permute-start | bytes 196616 | tf_op jit(solution)/shard_map/ppermute | solution.py:155
  22.8 5.5 %collective-permute-start.2 = (bf16[2,128,128]{2,1,0:T(8,128)(2,1)S(1)}, bf16[2,128,128]{2,1,0:T(8,128)(2,1)S(1)}, u32[]{:S(2)}, u32[]{:S(2)}) collective-permute-start(bf16[2,128,128]{2,1,0:T(8,128)(2,1)S(1)} %get-tuple-element.47), channel_id=1, source_target_pairs={{0,6},{2,0},{4,2},{6,4},{1,7},{3,1},{5,3},{7,5},{8,14},{10,8},{12,... | collective-permute-start | bytes 196616 | tf_op jit(solution)/shard_map/ppermute | solution.py:155
  25.1 9.3 %collective-permute-start.10 = (bf16[4,2,128,128]{3,2,1,0:T(8,128)(2,1)S(1)}, bf16[4,2,128,128]{3,2,1,0:T(8,128)(2,1)S(1)}, u32[]{:S(2)}, u32[]{:S(2)}) collective-permute-start(bf16[4,2,128,128]{3,2,1,0:T(8,128)(2,1)S(1)} %pad_maximum_fusion.2.refs_0_), channel_id=1, source_target_pairs={{0,16},{8,24},{16,0},{24,8},{1,17},{9,25},{17,1},{25,9},{2,18},{10... | collective-permute-start | bytes 786440 | tf_op jit(solution)/shard_map/ppermute | solution.py:182
  26.8 9.3 %collective-permute-start.9 = (bf16[4,2,128,128]{3,2,1,0:T(8,128)(2,1)S(1)}, bf16[4,2,128,128]{3,2,1,0:T(8,128)(2,1)S(1)}, u32[]{:S(2)}, u32[]{:S(2)}) collective-permute-start(bf16[4,2,128,128]{3,2,1,0:T(8,128)(2,1)S(1)} %pad_maximum_fusion.2.refs_0_), channel_id=1, source_target_pairs={{0,8},{8,0},{16,24},{24,16},{1,9},{9,1},{17,25},{25,17},{2,10},{10... | collective-permute-start | bytes 786440 | tf_op jit(solution)/shard_map/ppermute | solution.py:181
  28.4 13.3 %collective-permute-start.3 = (bf16[4,2,128,128]{3,2,1,0:T(8,128)(2,1)S(1)}, bf16[4,2,128,128]{3,2,1,0:T(8,128)(2,1)S(1)}, u32[]{:S(2)}, u32[]{:S(2)}) collective-permute-start(bf16[4,2,128,128]{3,2,1,0:T(8,128)(2,1)S(1)} %pad_maximum_fusion.1.refs_0_), channel_id=1, source_target_pairs={{0,8},{8,0},{16,24},{24,16},{1,9},{9,1},{17,25},{25,17},{2,10},{10... | collective-permute-start | bytes 786440 | tf_op jit(solution)/shard_map/ppermute | solution.py:178
  29.2 14.9 %collective-permute-start.4 = (bf16[4,2,128,128]{3,2,1,0:T(8,128)(2,1)S(1)}, bf16[4,2,128,128]{3,2,1,0:T(8,128)(2,1)S(1)}, u32[]{:S(2)}, u32[]{:S(2)}) collective-permute-start(bf16[4,2,128,128]{3,2,1,0:T(8,128)(2,1)S(1)} %pad_maximum_fusion.1.refs_0_), channel_id=1, source_target_pairs={{0,16},{8,24},{16,0},{24,8},{1,17},{9,25},{17,1},{25,9},{2,18},{10... | collective-permute-start | bytes 786440 | tf_op jit(solution)/shard_map/ppermute | solution.py:178
  30.7 16.2 %collective-permute-start.5 = (bf16[4,2,128,128]{3,2,1,0:T(8,128)(2,1)S(1)}, bf16[4,2,128,128]{3,2,1,0:T(8,128)(2,1)S(1)}, u32[]{:S(2)}, u32[]{:S(2)}) collective-permute-start(bf16[4,2,128,128]{3,2,1,0:T(8,128)(2,1)S(1)} %pad_maximum_fusion.1.refs_0_), channel_id=1, source_target_pairs={{0,24},{8,16},{16,8},{24,0},{1,25},{9,17},{17,9},{25,1},{2,26},{10... | collective-permute-start | bytes 786440 | tf_op jit(solution)/shard_map/ppermute | solution.py:178
  34.4 24.1 %collective-permute-start.11 = (bf16[4,2,64,128]{3,2,1,0:T(8,128)(2,1)S(1)}, bf16[4,2,64,128]{3,2,1,0:T(8,128)(2,1)S(1)}, u32[]{:S(2)}, u32[]{:S(2)}) collective-permute-start(bf16[4,2,64,128]{3,2,1,0:T(8,128)(2,1)S(1)} %slice.72), channel_id=1, source_target_pairs={{0,8},{8,0},{16,24},{24,16},{1,9},{9,1},{17,25},{25,17},{2,10},{10... | collective-permute-start | bytes 393224 | tf_op jit(solution)/shard_map/ppermute | solution.py:184
  36.1 22.4 %collective-permute-start.12 = (bf16[4,2,64,128]{3,2,1,0:T(8,128)(2,1)S(1)}, bf16[4,2,64,128]{3,2,1,0:T(8,128)(2,1)S(1)}, u32[]{:S(2)}, u32[]{:S(2)}) collective-permute-start(bf16[4,2,64,128]{3,2,1,0:T(8,128)(2,1)S(1)} %slice.73), channel_id=1, source_target_pairs={{0,16},{8,24},{16,0},{24,8},{1,17},{9,25},{17,1},{25,9},{2,18},{10... | collective-permute-start | bytes 393224 | tf_op jit(solution)/shard_map/ppermute | solution.py:185
  55.0 16.5 %collective-permute-start.19 = (bf16[4,2,128,128]{3,2,1,0:T(8,128)(2,1)}, bf16[4,2,128,128]{3,2,1,0:T(8,128)(2,1)S(1)}, u32[]{:S(2)}, u32[]{:S(2)}) collective-permute-start(bf16[4,2,128,128]{3,2,1,0:T(8,128)(2,1)} %get-tuple-element.29), channel_id=1, source_target_pairs={{0,8},{8,0},{16,24},{24,16},{1,9},{9,1},{17,25},{25,17},{2,10},{10... | collective-permute-start | bytes 786440 | tf_op jit(solution)/shard_map/ppermute | solution.py:199
  56.3 16.0 %collective-permute-start.20 = (bf16[4,2,128,128]{3,2,1,0:T(8,128)(2,1)}, bf16[4,2,128,128]{3,2,1,0:T(8,128)(2,1)S(1)}, u32[]{:S(2)}, u32[]{:S(2)}) collective-permute-start(bf16[4,2,128,128]{3,2,1,0:T(8,128)(2,1)} %get-tuple-element.30), channel_id=1, source_target_pairs={{0,16},{8,24},{16,0},{24,8},{1,17},{9,25},{17,1},{25,9},{2,18},{10... | collective-permute-start | bytes 786440 | tf_op jit(solution)/shard_map/ppermute | solution.py:199
  57.8 14.5 %collective-permute-start.21 = (bf16[4,2,128,128]{3,2,1,0:T(8,128)(2,1)}, bf16[4,2,128,128]{3,2,1,0:T(8,128)(2,1)S(1)}, u32[]{:S(2)}, u32[]{:S(2)}) collective-permute-start(bf16[4,2,128,128]{3,2,1,0:T(8,128)(2,1)} %get-tuple-element.31), channel_id=1, source_target_pairs={{0,24},{8,16},{16,8},{24,0},{1,25},{9,17},{17,9},{25,1},{2,26},{10... | collective-permute-start | bytes 786440 | tf_op jit(solution)/shard_map/ppermute | solution.py:199
  66.7 15.9 %collective-permute-start.13 = (bf16[4,2,128,128]{3,2,1,0:T(8,128)(2,1)}, bf16[4,2,128,128]{3,2,1,0:T(8,128)(2,1)S(1)}, u32[]{:S(2)}, u32[]{:S(2)}) collective-permute-start(bf16[4,2,128,128]{3,2,1,0:T(8,128)(2,1)} %get-tuple-element.25), channel_id=1, source_target_pairs={{0,8},{8,0},{16,24},{24,16},{1,9},{9,1},{17,25},{25,17},{2,10},{10... | collective-permute-start | bytes 786440 | tf_op jit(solution)/shard_map/ppermute | solution.py:199
  68.0 14.7 %collective-permute-start.14 = (bf16[4,2,128,128]{3,2,1,0:T(8,128)(2,1)}, bf16[4,2,128,128]{3,2,1,0:T(8,128)(2,1)S(1)}, u32[]{:S(2)}, u32[]{:S(2)}) collective-permute-start(bf16[4,2,128,128]{3,2,1,0:T(8,128)(2,1)} %get-tuple-element.26), channel_id=1, source_target_pairs={{0,16},{8,24},{16,0},{24,8},{1,17},{9,25},{17,1},{25,9},{2,18},{10... | collective-permute-start | bytes 786440 | tf_op jit(solution)/shard_map/ppermute | solution.py:199
  71.5 11.2 %collective-permute-start.15 = (bf16[4,2,128,128]{3,2,1,0:T(8,128)(2,1)S(1)}, bf16[4,2,128,128]{3,2,1,0:T(8,128)(2,1)S(1)}, u32[]{:S(2)}, u32[]{:S(2)}) collective-permute-start(bf16[4,2,128,128]{3,2,1,0:T(8,128)(2,1)S(1)} %copy-done.12), channel_id=1, source_target_pairs={{0,24},{8,16},{16,8},{24,0},{1,25},{9,17},{17,9},{25,1},{2,26},{10... | collective-permute-start | bytes 786440 | tf_op jit(solution)/shard_map/ppermute | solution.py:199
  72.5 6.1 %collective-permute-start.22 = (bf16[2,128,128]{2,1,0:T(8,128)(2,1)S(1)}, bf16[2,128,128]{2,1,0:T(8,128)(2,1)S(1)}, u32[]{:S(2)}, u32[]{:S(2)}) collective-permute-start(bf16[2,128,128]{2,1,0:T(8,128)(2,1)S(1)} %get-tuple-element.39), channel_id=1, source_target_pairs={{0,2},{2,4},{4,6},{6,0},{1,3},{3,5},{5,7},{7,1},{8,10},{10,12},{12... | collective-permute-start | bytes 196616 | tf_op jit(solution)/shard_map/ppermute | solution.py:155
  75.3 7.3 %collective-permute-start.23 = (bf16[2,128,128]{2,1,0:T(8,128)(2,1)S(1)}, bf16[2,128,128]{2,1,0:T(8,128)(2,1)S(1)}, u32[]{:S(2)}, u32[]{:S(2)}) collective-permute-start(bf16[2,128,128]{2,1,0:T(8,128)(2,1)S(1)} %get-tuple-element.38), channel_id=1, source_target_pairs={{0,4},{2,6},{4,0},{6,2},{1,5},{3,7},{5,1},{7,3},{8,12},{10,14},{12... | collective-permute-start | bytes 196616 | tf_op jit(solution)/shard_map/ppermute | solution.py:155
  78.6 4.9 %collective-permute-start.24 = (bf16[2,128,128]{2,1,0:T(8,128)(2,1)S(1)}, bf16[2,128,128]{2,1,0:T(8,128)(2,1)S(1)}, u32[]{:S(2)}, u32[]{:S(2)}) collective-permute-start(bf16[2,128,128]{2,1,0:T(8,128)(2,1)S(1)} %get-tuple-element.37), channel_id=1, source_target_pairs={{0,6},{2,0},{4,2},{6,4},{1,7},{3,1},{5,3},{7,5},{8,14},{10,8},{12,... | collective-permute-start | bytes 196616 | tf_op jit(solution)/shard_map/ppermute | solution.py:155
  82.9 6.2 %collective-permute-start.16 = (bf16[2,128,128]{2,1,0:T(8,128)(2,1)S(1)}, bf16[2,128,128]{2,1,0:T(8,128)(2,1)S(1)}, u32[]{:S(2)}, u32[]{:S(2)}) collective-permute-start(bf16[2,128,128]{2,1,0:T(8,128)(2,1)S(1)} %get-tuple-element.35), channel_id=1, source_target_pairs={{0,2},{2,4},{4,6},{6,0},{1,3},{3,5},{5,7},{7,1},{8,10},{10,12},{12... | collective-permute-start | bytes 196616 | tf_op jit(solution)/shard_map/ppermute | solution.py:155
  83.9 6.6 %collective-permute-start.17 = (bf16[2,128,128]{2,1,0:T(8,128)(2,1)S(1)}, bf16[2,128,128]{2,1,0:T(8,128)(2,1)S(1)}, u32[]{:S(2)}, u32[]{:S(2)}) collective-permute-start(bf16[2,128,128]{2,1,0:T(8,128)(2,1)S(1)} %get-tuple-element.34), channel_id=1, source_target_pairs={{0,4},{2,6},{4,0},{6,2},{1,5},{3,7},{5,1},{7,3},{8,12},{10,14},{12... | collective-permute-start | bytes 196616 | tf_op jit(solution)/shard_map/ppermute | solution.py:155
  (19 other events, 75.9 us)
